TPU v7x, 32 devices: a whole 2x2x4 slice. The times are simulated.
32 devices in a mesh: groups: 2 (over x), wide: 16 (over z, y, core).
Axes of the slice: x: 2, y: 2, z: 4, core: 2. Of those that a mesh axis runs over, the one named last changes fastest.
Arguments:
- activity: bfloat16 [1024, 16, 512], P(('groups', 'wide')), parts along dimension 0, may hold values from -6 to 6
- grad_out: bfloat16 [1024, 16, 512], P('groups', 'wide'), parts along dimension 0, may hold values from -6 to 6
- spatial_weights: bfloat16 [512, 2048], replicated, may hold values from -8 to 8
- temporal_weights: bfloat16 [512, 2048], replicated, may hold values from -8 to 8
- spatial_gain: float32 [512], replicated, may hold values from 0.25 to 1.75
- temporal_gain: float32 [512], replicated, may hold values from 0.25 to 1.75
- adjacency: int32 [16, 16], replicated, may hold values from 0 to 1
- channel_count: int32 [8], P('groups'), parts along dimension 0, may hold values from 128 to 2048
- session_id: int32 [1024], P('groups'), parts along dimension 0, may hold values from 0 to 3, never falling along the last dimension, each value on 1 to 256 neighbouring positions
Outputs:
- layer_out: bfloat16 [1024, 16, 512], P('groups', 'wide'), parts along dimension 0
- grad_activity: bfloat16 [1024, 16, 512], P(('groups', 'wide')), parts along dimension 0
- spatial_grad: float32 [1024, 2048], P(('groups', 'wide')), parts along dimension 0
- temporal_grad: float32 [1024, 2048], P(('groups', 'wide')), parts along dimension 0
There are 2 independent parts, one for each index of `groups`. A program takes and returns all parts, laid end to end along the dimension named above; an argument that names none is the same for every part. Nothing has to cross between parts.
Inputs may be any that keep to these rules, and one draw needn't show every extreme that they name: `session_id`: session ids never fall along time; every session holds 1 to 256 bins, one exactly 256.
All inputs are finite; a program needn't handle non-finite values.
Results may differ from a plain program's by a relative error of at most 0.015.
Values may be sent and summed in bfloat16 or wider, within the bound.
No kernel may reach another device: no remote copies, remote signals or barrier semaphores. Data moves between devices by JAX's collectives and lax.ppermute only.
A program may use at most 192 MiB of HBM per device.

v0:
```python
import jax
import jax.numpy as jnp
from jax import lax
from jax.sharding import PartitionSpec as P

HEADS = 8


eps_norm = 1e-05
block_channels = 128


def norm_inverse(rows):
    values = rows.astype(jnp.float32)
    return lax.rsqrt(jnp.mean(values * values, axis=-1, keepdims=True) + eps_norm)


def norm_forward(rows, gain):
    inverse = norm_inverse(rows)
    return ((rows.astype(jnp.float32) * inverse * gain).astype(jnp.bfloat16), inverse)


def norm_backward(rows, gain, inverse, grad_normed):
    values = rows.astype(jnp.float32)
    scaled = grad_normed * gain
    inner = jnp.mean(values * scaled, axis=-1, keepdims=True)
    return inverse * scaled - values * inverse * inverse * inverse * inner


def normalized_affinity(asking_vectors, lookup_array, admissible_pairs, sharpness_divisor):
    unnormalized_affinities = (
        jnp.einsum(
            "...uo,...ao->...ua", asking_vectors, lookup_array, preferred_element_type=jnp.float32
        )
        * sharpness_divisor
    )
    unnormalized_affinities = jnp.where(admissible_pairs, unnormalized_affinities, -1e30)
    row_max = jnp.max(unnormalized_affinities, axis=-1, keepdims=True)
    expo = jnp.exp(unnormalized_affinities - row_max)
    return expo / jnp.sum(expo, axis=-1, keepdims=True)


def compute_affinity_outputs(
    asking_vectors, lookup_array, payload_array, admissible_pairs, sharpness_divisor
):
    truncated_outcome = normalized_affinity(
        asking_vectors, lookup_array, admissible_pairs, sharpness_divisor
    ).astype(jnp.bfloat16)
    return jnp.einsum(
        "...qk,...kd->...qd", truncated_outcome, payload_array, preferred_element_type=jnp.float32
    ).astype(jnp.bfloat16)


def compute_affinity_derivatives(
    asking_vectors,
    lookup_array,
    payload_array,
    admissible_pairs,
    sharpness_divisor,
    combined_output,
    blended_output_derivative,
):
    coefficient_array = normalized_affinity(
        asking_vectors, lookup_array, admissible_pairs, sharpness_divisor
    )
    truncated_outcome = coefficient_array.astype(jnp.bfloat16)
    grad_values = jnp.einsum(
        "...qk,...qd->...kd",
        truncated_outcome,
        blended_output_derivative,
        preferred_element_type=jnp.float32,
    )
    coefficient_derivative = jnp.einsum(
        "...uo,...ao->...ua",
        blended_output_derivative,
        payload_array,
        preferred_element_type=jnp.float32,
    )
    paired_inner_sums = jnp.sum(
        blended_output_derivative.astype(jnp.float32) * combined_output.astype(jnp.float32),
        axis=-1,
        keepdims=True,
    )
    affinity_derivative = (
        coefficient_array * (coefficient_derivative - paired_inner_sums) * sharpness_divisor
    ).astype(jnp.bfloat16)
    grad_queries = jnp.einsum(
        "...qk,...kd->...qd", affinity_derivative, lookup_array, preferred_element_type=jnp.float32
    )
    grad_keys = jnp.einsum(
        "...qk,...qd->...kd",
        affinity_derivative,
        asking_vectors,
        preferred_element_type=jnp.float32,
    )
    return (
        grad_queries.astype(jnp.bfloat16),
        grad_keys.astype(jnp.bfloat16),
        grad_values.astype(jnp.bfloat16),
    )


def temporal_split(projected):
    pieces = projected.reshape(projected.shape[0], 3, HEADS, projected.shape[1] // (3 * HEADS))
    return [pieces[:, index].transpose(1, 0, 2) for index in range(3)]


def temporal_forward(projected, admissible_pairs):
    asking_vectors, lookup_array, payload_array = temporal_split(projected)
    sharpness_divisor = float(asking_vectors.shape[-1]) ** (-0.5)
    combined_output = compute_affinity_outputs(
        asking_vectors, lookup_array, payload_array, admissible_pairs[None], sharpness_divisor
    )
    return combined_output.transpose(1, 0, 2).reshape(projected.shape[0], -1)


def temporal_backward(projected, admissible_pairs, combined_output, blended_output_derivative):
    asking_vectors, lookup_array, payload_array = temporal_split(projected)
    sharpness_divisor = float(asking_vectors.shape[-1]) ** (-0.5)
    bins = projected.shape[0]
    subspace_outputs = combined_output.reshape(bins, HEADS, -1).transpose(1, 0, 2)
    subspace_derivative = blended_output_derivative.reshape(bins, HEADS, -1).transpose(1, 0, 2)
    derivative_collection = compute_affinity_derivatives(
        asking_vectors,
        lookup_array,
        payload_array,
        admissible_pairs[None],
        sharpness_divisor,
        subspace_outputs,
        subspace_derivative,
    )
    return jnp.stack(derivative_collection, axis=0).transpose(2, 0, 1, 3).reshape(bins, -1)


def spatial_split(projected):
    pieces = projected.reshape(
        projected.shape[0], projected.shape[1], 3, HEADS, projected.shape[2] // (3 * HEADS)
    )
    return [pieces[:, :, index].transpose(0, 2, 1, 3) for index in range(3)]


def spatial_forward(projected, admissible_pairs):
    asking_vectors, lookup_array, payload_array = spatial_split(projected)
    sharpness_divisor = float(asking_vectors.shape[-1]) ** (-0.5)
    combined_output = compute_affinity_outputs(
        asking_vectors, lookup_array, payload_array, admissible_pairs, sharpness_divisor
    )
    return combined_output.transpose(0, 2, 1, 3).reshape(projected.shape[0], projected.shape[1], -1)


def spatial_backward(projected, admissible_pairs, combined_output, blended_output_derivative):
    asking_vectors, lookup_array, payload_array = spatial_split(projected)
    sharpness_divisor = float(asking_vectors.shape[-1]) ** (-0.5)
    bins, blocks = (projected.shape[0], projected.shape[1])
    subspace_outputs = combined_output.reshape(bins, blocks, HEADS, -1).transpose(0, 2, 1, 3)
    subspace_derivative = blended_output_derivative.reshape(bins, blocks, HEADS, -1).transpose(
        0, 2, 1, 3
    )
    derivative_collection = compute_affinity_derivatives(
        asking_vectors,
        lookup_array,
        payload_array,
        admissible_pairs,
        sharpness_divisor,
        subspace_outputs,
        subspace_derivative,
    )
    return (
        jnp.stack(derivative_collection, axis=0).transpose(1, 3, 0, 2, 4).reshape(bins, blocks, -1)
    )


def spatial_allowed(sessions_here, channel_count, adjacency):
    block_count = adjacency.shape[0]
    block_ids = jnp.arange(block_count, dtype=jnp.int32)
    session_pick = (
        sessions_here[:, None] == jnp.arange(channel_count.shape[0], dtype=jnp.int32)[None, :]
    ).astype(jnp.int32)
    count_rows = jnp.sum(session_pick * channel_count[None, :], axis=1)
    live_block = block_ids[None, :] * block_channels < count_rows[:, None]
    linked = adjacency > 0
    itself = block_ids[:, None] == block_ids[None, :]
    admissible_pairs = linked[None, :, :] & live_block[:, None, :] | itself[None, :, :]
    return admissible_pairs[:, None, :, :]


def project(rows, coefficient_array):
    return jnp.einsum("tbd,de->tbe", rows, coefficient_array, preferred_element_type=jnp.float32)


def project_back(derivative_collection, coefficient_array):
    return jnp.einsum(
        "tbe,de->tbd", derivative_collection, coefficient_array, preferred_element_type=jnp.float32
    )


def weight_term(left, right):
    return jnp.einsum("tbd,tbe->de", left, right, preferred_element_type=jnp.float32)


def per_device(
    activity,
    grad_out,
    spatial_weights,
    temporal_weights,
    spatial_gain,
    temporal_gain,
    adjacency,
    channel_count,
    session_id,
):
    local_bins = activity.shape[0]
    model_width = activity.shape[2]
    first_bin = lax.axis_index("wide") * local_bins
    sessions_here = lax.dynamic_slice_in_dim(session_id, first_bin, local_bins)
    normed_one, inverse_one = norm_forward(activity, spatial_gain)
    spatial_proj = project(normed_one, spatial_weights[:, : 3 * model_width]).astype(jnp.bfloat16)
    allowed_space = spatial_allowed(sessions_here, channel_count, adjacency)
    spatial_context = spatial_forward(spatial_proj, allowed_space)
    middle = (
        activity.astype(jnp.float32)
        + project(spatial_context, spatial_weights[:, 3 * model_width :])
    ).astype(jnp.bfloat16)
    middle_block = lax.all_to_all(middle, "wide", split_axis=1, concat_axis=0, tiled=True)
    normed_two, inverse_two = norm_forward(middle_block, temporal_gain)
    temporal_proj = project(normed_two, temporal_weights[:, : 3 * model_width]).astype(jnp.bfloat16)
    allowed_time = session_id[:, None] == session_id[None, :]
    by_block = jnp.moveaxis(temporal_proj, 1, 0)
    temporal_context = jnp.moveaxis(
        lax.map(lambda block_rows: temporal_forward(block_rows, allowed_time), by_block), 0, 1
    )
    layer_out = (
        middle_block.astype(jnp.float32)
        + project(temporal_context, temporal_weights[:, 3 * model_width :])
    ).astype(jnp.bfloat16)
    grad_temporal_context = project_back(grad_out, temporal_weights[:, 3 * model_width :]).astype(
        jnp.bfloat16
    )
    stacked = (
        by_block,
        jnp.moveaxis(temporal_context, 1, 0),
        jnp.moveaxis(grad_temporal_context, 1, 0),
    )
    grad_temporal_proj = jnp.moveaxis(
        lax.map(
            lambda items: temporal_backward(items[0], allowed_time, items[1], items[2]), stacked
        ),
        0,
        1,
    )
    grad_normed_two = project_back(grad_temporal_proj, temporal_weights[:, : 3 * model_width])
    grad_middle = (
        grad_out.astype(jnp.float32)
        + norm_backward(middle_block, temporal_gain, inverse_two, grad_normed_two)
    ).astype(jnp.bfloat16)
    grad_middle_time = lax.all_to_all(grad_middle, "wide", split_axis=0, concat_axis=1, tiled=True)
    normed_cols = normed_two
    context_cols = temporal_context
    temporal_grad = lax.psum_scatter(
        jnp.concatenate(
            [weight_term(normed_cols, grad_temporal_proj), weight_term(context_cols, grad_out)],
            axis=1,
        ).astype(jnp.bfloat16),
        "wide",
        scatter_dimension=0,
        tiled=True,
    ).astype(jnp.float32)
    grad_spatial_context = project_back(
        grad_middle_time, spatial_weights[:, 3 * model_width :]
    ).astype(jnp.bfloat16)
    grad_spatial_proj = spatial_backward(
        spatial_proj, allowed_space, spatial_context, grad_spatial_context
    )
    grad_normed_one = project_back(grad_spatial_proj, spatial_weights[:, : 3 * model_width])
    grad_activity = (
        grad_middle_time.astype(jnp.float32)
        + norm_backward(activity, spatial_gain, inverse_one, grad_normed_one)
    ).astype(jnp.bfloat16)
    normed_cols = normed_one
    context_cols = spatial_context
    spatial_grad = lax.psum_scatter(
        jnp.concatenate(
            [
                weight_term(normed_cols, grad_spatial_proj),
                weight_term(context_cols, grad_middle_time),
            ],
            axis=1,
        ).astype(jnp.bfloat16),
        "wide",
        scatter_dimension=0,
        tiled=True,
    ).astype(jnp.float32)
    return (layer_out, grad_activity, spatial_grad, temporal_grad)


def solution(mesh):
    placed = (
        P(("groups", "wide"), None, None),
        P("groups", "wide", None),
        P(),
        P(),
        P(),
        P(),
        P(),
        P("groups"),
        P("groups"),
    )
    return jax.shard_map(
        per_device,
        mesh=mesh,
        in_specs=placed,
        out_specs=(
            P("groups", "wide", None),
            P(("groups", "wide"), None, None),
            P(("groups", "wide"), None),
            P(("groups", "wide"), None),
        ),
        check_vma=False,
    )
```

profile of v0, /device:TPU:0, one launch (start us, length us, event | category | flops | bytes accessed | tf_op | source)
XLA Modules:
  0.0 230.5 jit_solution(11808287719107655246)
XLA Ops:
  7.2 1.2 fusion.41
  8.4 3.8 %convolution_convert_fusion.2 = bf16[32,16,1536]{2,1,0:T(8,128)(2,1)} fusion(bf16[512,2048]{1,0:T(8,128)(2,1)} %param.11, bf16[32,16,512]{2,1,0:T(8,128)(2,1)} %param.9, f32[512]{0:T(512)} %param.13, f32[32,16]{1,0:T(8,128)S(1)} %add_rsqrt_fusion), kind=kOutput, calls=%fused_computation.15 | convolution fusion | flops 807141376 | bytes 3674112 | tf_op jit(solution)/shard_map/tbd,de->tbe/dot_general | solution.py:188
  12.2 4.0 %reshape.297 = bf16[32,16,3,8,64]{4,3,2,1,0:T(8,128)(2,1)S(1)} reshape(bf16[32,16,1536]{2,1,0:T(8,128)(2,1)} %convolution_convert_fusion.2) | data formatting | bytes 3145728 | tf_op jit(solution)/shard_map/reshape | solution.py:136
  16.2 2.1 fusion.82
  18.9 4.3 %fusion.83 = (f32[32,8,16]{2,1,0:T(8,128)S(1)}, f32[32,8,16,16]{2,3,1,0:T(8,128)}) fusion(pred[32,16,16]{1,2,0:T(8,128)(4,1)S(1)} %and_or_fusion, bf16[32,16,1,8,64]{4,3,2,1,0:T(8,128)(2,1)} %get-tuple-element.29, bf16[32,16,1,8,64]{4,3,2,1,0:T(8,128)(2,1)} %get-tuple-element.28), kind=kOutput, calls=%fused_computation.131 | convolution fusion | flops 8650767 | bytes 1335296 | tf_op jit(solution)/shard_map/sub | solution.py:39
  23.1 2.2 convolution_convert_fusion.6
  25.3 1.0 copy-done.7
  27.2 1.7 fusion.26
  28.9 1.1 copy.98
  30.0 7.4 %all-to-all-start = ((bf16[32,16,512]{2,0,1:T(8,128)(2,1)}), bf16[32,16,512]{2,0,1:T(8,128)(2,1)S(1)}, u32[]{:S(2)}, u32[]{:S(2)}) async-start(bf16[32,16,512]{2,0,1:T(8,128)(2,1)} %copy.98), calls=%async_computation | async-start | bytes 1048576 | tf_op jit(solution)/shard_map/all_to_all | solution.py:224
  37.4 1.0 copy.104
  38.6 2.3 %convolution_convert_fusion.13 = bf16[512,512]{0,1:T(8,128)(2,1)} fusion(bf16[512,1,512]{2,0,1:T(8,128)(2,1)S(1)} %copy-done.11, bf16[512,2048]{1,0:T(8,128)(2,1)} %param.12), kind=kOutput, calls=%fused_computation.54 | convolution fusion | flops 268697600 | bytes 1572864 | tf_op jit(solution)/shard_map/tbe,de->tbd/dot_general | solution.py:192
  40.9 10.9 %all-to-all-done = bf16[32,16,512]{2,0,1:T(8,128)(2,1)S(1)} async-done(((bf16[32,16,512]{2,0,1:T(8,128)(2,1)}), bf16[32,16,512]{2,0,1:T(8,128)(2,1)S(1)}, u32[]{:S(2)}, u32[]{:S(2)}) %all-to-all-start) | async-done | bytes 524320 | tf_op jit(solution)/shard_map/all_to_all | solution.py:224
  53.3 3.7 %convolution_convert_fusion.1 = bf16[512,1536]{1,0:T(8,128)(2,1)} fusion(bf16[512,2048]{1,0:T(8,128)(2,1)} %param.12, f32[512,512]{0,1:T(8,128)S(1)} %copy.101, f32[512]{0:T(512)S(1)} %copy-done.26, f32[512]{0:T(512)S(1)} %rsqrt.21), kind=kOutput, calls=%fused_computation.14 | convolution fusion | flops 806879232 | bytes 4198400 | tf_op jit(solution)/shard_map/tbd,de->tbe/dot_general | solution.py:188
  57.0 1.7 copy.102
  58.7 5.4 %fusion.84 = (f32[8,512]{1,0:T(8,128)S(1)}, f32[8,512,512]{1,2,0:T(8,128)}) fusion(pred[512,512]{0,1:T(8,128)(4,1)S(1)} %broadcast_compare_fusion, bf16[512,3,8,64]{0,3,2,1:T(8,128)(2,1)S(1)} %bitcast.171), kind=kOutput, calls=%fused_computation.132 | convolution fusion | flops 276824576 | bytes 9715712 | tf_op jit(solution)/shard_map/while/body/eval_jaxpr/sub | solution.py:39
  64.1 4.7 %fusion.6 = bf16[8,512,512]{1,2,0:T(8,128)(2,1)S(1)} fusion(f32[8,512,512]{1,2,0:T(8,128)} %get-tuple-element.40, f32[8,512]{1,0:T(8,128)S(1)} %get-tuple-element.33), kind=kLoop, calls=%fused_computation.10 | loop fusion | flops 4194304 | bytes 12599296 | tf_op jit(solution)/shard_map/while/body/eval_jaxpr/convert_element_type | solution.py:48
  69.6 1.4 fusion.33
  71.0 1.4 copy-done.2
  72.3 1.8 multiply_convert_fusion
  74.1 1.4 fusion.32
  76.5 1.2 copy-done.10
  77.8 1.0 copy-done.23
  78.8 1.0 multiply_reduce_fusion.1
  79.8 1.1 fusion.45
  81.5 2.1 reduce.6
  83.8 1.2 reshape.314
  85.0 4.1 %all-to-all-start.1 = ((bf16[16,2,8192]{2,1,0:T(2,128)(2,1)}), bf16[16,2,8192]{2,1,0:T(2,128)(2,1)S(1)}, u32[]{:S(2)}, u32[]{:S(2)}) async-start(bf16[16,2,8192]{2,1,0:T(2,128)(2,1)} %reshape.314), calls=%async_computation.1 | async-start | bytes 1048576 | tf_op jit(solution)/shard_map/all_to_all | solution.py:256
  89.9 2.6 %convolution_convert_fusion = bf16[512,1536]{1,0:T(8,128)(2,1)S(1)} fusion(bf16[512,1536]{0,1:T(8,128)(2,1)} %bitcast.182, f32[512,1,1,1,1,1,512]{6,0,5,4,3,2,1:T(8,128)S(1)} %bitcast.169, f32[512]{0:T(512)S(1)} %copy-done.26, f32[512]{0:T(512)S(1)} %rsqrt.21), kind=kOutput, calls=%fused_computation.13 | convolution fusion | flops 806879232 | bytes 4198400 | tf_op jit(solution)/shard_map/tbd,tbe->de/dot_general | solution.py:198
  92.5 1.6 pad_maximum_fusion.1
  94.1 9.4 %all-to-all-done.1 = bf16[16,2,8192]{2,1,0:T(2,128)(2,1)S(1)} async-done(((bf16[16,2,8192]{2,1,0:T(2,128)(2,1)}), bf16[16,2,8192]{2,1,0:T(2,128)(2,1)S(1)}, u32[]{:S(2)}, u32[]{:S(2)}) %all-to-all-start.1) | async-done | bytes 524320 | tf_op jit(solution)/shard_map/all_to_all | solution.py:256
  104.1 0.9 copy.129
  105.0 2.6 %convolution_convert_fusion.10 = bf16[32,16,512]{2,1,0:T(8,128)(2,1)} fusion(bf16[512,2048]{1,0:T(8,128)(2,1)} %param.11, bf16[16,32,1,512]{3,1,0,2:T(8,128)(2,1)} %bitcast.56), kind=kOutput, calls=%fused_computation.51 | convolution fusion | flops 268697600 | bytes 1572864 | tf_op jit(solution)/shard_map/tbe,de->tbd/dot_general | solution.py:192
  107.6 1.7 reshape.304
  110.0 1.0 copy-done.29
  115.7 0.8 copy.115
  116.5 3.0 %reshape.305 = bf16[32,16,1536]{2,1,0:T(8,128)(2,1)} reshape(bf16[32,16,3,8,64]{4,3,2,1,0:T(8,128)(2,1)S(1)} %copy.115) | data formatting | bytes 3145728 | tf_op jit(solution)/shard_map/reshape | solution.py:169
  119.5 1.9 fusion.28
  121.5 1.1 fusion.7
  122.6 1.6 pad_maximum_fusion
  124.2 1.2 copy-done.1
  125.5 2.4 %fusion.31 = bf16[512,1,512]{2,0,1:T(8,128)(2,1)} fusion(f32[512,512]{1,0:T(8,128)S(1)} %bitcast.170, bf16[512,512]{0,1:T(8,128)(2,1)S(1)} %bitcast.177, bf16[512,2048]{1,0:T(8,128)(2,1)} %param.12), kind=kOutput, calls=%fused_computation.60 | convolution fusion | flops 268959744 | bytes 2621440 | tf_op jit(solution)/shard_map/tbd,de->tbe/dot_general | solution.py:188
  127.9 2.5 %fusion.42 = (f32[32,16]{1,0:T(8,128)S(1)}, f32[32,16,512]{2,1,0:T(8,128)S(1)}) fusion(bf16[32,16,512]{2,1,0:T(8,128)(2,1)S(1)} %copy-done.14, f32[512]{0:T(512)S(1)} %copy-done.27, bf16[32,16,1536]{2,1,0:T(8,128)(2,1)S(1)} %copy-done.19, bf16[512,2048]{1,0:T(8,128)(2,1)} %param.11), kind=kOutput, calls=%fused_computation.71 | convolution fusion | flops 806354432 | bytes 4722688 | tf_op jit(solution)/shard_map/tbe,de->tbd/dot_general | solution.py:192
  130.4 2.3 %fusion.40 = bf16[32,16,512]{2,1,0:T(8,128)(2,1)} fusion(bf16[32,16,512]{2,1,0:T(8,128)(2,1)S(1)} %copy-done.14, f32[32,16,512]{2,1,0:T(8,128)S(1)} %get-tuple-element.46, f32[32,16]{1,0:T(8,128)S(1)} %broadcast_multiply_fusion, f32[32,16]{1,0:T(8,128)S(1)} %add_rsqrt_fusion, bf16[16,32,1,512]{3,1,0,2:T(8,128)(2,1)} %bitcast.56), kind=kLoop, calls=%fused_computation.69 | loop fusion | flops 2621440 | bytes 2625536 | tf_op jit(solution)/shard_map/convert_element_type | solution.py:278
  132.8 24.4 %reduce-scatter.5.cloned.1.call-done = bf16[32,2048]{1,0:T(8,128)(2,1)} async-done(((bf16[512,2048]{1,0:T(8,128)(2,1)}), bf16[32,2048]{1,0:T(8,128)(2,1)}) %reduce-scatter.5.cloned.1.call-update) | async-done | bytes 131088 | tf_op jit(solution)/shard_map/reduce_scatter | solution.py:259
  157.2 1.6 convert_element_type.231
  158.8 63.2 %reduce-scatter.3.cloned.1.call-done = bf16[32,2048]{1,0:T(8,128)(2,1)} async-done(((bf16[512,2048]{1,0:T(8,128)(2,1)}), bf16[32,2048]{1,0:T(8,128)(2,1)}) %reduce-scatter.3.cloned.1.call-update) | async-done | bytes 131088 | tf_op jit(solution)/shard_map/reduce_scatter | solution.py:281
  222.0 1.6 convert_element_type.226
  (92 shorter events, 12.3 us)
Async XLA Ops:
  16.2 2.2 copy-start.25
  16.2 2.2 copy-start.24
  16.2 2.3 %copy-start.28 = (s32[4]{0:T(128)S(1)}, s32[4]{0:T(128)}, u32[]{:S(2)}) copy-start(s32[4]{0:T(128)} %param.16) | copy-start | bytes 52
  18.8 4.3 %copy-start.20 = (bf16[32,16,1,8,64]{4,3,2,1,0:T(8,128)(2,1)S(1)}, bf16[32,16,1,8,64]{4,3,2,1,0:T(8,128)(2,1)}, u32[]{:S(2)}) copy-start(bf16[32,16,1,8,64]{4,3,2,1,0:T(8,128)(2,1)} %get-tuple-element.30) | copy-start | bytes 1572868
  25.3 1.0 copy-start.7
  25.3 1.9 copy-start.13
  27.2 2.8 %copy-start.22 = (bf16[32,16,512]{2,1,0:T(8,128)(2,1)}, bf16[32,16,512]{2,1,0:T(8,128)(2,1)S(1)}, u32[]{:S(2)}) copy-start(bf16[32,16,512]{2,1,0:T(8,128)(2,1)S(1)} %reshape.298) | copy-start | bytes 1572868
  27.2 10.2 %copy-start.11 = (bf16[512,1,512]{2,0,1:T(8,128)(2,1)S(1)}, bf16[512,1,512]{2,0,1:T(8,128)(2,1)}, u32[]{:S(2)}) copy-start(bf16[512,1,512]{2,0,1:T(8,128)(2,1)} %param.10) | copy-start | bytes 1572868
  30.0 21.9 %all-to-all-start = ((bf16[32,16,512]{2,0,1:T(8,128)(2,1)}), bf16[32,16,512]{2,0,1:T(8,128)(2,1)S(1)}, u32[]{:S(2)}, u32[]{:S(2)}) async-start(bf16[32,16,512]{2,0,1:T(8,128)(2,1)} %copy.98), calls=%async_computation | async-start | bytes 1048576 | tf_op jit(solution)/shard_map/all_to_all | solution.py:224
  40.9 12.4 %copy-start.26 = (f32[512]{0:T(512)S(1)}, f32[512]{0:T(512)}, u32[]{:S(2)}) copy-start(f32[512]{0:T(512)} %param.14) | copy-start | bytes 6148
  52.0 37.9 %copy-start = (f32[32,16,512]{2,0,1:T(8,128)}, f32[32,16,512]{2,0,1:T(8,128)S(1)}, u32[]{:S(2)}) copy-start(f32[32,16,512]{2,0,1:T(8,128)S(1)} %convert_element_type.236) | copy-start | bytes 3145732
  52.3 1.0 copy-start.9
  64.1 4.7 %copy-start.16 = (bf16[512,512]{0,1:T(8,128)(2,1)S(1)}, bf16[512,512]{0,1:T(8,128)(2,1)}, u32[]{:S(2)}) copy-start(bf16[512,512]{0,1:T(8,128)(2,1)} %convolution_convert_fusion.13) | copy-start | bytes 1572868
  68.8 3.6 %copy-start.2 = (f32[8,512,512]{1,2,0:T(8,128)S(1)}, f32[8,512,512]{1,2,0:T(8,128)}, u32[]{:S(2)}) copy-start(f32[8,512,512]{1,2,0:T(8,128)} %get-tuple-element.40) | copy-start | bytes 25165828
  69.6 19.8 %copy-start.3 = (bf16[8,512,64]{1,2,0:T(8,128)(2,1)}, bf16[8,512,64]{1,2,0:T(8,128)(2,1)S(1)}, u32[]{:S(2)}) copy-start(bf16[8,512,64]{1,2,0:T(8,128)(2,1)S(1)} %get-tuple-element.42) | copy-start | bytes 1572868
  76.3 1.5 copy-start.10
  76.3 2.5 %copy-start.23 = (bf16[512,2048]{1,0:T(8,128)(2,1)S(1)}, bf16[512,2048]{1,0:T(8,128)(2,1)}, u32[]{:S(2)}) copy-start(bf16[512,2048]{1,0:T(8,128)(2,1)} %param.12) | copy-start | bytes 6291460
  76.5 3.3 %copy-start.17 = (bf16[3,8,512,64]{2,3,1,0:T(8,128)(2,1)}, bf16[3,8,512,64]{2,3,1,0:T(8,128)(2,1)S(1)}, u32[]{:S(2)}) copy-start(bf16[3,8,512,64]{2,3,1,0:T(8,128)(2,1)S(1)} %pad_maximum_fusion.2) | copy-start | bytes 4718596
  78.8 1.0 copy-start.15
  81.5 7.9 %copy-start.12 = (bf16[512,1,512]{2,0,1:T(8,128)(2,1)S(1)}, bf16[512,1,512]{2,0,1:T(8,128)(2,1)}, u32[]{:S(2)}) copy-start(bf16[512,1,512]{2,0,1:T(8,128)(2,1)} %param.10) | copy-start | bytes 1572868
  85.0 18.6 %all-to-all-start.1 = ((bf16[16,2,8192]{2,1,0:T(2,128)(2,1)}), bf16[16,2,8192]{2,1,0:T(2,128)(2,1)S(1)}, u32[]{:S(2)}, u32[]{:S(2)}) async-start(bf16[16,2,8192]{2,1,0:T(2,128)(2,1)} %reshape.314), calls=%async_computation.1 | async-start | bytes 1048576 | tf_op jit(solution)/shard_map/all_to_all | solution.py:256
  89.1 68.1 %reduce-scatter.5.cloned.1.call-start = ((), (), s32[]{:S(2)}) async-start(), calls=%async_computation.5 | async-start | bytes 2228224 | tf_op jit(solution)/shard_map/reduce_scatter | solution.py:259
  94.1 127.9 %reduce-scatter.3.cloned.1.call-start = ((), (), s32[]{:S(2)}) async-start(), calls=%async_computation.4 | async-start | bytes 2228224 | tf_op jit(solution)/shard_map/reduce_scatter | solution.py:281
  105.0 4.3 %copy-start.8 = (bf16[32,8,16,64]{3,2,1,0:T(8,128)(2,1)S(1)}, bf16[32,8,16,64]{3,2,1,0:T(8,128)(2,1)}, u32[]{:S(2)}) copy-start(bf16[32,8,16,64]{3,2,1,0:T(8,128)(2,1)} %copy-done.7) | copy-start | bytes 1572868
  107.6 2.4 %copy-start.21 = (bf16[32,16,1,8,64]{4,3,2,1,0:T(8,128)(2,1)S(1)}, bf16[32,16,1,8,64]{4,3,2,1,0:T(8,128)(2,1)}, u32[]{:S(2)}) copy-start(bf16[32,16,1,8,64]{4,3,2,1,0:T(8,128)(2,1)} %get-tuple-element.30) | copy-start | bytes 1572868
  109.4 1.6 copy-start.29
  111.0 1.2 copy-start.6
  112.3 1.2 copy-start.5
  119.5 1.9 copy-start.14
  119.5 2.0 copy-start.18
  119.5 2.0 copy-start.27
  124.1 1.2 copy-start.1
  124.1 1.4 copy-start.4
  125.5 2.4 %copy-start.19 = (bf16[32,16,1536]{2,1,0:T(8,128)(2,1)S(1)}, bf16[32,16,1536]{2,1,0:T(8,128)(2,1)}, u32[]{:S(2)}) copy-start(bf16[32,16,1536]{2,1,0:T(8,128)(2,1)} %reshape.305) | copy-start | bytes 4718596
Sparse Core Ops, SparseCore 0:
  94.2 62.9 reduce-scatter.4
  161.4 60.6 reduce-scatter.2
where the time goes:
time: 232 us; the launch traced here: 230 us
  waiting for transfers between devices  108 us (47%)
  matrix products  46.6 us (20%)
  local copies, waits for them, and re-layouts  29.2 us (13%)
  other arithmetic  20.3 us (9%)
  between operations  14.6 us (6%)
  starting transfers between devices  11.8 us (5%)
    reduce_scatter x1, waiting for transfers between devices, per_device(): lax.psum_scatter(jnp.concatenate([weight_term(normed_cols, grad_spatial_p...  63.2 us
    reduce_scatter x1, waiting for transfers between devices, per_device(): lax.psum_scatter(jnp.concatenate([weight_term(normed_cols, grad_temporal_...  24.4 us
    unnamed x66, local copies, waits for them, and re-layouts  12.8 us
    dot_general x4, matrix products, project(): jnp.einsum('tbd,de->tbe', rows, coefficient_array, preferred_element_type...  11.6 us
    all_to_all x1, waiting for transfers between devices, per_device(): lax.all_to_all(middle, 'wide', split_axis=1, concat_axis=0, tiled=True)  10.9 us
    sub x2, matrix products, normalized_affinity(): expo = jnp.exp(unnormalized_affinities - row_max)  9.67 us
    all_to_all x1, waiting for transfers between devices, per_device(): lax.all_to_all(grad_middle, 'wide', split_axis=0, concat_axis=1, tiled=True)  9.45 us
    dot_general x4, matrix products, project_back(): jnp.einsum('tbe,de->tbd', derivative_collection, coefficient_array, prefe...  8.39 us
  transfers between devices with their start and end apart: 4, of which 4 were waited for; matrix products, arithmetic and copies ran while one was open for 15% of the time, Pallas kernels for 0%

commit v1 on v0

--- a/solution.py
+++ b/solution.py
@@ -1,7 +1,7 @@
 import jax
 import jax.numpy as jnp
 from jax import lax
-from jax.sharding import PartitionSpec as P
+from jax.sharding import Mesh, PartitionSpec as P
 
 HEADS = 8
 
@@ -198,6 +198,16 @@
     return jnp.einsum("tbd,tbe->de", left, right, preferred_element_type=jnp.float32)
 
 
+def reduce_rows(partial):
+    rows, cols = partial.shape
+    outer = lax.psum(1, "outer")
+    pieces = partial.astype(jnp.bfloat16).reshape(outer, 2, rows // (2 * outer), cols)
+    pieces = lax.all_to_all(pieces, "core", 1, 1, tiled=True)
+    pieces = jnp.sum(pieces.astype(jnp.float32), axis=1).astype(jnp.bfloat16)
+    pieces = lax.all_to_all(pieces, "outer", 0, 0, tiled=True)
+    return jnp.sum(pieces.astype(jnp.float32), axis=0)
+
+
 def per_device(
     activity,
     grad_out,
@@ -211,7 +221,7 @@
 ):
     local_bins = activity.shape[0]
     model_width = activity.shape[2]
-    first_bin = lax.axis_index("wide") * local_bins
+    first_bin = (lax.axis_index("outer") * 2 + lax.axis_index("core")) * local_bins
     sessions_here = lax.dynamic_slice_in_dim(session_id, first_bin, local_bins)
     normed_one, inverse_one = norm_forward(activity, spatial_gain)
     spatial_proj = project(normed_one, spatial_weights[:, : 3 * model_width]).astype(jnp.bfloat16)
@@ -221,7 +231,7 @@
         activity.astype(jnp.float32)
         + project(spatial_context, spatial_weights[:, 3 * model_width :])
     ).astype(jnp.bfloat16)
-    middle_block = lax.all_to_all(middle, "wide", split_axis=1, concat_axis=0, tiled=True)
+    middle_block = lax.all_to_all(middle, ("outer", "core"), split_axis=1, concat_axis=0, tiled=True)
     normed_two, inverse_two = norm_forward(middle_block, temporal_gain)
     temporal_proj = project(normed_two, temporal_weights[:, : 3 * model_width]).astype(jnp.bfloat16)
     allowed_time = session_id[:, None] == session_id[None, :]
@@ -253,18 +263,15 @@
         grad_out.astype(jnp.float32)
         + norm_backward(middle_block, temporal_gain, inverse_two, grad_normed_two)
     ).astype(jnp.bfloat16)
-    grad_middle_time = lax.all_to_all(grad_middle, "wide", split_axis=0, concat_axis=1, tiled=True)
+    grad_middle_time = lax.all_to_all(grad_middle, ("outer", "core"), split_axis=0, concat_axis=1, tiled=True)
     normed_cols = normed_two
     context_cols = temporal_context
-    temporal_grad = lax.psum_scatter(
+    temporal_grad = reduce_rows(
         jnp.concatenate(
             [weight_term(normed_cols, grad_temporal_proj), weight_term(context_cols, grad_out)],
             axis=1,
-        ).astype(jnp.bfloat16),
-        "wide",
-        scatter_dimension=0,
-        tiled=True,
-    ).astype(jnp.float32)
+        )
+    )
     grad_spatial_context = project_back(
         grad_middle_time, spatial_weights[:, 3 * model_width :]
     ).astype(jnp.bfloat16)
@@ -278,25 +285,24 @@
     ).astype(jnp.bfloat16)
     normed_cols = normed_one
     context_cols = spatial_context
-    spatial_grad = lax.psum_scatter(
+    spatial_grad = reduce_rows(
         jnp.concatenate(
             [
                 weight_term(normed_cols, grad_spatial_proj),
                 weight_term(context_cols, grad_middle_time),
             ],
             axis=1,
-        ).astype(jnp.bfloat16),
-        "wide",
-        scatter_dimension=0,
-        tiled=True,
-    ).astype(jnp.float32)
+        )
+    )
     return (layer_out, grad_activity, spatial_grad, temporal_grad)
 
 
 def solution(mesh):
+    groups, wide = mesh.devices.shape
+    mesh = Mesh(mesh.devices.reshape(groups, wide // 2, 2), ("groups", "outer", "core"))
     placed = (
-        P(("groups", "wide"), None, None),
-        P("groups", "wide", None),
+        P(("groups", "outer", "core"), None, None),
+        P("groups", ("outer", "core"), None),
         P(),
         P(),
         P(),
@@ -310,10 +316,10 @@
         mesh=mesh,
         in_specs=placed,
         out_specs=(
-            P("groups", "wide", None),
-            P(("groups", "wide"), None, None),
-            P(("groups", "wide"), None),
-            P(("groups", "wide"), None),
+            P("groups", ("outer", "core"), None),
+            P(("groups", "outer", "core"), None, None),
+            P(("groups", "outer", "core"), None),
+            P(("groups", "outer", "core"), None),
         ),
         check_vma=False,
     )

time: 232 us -> 200 us (0.86)
  waiting for transfers between devices: 108 us -> 67.5 us
  between operations: 14.6 us -> 1.3 us
  blocking collectives: 0 us -> 11 us
  starting transfers between devices: 11.8 us -> 19.4 us
  local copies, waits for them, and re-layouts: 29.2 us -> 35.8 us
    reduce_scatter x2 -> x0, waiting for transfers between devices: 87.6 us -> none  [the longest x1 63.2 us: per_device(): lax.psum_scatter(jnp.concatenate([weight_term(normed_cols, grad_spatial_p...]
    all_to_all x2 -> x4, waiting for transfers between devices: 20.4 us -> 67.5 us  [the longest x2 46.1 us: reduce_rows(): pieces = lax.all_to_all(pieces, 'outer', 0, 0, tiled=True)]
    all_to_all x0 -> x2, blocking collectives: none -> 11 us  [reduce_rows(): pieces = lax.all_to_all(pieces, 'core', 1, 1, tiled=True)]
    all_to_all x2 -> x4, starting transfers between devices: 11.5 us -> 19.4 us  [the longest x2 7.87 us: reduce_rows(): pieces = lax.all_to_all(pieces, 'outer', 0, 0, tiled=True)]
    reduce_sum x0 -> x4, other arithmetic: none -> 6.46 us  [the longest x2 3.52 us: reduce_rows(): pieces = jnp.sum(pieces.astype(jnp.float32), axis=1).astype(jnp.bfloat16)]
    convert_element_type x3 -> x1, other arithmetic: 5.59 us -> 0.16 us  [norm_forward(): (rows.astype(jnp.float32) * inverse * gain).astype(jnp.bfloat16)]
    dot_general x0 -> x2, local copies, waits for them, and re-layouts: none -> 4.39 us  [weight_term(): jnp.einsum('tbd,tbe->de', left, right, preferred_element_type=jnp.float32)]
    reshape x1 -> x2, local copies, waits for them, and re-layouts: 2.98 us -> 5.9 us  [spatial_backward(): jnp.stack(derivative_collection, axis=0).transpose(1, 3, 0, 2, 4)]
  transfers between devices with their start and end apart: 4 -> 4, of which waited for: 4 -> 4; matrix products, arithmetic and copies ran while one was open for 15% -> 7% of each run, Pallas kernels for 0% -> 0%
where the time goes in v1:
time: 200 us; the launch traced here: 198 us
  waiting for transfers between devices  67.5 us (34%)
  matrix products  45.2 us (23%)
  local copies, waits for them, and re-layouts  35.8 us (18%)
  starting transfers between devices  19.4 us (10%)
  other arithmetic  18.1 us (9%)
  blocking collectives  11 us (6%)
    all_to_all x2, waiting for transfers between devices, reduce_rows(): pieces = lax.all_to_all(pieces, 'outer', 0, 0, tiled=True)  46.1 us
    unnamed x78, local copies, waits for them, and re-layouts  12.7 us
    dot_general x4, matrix products, project(): jnp.einsum('tbd,de->tbe', rows, coefficient_array, preferred_element_type...  11.4 us
    all_to_all x2, blocking collectives, reduce_rows(): pieces = lax.all_to_all(pieces, 'core', 1, 1, tiled=True)  11 us
    all_to_all x1, waiting for transfers between devices, per_device(): lax.all_to_all(middle, ('outer', 'core'), split_axis=1, concat_axis=0, ti...  10.9 us
    all_to_all x1, waiting for transfers between devices, per_device(): lax.all_to_all(grad_middle, ('outer', 'core'), split_axis=0, concat_axis=...  10.5 us
    sub x2, matrix products, normalized_affinity(): expo = jnp.exp(unnormalized_affinities - row_max)  8.34 us
    dot_general x4, matrix products, project_back(): jnp.einsum('tbe,de->tbd', derivative_collection, coefficient_array, prefe...  7.98 us
  transfers between devices with their start and end apart: 4, of which 4 were waited for; matrix products, arithmetic and copies ran while one was open for 7% of the time, Pallas kernels for 0%

profile of v1, /device:TPU:0, one launch (start us, length us, event | category | flops | bytes accessed | tf_op | source)
XLA Modules:
  0.0 198.3 jit_solution(773313142242042754)
XLA Ops:
  0.7 1.2 fusion.50
  1.9 3.8 %convolution_convert_fusion.2 = bf16[32,16,1536]{2,1,0:T(8,128)(2,1)} fusion(bf16[512,2048]{1,0:T(8,128)(2,1)} %param.11, bf16[32,16,512]{2,1,0:T(8,128)(2,1)} %param.9, f32[512]{0:T(512)} %param.13, f32[32,16]{1,0:T(8,128)S(1)} %add_rsqrt_fusion), kind=kOutput, calls=%fused_computation.15 | convolution fusion | flops 807141376 | bytes 3674112 | tf_op jit(solution)/shard_map/tbd,de->tbe/dot_general | solution.py:188
  5.7 4.0 %reshape.269 = bf16[32,16,3,8,64]{4,3,2,1,0:T(8,128)(2,1)S(1)} reshape(bf16[32,16,1536]{2,1,0:T(8,128)(2,1)} %convolution_convert_fusion.2) | data formatting | bytes 3145728 | tf_op jit(solution)/shard_map/reshape | solution.py:136
  9.7 2.1 %fusion.84 = (bf16[32,16,1,8,64]{4,3,2,1,0:T(8,128)(2,1)}, bf16[32,16,1,8,64]{4,3,2,1,0:T(8,128)(2,1)}, bf16[32,16,1,8,64]{4,3,2,1,0:T(8,128)(2,1)}) fusion(bf16[32,16,3,8,64]{4,3,2,1,0:T(8,128)(2,1)S(1)} %reshape.269), kind=kLoop, calls=%fused_computation.130 | loop fusion | bytes 3145728 | tf_op jit(solution)/shard_map/slice | solution.py:139
  12.3 2.9 %fusion.85 = (f32[32,8,16]{2,1,0:T(8,128)S(1)}, f32[32,8,16,16]{2,3,1,0:T(8,128)S(1)}) fusion(pred[32,16,16]{1,2,0:T(8,128)(4,1)S(1)} %and_or_fusion, bf16[32,16,1,8,64]{4,3,2,1,0:T(8,128)(2,1)} %get-tuple-element.29, bf16[32,16,1,8,64]{4,3,2,1,0:T(8,128)(2,1)} %get-tuple-element.28), kind=kOutput, calls=%fused_computation.131 | convolution fusion | flops 8650767 | bytes 1335296 | tf_op jit(solution)/shard_map/sub | solution.py:39
  15.3 1.3 copy-done.32
  17.2 1.0 copy-done.10
  19.1 1.7 fusion.36
  20.8 1.1 copy.101
  21.9 7.4 %all-to-all-start = ((bf16[32,16,512]{2,0,1:T(8,128)(2,1)}), bf16[32,16,512]{2,0,1:T(8,128)(2,1)S(1)}, u32[]{:S(2)}, u32[]{:S(2)}) async-start(bf16[32,16,512]{2,0,1:T(8,128)(2,1)} %copy.101), calls=%async_computation | async-start | bytes 1048576 | tf_op jit(solution)/shard_map/all_to_all | solution.py:234
  29.3 1.0 copy.107
  30.5 2.3 %convolution_convert_fusion.13 = bf16[512,512]{0,1:T(8,128)(2,1)} fusion(bf16[512,1,512]{2,0,1:T(8,128)(2,1)S(1)} %copy-done.15, bf16[512,2048]{1,0:T(8,128)(2,1)} %param.12), kind=kOutput, calls=%fused_computation.60 | convolution fusion | flops 268697600 | bytes 1572864 | tf_op jit(solution)/shard_map/tbe,de->tbd/dot_general | solution.py:192
  32.8 10.9 %all-to-all-done = bf16[32,16,512]{2,0,1:T(8,128)(2,1)S(1)} async-done(((bf16[32,16,512]{2,0,1:T(8,128)(2,1)}), bf16[32,16,512]{2,0,1:T(8,128)(2,1)S(1)}, u32[]{:S(2)}, u32[]{:S(2)}) %all-to-all-start) | async-done | bytes 524320 | tf_op jit(solution)/shard_map/all_to_all | solution.py:234
  45.6 3.6 %convolution_convert_fusion.1 = bf16[512,1536]{1,0:T(8,128)(2,1)} fusion(bf16[512,512]{0,1:T(8,128)(2,1)S(1)} %multiply_convert_fusion.2, bf16[512,2048]{1,0:T(8,128)(2,1)} %param.12), kind=kOutput, calls=%fused_computation.14 | convolution fusion | flops 806092800 | bytes 3670016 | tf_op jit(solution)/shard_map/tbd,de->tbe/dot_general | solution.py:188
  49.2 1.7 copy.105
  50.9 5.4 %fusion.86 = (f32[8,512]{1,0:T(8,128)S(1)}, f32[8,512,512]{1,2,0:T(8,128)}) fusion(pred[512,512]{0,1:T(8,128)(4,1)S(1)} %broadcast_compare_fusion, bf16[512,3,8,64]{0,3,2,1:T(8,128)(2,1)S(1)} %bitcast.194), kind=kOutput, calls=%fused_computation.132 | convolution fusion | flops 276824576 | bytes 9715712 | tf_op jit(solution)/shard_map/while/body/eval_jaxpr/sub | solution.py:39
  56.4 4.7 %fusion.6 = bf16[8,512,512]{1,2,0:T(8,128)(2,1)S(1)} fusion(f32[8,512,512]{1,2,0:T(8,128)} %get-tuple-element.42, f32[8,512]{1,0:T(8,128)S(1)} %get-tuple-element.41), kind=kLoop, calls=%fused_computation.10 | loop fusion | flops 4194304 | bytes 12599296 | tf_op jit(solution)/shard_map/while/body/eval_jaxpr/convert_element_type | solution.py:48
  61.9 1.4 fusion.42
  63.2 1.4 copy-done.3
  64.6 1.8 multiply_convert_fusion
  66.4 1.4 fusion.41
  68.8 2.0 copy-done.26
  70.8 1.0 multiply_reduce_fusion.1
  72.7 1.0 reduce.8
  73.9 1.2 reshape.290
  75.5 2.4 %convolution_convert_fusion = bf16[8,2,32,1536]{3,2,1,0:T(8,128)(2,1)S(1)} fusion(bf16[8,2,32,512]{3,2,1,0:T(8,128)(2,1)S(1)} %bitcast.210, bf16[512,1536,1,1]{0,1,3,2:T(8,128)(2,1)} %bitcast.209), kind=kOutput, calls=%fused_computation.13 | convolution fusion | flops 806092800 | bytes 3670016 | tf_op jit(solution)/shard_map/tbd,tbe->de/dot_general | solution.py:198
  78.5 5.5 %all_to_all.47 = bf16[8,2,32,2048]{3,2,0,1:T(8,128)(2,1)S(1)} all-to-all(bf16[8,2,32,2048]{3,2,0,1:T(8,128)(2,1)S(1)} %copy.125), channel_id=1, replica_groups=mesh['groups'=2,'outer'=8,'core'=2] {'core'}, dimensions={1} | all-to-all | bytes 4194304 | tf_op jit(solution)/shard_map/all_to_all | solution.py:205
  84.1 4.1 %all-to-all-start.1 = ((bf16[16,2,8192]{2,1,0:T(2,128)(2,1)}), bf16[16,2,8192]{2,1,0:T(2,128)(2,1)S(1)}, u32[]{:S(2)}, u32[]{:S(2)}) async-start(bf16[16,2,8192]{2,1,0:T(2,128)(2,1)} %reshape.290), calls=%async_computation.1 | async-start | bytes 1048576 | tf_op jit(solution)/shard_map/all_to_all | solution.py:266
  88.2 2.2 %reshape.289 = bf16[8,2,32,16,32]{2,1,0,3,4:T(2,128)(2,1)} reshape(bf16[512,16,32]{0,1,2:T(8,128)(2,1)S(1)} %bitcast.205) | data formatting | bytes 1048576 | tf_op jit(solution)/shard_map/tbd,tbe->de/dot_general | solution.py:198
  90.4 1.7 reduce_sum.145
  92.1 10.5 %all-to-all-done.1 = bf16[16,2,8192]{2,1,0:T(2,128)(2,1)S(1)} async-done(((bf16[16,2,8192]{2,1,0:T(2,128)(2,1)}), bf16[16,2,8192]{2,1,0:T(2,128)(2,1)S(1)}, u32[]{:S(2)}, u32[]{:S(2)}) %all-to-all-start.1) | async-done | bytes 524320 | tf_op jit(solution)/shard_map/all_to_all | solution.py:266
  104.1 1.5 convolution_convert_fusion.10
  106.2 2.4 %fusion.29 = bf16[1,32,8,16,64]{4,3,2,1,0:T(8,128)(2,1)S(1)} fusion(bf16[32,16,8,64]{3,2,1,0:T(8,128)(2,1)S(1)} %reshape.276, f32[32,8,16,16]{2,3,1,0:T(8,128)} %copy-done.32, f32[32,8,16]{2,1,0:T(8,128)S(1)} %copy-done.35), kind=kOutput, calls=%fused_computation.51 | convolution fusion | flops 8781824 | bytes 1327104 | tf_op jit(solution)/shard_map/...qk,...qd->...kd/dot_general | solution.py:67
  114.5 2.9 %reshape.277 = bf16[32,16,1536]{2,1,0:T(8,128)(2,1)} reshape(bf16[32,16,3,8,64]{4,3,2,1,0:T(8,128)(2,1)S(1)} %copy.118) | data formatting | bytes 3145728 | tf_op jit(solution)/shard_map/reshape | solution.py:169
  117.4 3.0 %reshape.282 = bf16[32,16,1536,1,1]{2,1,0,3,4:T(8,128)(2,1)} reshape(bf16[32,16,3,8,64]{4,3,2,1,0:T(8,128)(2,1)S(1)} %copy.118) | data formatting | bytes 3145728 | tf_op jit(solution)/shard_map/reshape | solution.py:169
  120.4 3.2 %fusion.51 = (f32[32,16]{1,0:T(8,128)S(1)}, f32[32,16,512]{2,1,0:T(8,128)S(1)}) fusion(bf16[32,16,512]{2,1,0:T(8,128)(2,1)} %param.9, f32[512]{0:T(512)S(1)} %copy-done.30, bf16[32,16,1536]{2,1,0:T(8,128)(2,1)} %reshape.277, bf16[512,2048]{1,0:T(8,128)(2,1)} %param.11), kind=kOutput, calls=%fused_computation.77 | convolution fusion | flops 806354432 | bytes 4722688 | tf_op jit(solution)/shard_map/tbe,de->tbd/dot_general | solution.py:192
  123.6 1.3 fusion.76
  124.9 2.2 %dot_general.118 = bf16[8,2,32,16,32]{2,1,0,3,4:T(2,128)(2,1)} reshape(bf16[512,16,32]{0,1,2:T(8,128)(2,1)S(1)} %get-tuple-element.31) | data formatting | bytes 1048576 | tf_op jit(solution)/shard_map/tbd,tbe->de/dot_general | solution.py:198
  127.1 1.0 fusion.33
  128.6 2.7 %fusion.7 = bf16[8,2,32,1536]{3,2,1,0:T(8,128)(2,1)S(1)} fusion(bf16[8,2,32,16,32]{2,1,0,3,4:T(2,128)(2,1)S(1)} %copy-done.14, bf16[32,16,1536,1,1]{2,1,0,3,4:T(8,128)(2,1)} %reshape.282), kind=kOutput, calls=%fused_computation.16 | convolution fusion | flops 806092800 | bytes 3670016 | tf_op jit(solution)/shard_map/tbd,tbe->de/dot_general | solution.py:198
  131.9 5.4 %all_to_all.48 = bf16[8,2,32,2048]{3,2,0,1:T(8,128)(2,1)S(1)} all-to-all(bf16[8,2,32,2048]{3,2,0,1:T(8,128)(2,1)S(1)} %copy.123), channel_id=1, replica_groups=mesh['groups'=2,'outer'=8,'core'=2] {'core'}, dimensions={1} | all-to-all | bytes 4194304 | tf_op jit(solution)/shard_map/all_to_all | solution.py:205
  137.3 4.2 %all-to-all-start.5 = ((bf16[8,32,2048]{2,1,0:T(8,128)(2,1)}), bf16[8,32,2048]{2,1,0:T(8,128)(2,1)}, u32[]{:S(2)}, u32[]{:S(2)}) async-start(bf16[8,32,2048]{2,1,0:T(8,128)(2,1)} %reduce_sum.145), calls=%async_computation.5 | async-start | bytes 2097152 | tf_op jit(solution)/shard_map/all_to_all | solution.py:207
  141.5 1.8 reduce_sum.143
  143.4 24.5 %all-to-all-done.5 = bf16[8,32,2048]{2,1,0:T(8,128)(2,1)} async-done(((bf16[8,32,2048]{2,1,0:T(8,128)(2,1)}), bf16[8,32,2048]{2,1,0:T(8,128)(2,1)}, u32[]{:S(2)}, u32[]{:S(2)}) %all-to-all-start.5) | async-done | bytes 1048608 | tf_op jit(solution)/shard_map/all_to_all | solution.py:207
  167.9 3.6 %all-to-all-start.3 = ((bf16[8,32,2048]{2,1,0:T(8,128)(2,1)}), bf16[8,32,2048]{2,1,0:T(8,128)(2,1)S(1)}, u32[]{:S(2)}, u32[]{:S(2)}) async-start(bf16[8,32,2048]{2,1,0:T(8,128)(2,1)} %reduce_sum.143), calls=%async_computation.3 | async-start | bytes 2097152 | tf_op jit(solution)/shard_map/all_to_all | solution.py:207
  171.5 2.3 %fusion.40 = bf16[512,1,512]{2,0,1:T(8,128)(2,1)} fusion(f32[512,512]{1,0:T(8,128)S(1)} %bitcast.193, bf16[512,512]{0,1:T(8,128)(2,1)S(1)} %bitcast.200, bf16[512,2048]{1,0:T(8,128)(2,1)} %param.12), kind=kOutput, calls=%fused_computation.66 | convolution fusion | flops 268959744 | bytes 2621440 | tf_op jit(solution)/shard_map/tbd,de->tbe/dot_general | solution.py:188
  173.8 2.1 %convert_reduce_fusion = f32[32,2048]{1,0:T(8,128)} fusion(bf16[8,32,2048]{2,1,0:T(8,128)(2,1)} %all-to-all-done.5), kind=kLoop, calls=%fused_computation.22 | loop fusion | flops 983040 | bytes 1310720 | tf_op jit(solution)/shard_map/reduce_sum | solution.py:208
  175.9 21.6 %all-to-all-done.3 = bf16[8,32,2048]{2,1,0:T(8,128)(2,1)S(1)} async-done(((bf16[8,32,2048]{2,1,0:T(8,128)(2,1)}), bf16[8,32,2048]{2,1,0:T(8,128)(2,1)S(1)}, u32[]{:S(2)}, u32[]{:S(2)}) %all-to-all-start.3) | async-done | bytes 1048608 | tf_op jit(solution)/shard_map/all_to_all | solution.py:207
  (112 shorter events, 17.6 us)
Async XLA Ops:
  9.7 2.2 %copy-start.28 = (s32[16,16]{1,0:T(8,128)S(1)}, s32[16,16]{1,0:T(8,128)}, u32[]{:S(2)}) copy-start(s32[16,16]{1,0:T(8,128)} %param.15) | copy-start | bytes 3076
  9.7 2.3 %copy-start.27 = (s32[512]{0:T(512)S(1)}, s32[512]{0:T(512)}, u32[]{:S(2)}) copy-start(s32[512]{0:T(512)} %param.17) | copy-start | bytes 6148
  9.7 2.3 %copy-start.31 = (s32[4]{0:T(128)S(1)}, s32[4]{0:T(128)}, u32[]{:S(2)}) copy-start(s32[4]{0:T(128)} %param.16) | copy-start | bytes 52
  12.3 4.3 %copy-start.22 = (bf16[32,16,1,8,64]{4,3,2,1,0:T(8,128)(2,1)S(1)}, bf16[32,16,1,8,64]{4,3,2,1,0:T(8,128)(2,1)}, u32[]{:S(2)}) copy-start(bf16[32,16,1,8,64]{4,3,2,1,0:T(8,128)(2,1)} %get-tuple-element.30) | copy-start | bytes 1572868
  15.3 1.4 copy-start.32
  15.3 1.9 copy-start.34
  17.2 1.0 copy-start.10
  17.2 1.9 copy-start.17
  19.1 2.8 %copy-start.12 = (bf16[32,16,512]{2,1,0:T(8,128)(2,1)}, bf16[32,16,512]{2,1,0:T(8,128)(2,1)S(1)}, u32[]{:S(2)}) copy-start(bf16[32,16,512]{2,1,0:T(8,128)(2,1)S(1)} %reshape.270) | copy-start | bytes 1572868
  19.1 10.2 %copy-start.15 = (bf16[512,1,512]{2,0,1:T(8,128)(2,1)S(1)}, bf16[512,1,512]{2,0,1:T(8,128)(2,1)}, u32[]{:S(2)}) copy-start(bf16[512,1,512]{2,0,1:T(8,128)(2,1)} %param.10) | copy-start | bytes 1572868
  21.9 21.8 %all-to-all-start = ((bf16[32,16,512]{2,0,1:T(8,128)(2,1)}), bf16[32,16,512]{2,0,1:T(8,128)(2,1)S(1)}, u32[]{:S(2)}, u32[]{:S(2)}) async-start(bf16[32,16,512]{2,0,1:T(8,128)(2,1)} %copy.101), calls=%async_computation | async-start | bytes 1048576 | tf_op jit(solution)/shard_map/all_to_all | solution.py:234
  32.8 11.8 %copy-start.29 = (f32[512]{0:T(512)S(1)}, f32[512]{0:T(512)}, u32[]{:S(2)}) copy-start(f32[512]{0:T(512)} %param.14) | copy-start | bytes 6148
  43.8 1.0 copy-start
  44.8 0.8 copy-start.24
  56.4 4.7 %copy-start.20 = (bf16[512,512]{0,1:T(8,128)(2,1)S(1)}, bf16[512,512]{0,1:T(8,128)(2,1)}, u32[]{:S(2)}) copy-start(bf16[512,512]{0,1:T(8,128)(2,1)} %convolution_convert_fusion.13) | copy-start | bytes 1572868
  61.0 3.6 %copy-start.3 = (f32[8,512,512]{1,2,0:T(8,128)S(1)}, f32[8,512,512]{1,2,0:T(8,128)}, u32[]{:S(2)}) copy-start(f32[8,512,512]{1,2,0:T(8,128)} %get-tuple-element.42) | copy-start | bytes 25165828
  61.8 13.3 %copy-start.4 = (bf16[8,512,64]{1,2,0:T(8,128)(2,1)}, bf16[8,512,64]{1,2,0:T(8,128)(2,1)S(1)}, u32[]{:S(2)}) copy-start(bf16[8,512,64]{1,2,0:T(8,128)(2,1)S(1)} %get-tuple-element.44) | copy-start | bytes 1572868
  68.6 2.2 %copy-start.26 = (bf16[512,2048]{1,0:T(8,128)(2,1)S(1)}, bf16[512,2048]{1,0:T(8,128)(2,1)}, u32[]{:S(2)}) copy-start(bf16[512,2048]{1,0:T(8,128)(2,1)} %param.12) | copy-start | bytes 6291460
  68.8 3.0 %copy-start.21 = (bf16[3,8,512,64]{2,3,1,0:T(8,128)(2,1)}, bf16[3,8,512,64]{2,3,1,0:T(8,128)(2,1)S(1)}, u32[]{:S(2)}) copy-start(bf16[3,8,512,64]{2,3,1,0:T(8,128)(2,1)S(1)} %pad_maximum_fusion.2) | copy-start | bytes 4718596
  70.7 1.0 copy-start.19
  72.1 3.0 %copy-start.16 = (bf16[512,1,512]{2,0,1:T(8,128)(2,1)S(1)}, bf16[512,1,512]{2,0,1:T(8,128)(2,1)}, u32[]{:S(2)}) copy-start(bf16[512,1,512]{2,0,1:T(8,128)(2,1)} %param.10) | copy-start | bytes 1572868
  73.7 1.8 copy-start.25
  78.5 9.7 %copy-start.13 = (bf16[32,16,512]{2,1,0:T(8,128)(2,1)S(1)}, bf16[32,16,512]{2,1,0:T(8,128)(2,1)}, u32[]{:S(2)}) copy-start(bf16[32,16,512]{2,1,0:T(8,128)(2,1)} %copy-done.12) | copy-start | bytes 1572868
  84.1 18.6 %all-to-all-start.1 = ((bf16[16,2,8192]{2,1,0:T(2,128)(2,1)}), bf16[16,2,8192]{2,1,0:T(2,128)(2,1)S(1)}, u32[]{:S(2)}, u32[]{:S(2)}) async-start(bf16[16,2,8192]{2,1,0:T(2,128)(2,1)} %reshape.290), calls=%async_computation.1 | async-start | bytes 1048576 | tf_op jit(solution)/shard_map/all_to_all | solution.py:266
  103.3 0.8 copy-start.6
  103.3 2.8 %copy-start.35 = (f32[32,8,16]{2,1,0:T(8,128)S(1)}, f32[32,8,16]{2,1,0:T(8,128)}, u32[]{:S(2)}) copy-start(f32[32,8,16]{2,1,0:T(8,128)} %copy-done.34) | copy-start | bytes 49156
  106.2 2.5 %copy-start.11 = (bf16[32,8,16,64]{3,2,1,0:T(8,128)(2,1)S(1)}, bf16[32,8,16,64]{3,2,1,0:T(8,128)(2,1)}, u32[]{:S(2)}) copy-start(bf16[32,8,16,64]{3,2,1,0:T(8,128)(2,1)} %copy-done.10) | copy-start | bytes 1572868
  106.2 3.1 %copy-start.33 = (f32[32,8,16,16]{2,3,1,0:T(8,128)S(1)}, f32[32,8,16,16]{2,3,1,0:T(8,128)}, u32[]{:S(2)}) copy-start(f32[32,8,16,16]{2,3,1,0:T(8,128)} %copy-done.32) | copy-start | bytes 786436
  108.6 1.2 copy-start.23
  109.9 1.2 copy-start.9
  111.1 1.2 copy-start.8
  117.4 3.0 %copy-start.30 = (f32[512]{0:T(512)S(1)}, f32[512]{0:T(512)}, u32[]{:S(2)}) copy-start(f32[512]{0:T(512)} %param.13) | copy-start | bytes 6148
  120.4 3.2 %copy-start.7 = (bf16[512,1,512]{2,0,1:T(8,128)(2,1)S(1)}, bf16[512,1,512]{2,0,1:T(8,128)(2,1)}, u32[]{:S(2)}) copy-start(bf16[512,1,512]{2,0,1:T(8,128)(2,1)} %copy-done.6) | copy-start | bytes 1572868
  120.4 3.2 %copy-start.18 = (bf16[32,16,512]{2,1,0:T(8,128)(2,1)S(1)}, bf16[32,16,512]{2,1,0:T(8,128)(2,1)}, u32[]{:S(2)}) copy-start(bf16[32,16,512]{2,1,0:T(8,128)(2,1)} %param.9) | copy-start | bytes 1572868
  124.9 2.2 %copy-start.2 = (bf16[8,2,32,16,32]{2,1,0,3,4:T(2,128)(2,1)S(1)}, bf16[8,2,32,16,32]{2,1,0,3,4:T(2,128)(2,1)}, u32[]{:S(2)}) copy-start(bf16[8,2,32,16,32]{2,1,0,3,4:T(2,128)(2,1)} %reshape.289) | copy-start | bytes 1572868
  127.1 1.6 copy-start.14
  137.3 30.6 %all-to-all-start.5 = ((bf16[8,32,2048]{2,1,0:T(8,128)(2,1)}), bf16[8,32,2048]{2,1,0:T(8,128)(2,1)}, u32[]{:S(2)}, u32[]{:S(2)}) async-start(bf16[8,32,2048]{2,1,0:T(8,128)(2,1)} %reduce_sum.145), calls=%async_computation.5 | async-start | bytes 2097152 | tf_op jit(solution)/shard_map/all_to_all | solution.py:207
  141.5 30.0 %copy-start.1 = (f32[32,16,512]{2,0,1:T(8,128)S(1)}, f32[32,16,512]{2,0,1:T(8,128)}, u32[]{:S(2)}) copy-start(f32[32,16,512]{2,0,1:T(8,128)} %copy-done) | copy-start | bytes 3145732
  143.4 28.2 %copy-start.5 = (bf16[8,512,64]{1,2,0:T(8,128)(2,1)S(1)}, bf16[8,512,64]{1,2,0:T(8,128)(2,1)}, u32[]{:S(2)}) copy-start(bf16[8,512,64]{1,2,0:T(8,128)(2,1)} %copy-done.4) | copy-start | bytes 1572868
  167.9 29.6 %all-to-all-start.3 = ((bf16[8,32,2048]{2,1,0:T(8,128)(2,1)}), bf16[8,32,2048]{2,1,0:T(8,128)(2,1)S(1)}, u32[]{:S(2)}, u32[]{:S(2)}) async-start(bf16[8,32,2048]{2,1,0:T(8,128)(2,1)} %reduce_sum.143), calls=%async_computation.3 | async-start | bytes 2097152 | tf_op jit(solution)/shard_map/all_to_all | solution.py:207

commit v2 on v1

--- a/solution.py
+++ b/solution.py
@@ -266,12 +266,15 @@
     grad_middle_time = lax.all_to_all(grad_middle, ("outer", "core"), split_axis=0, concat_axis=1, tiled=True)
     normed_cols = normed_two
     context_cols = temporal_context
-    temporal_grad = reduce_rows(
+    temporal_grad = lax.psum_scatter(
         jnp.concatenate(
             [weight_term(normed_cols, grad_temporal_proj), weight_term(context_cols, grad_out)],
             axis=1,
-        )
-    )
+        ).astype(jnp.bfloat16),
+        ("outer", "core"),
+        scatter_dimension=0,
+        tiled=True,
+    ).astype(jnp.float32)
     grad_spatial_context = project_back(
         grad_middle_time, spatial_weights[:, 3 * model_width :]
     ).astype(jnp.bfloat16)

time: 200 us -> 182 us (0.910)
  waiting for transfers between devices: 67.5 us -> 46.2 us
  between operations: 1.3 us -> 14.7 us
  blocking collectives: 11 us -> 5.42 us
  starting transfers between devices: 19.4 us -> 16 us
    all_to_all x2 -> x1, waiting for transfers between devices: 46.1 us -> 28 us  [reduce_rows(): pieces = lax.all_to_all(pieces, 'outer', 0, 0, tiled=True)]
    all_to_all x2 -> x1, blocking collectives: 11 us -> 5.42 us  [reduce_rows(): pieces = lax.all_to_all(pieces, 'core', 1, 1, tiled=True)]
    all_to_all x2 -> x1, starting transfers between devices: 7.87 us -> 4.07 us  [reduce_rows(): pieces = lax.all_to_all(pieces, 'outer', 0, 0, tiled=True)]
    all_to_all x1, waiting for transfers between devices: 10.5 us -> 7.29 us  [per_device(): lax.all_to_all(grad_middle, ('outer', 'core'), split_axis=0, concat_axis=...]
    reduce_sum x2 -> x1, other arithmetic: 2.93 us -> 0.84 us  [reduce_rows(): return jnp.sum(pieces.astype(jnp.float32), axis=0)]
  transfers between devices with their start and end apart: 4 -> 4, of which waited for: 4 -> 3; matrix products, arithmetic and copies ran while one was open for 7% -> 23% of each run, Pallas kernels for 0% -> 0%
where the time goes in v2:
time: 182 us; the launch traced here: 181 us
  waiting for transfers between devices  46.2 us (25%)
  matrix products  45.5 us (25%)
  local copies, waits for them, and re-layouts  35.8 us (20%)
  other arithmetic  17.1 us (9%)
  starting transfers between devices  16 us (9%)
  between operations  14.7 us (8%)
  blocking collectives  5.42 us (3%)
    all_to_all x1, waiting for transfers between devices, reduce_rows(): pieces = lax.all_to_all(pieces, 'outer', 0, 0, tiled=True)  28 us
    unnamed x78, local copies, waits for them, and re-layouts  12.9 us
    dot_general x4, matrix products, project(): jnp.einsum('tbd,de->tbe', rows, coefficient_array, preferred_element_type...  11.4 us
    all_to_all x1, waiting for transfers between devices, per_device(): lax.all_to_all(middle, ('outer', 'core'), split_axis=1, concat_axis=0, ti...  10.9 us
    sub x2, matrix products, normalized_affinity(): expo = jnp.exp(unnormalized_affinities - row_max)  8.34 us
    dot_general x4, matrix products, project_back(): jnp.einsum('tbe,de->tbd', derivative_collection, coefficient_array, prefe...  7.99 us
    all_to_all x1, starting transfers between devices, per_device(): lax.all_to_all(middle, ('outer', 'core'), split_axis=1, concat_axis=0, ti...  7.39 us
    all_to_all x1, waiting for transfers between devices, per_device(): lax.all_to_all(grad_middle, ('outer', 'core'), split_axis=0, concat_axis=...  7.29 us
  transfers between devices with their start and end apart: 4, of which 3 were waited for; matrix products, arithmetic and copies ran while one was open for 23% of the time, Pallas kernels for 0%

profile of v2, /device:TPU:0, one launch (start us, length us, event | category | flops | bytes accessed | tf_op | source)
XLA Modules:
  0.0 180.6 jit_solution(17590320432922437677)
XLA Ops:
  7.2 1.2 fusion.50
  8.4 3.8 %convolution_convert_fusion.2 = bf16[32,16,1536]{2,1,0:T(8,128)(2,1)} fusion(bf16[512,2048]{1,0:T(8,128)(2,1)} %param.11, bf16[32,16,512]{2,1,0:T(8,128)(2,1)} %param.9, f32[512]{0:T(512)} %param.13, f32[32,16]{1,0:T(8,128)S(1)} %add_rsqrt_fusion), kind=kOutput, calls=%fused_computation.15 | convolution fusion | flops 807141376 | bytes 3674112 | tf_op jit(solution)/shard_map/tbd,de->tbe/dot_general | solution.py:188
  12.2 4.0 %reshape.302 = bf16[32,16,3,8,64]{4,3,2,1,0:T(8,128)(2,1)S(1)} reshape(bf16[32,16,1536]{2,1,0:T(8,128)(2,1)} %convolution_convert_fusion.2) | data formatting | bytes 3145728 | tf_op jit(solution)/shard_map/reshape | solution.py:136
  16.2 2.1 %fusion.90 = (bf16[32,16,1,8,64]{4,3,2,1,0:T(8,128)(2,1)}, bf16[32,16,1,8,64]{4,3,2,1,0:T(8,128)(2,1)}, bf16[32,16,1,8,64]{4,3,2,1,0:T(8,128)(2,1)}) fusion(bf16[32,16,3,8,64]{4,3,2,1,0:T(8,128)(2,1)S(1)} %reshape.302), kind=kLoop, calls=%fused_computation.135 | loop fusion | bytes 3145728 | tf_op jit(solution)/shard_map/slice | solution.py:139
  18.8 2.9 %fusion.91 = (f32[32,8,16]{2,1,0:T(8,128)S(1)}, f32[32,8,16,16]{2,3,1,0:T(8,128)S(1)}) fusion(pred[32,16,16]{1,2,0:T(8,128)(4,1)S(1)} %and_or_fusion, bf16[32,16,1,8,64]{4,3,2,1,0:T(8,128)(2,1)} %get-tuple-element.29, bf16[32,16,1,8,64]{4,3,2,1,0:T(8,128)(2,1)} %get-tuple-element.28), kind=kOutput, calls=%fused_computation.136 | convolution fusion | flops 8650767 | bytes 1335296 | tf_op jit(solution)/shard_map/sub | solution.py:39
  21.8 1.3 copy-done.32
  23.7 1.0 copy-done.10
  25.6 1.7 fusion.36
  27.3 1.1 copy.100
  28.4 7.4 %all-to-all-start = ((bf16[32,16,512]{2,0,1:T(8,128)(2,1)}), bf16[32,16,512]{2,0,1:T(8,128)(2,1)S(1)}, u32[]{:S(2)}, u32[]{:S(2)}) async-start(bf16[32,16,512]{2,0,1:T(8,128)(2,1)} %copy.100), calls=%async_computation | async-start | bytes 1048576 | tf_op jit(solution)/shard_map/all_to_all | solution.py:234
  35.8 1.0 copy.106
  37.0 2.3 %convolution_convert_fusion.13 = bf16[512,512]{0,1:T(8,128)(2,1)} fusion(bf16[512,1,512]{2,0,1:T(8,128)(2,1)S(1)} %copy-done.17, bf16[512,2048]{1,0:T(8,128)(2,1)} %param.12), kind=kOutput, calls=%fused_computation.59 | convolution fusion | flops 268697600 | bytes 1572864 | tf_op jit(solution)/shard_map/tbe,de->tbd/dot_general | solution.py:192
  39.3 10.9 %all-to-all-done = bf16[32,16,512]{2,0,1:T(8,128)(2,1)S(1)} async-done(((bf16[32,16,512]{2,0,1:T(8,128)(2,1)}), bf16[32,16,512]{2,0,1:T(8,128)(2,1)S(1)}, u32[]{:S(2)}, u32[]{:S(2)}) %all-to-all-start) | async-done | bytes 524320 | tf_op jit(solution)/shard_map/all_to_all | solution.py:234
  51.7 3.6 %convolution_convert_fusion.1 = bf16[512,1536]{1,0:T(8,128)(2,1)} fusion(bf16[512,2048]{1,0:T(8,128)(2,1)} %param.12, f32[512,512]{0,1:T(8,128)S(1)} %copy.103, f32[512]{0:T(512)S(1)} %copy-done.30, f32[512]{0:T(512)S(1)} %rsqrt.21), kind=kOutput, calls=%fused_computation.14 | convolution fusion | flops 806879232 | bytes 4198400 | tf_op jit(solution)/shard_map/tbd,de->tbe/dot_general | solution.py:188
  55.4 1.7 copy.104
  57.1 5.4 %fusion.92 = (f32[8,512]{1,0:T(8,128)S(1)}, f32[8,512,512]{1,2,0:T(8,128)}) fusion(pred[512,512]{0,1:T(8,128)(4,1)S(1)} %broadcast_compare_fusion, bf16[512,3,8,64]{0,3,2,1:T(8,128)(2,1)S(1)} %bitcast.185), kind=kOutput, calls=%fused_computation.137 | convolution fusion | flops 276824576 | bytes 9715712 | tf_op jit(solution)/shard_map/while/body/eval_jaxpr/sub | solution.py:39
  62.5 4.7 %fusion.6 = bf16[8,512,512]{1,2,0:T(8,128)(2,1)S(1)} fusion(f32[8,512,512]{1,2,0:T(8,128)} %get-tuple-element.42, f32[8,512]{1,0:T(8,128)S(1)} %get-tuple-element.41), kind=kLoop, calls=%fused_computation.10 | loop fusion | flops 4194304 | bytes 12599296 | tf_op jit(solution)/shard_map/while/body/eval_jaxpr/convert_element_type | solution.py:48
  68.0 1.4 fusion.42
  69.4 1.4 copy-done.3
  70.8 1.8 multiply_convert_fusion
  72.6 1.4 fusion.41
  75.0 1.2 copy-done.13
  76.2 1.0 copy-done.26
  77.2 1.0 multiply_reduce_fusion.1
  79.1 1.1 reduce.7
  80.4 1.2 reshape.323
  81.6 4.2 %all-to-all-start.1 = ((bf16[16,2,8192]{2,1,0:T(2,128)(2,1)}), bf16[16,2,8192]{2,1,0:T(2,128)(2,1)S(1)}, u32[]{:S(2)}, u32[]{:S(2)}) async-start(bf16[16,2,8192]{2,1,0:T(2,128)(2,1)} %reshape.323), calls=%async_computation.1 | async-start | bytes 1048576 | tf_op jit(solution)/shard_map/all_to_all | solution.py:266
  86.1 2.2 %reshape.322 = bf16[8,2,32,16,32]{2,1,0,3,4:T(2,128)(2,1)} reshape(bf16[512,16,32]{0,1,2:T(8,128)(2,1)S(1)} %bitcast.196) | data formatting | bytes 1048576 | tf_op jit(solution)/shard_map/tbd,tbe->de/dot_general | solution.py:198
  88.8 2.6 %convolution_convert_fusion = bf16[512,1536]{1,0:T(8,128)(2,1)S(1)} fusion(bf16[512,1536]{0,1:T(8,128)(2,1)} %bitcast.200, f32[512,1,1,1,1,1,512]{6,0,5,4,3,2,1:T(8,128)S(1)} %bitcast.183, f32[512]{0:T(512)S(1)} %copy-done.30, f32[512]{0:T(512)S(1)} %rsqrt.21), kind=kOutput, calls=%fused_computation.13 | convolution fusion | flops 806879232 | bytes 4198400 | tf_op jit(solution)/shard_map/tbd,tbe->de/dot_general | solution.py:198
  91.4 1.6 pad_maximum_fusion.1
  93.0 7.3 %all-to-all-done.1 = bf16[16,2,8192]{2,1,0:T(2,128)(2,1)S(1)} async-done(((bf16[16,2,8192]{2,1,0:T(2,128)(2,1)}), bf16[16,2,8192]{2,1,0:T(2,128)(2,1)S(1)}, u32[]{:S(2)}, u32[]{:S(2)}) %all-to-all-start.1) | async-done | bytes 524320 | tf_op jit(solution)/shard_map/all_to_all | solution.py:266
  101.8 1.5 convolution_convert_fusion.10
  103.9 2.5 %fusion.29 = bf16[1,32,8,16,64]{4,3,2,1,0:T(8,128)(2,1)S(1)} fusion(bf16[32,16,8,64]{3,2,1,0:T(8,128)(2,1)S(1)} %reshape.309, f32[32,8,16,16]{2,3,1,0:T(8,128)} %copy-done.32, f32[32,8,16]{2,1,0:T(8,128)S(1)} %copy-done.35), kind=kOutput, calls=%fused_computation.50 | convolution fusion | flops 8781824 | bytes 1327104 | tf_op jit(solution)/shard_map/...qk,...qd->...kd/dot_general | solution.py:67
  111.5 0.8 copy.117
  112.3 3.0 %reshape.310 = bf16[32,16,1536]{2,1,0:T(8,128)(2,1)} reshape(bf16[32,16,3,8,64]{4,3,2,1,0:T(8,128)(2,1)S(1)} %copy.117) | data formatting | bytes 3145728 | tf_op jit(solution)/shard_map/reshape | solution.py:169
  115.3 2.9 %reshape.317 = bf16[32,16,1536,1,1]{2,1,0,3,4:T(8,128)(2,1)} reshape(bf16[32,16,3,8,64]{4,3,2,1,0:T(8,128)(2,1)S(1)} %copy.117) | data formatting | bytes 3145728 | tf_op jit(solution)/shard_map/reshape | solution.py:169
  118.2 3.2 %fusion.51 = (f32[32,16]{1,0:T(8,128)S(1)}, f32[32,16,512]{2,1,0:T(8,128)S(1)}) fusion(bf16[32,16,512]{2,1,0:T(8,128)(2,1)} %param.9, f32[512]{0:T(512)S(1)} %copy-done.29, bf16[32,16,1536]{2,1,0:T(8,128)(2,1)} %reshape.310, bf16[512,2048]{1,0:T(8,128)(2,1)} %param.11), kind=kOutput, calls=%fused_computation.76 | convolution fusion | flops 806354432 | bytes 4722688 | tf_op jit(solution)/shard_map/tbe,de->tbd/dot_general | solution.py:192
  121.4 1.3 fusion.82
  122.8 2.2 %dot_general.110 = bf16[8,2,32,16,32]{2,1,0,3,4:T(2,128)(2,1)} reshape(bf16[512,16,32]{0,1,2:T(8,128)(2,1)S(1)} %get-tuple-element.31) | data formatting | bytes 1048576 | tf_op jit(solution)/shard_map/tbd,tbe->de/dot_general | solution.py:198
  125.0 1.0 fusion.33
  126.5 2.7 %fusion.7 = bf16[8,2,32,1536]{3,2,1,0:T(8,128)(2,1)S(1)} fusion(bf16[8,2,32,16,32]{2,1,0,3,4:T(2,128)(2,1)S(1)} %copy-done.16, bf16[32,16,1536,1,1]{2,1,0,3,4:T(8,128)(2,1)} %reshape.317), kind=kOutput, calls=%fused_computation.16 | convolution fusion | flops 806092800 | bytes 3670016 | tf_op jit(solution)/shard_map/tbd,tbe->de/dot_general | solution.py:198
  129.8 5.4 %all_to_all.37 = bf16[8,2,32,2048]{3,2,0,1:T(8,128)(2,1)S(1)} all-to-all(bf16[8,2,32,2048]{3,2,0,1:T(8,128)(2,1)S(1)} %copy.122), channel_id=1, replica_groups=mesh['groups'=2,'outer'=8,'core'=2] {'core'}, dimensions={1} | all-to-all | bytes 4194304 | tf_op jit(solution)/shard_map/all_to_all | solution.py:205
  135.2 1.7 reduce_sum.122
  136.9 4.1 %all-to-all-start.3 = ((bf16[8,32,2048]{2,1,0:T(8,128)(2,1)}), bf16[8,32,2048]{2,1,0:T(8,128)(2,1)S(1)}, u32[]{:S(2)}, u32[]{:S(2)}) async-start(bf16[8,32,2048]{2,1,0:T(8,128)(2,1)} %reduce_sum.122), calls=%async_computation.3 | async-start | bytes 2097152 | tf_op jit(solution)/shard_map/all_to_all | solution.py:207
  141.0 2.3 %fusion.40 = bf16[512,1,512]{2,0,1:T(8,128)(2,1)} fusion(f32[512,512]{1,0:T(8,128)S(1)} %bitcast.184, bf16[512,512]{0,1:T(8,128)(2,1)S(1)} %bitcast.191, bf16[512,2048]{1,0:T(8,128)(2,1)} %param.12), kind=kOutput, calls=%fused_computation.65 | convolution fusion | flops 268959744 | bytes 2621440 | tf_op jit(solution)/shard_map/tbd,de->tbe/dot_general | solution.py:188
  143.3 28.0 %all-to-all-done.3 = bf16[8,32,2048]{2,1,0:T(8,128)(2,1)S(1)} async-done(((bf16[8,32,2048]{2,1,0:T(8,128)(2,1)}), bf16[8,32,2048]{2,1,0:T(8,128)(2,1)S(1)}, u32[]{:S(2)}, u32[]{:S(2)}) %all-to-all-start.3) | async-done | bytes 1048608 | tf_op jit(solution)/shard_map/all_to_all | solution.py:207
  171.3 0.8 convert_reduce_fusion
  172.1 1.6 convert_element_type.234
  (109 shorter events, 15.4 us)
Async XLA Ops:
  16.2 2.2 %copy-start.28 = (s32[16,16]{1,0:T(8,128)S(1)}, s32[16,16]{1,0:T(8,128)}, u32[]{:S(2)}) copy-start(s32[16,16]{1,0:T(8,128)} %param.15) | copy-start | bytes 3076
  16.2 2.3 %copy-start.27 = (s32[512]{0:T(512)S(1)}, s32[512]{0:T(512)}, u32[]{:S(2)}) copy-start(s32[512]{0:T(512)} %param.17) | copy-start | bytes 6148
  16.2 2.3 %copy-start.31 = (s32[4]{0:T(128)S(1)}, s32[4]{0:T(128)}, u32[]{:S(2)}) copy-start(s32[4]{0:T(128)} %param.16) | copy-start | bytes 52
  18.8 4.3 %copy-start.24 = (bf16[32,16,1,8,64]{4,3,2,1,0:T(8,128)(2,1)S(1)}, bf16[32,16,1,8,64]{4,3,2,1,0:T(8,128)(2,1)}, u32[]{:S(2)}) copy-start(bf16[32,16,1,8,64]{4,3,2,1,0:T(8,128)(2,1)} %get-tuple-element.30) | copy-start | bytes 1572868
  21.8 1.4 copy-start.32
  21.8 1.9 %copy-start.34 = (f32[32,8,16]{2,1,0:T(8,128)}, f32[32,8,16]{2,1,0:T(8,128)S(1)}, u32[]{:S(2)}) copy-start(f32[32,8,16]{2,1,0:T(8,128)S(1)} %get-tuple-element.33) | copy-start | bytes 49156
  23.7 1.0 copy-start.10
  23.7 1.9 %copy-start.19 = (bf16[32,16,512]{2,1,0:T(8,128)(2,1)S(1)}, bf16[32,16,512]{2,1,0:T(8,128)(2,1)}, u32[]{:S(2)}) copy-start(bf16[32,16,512]{2,1,0:T(8,128)(2,1)} %param.9) | copy-start | bytes 1572868
  25.6 2.8 %copy-start.14 = (bf16[32,16,512]{2,1,0:T(8,128)(2,1)}, bf16[32,16,512]{2,1,0:T(8,128)(2,1)S(1)}, u32[]{:S(2)}) copy-start(bf16[32,16,512]{2,1,0:T(8,128)(2,1)S(1)} %reshape.303) | copy-start | bytes 1572868
  25.6 10.2 %copy-start.17 = (bf16[512,1,512]{2,0,1:T(8,128)(2,1)S(1)}, bf16[512,1,512]{2,0,1:T(8,128)(2,1)}, u32[]{:S(2)}) copy-start(bf16[512,1,512]{2,0,1:T(8,128)(2,1)} %param.10) | copy-start | bytes 1572868
  28.4 21.9 %all-to-all-start = ((bf16[32,16,512]{2,0,1:T(8,128)(2,1)}), bf16[32,16,512]{2,0,1:T(8,128)(2,1)S(1)}, u32[]{:S(2)}, u32[]{:S(2)}) async-start(bf16[32,16,512]{2,0,1:T(8,128)(2,1)} %copy.100), calls=%async_computation | async-start | bytes 1048576 | tf_op jit(solution)/shard_map/all_to_all | solution.py:234
  39.3 12.4 %copy-start.30 = (f32[512]{0:T(512)S(1)}, f32[512]{0:T(512)}, u32[]{:S(2)}) copy-start(f32[512]{0:T(512)} %param.14) | copy-start | bytes 6148
  50.4 38.4 %copy-start = (f32[32,16,512]{2,0,1:T(8,128)}, f32[32,16,512]{2,0,1:T(8,128)S(1)}, u32[]{:S(2)}) copy-start(f32[32,16,512]{2,0,1:T(8,128)S(1)} %convert_element_type.239) | copy-start | bytes 3145732
  50.7 1.0 copy-start.12
  62.5 4.7 %copy-start.22 = (bf16[512,512]{0,1:T(8,128)(2,1)S(1)}, bf16[512,512]{0,1:T(8,128)(2,1)}, u32[]{:S(2)}) copy-start(bf16[512,512]{0,1:T(8,128)(2,1)} %convolution_convert_fusion.13) | copy-start | bytes 1572868
  67.2 3.6 %copy-start.3 = (f32[8,512,512]{1,2,0:T(8,128)S(1)}, f32[8,512,512]{1,2,0:T(8,128)}, u32[]{:S(2)}) copy-start(f32[8,512,512]{1,2,0:T(8,128)} %get-tuple-element.42) | copy-start | bytes 25165828
  68.0 20.3 %copy-start.4 = (bf16[8,512,64]{1,2,0:T(8,128)(2,1)}, bf16[8,512,64]{1,2,0:T(8,128)(2,1)S(1)}, u32[]{:S(2)}) copy-start(bf16[8,512,64]{1,2,0:T(8,128)(2,1)S(1)} %get-tuple-element.44) | copy-start | bytes 1572868
  74.7 1.5 copy-start.13
  74.8 2.5 %copy-start.26 = (bf16[512,2048]{1,0:T(8,128)(2,1)S(1)}, bf16[512,2048]{1,0:T(8,128)(2,1)}, u32[]{:S(2)}) copy-start(bf16[512,2048]{1,0:T(8,128)(2,1)} %param.12) | copy-start | bytes 6291460
  75.0 3.3 %copy-start.23 = (bf16[3,8,512,64]{2,3,1,0:T(8,128)(2,1)}, bf16[3,8,512,64]{2,3,1,0:T(8,128)(2,1)S(1)}, u32[]{:S(2)}) copy-start(bf16[3,8,512,64]{2,3,1,0:T(8,128)(2,1)S(1)} %pad_maximum_fusion.2) | copy-start | bytes 4718596
  77.2 1.0 copy-start.21
  79.1 7.0 %copy-start.15 = (bf16[32,16,512]{2,1,0:T(8,128)(2,1)S(1)}, bf16[32,16,512]{2,1,0:T(8,128)(2,1)}, u32[]{:S(2)}) copy-start(bf16[32,16,512]{2,1,0:T(8,128)(2,1)} %copy-done.14) | copy-start | bytes 1572868
  81.6 6.7 %copy-start.18 = (bf16[512,1,512]{2,0,1:T(8,128)(2,1)S(1)}, bf16[512,1,512]{2,0,1:T(8,128)(2,1)}, u32[]{:S(2)}) copy-start(bf16[512,1,512]{2,0,1:T(8,128)(2,1)} %param.10) | copy-start | bytes 1572868
  81.6 18.7 %all-to-all-start.1 = ((bf16[16,2,8192]{2,1,0:T(2,128)(2,1)}), bf16[16,2,8192]{2,1,0:T(2,128)(2,1)S(1)}, u32[]{:S(2)}, u32[]{:S(2)}) async-start(bf16[16,2,8192]{2,1,0:T(2,128)(2,1)} %reshape.323), calls=%async_computation.1 | async-start | bytes 1048576 | tf_op jit(solution)/shard_map/all_to_all | solution.py:266
  85.9 86.3 %reduce-scatter.2.cloned.1.call-start = ((), (), s32[]{:S(2)}) async-start(), calls=%async_computation.5 | async-start | bytes 2228224 | tf_op jit(solution)/shard_map/reduce_scatter | solution.py:269
  101.0 0.8 copy-start.6
  101.0 2.9 %copy-start.35 = (f32[32,8,16]{2,1,0:T(8,128)S(1)}, f32[32,8,16]{2,1,0:T(8,128)}, u32[]{:S(2)}) copy-start(f32[32,8,16]{2,1,0:T(8,128)} %copy-done.34) | copy-start | bytes 49156
  103.9 2.5 %copy-start.11 = (bf16[32,8,16,64]{3,2,1,0:T(8,128)(2,1)S(1)}, bf16[32,8,16,64]{3,2,1,0:T(8,128)(2,1)}, u32[]{:S(2)}) copy-start(bf16[32,8,16,64]{3,2,1,0:T(8,128)(2,1)} %copy-done.10) | copy-start | bytes 1572868
  103.9 3.1 %copy-start.33 = (f32[32,8,16,16]{2,3,1,0:T(8,128)S(1)}, f32[32,8,16,16]{2,3,1,0:T(8,128)}, u32[]{:S(2)}) copy-start(f32[32,8,16,16]{2,3,1,0:T(8,128)} %copy-done.32) | copy-start | bytes 786436
  106.4 1.3 copy-start.25
  107.7 1.3 copy-start.9
  108.9 1.3 copy-start.8
  115.3 2.9 %copy-start.29 = (f32[512]{0:T(512)S(1)}, f32[512]{0:T(512)}, u32[]{:S(2)}) copy-start(f32[512]{0:T(512)} %param.13) | copy-start | bytes 6148
  118.2 3.2 %copy-start.7 = (bf16[512,1,512]{2,0,1:T(8,128)(2,1)S(1)}, bf16[512,1,512]{2,0,1:T(8,128)(2,1)}, u32[]{:S(2)}) copy-start(bf16[512,1,512]{2,0,1:T(8,128)(2,1)} %copy-done.6) | copy-start | bytes 1572868
  118.2 3.2 %copy-start.20 = (bf16[32,16,512]{2,1,0:T(8,128)(2,1)S(1)}, bf16[32,16,512]{2,1,0:T(8,128)(2,1)}, u32[]{:S(2)}) copy-start(bf16[32,16,512]{2,1,0:T(8,128)(2,1)} %param.9) | copy-start | bytes 1572868
  122.8 2.2 %copy-start.2 = (bf16[8,2,32,16,32]{2,1,0,3,4:T(2,128)(2,1)S(1)}, bf16[8,2,32,16,32]{2,1,0,3,4:T(2,128)(2,1)}, u32[]{:S(2)}) copy-start(bf16[8,2,32,16,32]{2,1,0,3,4:T(2,128)(2,1)} %reshape.322) | copy-start | bytes 1572868
  125.0 1.6 copy-start.16
  135.2 5.8 %copy-start.1 = (f32[32,16,512]{2,0,1:T(8,128)S(1)}, f32[32,16,512]{2,0,1:T(8,128)}, u32[]{:S(2)}) copy-start(f32[32,16,512]{2,0,1:T(8,128)} %copy-done) | copy-start | bytes 3145732
  136.9 4.1 %copy-start.5 = (bf16[8,512,64]{1,2,0:T(8,128)(2,1)S(1)}, bf16[8,512,64]{1,2,0:T(8,128)(2,1)}, u32[]{:S(2)}) copy-start(bf16[8,512,64]{1,2,0:T(8,128)(2,1)} %copy-done.4) | copy-start | bytes 1572868
  136.9 34.4 %all-to-all-start.3 = ((bf16[8,32,2048]{2,1,0:T(8,128)(2,1)}), bf16[8,32,2048]{2,1,0:T(8,128)(2,1)S(1)}, u32[]{:S(2)}, u32[]{:S(2)}) async-start(bf16[8,32,2048]{2,1,0:T(8,128)(2,1)} %reduce_sum.122), calls=%async_computation.3 | async-start | bytes 2097152 | tf_op jit(solution)/shard_map/all_to_all | solution.py:207
Sparse Core Ops, SparseCore 0:
  93.1 64.6 reduce-scatter.1

commit v3 on v1

--- a/solution.py
+++ b/solution.py
@@ -206,6 +206,12 @@
     pieces = jnp.sum(pieces.astype(jnp.float32), axis=1).astype(jnp.bfloat16)
     pieces = lax.all_to_all(pieces, "outer", 0, 0, tiled=True)
     return jnp.sum(pieces.astype(jnp.float32), axis=0)
+
+
+def scatter_rows(partial):
+    return lax.psum_scatter(
+        partial.astype(jnp.bfloat16), ("outer", "core"), scatter_dimension=0, tiled=True
+    ).astype(jnp.float32)
 
 
 def per_device(
@@ -266,18 +272,22 @@
     grad_middle_time = lax.all_to_all(grad_middle, ("outer", "core"), split_axis=0, concat_axis=1, tiled=True)
     normed_cols = normed_two
     context_cols = temporal_context
-    temporal_grad = reduce_rows(
+    temporal_grad = scatter_rows(
         jnp.concatenate(
             [weight_term(normed_cols, grad_temporal_proj), weight_term(context_cols, grad_out)],
             axis=1,
         )
     )
+    spatial_term = weight_term(spatial_context, grad_middle_time)
+    spatial_term, grad_middle_time = lax.optimization_barrier((spatial_term, grad_middle_time))
     grad_spatial_context = project_back(
         grad_middle_time, spatial_weights[:, 3 * model_width :]
     ).astype(jnp.bfloat16)
     grad_spatial_proj = spatial_backward(
         spatial_proj, allowed_space, spatial_context, grad_spatial_context
     )
+    spatial_term = reduce_rows(spatial_term)
+    spatial_term, grad_spatial_proj = lax.optimization_barrier((spatial_term, grad_spatial_proj))
     grad_normed_one = project_back(grad_spatial_proj, spatial_weights[:, : 3 * model_width])
     grad_activity = (
         grad_middle_time.astype(jnp.float32)
@@ -285,14 +295,12 @@
     ).astype(jnp.bfloat16)
     normed_cols = normed_one
     context_cols = spatial_context
-    spatial_grad = reduce_rows(
-        jnp.concatenate(
-            [
-                weight_term(normed_cols, grad_spatial_proj),
-                weight_term(context_cols, grad_middle_time),
-            ],
-            axis=1,
-        )
+    spatial_grad = jnp.concatenate(
+        [
+            reduce_rows(weight_term(normed_cols, grad_spatial_proj)),
+            spatial_term,
+        ],
+        axis=1,
     )
     return (layer_out, grad_activity, spatial_grad, temporal_grad)
 

time: 200 us -> 179 us (0.90)
  waiting for transfers between devices: 67.5 us -> 41 us
  between operations: 1.3 us -> 14.7 us
  local copies, waits for them, and re-layouts: 35.8 us -> 27.5 us
  matrix products: 45.2 us -> 47.2 us
    all_to_all x2, waiting for transfers between devices: 46.1 us -> 20.6 us  [reduce_rows(): pieces = lax.all_to_all(pieces, 'outer', 0, 0, tiled=True)]
    dot_general x2 -> x0, local copies, waits for them, and re-layouts: 4.39 us -> none  [weight_term(): jnp.einsum('tbd,tbe->de', left, right, preferred_element_type=jnp.float32)]
    reshape x2 -> x1, local copies, waits for them, and re-layouts: 5.9 us -> 2.95 us  [spatial_backward(): jnp.stack(derivative_collection, axis=0).transpose(1, 3, 0, 2, 4)]
    reduce_sum x2, other arithmetic: 2.93 us -> 0.14 us  [reduce_rows(): return jnp.sum(pieces.astype(jnp.float32), axis=0)]
    convert_element_type x1 -> x2, other arithmetic: 0.16 us -> 2.83 us  [the longest x1 1.62 us: scatter_rows(): return lax.psum_scatter(partial.astype(jnp.bfloat16), ('outer', 'core'),...]
    unnamed x78 -> x76, local copies, waits for them, and re-layouts: 12.7 us -> 11.8 us
  transfers between devices with their start and end apart: 4 -> 5, of which waited for: 4 -> 4; matrix products, arithmetic and copies ran while one was open for 7% -> 20% of each run, Pallas kernels for 0% -> 0%
where the time goes in v3:
time: 179 us; the launch traced here: 177 us
  matrix products  47.2 us (26%)
  waiting for transfers between devices  41 us (23%)
  local copies, waits for them, and re-layouts  27.5 us (15%)
  starting transfers between devices  20.4 us (11%)
  other arithmetic  17.2 us (10%)
  between operations  14.7 us (8%)
  blocking collectives  9.28 us (5%)
    all_to_all x2, waiting for transfers between devices, reduce_rows(): pieces = lax.all_to_all(pieces, 'outer', 0, 0, tiled=True)  20.6 us
    unnamed x76, local copies, waits for them, and re-layouts  11.8 us
    dot_general x4, matrix products, project(): jnp.einsum('tbd,de->tbe', rows, coefficient_array, preferred_element_type...  11.5 us
    all_to_all x1, waiting for transfers between devices, per_device(): lax.all_to_all(middle, ('outer', 'core'), split_axis=1, concat_axis=0, ti...  10.9 us
    all_to_all x1, waiting for transfers between devices, per_device(): lax.all_to_all(grad_middle, ('outer', 'core'), split_axis=0, concat_axis=...  9.48 us
    all_to_all x2, blocking collectives, reduce_rows(): pieces = lax.all_to_all(pieces, 'core', 1, 1, tiled=True)  9.28 us
    all_to_all x2, starting transfers between devices, reduce_rows(): pieces = lax.all_to_all(pieces, 'outer', 0, 0, tiled=True)  8.67 us
    sub x2, matrix products, normalized_affinity(): expo = jnp.exp(unnormalized_affinities - row_max)  8.32 us
  transfers between devices with their start and end apart: 5, of which 4 were waited for; matrix products, arithmetic and copies ran while one was open for 20% of the time, Pallas kernels for 0%

profile of v3, /device:TPU:0, one launch (start us, length us, event | category | flops | bytes accessed | tf_op | source)
XLA Modules:
  0.0 177.4 jit_solution(9739659558736357842)
XLA Ops:
  7.2 1.2 fusion.40
  8.4 3.8 %convolution_convert_fusion.2 = bf16[32,16,1536]{2,1,0:T(8,128)(2,1)} fusion(bf16[512,2048]{1,0:T(8,128)(2,1)} %param.11, bf16[32,16,512]{2,1,0:T(8,128)(2,1)} %param.9, f32[512]{0:T(512)} %param.13, f32[32,16]{1,0:T(8,128)S(1)} %add_rsqrt_fusion), kind=kOutput, calls=%fused_computation.15 | convolution fusion | flops 807141376 | bytes 3674112 | tf_op jit(solution)/shard_map/tbd,de->tbe/dot_general | solution.py:188
  12.2 4.0 %reshape.303 = bf16[32,16,3,8,64]{4,3,2,1,0:T(8,128)(2,1)S(1)} reshape(bf16[32,16,1536]{2,1,0:T(8,128)(2,1)} %convolution_convert_fusion.2) | data formatting | bytes 3145728 | tf_op jit(solution)/shard_map/reshape | solution.py:136
  16.2 2.2 %fusion.77 = (bf16[32,16,1,8,64]{4,3,2,1,0:T(8,128)(2,1)}, bf16[32,16,1,8,64]{4,3,2,1,0:T(8,128)(2,1)}, bf16[32,16,1,8,64]{4,3,2,1,0:T(8,128)(2,1)}) fusion(bf16[32,16,3,8,64]{4,3,2,1,0:T(8,128)(2,1)S(1)} %reshape.303), kind=kLoop, calls=%fused_computation.128 | loop fusion | bytes 3145728 | tf_op jit(solution)/shard_map/slice | solution.py:139
  18.9 2.9 %fusion.78 = (f32[32,8,16]{2,1,0:T(8,128)S(1)}, f32[32,8,16,16]{2,3,1,0:T(8,128)S(1)}) fusion(pred[32,16,16]{1,2,0:T(8,128)(4,1)S(1)} %and_or_fusion, bf16[32,16,1,8,64]{4,3,2,1,0:T(8,128)(2,1)} %get-tuple-element.43, bf16[32,16,1,8,64]{4,3,2,1,0:T(8,128)(2,1)} %get-tuple-element.42), kind=kOutput, calls=%fused_computation.129 | convolution fusion | flops 8650767 | bytes 1335296 | tf_op jit(solution)/shard_map/sub | solution.py:39
  21.8 1.4 copy-done.32
  23.8 1.0 copy-done.7
  25.6 1.7 fusion.26
  27.3 1.1 copy.97
  28.4 7.4 %all-to-all-start = ((bf16[32,16,512]{2,0,1:T(8,128)(2,1)}), bf16[32,16,512]{2,0,1:T(8,128)(2,1)S(1)}, u32[]{:S(2)}, u32[]{:S(2)}) async-start(bf16[32,16,512]{2,0,1:T(8,128)(2,1)} %copy.97), calls=%async_computation | async-start | bytes 1048576 | tf_op jit(solution)/shard_map/all_to_all | solution.py:240
  35.8 1.0 copy.103
  37.0 2.3 %convolution_convert_fusion.13 = bf16[512,512]{0,1:T(8,128)(2,1)} fusion(bf16[512,1,512]{2,0,1:T(8,128)(2,1)S(1)} %copy-done.11, bf16[512,2048]{1,0:T(8,128)(2,1)} %param.12), kind=kOutput, calls=%fused_computation.54 | convolution fusion | flops 268697600 | bytes 1572864 | tf_op jit(solution)/shard_map/tbe,de->tbd/dot_general | solution.py:192
  39.4 10.9 %all-to-all-done = bf16[32,16,512]{2,0,1:T(8,128)(2,1)S(1)} async-done(((bf16[32,16,512]{2,0,1:T(8,128)(2,1)}), bf16[32,16,512]{2,0,1:T(8,128)(2,1)S(1)}, u32[]{:S(2)}, u32[]{:S(2)}) %all-to-all-start) | async-done | bytes 524320 | tf_op jit(solution)/shard_map/all_to_all | solution.py:240
  51.7 3.7 %convolution_convert_fusion.1 = bf16[512,1536]{1,0:T(8,128)(2,1)} fusion(bf16[512,2048]{1,0:T(8,128)(2,1)} %param.12, f32[512,512]{0,1:T(8,128)S(1)} %copy.100, f32[512]{0:T(512)S(1)} %copy-done.29, f32[512]{0:T(512)S(1)} %rsqrt.21), kind=kOutput, calls=%fused_computation.14 | convolution fusion | flops 806879232 | bytes 4198400 | tf_op jit(solution)/shard_map/tbd,de->tbe/dot_general | solution.py:188
  55.4 1.7 copy.101
  57.1 5.4 %fusion.79 = (f32[8,512]{1,0:T(8,128)S(1)}, f32[8,512,512]{1,2,0:T(8,128)}) fusion(pred[512,512]{0,1:T(8,128)(4,1)S(1)} %broadcast_compare_fusion, bf16[512,3,8,64]{0,3,2,1:T(8,128)(2,1)S(1)} %bitcast.170), kind=kOutput, calls=%fused_computation.130 | convolution fusion | flops 276824576 | bytes 9715712 | tf_op jit(solution)/shard_map/while/body/eval_jaxpr/sub | solution.py:39
  62.5 4.7 %fusion.6 = bf16[8,512,512]{1,2,0:T(8,128)(2,1)S(1)} fusion(f32[8,512,512]{1,2,0:T(8,128)} %get-tuple-element.48, f32[8,512]{1,0:T(8,128)S(1)} %get-tuple-element.47), kind=kLoop, calls=%fused_computation.10 | loop fusion | flops 4194304 | bytes 12599296 | tf_op jit(solution)/shard_map/while/body/eval_jaxpr/convert_element_type | solution.py:48
  68.0 1.4 fusion.32
  69.4 1.4 copy-done.2
  70.8 1.8 %multiply_convert_fusion = bf16[8,512,512]{1,2,0:T(8,128)(2,1)S(1)} fusion(f32[8,512]{1,0:T(8,128)S(1)} %get-tuple-element.49, f32[8,512,512]{1,2,0:T(8,128)S(1)} %copy-done.2, f32[8,512]{1,0:T(8,128)S(1)} %get-tuple-element.47, bf16[8,512,64]{1,2,0:T(8,128)(2,1)S(1)} %bitcast.183, bf16[512,3,8,64]{0,3,2,1:T(8,128)(2,1)S(1)} %bitcast.172), kind=kOutput, calls=%fused_computation.2 | convolution fusion | flops 278921216 | bytes 13664256 | tf_op jit(solution)/shard_map/while/body/eval_jaxpr/...uo,...ao->...ua/dot_general | solution.py:73
  72.6 1.4 fusion.31
  75.0 1.2 copy-done.10
  76.2 1.0 copy-done.26
  77.3 1.0 multiply_reduce_fusion.1
  79.2 1.1 reduce.8
  80.5 1.2 reshape.322
  81.6 4.1 %all-to-all-start.1 = ((bf16[16,2,8192]{2,1,0:T(2,128)(2,1)}), bf16[16,2,8192]{2,1,0:T(2,128)(2,1)S(1)}, u32[]{:S(2)}, u32[]{:S(2)}) async-start(bf16[16,2,8192]{2,1,0:T(2,128)(2,1)} %reshape.322), calls=%async_computation.1 | async-start | bytes 1048576 | tf_op jit(solution)/shard_map/all_to_all | solution.py:272
  86.5 2.6 %convolution_convert_fusion = bf16[512,1536]{1,0:T(8,128)(2,1)S(1)} fusion(bf16[512,1536]{0,1:T(8,128)(2,1)} %bitcast.185, f32[512,1,1,1,1,1,512]{6,0,5,4,3,2,1:T(8,128)S(1)} %bitcast.168, f32[512]{0:T(512)S(1)} %copy-done.29, f32[512]{0:T(512)S(1)} %rsqrt.21), kind=kOutput, calls=%fused_computation.13 | convolution fusion | flops 806879232 | bytes 4198400 | tf_op jit(solution)/shard_map/tbd,tbe->de/dot_general | solution.py:198
  89.1 1.6 pad_maximum_fusion
  90.7 9.5 %all-to-all-done.1 = bf16[16,2,8192]{2,1,0:T(2,128)(2,1)S(1)} async-done(((bf16[16,2,8192]{2,1,0:T(2,128)(2,1)}), bf16[16,2,8192]{2,1,0:T(2,128)(2,1)S(1)}, u32[]{:S(2)}, u32[]{:S(2)}) %all-to-all-start.1) | async-done | bytes 524320 | tf_op jit(solution)/shard_map/all_to_all | solution.py:272
  102.6 1.5 convolution_convert_fusion.10
  104.7 3.4 %fusion.22 = bf16[1,32,8,16,64]{4,3,2,1,0:T(8,128)(2,1)} fusion(bf16[32,16,8,64]{3,2,1,0:T(8,128)(2,1)S(1)} %reshape.311, f32[32,8,16,16]{2,3,1,0:T(8,128)} %copy-done.32, f32[32,8,16]{2,1,0:T(8,128)S(1)} %copy-done.34), kind=kOutput, calls=%fused_computation.45 | convolution fusion | flops 8781824 | bytes 1327104 | tf_op jit(solution)/shard_map/...qk,...qd->...kd/dot_general | solution.py:67
  108.8 4.3 %all_to_all.47 = bf16[8,2,32,512]{3,2,0,1:T(8,128)(2,1)S(1)} all-to-all(bf16[8,2,32,512]{3,2,0,1:T(8,128)(2,1)S(1)} %copy.111), channel_id=1, replica_groups=mesh['groups'=2,'outer'=8,'core'=2] {'core'}, dimensions={1} | all-to-all | bytes 1048576 | tf_op jit(solution)/shard_map/all_to_all | solution.py:205
  113.0 0.8 reduce_sum.141
  113.9 4.0 %all-to-all-start.3 = ((bf16[8,32,512]{2,1,0:T(8,128)(2,1)}), bf16[8,32,512]{2,1,0:T(8,128)(2,1)S(1)}, u32[]{:S(2)}, u32[]{:S(2)}) async-start(bf16[8,32,512]{2,1,0:T(8,128)(2,1)} %reduce_sum.141), calls=%async_computation.3 | async-start | bytes 524288 | tf_op jit(solution)/shard_map/all_to_all | solution.py:207
  117.9 2.4 %multiply_convert_fusion.1 = bf16[32,8,16,16]{2,3,1,0:T(8,128)(2,1)S(1)} fusion(f32[32,8,16]{2,1,0:T(8,128)S(1)} %multiply_reduce_fusion, bf16[32,16,1,8,64]{4,3,2,1,0:T(8,128)(2,1)S(1)} %copy-done.22, bf16[32,16,8,64]{3,2,1,0:T(8,128)(2,1)S(1)} %reshape.311, f32[32,8,16,16]{2,3,1,0:T(8,128)} %copy-done.32, f32[32,8,16]{2,1,0:T(8,128)} %copy-done.33), kind=kOutput, calls=%fused_computation.18 | convolution fusion | flops 8716288 | bytes 1474560 | tf_op jit(solution)/shard_map/...uo,...ao->...ua/dot_general | solution.py:73
  123.5 0.8 copy.115
  124.4 2.9 %reshape.312 = bf16[32,16,1536]{2,1,0:T(8,128)(2,1)} reshape(bf16[32,16,3,8,64]{4,3,2,1,0:T(8,128)(2,1)S(1)} %copy.115) | data formatting | bytes 3145728 | tf_op jit(solution)/shard_map/reshape | solution.py:169
  127.3 3.7 %all-to-all-done.3 = bf16[8,32,512]{2,1,0:T(8,128)(2,1)S(1)} async-done(((bf16[8,32,512]{2,1,0:T(8,128)(2,1)}), bf16[8,32,512]{2,1,0:T(8,128)(2,1)S(1)}, u32[]{:S(2)}, u32[]{:S(2)}) %all-to-all-start.3) | async-done | bytes 262176 | tf_op jit(solution)/shard_map/all_to_all | solution.py:207
  131.0 2.7 %fusion.7 = bf16[512,1536]{1,0:T(8,128)(2,1)S(1)} fusion(bf16[32,16,1536]{2,1,0:T(8,128)(2,1)} %reshape.312, bf16[32,16,512]{2,1,0:T(8,128)(2,1)} %param.9, f32[512]{0:T(512)S(1)} %copy-done.30, f32[32,16]{1,0:T(8,128)S(1)} %add_rsqrt_fusion), kind=kOutput, calls=%fused_computation.16 | convolution fusion | flops 807141376 | bytes 3674112 | tf_op jit(solution)/shard_map/tbd,tbe->de/dot_general | solution.py:198
  133.9 5.0 %all_to_all.48 = bf16[8,2,32,1536]{3,2,0,1:T(8,128)(2,1)S(1)} all-to-all(bf16[8,2,32,1536]{3,2,0,1:T(8,128)(2,1)S(1)} %copy.116), channel_id=1, replica_groups=mesh['groups'=2,'outer'=8,'core'=2] {'core'}, dimensions={1} | all-to-all | bytes 3145728 | tf_op jit(solution)/shard_map/all_to_all | solution.py:205
  138.9 1.4 reduce_sum.145
  140.3 4.7 %all-to-all-start.5 = ((bf16[8,32,1536]{2,1,0:T(8,128)(2,1)}), bf16[8,32,1536]{2,1,0:T(8,128)(2,1)S(1)}, u32[]{:S(2)}, u32[]{:S(2)}) async-start(bf16[8,32,1536]{2,1,0:T(8,128)(2,1)} %reduce_sum.145), calls=%async_computation.5 | async-start | bytes 1572864 | tf_op jit(solution)/shard_map/all_to_all | solution.py:207
  144.9 2.4 %fusion.30 = bf16[512,1,512]{2,0,1:T(8,128)(2,1)} fusion(f32[512,512]{1,0:T(8,128)S(1)} %bitcast.169, bf16[512,512]{0,1:T(8,128)(2,1)S(1)} %bitcast.176, bf16[512,2048]{1,0:T(8,128)(2,1)} %param.12), kind=kOutput, calls=%fused_computation.59 | convolution fusion | flops 268959744 | bytes 2621440 | tf_op jit(solution)/shard_map/tbd,de->tbe/dot_general | solution.py:188
  147.4 2.6 %fusion.41 = (f32[32,16]{1,0:T(8,128)S(1)}, f32[32,16,512]{2,1,0:T(8,128)S(1)}) fusion(bf16[32,16,512]{2,1,0:T(8,128)(2,1)S(1)} %copy-done.14, f32[512]{0:T(512)S(1)} %copy-done.30, bf16[32,16,1536]{2,1,0:T(8,128)(2,1)S(1)} %copy-done.20, bf16[512,2048]{1,0:T(8,128)(2,1)} %param.11), kind=kOutput, calls=%fused_computation.70 | convolution fusion | flops 806354432 | bytes 4722688 | tf_op jit(solution)/shard_map/tbe,de->tbd/dot_general | solution.py:192
  150.0 1.2 fusion.39
  151.2 17.0 %all-to-all-done.5 = bf16[8,32,1536]{2,1,0:T(8,128)(2,1)S(1)} async-done(((bf16[8,32,1536]{2,1,0:T(8,128)(2,1)}), bf16[8,32,1536]{2,1,0:T(8,128)(2,1)S(1)}, u32[]{:S(2)}, u32[]{:S(2)}) %all-to-all-start.5) | async-done | bytes 786464 | tf_op jit(solution)/shard_map/all_to_all | solution.py:207
  169.0 1.6 convert_element_type.246
  (111 shorter events, 15.0 us)
Async XLA Ops:
  16.2 2.2 %copy-start.28 = (s32[16,16]{1,0:T(8,128)S(1)}, s32[16,16]{1,0:T(8,128)}, u32[]{:S(2)}) copy-start(s32[16,16]{1,0:T(8,128)} %param.15) | copy-start | bytes 3076
  16.2 2.3 %copy-start.27 = (s32[512]{0:T(512)S(1)}, s32[512]{0:T(512)}, u32[]{:S(2)}) copy-start(s32[512]{0:T(512)} %param.17) | copy-start | bytes 6148
  16.2 2.3 %copy-start.31 = (s32[4]{0:T(128)S(1)}, s32[4]{0:T(128)}, u32[]{:S(2)}) copy-start(s32[4]{0:T(128)} %param.16) | copy-start | bytes 52
  18.9 4.3 %copy-start.21 = (bf16[32,16,1,8,64]{4,3,2,1,0:T(8,128)(2,1)S(1)}, bf16[32,16,1,8,64]{4,3,2,1,0:T(8,128)(2,1)}, u32[]{:S(2)}) copy-start(bf16[32,16,1,8,64]{4,3,2,1,0:T(8,128)(2,1)} %get-tuple-element.44) | copy-start | bytes 1572868
  21.8 1.4 copy-start.32
  21.8 1.9 %copy-start.33 = (f32[32,8,16]{2,1,0:T(8,128)}, f32[32,8,16]{2,1,0:T(8,128)S(1)}, u32[]{:S(2)}) copy-start(f32[32,8,16]{2,1,0:T(8,128)S(1)} %get-tuple-element.45) | copy-start | bytes 49156
  23.7 1.0 copy-start.7
  23.7 1.9 %copy-start.13 = (bf16[32,16,512]{2,1,0:T(8,128)(2,1)S(1)}, bf16[32,16,512]{2,1,0:T(8,128)(2,1)}, u32[]{:S(2)}) copy-start(bf16[32,16,512]{2,1,0:T(8,128)(2,1)} %param.9) | copy-start | bytes 1572868
  25.6 2.8 %copy-start.24 = (bf16[32,16,512]{2,1,0:T(8,128)(2,1)}, bf16[32,16,512]{2,1,0:T(8,128)(2,1)S(1)}, u32[]{:S(2)}) copy-start(bf16[32,16,512]{2,1,0:T(8,128)(2,1)S(1)} %reshape.304) | copy-start | bytes 1572868
  25.6 10.2 %copy-start.11 = (bf16[512,1,512]{2,0,1:T(8,128)(2,1)S(1)}, bf16[512,1,512]{2,0,1:T(8,128)(2,1)}, u32[]{:S(2)}) copy-start(bf16[512,1,512]{2,0,1:T(8,128)(2,1)} %param.10) | copy-start | bytes 1572868
  28.4 21.8 %all-to-all-start = ((bf16[32,16,512]{2,0,1:T(8,128)(2,1)}), bf16[32,16,512]{2,0,1:T(8,128)(2,1)S(1)}, u32[]{:S(2)}, u32[]{:S(2)}) async-start(bf16[32,16,512]{2,0,1:T(8,128)(2,1)} %copy.97), calls=%async_computation | async-start | bytes 1048576 | tf_op jit(solution)/shard_map/all_to_all | solution.py:240
  39.3 12.4 %copy-start.29 = (f32[512]{0:T(512)S(1)}, f32[512]{0:T(512)}, u32[]{:S(2)}) copy-start(f32[512]{0:T(512)} %param.14) | copy-start | bytes 6148
  50.4 36.1 %copy-start = (f32[32,16,512]{2,0,1:T(8,128)}, f32[32,16,512]{2,0,1:T(8,128)S(1)}, u32[]{:S(2)}) copy-start(f32[32,16,512]{2,0,1:T(8,128)S(1)} %convert_element_type.251) | copy-start | bytes 3145732
  50.7 1.0 copy-start.9
  62.5 4.7 %copy-start.18 = (bf16[512,512]{0,1:T(8,128)(2,1)S(1)}, bf16[512,512]{0,1:T(8,128)(2,1)}, u32[]{:S(2)}) copy-start(bf16[512,512]{0,1:T(8,128)(2,1)} %convolution_convert_fusion.13) | copy-start | bytes 1572868
  67.2 3.6 %copy-start.2 = (f32[8,512,512]{1,2,0:T(8,128)S(1)}, f32[8,512,512]{1,2,0:T(8,128)}, u32[]{:S(2)}) copy-start(f32[8,512,512]{1,2,0:T(8,128)} %get-tuple-element.48) | copy-start | bytes 25165828
  68.0 18.0 %copy-start.3 = (bf16[8,512,64]{1,2,0:T(8,128)(2,1)}, bf16[8,512,64]{1,2,0:T(8,128)(2,1)S(1)}, u32[]{:S(2)}) copy-start(bf16[8,512,64]{1,2,0:T(8,128)(2,1)S(1)} %get-tuple-element.50) | copy-start | bytes 1572868
  74.8 1.5 copy-start.10
  74.8 2.5 %copy-start.26 = (bf16[512,2048]{1,0:T(8,128)(2,1)S(1)}, bf16[512,2048]{1,0:T(8,128)(2,1)}, u32[]{:S(2)}) copy-start(bf16[512,2048]{1,0:T(8,128)(2,1)} %param.12) | copy-start | bytes 6291460
  75.0 3.3 %copy-start.19 = (bf16[3,8,512,64]{2,3,1,0:T(8,128)(2,1)}, bf16[3,8,512,64]{2,3,1,0:T(8,128)(2,1)S(1)}, u32[]{:S(2)}) copy-start(bf16[3,8,512,64]{2,3,1,0:T(8,128)(2,1)S(1)} %pad_maximum_fusion.1) | copy-start | bytes 4718596
  77.3 1.0 copy-start.17
  79.2 6.9 %copy-start.12 = (bf16[512,1,512]{2,0,1:T(8,128)(2,1)S(1)}, bf16[512,1,512]{2,0,1:T(8,128)(2,1)}, u32[]{:S(2)}) copy-start(bf16[512,1,512]{2,0,1:T(8,128)(2,1)} %param.10) | copy-start | bytes 1572868
  81.6 18.6 %all-to-all-start.1 = ((bf16[16,2,8192]{2,1,0:T(2,128)(2,1)}), bf16[16,2,8192]{2,1,0:T(2,128)(2,1)S(1)}, u32[]{:S(2)}, u32[]{:S(2)}) async-start(bf16[16,2,8192]{2,1,0:T(2,128)(2,1)} %reshape.322), calls=%async_computation.1 | async-start | bytes 1048576 | tf_op jit(solution)/shard_map/all_to_all | solution.py:272
  85.7 83.2 %reduce-scatter.2.cloned.1.call-start = ((), (), s32[]{:S(2)}) async-start(), calls=%async_computation.7 | async-start | bytes 2228224 | tf_op jit(solution)/shard_map/reduce_scatter | solution.py:212
  90.7 10.2 %copy-start.25 = (bf16[32,16,512]{2,1,0:T(8,128)(2,1)S(1)}, bf16[32,16,512]{2,1,0:T(8,128)(2,1)}, u32[]{:S(2)}) copy-start(bf16[32,16,512]{2,1,0:T(8,128)(2,1)} %copy-done.24) | copy-start | bytes 1572868
  101.5 3.2 %copy-start.34 = (f32[32,8,16]{2,1,0:T(8,128)S(1)}, f32[32,8,16]{2,1,0:T(8,128)}, u32[]{:S(2)}) copy-start(f32[32,8,16]{2,1,0:T(8,128)} %copy-done.33) | copy-start | bytes 49156
  101.8 0.8 copy-start.15
  104.7 3.4 %copy-start.8 = (bf16[32,8,16,64]{3,2,1,0:T(8,128)(2,1)S(1)}, bf16[32,8,16,64]{3,2,1,0:T(8,128)(2,1)}, u32[]{:S(2)}) copy-start(bf16[32,8,16,64]{3,2,1,0:T(8,128)(2,1)} %copy-done.7) | copy-start | bytes 1572868
  108.7 9.2 %copy-start.22 = (bf16[32,16,1,8,64]{4,3,2,1,0:T(8,128)(2,1)S(1)}, bf16[32,16,1,8,64]{4,3,2,1,0:T(8,128)(2,1)}, u32[]{:S(2)}) copy-start(bf16[32,16,1,8,64]{4,3,2,1,0:T(8,128)(2,1)} %get-tuple-element.44) | copy-start | bytes 1572868
  113.9 17.1 %all-to-all-start.3 = ((bf16[8,32,512]{2,1,0:T(8,128)(2,1)}), bf16[8,32,512]{2,1,0:T(8,128)(2,1)S(1)}, u32[]{:S(2)}, u32[]{:S(2)}) async-start(bf16[8,32,512]{2,1,0:T(8,128)(2,1)} %reduce_sum.141), calls=%async_computation.3 | async-start | bytes 524288 | tf_op jit(solution)/shard_map/all_to_all | solution.py:207
  117.9 2.4 %copy-start.6 = (bf16[32,16,1,8,64]{4,3,2,1,0:T(8,128)(2,1)S(1)}, bf16[32,16,1,8,64]{4,3,2,1,0:T(8,128)(2,1)}, u32[]{:S(2)}) copy-start(bf16[32,16,1,8,64]{4,3,2,1,0:T(8,128)(2,1)} %get-tuple-element.42) | copy-start | bytes 1572868
  120.3 1.2 copy-start.5
  121.6 1.2 copy-start.23
  124.4 6.7 %copy-start.30 = (f32[512]{0:T(512)S(1)}, f32[512]{0:T(512)}, u32[]{:S(2)}) copy-start(f32[512]{0:T(512)} %param.13) | copy-start | bytes 6148
  138.9 6.0 %copy-start.1 = (f32[32,16,512]{2,0,1:T(8,128)S(1)}, f32[32,16,512]{2,0,1:T(8,128)}, u32[]{:S(2)}) copy-start(f32[32,16,512]{2,0,1:T(8,128)} %copy-done) | copy-start | bytes 3145732
  138.9 6.0 %copy-start.4 = (bf16[8,512,64]{1,2,0:T(8,128)(2,1)S(1)}, bf16[8,512,64]{1,2,0:T(8,128)(2,1)}, u32[]{:S(2)}) copy-start(bf16[8,512,64]{1,2,0:T(8,128)(2,1)} %copy-done.3) | copy-start | bytes 1572868
  140.3 7.1 %copy-start.14 = (bf16[32,16,512]{2,1,0:T(8,128)(2,1)S(1)}, bf16[32,16,512]{2,1,0:T(8,128)(2,1)}, u32[]{:S(2)}) copy-start(bf16[32,16,512]{2,1,0:T(8,128)(2,1)} %param.9) | copy-start | bytes 1572868
  140.3 27.9 %all-to-all-start.5 = ((bf16[8,32,1536]{2,1,0:T(8,128)(2,1)}), bf16[8,32,1536]{2,1,0:T(8,128)(2,1)S(1)}, u32[]{:S(2)}, u32[]{:S(2)}) async-start(bf16[8,32,1536]{2,1,0:T(8,128)(2,1)} %reduce_sum.145), calls=%async_computation.5 | async-start | bytes 1572864 | tf_op jit(solution)/shard_map/all_to_all | solution.py:207
  144.9 2.4 %copy-start.20 = (bf16[32,16,1536]{2,1,0:T(8,128)(2,1)S(1)}, bf16[32,16,1536]{2,1,0:T(8,128)(2,1)}, u32[]{:S(2)}) copy-start(bf16[32,16,1536]{2,1,0:T(8,128)(2,1)} %reshape.312) | copy-start | bytes 4718596
  147.4 2.6 %copy-start.16 = (bf16[16,32,1,512]{3,0,1,2:T(8,128)(2,1)S(1)}, bf16[16,32,1,512]{3,0,1,2:T(8,128)(2,1)}, u32[]{:S(2)}) copy-start(bf16[16,32,1,512]{3,0,1,2:T(8,128)(2,1)} %copy-done.15) | copy-start | bytes 1572868
Sparse Core Ops, SparseCore 0:
  90.8 66.5 reduce-scatter.1

commit v4 on v3

--- a/solution.py
+++ b/solution.py
@@ -229,15 +229,34 @@
     model_width = activity.shape[2]
     first_bin = (lax.axis_index("outer") * 2 + lax.axis_index("core")) * local_bins
     sessions_here = lax.dynamic_slice_in_dim(session_id, first_bin, local_bins)
-    normed_one, inverse_one = norm_forward(activity, spatial_gain)
-    spatial_proj = project(normed_one, spatial_weights[:, : 3 * model_width]).astype(jnp.bfloat16)
-    allowed_space = spatial_allowed(sessions_here, channel_count, adjacency)
-    spatial_context = spatial_forward(spatial_proj, allowed_space)
-    middle = (
-        activity.astype(jnp.float32)
-        + project(spatial_context, spatial_weights[:, 3 * model_width :])
-    ).astype(jnp.bfloat16)
-    middle_block = lax.all_to_all(middle, ("outer", "core"), split_axis=1, concat_axis=0, tiled=True)
+    halves = 2
+    half_bins = local_bins // halves
+    sent = session_id.shape[0] // local_bins
+    parts = []
+    for half in range(halves):
+        rows = activity[half * half_bins : (half + 1) * half_bins]
+        normed_half, inverse_half = norm_forward(rows, spatial_gain)
+        proj_half = project(normed_half, spatial_weights[:, : 3 * model_width]).astype(
+            jnp.bfloat16
+        )
+        allowed_half = spatial_allowed(
+            sessions_here[half * half_bins : (half + 1) * half_bins], channel_count, adjacency
+        )
+        context_half = spatial_forward(proj_half, allowed_half)
+        middle_half = (
+            rows.astype(jnp.float32)
+            + project(context_half, spatial_weights[:, 3 * model_width :])
+        ).astype(jnp.bfloat16)
+        moved = lax.all_to_all(
+            middle_half, ("outer", "core"), split_axis=1, concat_axis=0, tiled=True
+        )
+        parts.append((normed_half, inverse_half, proj_half, allowed_half, context_half, moved))
+    normed_one, inverse_one, spatial_proj, allowed_space, spatial_context = [
+        jnp.concatenate([part[index] for part in parts], axis=0) for index in range(5)
+    ]
+    middle_block = jnp.stack(
+        [part[5].reshape(sent, half_bins, 1, model_width) for part in parts], axis=1
+    ).reshape(sent * local_bins, 1, model_width)
     normed_two, inverse_two = norm_forward(middle_block, temporal_gain)
     temporal_proj = project(normed_two, temporal_weights[:, : 3 * model_width]).astype(jnp.bfloat16)
     allowed_time = session_id[:, None] == session_id[None, :]

time: 179 us -> 197 us (1.10)
  waiting for transfers between devices: 41 us -> 25 us
  local copies, waits for them, and re-layouts: 27.5 us -> 40.2 us
  other arithmetic: 17.2 us -> 25.8 us
  starting transfers between devices: 20.4 us -> 28.2 us
  matrix products: 47.2 us -> 52.3 us
    all_to_all x1 -> x2, waiting for transfers between devices: 10.9 us -> 2.79 us  [per_device(): lax.all_to_all(middle_half, ('outer', 'core'), split_axis=1, concat_axis=...]
    sub x2 -> x4, matrix products: 8.32 us -> 14.6 us  [normalized_affinity(): expo = jnp.exp(unnormalized_affinities - row_max)]
    all_to_all x1 -> x2, starting transfers between devices: 7.38 us -> 13.5 us  [per_device(): lax.all_to_all(middle_half, ('outer', 'core'), split_axis=1, concat_axis=...]
    all_to_all x1, waiting for transfers between devices: 9.48 us -> 4.37 us  [per_device(): lax.all_to_all(grad_middle, ('outer', 'core'), split_axis=0, concat_axis=...]
    reshape x1 -> x3, local copies, waits for them, and re-layouts: 3.97 us -> 7.29 us  [spatial_split(): projected.reshape(projected.shape[0], projected.shape[1], 3, HEADS, proje...]
    unnamed x76 -> x89, local copies, waits for them, and re-layouts: 11.8 us -> 14.8 us
    all_to_all x2, waiting for transfers between devices: 20.6 us -> 17.8 us  [reduce_rows(): pieces = lax.all_to_all(pieces, 'outer', 0, 0, tiled=True)]
    dot_general x2, matrix products: 4.79 us -> 2.07 us  [compute_affinity_derivatives(): jnp.einsum('...qk,...qd->...kd', truncated_outcome, blended_output_deriva...]
  transfers between devices with their start and end apart: 5 -> 6, of which waited for: 4 -> 3; matrix products, arithmetic and copies ran while one was open for 20% -> 33% of each run, Pallas kernels for 0% -> 0%
where the time goes in v4:
time: 197 us; the launch traced here: 195 us
  matrix products  52.3 us (27%)
  local copies, waits for them, and re-layouts  40.2 us (20%)
  starting transfers between devices  28.2 us (14%)
  other arithmetic  25.8 us (13%)
  waiting for transfers between devices  25 us (13%)
  between operations  14.7 us (7%)
  blocking collectives  9.2 us (5%)
    all_to_all x2, waiting for transfers between devices, reduce_rows(): pieces = lax.all_to_all(pieces, 'outer', 0, 0, tiled=True)  17.8 us
    unnamed x89, local copies, waits for them, and re-layouts  14.8 us
    sub x4, matrix products, normalized_affinity(): expo = jnp.exp(unnormalized_affinities - row_max)  14.6 us
    dot_general x6, matrix products, project(): jnp.einsum('tbd,de->tbe', rows, coefficient_array, preferred_element_type...  13.9 us
    all_to_all x2, starting transfers between devices, per_device(): lax.all_to_all(middle_half, ('outer', 'core'), split_axis=1, concat_axis=...  13.5 us
    all_to_all x2, starting transfers between devices, reduce_rows(): pieces = lax.all_to_all(pieces, 'outer', 0, 0, tiled=True)  10.2 us
    all_to_all x2, blocking collectives, reduce_rows(): pieces = lax.all_to_all(pieces, 'core', 1, 1, tiled=True)  9.2 us
    dot_general x4, matrix products, project_back(): jnp.einsum('tbe,de->tbd', derivative_collection, coefficient_array, prefe...  8.47 us
  transfers between devices with their start and end apart: 6, of which 3 were waited for; matrix products, arithmetic and copies ran while one was open for 33% of the time, Pallas kernels for 0%

profile of v4, /device:TPU:0, one launch (start us, length us, event | category | flops | bytes accessed | tf_op | source)
XLA Modules:
  0.0 195.3 jit_solution(12349369979869839455)
XLA Ops:
  8.4 1.9 fusion.70
  11.0 2.0 %convolution_convert_fusion.2 = bf16[16,16,1536]{2,1,0:T(8,128)(2,1)S(1)} fusion(bf16[16,16,512]{2,1,0:T(8,128)(2,1)S(1)} %get-tuple-element.80, bf16[512,2048]{1,0:T(8,128)(2,1)} %param.11), kind=kOutput, calls=%fused_computation.18 | convolution fusion | flops 403046400 | bytes 2621440 | tf_op jit(solution)/shard_map/tbd,de->tbe/dot_general | solution.py:188
  14.0 1.2 fusion.110
  15.8 1.7 fusion.112
  19.2 1.4 fusion.45
  21.5 7.4 %all-to-all-start.1 = ((bf16[16,16,512]{2,0,1:T(8,128)(2,1)}), bf16[16,16,512]{2,0,1:T(8,128)(2,1)S(1)}, u32[]{:S(2)}, u32[]{:S(2)}) async-start(bf16[16,16,512]{2,0,1:T(8,128)(2,1)} %copy.224), calls=%async_computation.1 | async-start | bytes 524288 | tf_op jit(solution)/shard_map/all_to_all | solution.py:250
  28.9 2.9 %convolution_convert_fusion.3 = bf16[16,16,1536]{2,1,0:T(8,128)(2,1)} fusion(bf16[16,16,512]{2,1,0:T(8,128)(2,1)S(1)} %copy-done.31, bf16[512,2048]{1,0:T(8,128)(2,1)} %param.11), kind=kOutput, calls=%fused_computation.19 | convolution fusion | flops 403046400 | bytes 2621440 | tf_op jit(solution)/shard_map/tbd,de->tbe/dot_general | solution.py:188
  31.8 2.4 %reshape.415 = bf16[16,16,3,8,64]{4,3,2,1,0:T(8,128)(2,1)S(1)} reshape(bf16[16,16,1536]{2,1,0:T(8,128)(2,1)} %convolution_convert_fusion.3) | data formatting | bytes 1572864 | tf_op jit(solution)/shard_map/reshape | solution.py:136
  34.2 1.4 fusion.109
  35.6 2.9 %fusion.113 = (f32[16,8,16]{2,1,0:T(8,128)S(1)}, f32[16,8,16,16]{2,3,1,0:T(8,128)}) fusion(bf16[16,16,1,8,64]{4,3,2,1,0:T(8,128)(2,1)} %get-tuple-element.74, bf16[16,16,1,8,64]{4,3,2,1,0:T(8,128)(2,1)} %get-tuple-element.75, pred[16,16,16]{1,2,0:T(8,128)(4,1)S(1)} %get-tuple-element.87), kind=kOutput, calls=%fused_computation.192 | convolution fusion | flops 4325391 | bytes 667648 | tf_op jit(solution)/shard_map/sub | solution.py:39
  38.5 1.6 fusion.39
  40.6 1.5 fusion.44
  42.9 2.3 %convolution_convert_fusion.13 = bf16[512,512]{0,1:T(8,128)(2,1)} fusion(bf16[512,1,512]{2,0,1:T(8,128)(2,1)S(1)} %copy-done.14, bf16[512,2048]{1,0:T(8,128)(2,1)} %param.12), kind=kOutput, calls=%fused_computation.64 | convolution fusion | flops 268697600 | bytes 1572864 | tf_op jit(solution)/shard_map/tbe,de->tbd/dot_general | solution.py:192
  46.1 1.3 pad_maximum_fusion.2
  47.4 6.1 %all-to-all-start = ((bf16[16,16,512]{2,0,1:T(8,128)(2,1)}), bf16[16,16,512]{2,0,1:T(8,128)(2,1)}, u32[]{:S(2)}, u32[]{:S(2)}) async-start(bf16[16,16,512]{2,0,1:T(8,128)(2,1)} %copy.218), calls=%async_computation | async-start | bytes 524288 | tf_op jit(solution)/shard_map/all_to_all | solution.py:250
  54.7 4.0 %reshape.425 = bf16[32,16,3,8,64]{4,3,2,1,0:T(8,128)(2,1)S(1)} reshape(bf16[32,16,1536]{2,1,0:T(8,128)(2,1)} %pad_maximum_fusion.2) | data formatting | bytes 3145728 | tf_op jit(solution)/shard_map/reshape | solution.py:136
  58.7 2.1 %fusion.108 = (bf16[32,16,1,8,64]{4,3,2,1,0:T(8,128)(2,1)}, bf16[32,16,1,8,64]{4,3,2,1,0:T(8,128)(2,1)}, bf16[32,16,1,8,64]{4,3,2,1,0:T(8,128)(2,1)}) fusion(bf16[32,16,3,8,64]{4,3,2,1,0:T(8,128)(2,1)S(1)} %reshape.425), kind=kLoop, calls=%fused_computation.187 | loop fusion | bytes 3145728 | tf_op jit(solution)/shard_map/slice | solution.py:139
  60.8 2.8 %all-to-all-done = bf16[16,16,512]{2,0,1:T(8,128)(2,1)} async-done(((bf16[16,16,512]{2,0,1:T(8,128)(2,1)}), bf16[16,16,512]{2,0,1:T(8,128)(2,1)}, u32[]{:S(2)}, u32[]{:S(2)}) %all-to-all-start) | async-done | bytes 262176 | tf_op jit(solution)/shard_map/all_to_all | solution.py:250
  64.7 1.4 multiply_reduce_fusion.2
  67.4 3.7 %convolution_convert_fusion.1 = bf16[512,1536]{1,0:T(8,128)(2,1)} fusion(bf16[512,2048]{1,0:T(8,128)(2,1)} %param.12, f32[512,512]{0,1:T(8,128)S(1)} %copy.227, f32[512]{0:T(512)S(1)} %copy-done.38, f32[512]{0:T(512)S(1)} %rsqrt.44), kind=kOutput, calls=%fused_computation.16 | convolution fusion | flops 806879232 | bytes 4198400 | tf_op jit(solution)/shard_map/tbd,de->tbe/dot_general | solution.py:188
  71.1 1.8 copy.228
  72.8 5.4 %fusion.114 = (f32[8,512]{1,0:T(8,128)S(1)}, f32[8,512,512]{1,2,0:T(8,128)}) fusion(pred[512,512]{0,1:T(8,128)(4,1)S(1)} %copy-done.29, bf16[512,3,8,64]{0,3,2,1:T(8,128)(2,1)S(1)} %bitcast.230), kind=kOutput, calls=%fused_computation.193 | convolution fusion | flops 276824576 | bytes 9715712 | tf_op jit(solution)/shard_map/while/body/eval_jaxpr/sub | solution.py:39
  78.3 4.7 %fusion.8 = bf16[8,512,512]{1,2,0:T(8,128)(2,1)S(1)} fusion(f32[8,512,512]{1,2,0:T(8,128)} %get-tuple-element.98, f32[8,512]{1,0:T(8,128)S(1)} %get-tuple-element.97), kind=kLoop, calls=%fused_computation.12 | loop fusion | flops 4194304 | bytes 12599296 | tf_op jit(solution)/shard_map/while/body/eval_jaxpr/convert_element_type | solution.py:48
  83.8 1.4 fusion.42
  85.1 1.4 copy-done.2
  86.5 1.8 multiply_convert_fusion
  88.3 1.4 fusion.41
  95.7 2.2 %reduce.6 = bf16[512,512]{0,1:T(8,128)(2,1)S(1)} reduce(bf16[512,1,512]{0,2,1:T(8,128)(2,1)} %fusion.58, bf16[]{:T(256)} %broadcast.319), dimensions={1}, to_apply=%copy.238.reduce_sub_computation | reduce | bytes 1048578 | tf_op jit(solution)/shard_map/convert_element_type | solution.py:290
  98.8 2.3 %reshape.435 = bf16[16,2,8192]{2,1,0:T(2,128)(2,1)} reshape(bf16[512,512]{1,0:T(8,128)(2,1)} %copy.333) | data formatting | bytes 1048576
  101.1 4.2 %all-to-all-start.2 = ((bf16[16,2,8192]{2,1,0:T(2,128)(2,1)}), bf16[16,2,8192]{2,1,0:T(2,128)(2,1)}, u32[]{:S(2)}, u32[]{:S(2)}) async-start(bf16[16,2,8192]{2,1,0:T(2,128)(2,1)} %reshape.435), calls=%async_computation.2 | async-start | bytes 1048576 | tf_op jit(solution)/shard_map/all_to_all | solution.py:291
  105.6 4.5 %fusion.115 = (f32[32,8,16]{2,1,0:T(8,128)}, f32[32,8,16,16]{2,3,1,0:T(8,128)}) fusion(pred[32,16,16]{1,2,0:T(8,128)(4,1)S(1)} %add_bitcast_fusion, bf16[32,16,1,8,64]{4,3,2,1,0:T(8,128)(2,1)S(1)} %copy-done.7, bf16[32,16,1,8,64]{4,3,2,1,0:T(8,128)(2,1)} %get-tuple-element.71), kind=kOutput, calls=%fused_computation.194 | convolution fusion | flops 8650767 | bytes 1335296 | tf_op jit(solution)/shard_map/sub | solution.py:39
  113.8 1.6 pad_maximum_fusion
  115.4 4.4 %all-to-all-done.2 = bf16[16,2,8192]{2,1,0:T(2,128)(2,1)} async-done(((bf16[16,2,8192]{2,1,0:T(2,128)(2,1)}), bf16[16,2,8192]{2,1,0:T(2,128)(2,1)}, u32[]{:S(2)}, u32[]{:S(2)}) %all-to-all-start.2) | async-done | bytes 524320 | tf_op jit(solution)/shard_map/all_to_all | solution.py:291
  119.8 2.2 %reshape.436 = bf16[512,1,512]{2,1,0:T(2,128)(2,1)S(1)} reshape(bf16[16,2,8192]{2,1,0:T(2,128)(2,1)} %all-to-all-done.2) | data formatting | bytes 1048576
  122.7 4.2 %all_to_all.68 = bf16[8,2,32,512]{3,2,0,1:T(8,128)(2,1)S(1)} all-to-all(bf16[8,2,32,512]{3,2,0,1:T(8,128)(2,1)S(1)} %copy.240), channel_id=1, replica_groups=mesh['groups'=2,'outer'=8,'core'=2] {'core'}, dimensions={1} | all-to-all | bytes 1048576 | tf_op jit(solution)/shard_map/all_to_all | solution.py:205
  127.7 4.1 %all-to-all-start.4 = ((bf16[8,32,512]{2,1,0:T(8,128)(2,1)}), bf16[8,32,512]{2,1,0:T(8,128)(2,1)S(1)}, u32[]{:S(2)}, u32[]{:S(2)}) async-start(bf16[8,32,512]{2,1,0:T(8,128)(2,1)} %reduce_sum.176), calls=%async_computation.4 | async-start | bytes 524288 | tf_op jit(solution)/shard_map/all_to_all | solution.py:207
  131.8 2.3 %convolution_convert_fusion.10 = bf16[32,16,512]{2,1,0:T(8,128)(2,1)} fusion(bf16[32,16,512]{2,0,1:T(8,128)(2,1)S(1)} %bitcast.240, bf16[512,2048]{1,0:T(8,128)(2,1)} %param.11), kind=kOutput, calls=%fused_computation.61 | convolution fusion | flops 268697600 | bytes 1572864 | tf_op jit(solution)/shard_map/tbe,de->tbd/dot_general | solution.py:192
  134.2 1.7 reshape.426
  135.9 1.8 fusion.10
  143.0 2.9 %reshape.427 = bf16[32,16,1536]{2,1,0:T(8,128)(2,1)} reshape(bf16[32,16,3,8,64]{4,3,2,1,0:T(8,128)(2,1)S(1)} %copy.249) | data formatting | bytes 3145728 | tf_op jit(solution)/shard_map/reshape | solution.py:169
  146.0 2.6 %fusion.9 = bf16[512,1536]{1,0:T(8,128)(2,1)S(1)} fusion(bf16[32,16,1536]{2,1,0:T(8,128)(2,1)} %reshape.427, bf16[16,16,512]{2,1,0:T(8,128)(2,1)} %copy-done.32, bf16[16,16,512]{2,1,0:T(8,128)(2,1)} %get-tuple-element.79), kind=kOutput, calls=%fused_computation.17 | convolution fusion | flops 806354944 | bytes 3670016 | tf_op jit(solution)/shard_map/tbd,tbe->de/dot_general | solution.py:198
  148.7 5.0 %all_to_all.69 = bf16[8,2,32,1536]{3,2,0,1:T(8,128)(2,1)S(1)} all-to-all(bf16[8,2,32,1536]{3,2,0,1:T(8,128)(2,1)S(1)} %copy.252), channel_id=1, replica_groups=mesh['groups'=2,'outer'=8,'core'=2] {'core'}, dimensions={1} | all-to-all | bytes 3145728 | tf_op jit(solution)/shard_map/all_to_all | solution.py:205
  153.7 1.4 reduce_sum.181
  155.1 6.1 %all-to-all-start.6 = ((bf16[8,32,1536]{2,1,0:T(8,128)(2,1)}), bf16[8,32,1536]{2,1,0:T(8,128)(2,1)S(1)}, u32[]{:S(2)}, u32[]{:S(2)}) async-start(bf16[8,32,1536]{2,1,0:T(8,128)(2,1)} %reduce_sum.181), calls=%async_computation.6 | async-start | bytes 1572864 | tf_op jit(solution)/shard_map/all_to_all | solution.py:207
  161.3 2.4 %fusion.38 = bf16[512,1,512]{2,0,1:T(8,128)(2,1)} fusion(f32[512,512]{1,0:T(8,128)S(1)} %bitcast.229, bf16[512,512]{0,1:T(8,128)(2,1)S(1)} %bitcast.236, bf16[512,2048]{1,0:T(8,128)(2,1)} %param.12), kind=kOutput, calls=%fused_computation.68 | convolution fusion | flops 268959744 | bytes 2621440 | tf_op jit(solution)/shard_map/tbd,de->tbe/dot_general | solution.py:188
  163.7 2.8 %fusion.55 = (f32[32,16]{0,1:T(8,128)S(1)}, f32[32,16,512]{2,0,1:T(8,128)S(1)}) fusion(bf16[32,16,512]{2,1,0:T(8,128)(2,1)S(1)} %copy-done.4, f32[512]{0:T(512)S(1)} %copy-done.36, bf16[512,2048]{1,0:T(8,128)(2,1)} %param.11, bf16[32,16,1536]{2,1,0:T(8,128)(2,1)S(1)} %copy-done.23), kind=kOutput, calls=%fused_computation.87 | convolution fusion | flops 806354432 | bytes 4722688 | tf_op jit(solution)/shard_map/tbe,de->tbd/dot_general | solution.py:192
  168.2 17.8 %all-to-all-done.6 = bf16[8,32,1536]{2,1,0:T(8,128)(2,1)S(1)} async-done(((bf16[8,32,1536]{2,1,0:T(8,128)(2,1)}), bf16[8,32,1536]{2,1,0:T(8,128)(2,1)S(1)}, u32[]{:S(2)}, u32[]{:S(2)}) %all-to-all-start.6) | async-done | bytes 786464 | tf_op jit(solution)/shard_map/all_to_all | solution.py:207
  186.8 1.6 convert_element_type.282
  (146 shorter events, 32.8 us)
Async XLA Ops:
  10.3 0.7 copy-start.32
  14.0 1.3 copy-start.34
  14.0 1.4 copy-start.35
  14.0 1.5 copy-start.37
  17.6 1.6 copy-start.3
  17.9 0.8 copy-start.16
  18.7 10.2 %copy-start.31 = (bf16[16,16,512]{2,1,0:T(8,128)(2,1)S(1)}, bf16[16,16,512]{2,1,0:T(8,128)(2,1)}, u32[]{:S(2)}) copy-start(bf16[16,16,512]{2,1,0:T(8,128)(2,1)} %get-tuple-element.79) | copy-start | bytes 786436
  19.2 9.7 %copy-start.24 = (bf16[16,16,512]{2,1,0:T(8,128)(2,1)}, bf16[16,16,512]{2,1,0:T(8,128)(2,1)S(1)}, u32[]{:S(2)}) copy-start(bf16[16,16,512]{2,1,0:T(8,128)(2,1)S(1)} %reshape.418) | copy-start | bytes 786436
  21.5 26.0 %all-to-all-start.1 = ((bf16[16,16,512]{2,0,1:T(8,128)(2,1)}), bf16[16,16,512]{2,0,1:T(8,128)(2,1)S(1)}, u32[]{:S(2)}, u32[]{:S(2)}) async-start(bf16[16,16,512]{2,0,1:T(8,128)(2,1)} %copy.224), calls=%async_computation.1 | async-start | bytes 524288 | tf_op jit(solution)/shard_map/all_to_all | solution.py:250
  35.6 2.9 %copy-start.28 = (bf16[16,16,1,8,64]{4,3,2,1,0:T(8,128)(2,1)S(1)}, bf16[16,16,1,8,64]{4,3,2,1,0:T(8,128)(2,1)}, u32[]{:S(2)}) copy-start(bf16[16,16,1,8,64]{4,3,2,1,0:T(8,128)(2,1)} %get-tuple-element.73) | copy-start | bytes 786436
  40.1 5.1 %copy-start.18 = (bf16[16,16,8,64]{3,1,2,0:T(8,128)(2,1)}, bf16[16,16,8,64]{3,1,2,0:T(8,128)(2,1)S(1)}, u32[]{:S(2)}) copy-start(bf16[16,16,8,64]{3,1,2,0:T(8,128)(2,1)S(1)} %fusion.39) | copy-start | bytes 786436
  40.1 2.8 %copy-start.14 = (bf16[512,1,512]{2,0,1:T(8,128)(2,1)S(1)}, bf16[512,1,512]{2,0,1:T(8,128)(2,1)}, u32[]{:S(2)}) copy-start(bf16[512,1,512]{2,0,1:T(8,128)(2,1)} %param.10) | copy-start | bytes 1572868
  40.6 6.9 %copy-start.26 = (bf16[16,16,512]{2,1,0:T(8,128)(2,1)}, bf16[16,16,512]{2,1,0:T(8,128)(2,1)S(1)}, u32[]{:S(2)}) copy-start(bf16[16,16,512]{2,1,0:T(8,128)(2,1)S(1)} %reshape.416) | copy-start | bytes 786436
  40.6 5.6 %copy-start.11 = (bf16[16,16,1536]{2,1,0:T(8,128)(2,1)S(1)}, bf16[16,16,1536]{2,1,0:T(8,128)(2,1)}, u32[]{:S(2)}) copy-start(bf16[16,16,1536]{2,1,0:T(8,128)(2,1)} %convolution_convert_fusion.3) | copy-start | bytes 2359300
  47.4 16.2 %all-to-all-start = ((bf16[16,16,512]{2,0,1:T(8,128)(2,1)}), bf16[16,16,512]{2,0,1:T(8,128)(2,1)}, u32[]{:S(2)}, u32[]{:S(2)}) async-start(bf16[16,16,512]{2,0,1:T(8,128)(2,1)} %copy.218), calls=%async_computation | async-start | bytes 524288 | tf_op jit(solution)/shard_map/all_to_all | solution.py:250
  63.6 3.8 %copy-start.38 = (f32[512]{0:T(512)S(1)}, f32[512]{0:T(512)}, u32[]{:S(2)}) copy-start(f32[512]{0:T(512)} %param.14) | copy-start | bytes 6148
  64.7 47.9 %copy-start = (f32[16,2,16,1,512]{4,2,1,0,3:T(8,128)}, f32[16,2,16,1,512]{4,2,1,0,3:T(8,128)S(1)}, u32[]{:S(2)}) copy-start(f32[16,2,16,1,512]{4,2,1,0,3:T(8,128)S(1)} %maximum_convert_fusion) | copy-start | bytes 3145732
  66.4 1.0 copy-start.9
  71.1 1.8 copy-start.29
  78.3 4.7 %copy-start.20 = (bf16[512,512]{0,1:T(8,128)(2,1)S(1)}, bf16[512,512]{0,1:T(8,128)(2,1)}, u32[]{:S(2)}) copy-start(bf16[512,512]{0,1:T(8,128)(2,1)} %convolution_convert_fusion.13) | copy-start | bytes 1572868
  82.9 3.6 %copy-start.2 = (f32[8,512,512]{1,2,0:T(8,128)S(1)}, f32[8,512,512]{1,2,0:T(8,128)}, u32[]{:S(2)}) copy-start(f32[8,512,512]{1,2,0:T(8,128)} %get-tuple-element.98) | copy-start | bytes 25165828
  83.7 28.4 %copy-start.5 = (bf16[8,512,64]{1,2,0:T(8,128)(2,1)}, bf16[8,512,64]{1,2,0:T(8,128)(2,1)S(1)}, u32[]{:S(2)}) copy-start(bf16[8,512,64]{1,2,0:T(8,128)(2,1)S(1)} %get-tuple-element.100) | copy-start | bytes 1572868
  90.5 1.5 copy-start.10
  90.5 2.5 %copy-start.33 = (bf16[512,2048]{1,0:T(8,128)(2,1)S(1)}, bf16[512,2048]{1,0:T(8,128)(2,1)}, u32[]{:S(2)}) copy-start(bf16[512,2048]{1,0:T(8,128)(2,1)} %param.12) | copy-start | bytes 6291460
  90.7 3.3 %copy-start.21 = (bf16[3,8,512,64]{2,3,1,0:T(8,128)(2,1)}, bf16[3,8,512,64]{2,3,1,0:T(8,128)(2,1)S(1)}, u32[]{:S(2)}) copy-start(bf16[3,8,512,64]{2,3,1,0:T(8,128)(2,1)S(1)} %pad_maximum_fusion.1) | copy-start | bytes 4718596
  93.0 1.0 copy-start.19
  95.7 9.9 %copy-start.7 = (bf16[32,16,1,8,64]{4,3,2,1,0:T(8,128)(2,1)S(1)}, bf16[32,16,1,8,64]{4,3,2,1,0:T(8,128)(2,1)}, u32[]{:S(2)}) copy-start(bf16[32,16,1,8,64]{4,3,2,1,0:T(8,128)(2,1)} %get-tuple-element.72) | copy-start | bytes 1572868
  101.1 18.7 %all-to-all-start.2 = ((bf16[16,2,8192]{2,1,0:T(2,128)(2,1)}), bf16[16,2,8192]{2,1,0:T(2,128)(2,1)}, u32[]{:S(2)}, u32[]{:S(2)}) async-start(bf16[16,2,8192]{2,1,0:T(2,128)(2,1)} %reshape.435), calls=%async_computation.2 | async-start | bytes 1048576 | tf_op jit(solution)/shard_map/all_to_all | solution.py:291
  105.3 81.5 %reduce-scatter.2.cloned.1.call-start = ((), (), s32[]{:S(2)}) async-start(), calls=%async_computation.8 | async-start | bytes 2228224 | tf_op jit(solution)/shard_map/reduce_scatter | solution.py:212
  105.6 4.6 %copy-start.25 = (bf16[16,16,512]{2,1,0:T(8,128)(2,1)S(1)}, bf16[16,16,512]{2,1,0:T(8,128)(2,1)}, u32[]{:S(2)}) copy-start(bf16[16,16,512]{2,1,0:T(8,128)(2,1)} %copy-done.24) | copy-start | bytes 786436
  105.6 6.5 %copy-start.15 = (bf16[512,1,512]{2,0,1:T(8,128)(2,1)S(1)}, bf16[512,1,512]{2,0,1:T(8,128)(2,1)}, u32[]{:S(2)}) copy-start(bf16[512,1,512]{2,0,1:T(8,128)(2,1)} %param.10) | copy-start | bytes 1572868
  110.2 2.4 %copy-start.22 = (bf16[3,8,512,64]{2,3,1,0:T(8,128)(2,1)S(1)}, bf16[3,8,512,64]{2,3,1,0:T(8,128)(2,1)}, u32[]{:S(2)}) copy-start(bf16[3,8,512,64]{2,3,1,0:T(8,128)(2,1)} %copy-done.21) | copy-start | bytes 4718596
  115.4 6.7 %copy-start.30 = (bf16[16,16,512]{2,0,1:T(8,128)(2,1)S(1)}, bf16[16,16,512]{2,0,1:T(8,128)(2,1)}, u32[]{:S(2)}) copy-start(bf16[16,16,512]{2,0,1:T(8,128)(2,1)} %copy.231) | copy-start | bytes 786436
  122.2 9.7 %copy-start.12 = (bf16[512,1,512]{2,0,1:T(8,128)(2,1)}, bf16[512,1,512]{2,0,1:T(8,128)(2,1)S(1)}, u32[]{:S(2)}) copy-start(bf16[512,1,512]{2,0,1:T(8,128)(2,1)S(1)} %copy.267) | copy-start | bytes 1572868
  127.7 8.1 %copy-start.17 = (bf16[16,16,8,64]{3,1,2,0:T(8,128)(2,1)S(1)}, bf16[16,16,8,64]{3,1,2,0:T(8,128)(2,1)}, u32[]{:S(2)}) copy-start(bf16[16,16,8,64]{3,1,2,0:T(8,128)(2,1)} %copy-done.16) | copy-start | bytes 786436
  127.7 18.2 %all-to-all-start.4 = ((bf16[8,32,512]{2,1,0:T(8,128)(2,1)}), bf16[8,32,512]{2,1,0:T(8,128)(2,1)S(1)}, u32[]{:S(2)}, u32[]{:S(2)}) async-start(bf16[8,32,512]{2,1,0:T(8,128)(2,1)} %reduce_sum.176), calls=%async_computation.4 | async-start | bytes 524288 | tf_op jit(solution)/shard_map/all_to_all | solution.py:207
  134.2 3.5 %copy-start.40 = (f32[32,8,16]{2,1,0:T(8,128)S(1)}, f32[32,8,16]{2,1,0:T(8,128)}, u32[]{:S(2)}) copy-start(f32[32,8,16]{2,1,0:T(8,128)} %get-tuple-element.103) | copy-start | bytes 49156
  135.9 1.8 copy-start.39
  137.7 1.2 copy-start.27
  139.0 1.2 copy-start.8
  153.7 7.6 %copy-start.1 = (f32[16,2,16,1,512]{4,2,1,0,3:T(8,128)S(1)}, f32[16,2,16,1,512]{4,2,1,0,3:T(8,128)}, u32[]{:S(2)}) copy-start(f32[16,2,16,1,512]{4,2,1,0,3:T(8,128)} %copy-done) | copy-start | bytes 3145732
  153.7 7.6 %copy-start.6 = (bf16[8,512,64]{1,2,0:T(8,128)(2,1)S(1)}, bf16[8,512,64]{1,2,0:T(8,128)(2,1)}, u32[]{:S(2)}) copy-start(bf16[8,512,64]{1,2,0:T(8,128)(2,1)} %copy-done.5) | copy-start | bytes 1572868
  155.1 8.7 %copy-start.4 = (bf16[32,16,512]{2,1,0:T(8,128)(2,1)S(1)}, bf16[32,16,512]{2,1,0:T(8,128)(2,1)}, u32[]{:S(2)}) copy-start(bf16[32,16,512]{2,1,0:T(8,128)(2,1)} %param.9) | copy-start | bytes 1572868
  155.1 8.7 %copy-start.36 = (f32[512]{0:T(512)S(1)}, f32[512]{0:T(512)}, u32[]{:S(2)}) copy-start(f32[512]{0:T(512)} %param.13) | copy-start | bytes 6148
  155.1 30.9 %all-to-all-start.6 = ((bf16[8,32,1536]{2,1,0:T(8,128)(2,1)}), bf16[8,32,1536]{2,1,0:T(8,128)(2,1)S(1)}, u32[]{:S(2)}, u32[]{:S(2)}) async-start(bf16[8,32,1536]{2,1,0:T(8,128)(2,1)} %reduce_sum.181), calls=%async_computation.6 | async-start | bytes 1572864 | tf_op jit(solution)/shard_map/all_to_all | solution.py:207
  161.3 2.4 %copy-start.23 = (bf16[32,16,1536]{2,1,0:T(8,128)(2,1)S(1)}, bf16[32,16,1536]{2,1,0:T(8,128)(2,1)}, u32[]{:S(2)}) copy-start(bf16[32,16,1536]{2,1,0:T(8,128)(2,1)} %reshape.427) | copy-start | bytes 4718596
  163.7 2.9 %copy-start.13 = (bf16[512,1,512]{2,0,1:T(8,128)(2,1)S(1)}, bf16[512,1,512]{2,0,1:T(8,128)(2,1)}, u32[]{:S(2)}) copy-start(bf16[512,1,512]{2,0,1:T(8,128)(2,1)} %copy-done.12) | copy-start | bytes 1572868
Sparse Core Ops, SparseCore 0:
  115.5 69.1 reduce-scatter.1

commit v5 on v3

--- a/solution.py
+++ b/solution.py
@@ -201,9 +201,12 @@
 def reduce_rows(partial):
     rows, cols = partial.shape
     outer = lax.psum(1, "outer")
-    pieces = partial.astype(jnp.bfloat16).reshape(outer, 2, rows // (2 * outer), cols)
-    pieces = lax.all_to_all(pieces, "core", 1, 1, tiled=True)
-    pieces = jnp.sum(pieces.astype(jnp.float32), axis=1).astype(jnp.bfloat16)
+    pieces = partial.reshape(outer, 2, rows // (2 * outer), cols)
+    first = lax.axis_index("core") == 0
+    kept = jnp.where(first, pieces[:, 0], pieces[:, 1])
+    given = jnp.where(first, pieces[:, 1], pieces[:, 0]).astype(jnp.bfloat16)
+    taken = lax.ppermute(given, "core", [(0, 1), (1, 0)])
+    pieces = (kept + taken.astype(jnp.float32)).astype(jnp.bfloat16)
     pieces = lax.all_to_all(pieces, "outer", 0, 0, tiled=True)
     return jnp.sum(pieces.astype(jnp.float32), axis=0)
 

time: 179 us -> 174 us (0.972)
  blocking collectives: 9.28 us -> 0 us
  waiting for transfers between devices: 41 us -> 45.6 us
  matrix products: 47.2 us -> 44.7 us
    reduce_scatter x1, waiting for transfers between devices: 0.01 us -> 10.7 us  [scatter_rows(): lax.psum_scatter(partial.astype(jnp.bfloat16), ('outer', 'core'), scatter...]
    all_to_all x2 -> x0, blocking collectives: 9.28 us -> none  [reduce_rows(): pieces = lax.all_to_all(pieces, 'core', 1, 1, tiled=True)]
    all_to_all x2, waiting for transfers between devices: 20.6 us -> 12.3 us  [reduce_rows(): pieces = lax.all_to_all(pieces, 'outer', 0, 0, tiled=True)]
    convert_element_type x0 -> x4, other arithmetic: none -> 2.98 us  [the longest x2 2.09 us: reduce_rows(): pieces = (kept + taken.astype(jnp.float32)).astype(jnp.bfloat16)]
    ppermute x0 -> x2, waiting for transfers between devices: none -> 2.27 us  [reduce_rows(): taken = lax.ppermute(given, 'core', [(0, 1), (1, 0)])]
    reduce_sum x2 -> x0, other arithmetic: 2.23 us -> none  [reduce_rows(): pieces = jnp.sum(pieces.astype(jnp.float32), axis=1).astype(jnp.bfloat16)]
    unnamed x76 -> x82, local copies, waits for them, and re-layouts: 11.8 us -> 12 us
  transfers between devices with their start and end apart: 5 -> 7, of which waited for: 4 -> 6; matrix products, arithmetic and copies ran while one was open for 20% -> 21% of each run, Pallas kernels for 0% -> 0%
where the time goes in v5:
time: 174 us; the launch traced here: 173 us
  waiting for transfers between devices  45.6 us (26%)
  matrix products  44.7 us (26%)
  local copies, waits for them, and re-layouts  28.8 us (17%)
  starting transfers between devices  20.9 us (12%)
  other arithmetic  18 us (10%)
  between operations  14.7 us (8%)
    all_to_all x2, waiting for transfers between devices, reduce_rows(): pieces = lax.all_to_all(pieces, 'outer', 0, 0, tiled=True)  12.3 us
    unnamed x82, local copies, waits for them, and re-layouts  12 us
    dot_general x4, matrix products, project(): jnp.einsum('tbd,de->tbe', rows, coefficient_array, preferred_element_type...  11.6 us
    all_to_all x1, waiting for transfers between devices, per_device(): lax.all_to_all(middle, ('outer', 'core'), split_axis=1, concat_axis=0, ti...  10.9 us
    reduce_scatter x1, waiting for transfers between devices, scatter_rows(): lax.psum_scatter(partial.astype(jnp.bfloat16), ('outer', 'core'), scatter...  10.7 us
    all_to_all x1, waiting for transfers between devices, per_device(): lax.all_to_all(grad_middle, ('outer', 'core'), split_axis=0, concat_axis=...  9.49 us
    all_to_all x2, starting transfers between devices, reduce_rows(): pieces = lax.all_to_all(pieces, 'outer', 0, 0, tiled=True)  9.09 us
    sub x2, matrix products, normalized_affinity(): expo = jnp.exp(unnormalized_affinities - row_max)  8.31 us
  transfers between devices with their start and end apart: 7, of which 6 were waited for; matrix products, arithmetic and copies ran while one was open for 21% of the time, Pallas kernels for 0%

profile of v5, /device:TPU:0, one launch (start us, length us, event | category | flops | bytes accessed | tf_op | source)
XLA Modules:
  0.0 172.6 jit_solution(10212849951422112386)
XLA Ops:
  7.2 1.2 fusion.42
  8.4 3.8 %convolution_convert_fusion.2 = bf16[32,16,1536]{2,1,0:T(8,128)(2,1)} fusion(bf16[512,2048]{1,0:T(8,128)(2,1)} %param.11, bf16[32,16,512]{2,1,0:T(8,128)(2,1)} %param.9, f32[512]{0:T(512)} %param.13, f32[32,16]{1,0:T(8,128)S(1)} %add_rsqrt_fusion), kind=kOutput, calls=%fused_computation.14 | convolution fusion | flops 807141376 | bytes 3674112 | tf_op jit(solution)/shard_map/tbd,de->tbe/dot_general | solution.py:188
  12.2 4.0 %reshape.313 = bf16[32,16,3,8,64]{4,3,2,1,0:T(8,128)(2,1)S(1)} reshape(bf16[32,16,1536]{2,1,0:T(8,128)(2,1)} %convolution_convert_fusion.2) | data formatting | bytes 3145728 | tf_op jit(solution)/shard_map/reshape | solution.py:136
  16.2 2.1 %fusion.85 = (bf16[32,16,1,8,64]{4,3,2,1,0:T(8,128)(2,1)}, bf16[32,16,1,8,64]{4,3,2,1,0:T(8,128)(2,1)}, bf16[32,16,1,8,64]{4,3,2,1,0:T(8,128)(2,1)}) fusion(bf16[32,16,3,8,64]{4,3,2,1,0:T(8,128)(2,1)S(1)} %reshape.313), kind=kLoop, calls=%fused_computation.139 | loop fusion | bytes 3145728 | tf_op jit(solution)/shard_map/slice | solution.py:139
  18.8 2.9 %fusion.86 = (f32[32,8,16]{2,1,0:T(8,128)S(1)}, f32[32,8,16,16]{2,3,1,0:T(8,128)S(1)}) fusion(pred[32,16,16]{1,2,0:T(8,128)(4,1)S(1)} %and_or_fusion, bf16[32,16,1,8,64]{4,3,2,1,0:T(8,128)(2,1)} %get-tuple-element.43, bf16[32,16,1,8,64]{4,3,2,1,0:T(8,128)(2,1)} %get-tuple-element.42), kind=kOutput, calls=%fused_computation.140 | convolution fusion | flops 8650767 | bytes 1335296 | tf_op jit(solution)/shard_map/sub | solution.py:39
  21.8 1.3 copy-done.34
  23.7 1.0 copy-done.7
  25.6 1.7 fusion.28
  27.3 1.1 copy.119
  28.4 7.4 %all-to-all-start = ((bf16[32,16,512]{2,0,1:T(8,128)(2,1)}), bf16[32,16,512]{2,0,1:T(8,128)(2,1)S(1)}, u32[]{:S(2)}, u32[]{:S(2)}) async-start(bf16[32,16,512]{2,0,1:T(8,128)(2,1)} %copy.119), calls=%async_computation | async-start | bytes 1048576 | tf_op jit(solution)/shard_map/all_to_all | solution.py:243
  35.8 1.0 copy.125
  37.0 2.3 %convolution_convert_fusion.13 = bf16[512,512]{0,1:T(8,128)(2,1)} fusion(bf16[512,1,512]{2,0,1:T(8,128)(2,1)S(1)} %copy-done.13, bf16[512,2048]{1,0:T(8,128)(2,1)} %param.12), kind=kOutput, calls=%fused_computation.57 | convolution fusion | flops 268697600 | bytes 1572864 | tf_op jit(solution)/shard_map/tbe,de->tbd/dot_general | solution.py:192
  39.3 10.9 %all-to-all-done = bf16[32,16,512]{2,0,1:T(8,128)(2,1)S(1)} async-done(((bf16[32,16,512]{2,0,1:T(8,128)(2,1)}), bf16[32,16,512]{2,0,1:T(8,128)(2,1)S(1)}, u32[]{:S(2)}, u32[]{:S(2)}) %all-to-all-start) | async-done | bytes 524320 | tf_op jit(solution)/shard_map/all_to_all | solution.py:243
  51.7 3.7 %convolution_convert_fusion.1 = bf16[512,1536]{1,0:T(8,128)(2,1)} fusion(bf16[512,2048]{1,0:T(8,128)(2,1)} %param.12, f32[512,512]{0,1:T(8,128)S(1)} %copy.122, f32[512]{0:T(512)S(1)} %copy-done.31, f32[512]{0:T(512)S(1)} %rsqrt.21), kind=kOutput, calls=%fused_computation.13 | convolution fusion | flops 806879232 | bytes 4198400 | tf_op jit(solution)/shard_map/tbd,de->tbe/dot_general | solution.py:188
  55.4 1.7 copy.123
  57.1 5.4 %fusion.87 = (f32[8,512]{1,0:T(8,128)S(1)}, f32[8,512,512]{1,2,0:T(8,128)}) fusion(pred[512,512]{0,1:T(8,128)(4,1)S(1)} %broadcast_compare_fusion, bf16[512,3,8,64]{0,3,2,1:T(8,128)(2,1)S(1)} %bitcast.218), kind=kOutput, calls=%fused_computation.141 | convolution fusion | flops 276824576 | bytes 9715712 | tf_op jit(solution)/shard_map/while/body/eval_jaxpr/sub | solution.py:39
  62.5 4.7 %fusion.6 = bf16[8,512,512]{1,2,0:T(8,128)(2,1)S(1)} fusion(f32[8,512,512]{1,2,0:T(8,128)} %get-tuple-element.48, f32[8,512]{1,0:T(8,128)S(1)} %get-tuple-element.47), kind=kLoop, calls=%fused_computation.10 | loop fusion | flops 4194304 | bytes 12599296 | tf_op jit(solution)/shard_map/while/body/eval_jaxpr/convert_element_type | solution.py:48
  68.0 1.4 fusion.34
  69.4 1.4 copy-done.2
  70.7 1.8 %multiply_convert_fusion = bf16[8,512,512]{1,2,0:T(8,128)(2,1)S(1)} fusion(f32[8,512]{1,0:T(8,128)S(1)} %get-tuple-element.49, f32[8,512,512]{1,2,0:T(8,128)S(1)} %copy-done.2, f32[8,512]{1,0:T(8,128)S(1)} %get-tuple-element.47, bf16[8,512,64]{1,2,0:T(8,128)(2,1)S(1)} %bitcast.233, bf16[512,3,8,64]{0,3,2,1:T(8,128)(2,1)S(1)} %bitcast.220), kind=kOutput, calls=%fused_computation.2 | convolution fusion | flops 278921216 | bytes 13664256 | tf_op jit(solution)/shard_map/while/body/eval_jaxpr/...uo,...ao->...ua/dot_general | solution.py:73
  72.6 1.4 fusion.33
  74.9 1.2 copy-done.10
  76.2 1.0 copy-done.28
  77.2 1.0 multiply_reduce_fusion.1
  79.1 1.1 reduce.6
  80.4 1.2 reshape.332
  81.6 4.1 %all-to-all-start.1 = ((bf16[16,2,8192]{2,1,0:T(2,128)(2,1)}), bf16[16,2,8192]{2,1,0:T(2,128)(2,1)S(1)}, u32[]{:S(2)}, u32[]{:S(2)}) async-start(bf16[16,2,8192]{2,1,0:T(2,128)(2,1)} %reshape.332), calls=%async_computation.1 | async-start | bytes 1048576 | tf_op jit(solution)/shard_map/all_to_all | solution.py:275
  86.5 2.6 %convolution_convert_fusion = bf16[512,1536]{1,0:T(8,128)(2,1)S(1)} fusion(bf16[512,1536]{0,1:T(8,128)(2,1)} %bitcast.235, f32[512,1,1,1,1,1,512]{6,0,5,4,3,2,1:T(8,128)S(1)} %bitcast.214, f32[512]{0:T(512)S(1)} %copy-done.31, f32[512]{0:T(512)S(1)} %rsqrt.21), kind=kOutput, calls=%fused_computation.12 | convolution fusion | flops 806879232 | bytes 4198400 | tf_op jit(solution)/shard_map/tbd,tbe->de/dot_general | solution.py:198
  89.1 1.6 pad_maximum_fusion
  90.7 9.5 %all-to-all-done.1 = bf16[16,2,8192]{2,1,0:T(2,128)(2,1)S(1)} async-done(((bf16[16,2,8192]{2,1,0:T(2,128)(2,1)}), bf16[16,2,8192]{2,1,0:T(2,128)(2,1)S(1)}, u32[]{:S(2)}, u32[]{:S(2)}) %all-to-all-start.1) | async-done | bytes 524320 | tf_op jit(solution)/shard_map/all_to_all | solution.py:275
  103.2 2.3 %convolution_convert_fusion.10 = bf16[32,16,512]{2,1,0:T(8,128)(2,1)} fusion(bf16[32,16,512]{2,1,0:T(8,128)(2,1)S(1)} %bitcast.230, bf16[512,2048]{1,0:T(8,128)(2,1)} %param.11), kind=kOutput, calls=%fused_computation.54 | convolution fusion | flops 268697600 | bytes 1572864 | tf_op jit(solution)/shard_map/tbe,de->tbd/dot_general | solution.py:192
  105.5 1.7 %reshape.321 = bf16[32,16,8,64]{3,2,1,0:T(8,128)(2,1)S(1)} reshape(bf16[32,16,512]{2,1,0:T(8,128)(2,1)} %convolution_convert_fusion.10) | data formatting | bytes 1048576 | tf_op jit(solution)/shard_map/reshape | solution.py:156
  107.9 1.0 copy-done.35
  109.7 1.7 fusion.24
  111.4 0.8 fusion.61
  112.2 4.4 %all-to-all-start.2 = ((bf16[8,32,512]{2,1,0:T(8,128)(2,1)}), bf16[8,32,512]{2,1,0:T(8,128)(2,1)S(1)}, u32[]{:S(2)}, u32[]{:S(2)}) async-start(bf16[8,32,512]{2,1,0:T(8,128)(2,1)} %fusion.61), calls=%async_computation.2 | async-start | bytes 524288 | tf_op jit(solution)/shard_map/all_to_all | solution.py:210
  120.0 3.0 %reshape.322 = bf16[32,16,1536]{2,1,0:T(8,128)(2,1)} reshape(bf16[32,16,3,8,64]{4,3,2,1,0:T(8,128)(2,1)S(1)} %copy.140) | data formatting | bytes 3145728 | tf_op jit(solution)/shard_map/reshape | solution.py:169
  123.0 6.2 %all-to-all-done.2 = bf16[8,32,512]{2,1,0:T(8,128)(2,1)S(1)} async-done(((bf16[8,32,512]{2,1,0:T(8,128)(2,1)}), bf16[8,32,512]{2,1,0:T(8,128)(2,1)S(1)}, u32[]{:S(2)}, u32[]{:S(2)}) %all-to-all-start.2) | async-done | bytes 262176 | tf_op jit(solution)/shard_map/all_to_all | solution.py:210
  129.2 2.7 %fusion.75 = f32[512,1536,1]{1,0,2:T(8,128)S(1)} fusion(bf16[32,16,1536]{2,1,0:T(8,128)(2,1)} %reshape.322, bf16[32,16,512]{2,1,0:T(8,128)(2,1)} %param.9, f32[512]{0:T(512)S(1)} %copy-done.32, f32[32,16]{1,0:T(8,128)S(1)} %add_rsqrt_fusion), kind=kOutput, calls=%fused_computation.121 | convolution fusion | flops 806354944 | bytes 5246976 | tf_op jit(solution)/shard_map/tbd,tbe->de/dot_general | solution.py:198
  132.1 2.3 %collective-permute-done.1 = bf16[8,32,1536]{2,1,0:T(8,128)(2,1)S(1)} collective-permute-done((bf16[8,32,1536]{2,1,0:T(8,128)(2,1)S(1)}, bf16[8,32,1536]{2,1,0:T(8,128)(2,1)S(1)}, u32[]{:S(2)}, u32[]{:S(2)}) %collective-permute-start.1) | collective-permute-done | bytes 786464 | tf_op jit(solution)/shard_map/ppermute | solution.py:208
  134.4 1.2 fusion.10
  135.7 4.7 %all-to-all-start.3 = ((bf16[8,32,1536]{2,1,0:T(8,128)(2,1)}), bf16[8,32,1536]{2,1,0:T(8,128)(2,1)S(1)}, u32[]{:S(2)}, u32[]{:S(2)}) async-start(bf16[8,32,1536]{2,1,0:T(8,128)(2,1)} %fusion.10), calls=%async_computation.3 | async-start | bytes 1572864 | tf_op jit(solution)/shard_map/all_to_all | solution.py:210
  140.4 2.4 %fusion.32 = bf16[512,1,512]{2,0,1:T(8,128)(2,1)} fusion(f32[512,512]{1,0:T(8,128)S(1)} %bitcast.215, bf16[512,512]{0,1:T(8,128)(2,1)S(1)} %bitcast.224, bf16[512,2048]{1,0:T(8,128)(2,1)} %param.12), kind=kOutput, calls=%fused_computation.62 | convolution fusion | flops 268959744 | bytes 2621440 | tf_op jit(solution)/shard_map/tbd,de->tbe/dot_general | solution.py:188
  142.8 2.6 %fusion.43 = (f32[32,16]{1,0:T(8,128)S(1)}, f32[32,16,512]{2,1,0:T(8,128)S(1)}) fusion(bf16[32,16,512]{2,1,0:T(8,128)(2,1)S(1)} %copy-done.16, f32[512]{0:T(512)S(1)} %copy-done.32, bf16[32,16,1536]{2,1,0:T(8,128)(2,1)S(1)} %copy-done.22, bf16[512,2048]{1,0:T(8,128)(2,1)} %param.11), kind=kOutput, calls=%fused_computation.73 | convolution fusion | flops 806354432 | bytes 4722688 | tf_op jit(solution)/shard_map/tbe,de->tbd/dot_general | solution.py:192
  145.4 1.2 fusion.41
  146.6 10.7 %reduce-scatter.2.cloned.1.call-done = bf16[32,2048]{1,0:T(8,128)(2,1)} async-done(((bf16[512,2048]{1,0:T(8,128)(2,1)}), bf16[32,2048]{1,0:T(8,128)(2,1)}) %reduce-scatter.2.cloned.1.call-update) | async-done | bytes 131088 | tf_op jit(solution)/shard_map/reduce_scatter | solution.py:215
  157.2 1.6 convert_element_type.266
  158.9 6.1 %all-to-all-done.3 = bf16[8,32,1536]{2,1,0:T(8,128)(2,1)S(1)} async-done(((bf16[8,32,1536]{2,1,0:T(8,128)(2,1)}), bf16[8,32,1536]{2,1,0:T(8,128)(2,1)S(1)}, u32[]{:S(2)}, u32[]{:S(2)}) %all-to-all-start.3) | async-done | bytes 786464 | tf_op jit(solution)/shard_map/all_to_all | solution.py:210
  (119 shorter events, 15.9 us)
Async XLA Ops:
  16.2 2.2 %copy-start.30 = (s32[16,16]{1,0:T(8,128)S(1)}, s32[16,16]{1,0:T(8,128)}, u32[]{:S(2)}) copy-start(s32[16,16]{1,0:T(8,128)} %param.15) | copy-start | bytes 3076
  16.2 2.2 %copy-start.29 = (s32[512]{0:T(512)S(1)}, s32[512]{0:T(512)}, u32[]{:S(2)}) copy-start(s32[512]{0:T(512)} %param.17) | copy-start | bytes 6148
  16.2 2.3 %copy-start.33 = (s32[4]{0:T(128)S(1)}, s32[4]{0:T(128)}, u32[]{:S(2)}) copy-start(s32[4]{0:T(128)} %param.16) | copy-start | bytes 52
  18.8 4.3 %copy-start.23 = (bf16[32,16,1,8,64]{4,3,2,1,0:T(8,128)(2,1)S(1)}, bf16[32,16,1,8,64]{4,3,2,1,0:T(8,128)(2,1)}, u32[]{:S(2)}) copy-start(bf16[32,16,1,8,64]{4,3,2,1,0:T(8,128)(2,1)} %get-tuple-element.44) | copy-start | bytes 1572868
  21.8 1.4 copy-start.34
  21.8 1.9 %copy-start.36 = (f32[32,8,16]{2,1,0:T(8,128)}, f32[32,8,16]{2,1,0:T(8,128)S(1)}, u32[]{:S(2)}) copy-start(f32[32,8,16]{2,1,0:T(8,128)S(1)} %get-tuple-element.45) | copy-start | bytes 49156
  23.7 1.0 copy-start.7
  23.7 1.9 %copy-start.15 = (bf16[32,16,512]{2,1,0:T(8,128)(2,1)S(1)}, bf16[32,16,512]{2,1,0:T(8,128)(2,1)}, u32[]{:S(2)}) copy-start(bf16[32,16,512]{2,1,0:T(8,128)(2,1)} %param.9) | copy-start | bytes 1572868
  25.6 2.8 %copy-start.26 = (bf16[32,16,512]{2,1,0:T(8,128)(2,1)}, bf16[32,16,512]{2,1,0:T(8,128)(2,1)S(1)}, u32[]{:S(2)}) copy-start(bf16[32,16,512]{2,1,0:T(8,128)(2,1)S(1)} %reshape.314) | copy-start | bytes 1572868
  25.6 10.2 %copy-start.13 = (bf16[512,1,512]{2,0,1:T(8,128)(2,1)S(1)}, bf16[512,1,512]{2,0,1:T(8,128)(2,1)}, u32[]{:S(2)}) copy-start(bf16[512,1,512]{2,0,1:T(8,128)(2,1)} %param.10) | copy-start | bytes 1572868
  28.4 21.9 %all-to-all-start = ((bf16[32,16,512]{2,0,1:T(8,128)(2,1)}), bf16[32,16,512]{2,0,1:T(8,128)(2,1)S(1)}, u32[]{:S(2)}, u32[]{:S(2)}) async-start(bf16[32,16,512]{2,0,1:T(8,128)(2,1)} %copy.119), calls=%async_computation | async-start | bytes 1048576 | tf_op jit(solution)/shard_map/all_to_all | solution.py:243
  39.3 12.4 %copy-start.31 = (f32[512]{0:T(512)S(1)}, f32[512]{0:T(512)}, u32[]{:S(2)}) copy-start(f32[512]{0:T(512)} %param.14) | copy-start | bytes 6148
  50.4 36.1 %copy-start = (f32[32,16,512]{2,0,1:T(8,128)}, f32[32,16,512]{2,0,1:T(8,128)S(1)}, u32[]{:S(2)}) copy-start(f32[32,16,512]{2,0,1:T(8,128)S(1)} %convert_element_type.271) | copy-start | bytes 3145732
  50.7 1.0 copy-start.9
  62.5 4.7 %copy-start.20 = (bf16[512,512]{0,1:T(8,128)(2,1)S(1)}, bf16[512,512]{0,1:T(8,128)(2,1)}, u32[]{:S(2)}) copy-start(bf16[512,512]{0,1:T(8,128)(2,1)} %convolution_convert_fusion.13) | copy-start | bytes 1572868
  67.2 3.6 %copy-start.2 = (f32[8,512,512]{1,2,0:T(8,128)S(1)}, f32[8,512,512]{1,2,0:T(8,128)}, u32[]{:S(2)}) copy-start(f32[8,512,512]{1,2,0:T(8,128)} %get-tuple-element.48) | copy-start | bytes 25165828
  68.0 18.0 %copy-start.3 = (bf16[8,512,64]{1,2,0:T(8,128)(2,1)}, bf16[8,512,64]{1,2,0:T(8,128)(2,1)S(1)}, u32[]{:S(2)}) copy-start(bf16[8,512,64]{1,2,0:T(8,128)(2,1)S(1)} %get-tuple-element.50) | copy-start | bytes 1572868
  74.7 1.5 copy-start.10
  74.7 2.5 %copy-start.28 = (bf16[512,2048]{1,0:T(8,128)(2,1)S(1)}, bf16[512,2048]{1,0:T(8,128)(2,1)}, u32[]{:S(2)}) copy-start(bf16[512,2048]{1,0:T(8,128)(2,1)} %param.12) | copy-start | bytes 6291460
  74.9 3.3 %copy-start.21 = (bf16[3,8,512,64]{2,3,1,0:T(8,128)(2,1)}, bf16[3,8,512,64]{2,3,1,0:T(8,128)(2,1)S(1)}, u32[]{:S(2)}) copy-start(bf16[3,8,512,64]{2,3,1,0:T(8,128)(2,1)S(1)} %pad_maximum_fusion.1) | copy-start | bytes 4718596
  77.2 1.0 copy-start.19
  79.1 6.9 %copy-start.14 = (bf16[512,1,512]{2,0,1:T(8,128)(2,1)S(1)}, bf16[512,1,512]{2,0,1:T(8,128)(2,1)}, u32[]{:S(2)}) copy-start(bf16[512,1,512]{2,0,1:T(8,128)(2,1)} %param.10) | copy-start | bytes 1572868
  81.6 18.6 %all-to-all-start.1 = ((bf16[16,2,8192]{2,1,0:T(2,128)(2,1)}), bf16[16,2,8192]{2,1,0:T(2,128)(2,1)S(1)}, u32[]{:S(2)}, u32[]{:S(2)}) async-start(bf16[16,2,8192]{2,1,0:T(2,128)(2,1)} %reshape.332), calls=%async_computation.1 | async-start | bytes 1048576 | tf_op jit(solution)/shard_map/all_to_all | solution.py:275
  85.7 71.5 %reduce-scatter.2.cloned.1.call-start = ((), (), s32[]{:S(2)}) async-start(), calls=%async_computation.5 | async-start | bytes 2228224 | tf_op jit(solution)/shard_map/reduce_scatter | solution.py:215
  90.7 10.2 %copy-start.27 = (bf16[32,16,512]{2,1,0:T(8,128)(2,1)S(1)}, bf16[32,16,512]{2,1,0:T(8,128)(2,1)}, u32[]{:S(2)}) copy-start(bf16[32,16,512]{2,1,0:T(8,128)(2,1)} %copy-done.26) | copy-start | bytes 1572868
  101.4 1.0 copy-start.11
  101.7 1.4 copy-start.17
  101.8 5.5 %copy-start.8 = (bf16[32,8,16,64]{3,2,1,0:T(8,128)(2,1)S(1)}, bf16[32,8,16,64]{3,2,1,0:T(8,128)(2,1)}, u32[]{:S(2)}) copy-start(bf16[32,8,16,64]{3,2,1,0:T(8,128)(2,1)} %copy-done.7) | copy-start | bytes 1572868
  103.2 8.2 %collective-permute-start = (bf16[8,32,512]{2,1,0:T(8,128)(2,1)}, bf16[8,32,512]{2,1,0:T(8,128)(2,1)S(1)}, u32[]{:S(2)}, u32[]{:S(2)}) collective-permute-start(bf16[8,32,512]{2,1,0:T(8,128)(2,1)} %fusion.78), channel_id=1, source_target_pairs={{0,1},{1,0},{2,3},{3,2},{4,5},{5,4},{6,7},{7,6},{8,9},{9,8},{10,11... | collective-permute-start | bytes 786440 | tf_op jit(solution)/shard_map/ppermute | solution.py:208
  105.5 2.4 %copy-start.24 = (bf16[32,16,1,8,64]{4,3,2,1,0:T(8,128)(2,1)S(1)}, bf16[32,16,1,8,64]{4,3,2,1,0:T(8,128)(2,1)}, u32[]{:S(2)}) copy-start(bf16[32,16,1,8,64]{4,3,2,1,0:T(8,128)(2,1)} %get-tuple-element.44) | copy-start | bytes 1572868
  105.5 2.4 %copy-start.37 = (f32[32,8,16]{2,1,0:T(8,128)S(1)}, f32[32,8,16]{2,1,0:T(8,128)}, u32[]{:S(2)}) copy-start(f32[32,8,16]{2,1,0:T(8,128)} %copy-done.36) | copy-start | bytes 49156
  107.3 1.6 copy-start.35
  109.7 1.7 copy-start.12
  111.4 5.3 %copy-start.6 = (bf16[32,16,1,8,64]{4,3,2,1,0:T(8,128)(2,1)S(1)}, bf16[32,16,1,8,64]{4,3,2,1,0:T(8,128)(2,1)}, u32[]{:S(2)}) copy-start(bf16[32,16,1,8,64]{4,3,2,1,0:T(8,128)(2,1)} %get-tuple-element.42) | copy-start | bytes 1572868
  112.2 4.9 %copy-start.5 = (bf16[32,16,1,8,64]{4,3,2,1,0:T(8,128)(2,1)S(1)}, bf16[32,16,1,8,64]{4,3,2,1,0:T(8,128)(2,1)}, u32[]{:S(2)}) copy-start(bf16[32,16,1,8,64]{4,3,2,1,0:T(8,128)(2,1)} %get-tuple-element.43) | copy-start | bytes 1572868
  112.2 16.9 %all-to-all-start.2 = ((bf16[8,32,512]{2,1,0:T(8,128)(2,1)}), bf16[8,32,512]{2,1,0:T(8,128)(2,1)S(1)}, u32[]{:S(2)}, u32[]{:S(2)}) async-start(bf16[8,32,512]{2,1,0:T(8,128)(2,1)} %fusion.61), calls=%async_computation.2 | async-start | bytes 524288 | tf_op jit(solution)/shard_map/all_to_all | solution.py:210
  117.2 1.2 copy-start.25
  120.0 9.2 %copy-start.32 = (f32[512]{0:T(512)S(1)}, f32[512]{0:T(512)}, u32[]{:S(2)}) copy-start(f32[512]{0:T(512)} %param.13) | copy-start | bytes 6148
  132.0 8.3 %copy-start.1 = (f32[32,16,512]{2,0,1:T(8,128)S(1)}, f32[32,16,512]{2,0,1:T(8,128)}, u32[]{:S(2)}) copy-start(f32[32,16,512]{2,0,1:T(8,128)} %copy-done) | copy-start | bytes 3145732
  132.0 8.3 %copy-start.4 = (bf16[8,512,64]{1,2,0:T(8,128)(2,1)S(1)}, bf16[8,512,64]{1,2,0:T(8,128)(2,1)}, u32[]{:S(2)}) copy-start(bf16[8,512,64]{1,2,0:T(8,128)(2,1)} %copy-done.3) | copy-start | bytes 1572868
  132.1 2.4 %collective-permute-start.1 = (bf16[8,32,1536]{2,1,0:T(8,128)(2,1)S(1)}, bf16[8,32,1536]{2,1,0:T(8,128)(2,1)S(1)}, u32[]{:S(2)}, u32[]{:S(2)}) collective-permute-start(bf16[8,32,1536]{2,1,0:T(8,128)(2,1)S(1)} %fusion.56), channel_id=1, source_target_pairs={{0,1},{1,0},{2,3},{3,2},{4,5},{5,4},{6,7},{7,6},{8,9},{9,8},{10,11... | collective-permute-start | bytes 2359304 | tf_op jit(solution)/shard_map/ppermute | solution.py:208
  135.7 7.1 %copy-start.16 = (bf16[32,16,512]{2,1,0:T(8,128)(2,1)S(1)}, bf16[32,16,512]{2,1,0:T(8,128)(2,1)}, u32[]{:S(2)}) copy-start(bf16[32,16,512]{2,1,0:T(8,128)(2,1)} %param.9) | copy-start | bytes 1572868
  135.7 29.3 %all-to-all-start.3 = ((bf16[8,32,1536]{2,1,0:T(8,128)(2,1)}), bf16[8,32,1536]{2,1,0:T(8,128)(2,1)S(1)}, u32[]{:S(2)}, u32[]{:S(2)}) async-start(bf16[8,32,1536]{2,1,0:T(8,128)(2,1)} %fusion.10), calls=%async_computation.3 | async-start | bytes 1572864 | tf_op jit(solution)/shard_map/all_to_all | solution.py:210
  140.4 2.4 %copy-start.22 = (bf16[32,16,1536]{2,1,0:T(8,128)(2,1)S(1)}, bf16[32,16,1536]{2,1,0:T(8,128)(2,1)}, u32[]{:S(2)}) copy-start(bf16[32,16,1536]{2,1,0:T(8,128)(2,1)} %reshape.322) | copy-start | bytes 4718596
  142.8 2.6 %copy-start.18 = (bf16[16,32,1,512]{3,0,1,2:T(8,128)(2,1)S(1)}, bf16[16,32,1,512]{3,0,1,2:T(8,128)(2,1)}, u32[]{:S(2)}) copy-start(bf16[16,32,1,512]{3,0,1,2:T(8,128)(2,1)} %copy-done.17) | copy-start | bytes 1572868
Sparse Core Ops, SparseCore 0:
  90.8 66.3 reduce-scatter.1

commit v6 on v5

--- a/solution.py
+++ b/solution.py
@@ -275,7 +275,7 @@
     grad_middle_time = lax.all_to_all(grad_middle, ("outer", "core"), split_axis=0, concat_axis=1, tiled=True)
     normed_cols = normed_two
     context_cols = temporal_context
-    temporal_grad = scatter_rows(
+    temporal_grad = reduce_rows(
         jnp.concatenate(
             [weight_term(normed_cols, grad_temporal_proj), weight_term(context_cols, grad_out)],
             axis=1,
@@ -290,7 +290,9 @@
         spatial_proj, allowed_space, spatial_context, grad_spatial_context
     )
     spatial_term = reduce_rows(spatial_term)
-    spatial_term, grad_spatial_proj = lax.optimization_barrier((spatial_term, grad_spatial_proj))
+    spatial_term, temporal_grad, grad_spatial_proj = lax.optimization_barrier(
+        (spatial_term, temporal_grad, grad_spatial_proj)
+    )
     grad_normed_one = project_back(grad_spatial_proj, spatial_weights[:, : 3 * model_width])
     grad_activity = (
         grad_middle_time.astype(jnp.float32)

time: 174 us -> 187 us (1.075)
  between operations: 14.7 us -> 1.22 us
  local copies, waits for them, and re-layouts: 28.8 us -> 38.6 us
  other arithmetic: 18 us -> 26.3 us
  waiting for transfers between devices: 45.6 us -> 50.7 us
  starting transfers between devices: 20.9 us -> 24 us
    all_to_all x2 -> x3, waiting for transfers between devices: 12.3 us -> 28.4 us  [reduce_rows(): pieces = lax.all_to_all(pieces, 'outer', 0, 0, tiled=True)]
    reduce_scatter x1 -> x0, waiting for transfers between devices: 10.7 us -> none  [scatter_rows(): lax.psum_scatter(partial.astype(jnp.bfloat16), ('outer', 'core'), scatter...]
    unnamed x82 -> x68, local copies, waits for them, and re-layouts: 12 us -> 17.1 us
    convert_element_type x2 -> x3, other arithmetic: 2.09 us -> 6.21 us  [reduce_rows(): pieces = (kept + taken.astype(jnp.float32)).astype(jnp.bfloat16)]
    all_to_all x2 -> x3, starting transfers between devices: 9.09 us -> 12 us  [reduce_rows(): pieces = lax.all_to_all(pieces, 'outer', 0, 0, tiled=True)]
    convert_element_type x2, other arithmetic: 1.43 us -> 3.84 us  [per_device(): grad_middle = (grad_out.astype(jnp.float32) + norm_backward(middle_block,...]
    reshape x1, local copies, waits for them, and re-layouts: 3 us -> 5.4 us  [spatial_backward(): jnp.stack(derivative_collection, axis=0).transpose(1, 3, 0, 2, 4)]
    reduce_sum x2 -> x3, other arithmetic: 0.14 us -> 2.24 us  [reduce_rows(): return jnp.sum(pieces.astype(jnp.float32), axis=0)]
  transfers between devices with their start and end apart: 7 -> 8, of which waited for: 6 -> 6; matrix products, arithmetic and copies ran while one was open for 21% -> 23% of each run, Pallas kernels for 0% -> 0%
where the time goes in v6:
time: 187 us; the launch traced here: 185 us
  waiting for transfers between devices  50.7 us (27%)
  matrix products  44.7 us (24%)
  local copies, waits for them, and re-layouts  38.6 us (21%)
  other arithmetic  26.3 us (14%)
  starting transfers between devices  24 us (13%)
    all_to_all x3, waiting for transfers between devices, reduce_rows(): pieces = lax.all_to_all(pieces, 'outer', 0, 0, tiled=True)  28.4 us
    unnamed x68, local copies, waits for them, and re-layouts  17.1 us
    all_to_all x3, starting transfers between devices, reduce_rows(): pieces = lax.all_to_all(pieces, 'outer', 0, 0, tiled=True)  12 us
    dot_general x4, matrix products, project(): jnp.einsum('tbd,de->tbe', rows, coefficient_array, preferred_element_type...  11.5 us
    all_to_all x1, waiting for transfers between devices, per_device(): lax.all_to_all(middle, ('outer', 'core'), split_axis=1, concat_axis=0, ti...  10.9 us
    all_to_all x1, waiting for transfers between devices, per_device(): lax.all_to_all(grad_middle, ('outer', 'core'), split_axis=0, concat_axis=...  9.09 us
    sub x2, matrix products, normalized_affinity(): expo = jnp.exp(unnormalized_affinities - row_max)  8.34 us
    dot_general x4, matrix products, project_back(): jnp.einsum('tbe,de->tbd', derivative_collection, coefficient_array, prefe...  8.1 us
  transfers between devices with their start and end apart: 8, of which 6 were waited for; matrix products, arithmetic and copies ran while one was open for 23% of the time, Pallas kernels for 0%

profile of v6, /device:TPU:0, one launch (start us, length us, event | category | flops | bytes accessed | tf_op | source)
XLA Modules:
  0.0 185.5 jit_solution(6402426490220170627)
XLA Ops:
  0.7 1.2 fusion.45
  1.9 3.8 %convolution_convert_fusion.1 = bf16[32,16,1536]{2,1,0:T(8,128)(2,1)} fusion(bf16[512,2048]{1,0:T(8,128)(2,1)} %param.11, bf16[32,16,512]{2,1,0:T(8,128)(2,1)} %param.9, f32[512]{0:T(512)} %param.13, f32[32,16]{1,0:T(8,128)S(1)} %add_rsqrt_fusion), kind=kOutput, calls=%fused_computation.14 | convolution fusion | flops 807141376 | bytes 3674112 | tf_op jit(solution)/shard_map/tbd,de->tbe/dot_general | solution.py:188
  5.7 4.0 %reshape.321 = bf16[32,16,3,8,64]{4,3,2,1,0:T(8,128)(2,1)S(1)} reshape(bf16[32,16,1536]{2,1,0:T(8,128)(2,1)} %convolution_convert_fusion.1) | data formatting | bytes 3145728 | tf_op jit(solution)/shard_map/reshape | solution.py:136
  9.7 2.2 %fusion.91 = (bf16[32,16,1,8,64]{4,3,2,1,0:T(8,128)(2,1)}, bf16[32,16,1,8,64]{4,3,2,1,0:T(8,128)(2,1)}, bf16[32,16,1,8,64]{4,3,2,1,0:T(8,128)(2,1)}) fusion(bf16[32,16,3,8,64]{4,3,2,1,0:T(8,128)(2,1)S(1)} %reshape.321), kind=kLoop, calls=%fused_computation.146 | loop fusion | bytes 3145728 | tf_op jit(solution)/shard_map/slice | solution.py:139
  12.3 2.9 %fusion.92 = (f32[32,8,16]{2,1,0:T(8,128)S(1)}, f32[32,8,16,16]{2,3,1,0:T(8,128)S(1)}) fusion(pred[32,16,16]{1,2,0:T(8,128)(4,1)S(1)} %and_or_fusion, bf16[32,16,1,8,64]{4,3,2,1,0:T(8,128)(2,1)} %get-tuple-element.45, bf16[32,16,1,8,64]{4,3,2,1,0:T(8,128)(2,1)} %get-tuple-element.44), kind=kOutput, calls=%fused_computation.147 | convolution fusion | flops 8650767 | bytes 1335296 | tf_op jit(solution)/shard_map/sub | solution.py:39
  15.3 1.3 copy-done.27
  19.1 1.7 fusion.31
  21.9 7.4 %all-to-all-start = ((bf16[32,16,512]{2,0,1:T(8,128)(2,1)}), bf16[32,16,512]{2,0,1:T(8,128)(2,1)S(1)}, u32[]{:S(2)}, u32[]{:S(2)}) async-start(bf16[32,16,512]{2,0,1:T(8,128)(2,1)} %copy.131), calls=%async_computation | async-start | bytes 1048576 | tf_op jit(solution)/shard_map/all_to_all | solution.py:243
  30.5 2.3 %convolution_convert_fusion.11 = bf16[512,512]{0,1:T(8,128)(2,1)} fusion(bf16[512,1,512]{2,0,1:T(8,128)(2,1)S(1)} %copy-done.9, bf16[512,2048]{1,0:T(8,128)(2,1)} %param.12), kind=kOutput, calls=%fused_computation.61 | convolution fusion | flops 268697600 | bytes 1572864 | tf_op jit(solution)/shard_map/tbe,de->tbd/dot_general | solution.py:192
  32.8 10.9 %all-to-all-done = bf16[32,16,512]{2,0,1:T(8,128)(2,1)S(1)} async-done(((bf16[32,16,512]{2,0,1:T(8,128)(2,1)}), bf16[32,16,512]{2,0,1:T(8,128)(2,1)S(1)}, u32[]{:S(2)}, u32[]{:S(2)}) %all-to-all-start) | async-done | bytes 524320 | tf_op jit(solution)/shard_map/all_to_all | solution.py:243
  45.2 3.7 %convolution_convert_fusion = bf16[512,1536]{1,0:T(8,128)(2,1)} fusion(bf16[512,2048]{1,0:T(8,128)(2,1)} %param.12, f32[512,512]{0,1:T(8,128)S(1)} %copy.134, f32[512]{0:T(512)S(1)} %copy-done.24, f32[512]{0:T(512)S(1)} %rsqrt.21), kind=kOutput, calls=%fused_computation.13 | convolution fusion | flops 806879232 | bytes 4198400 | tf_op jit(solution)/shard_map/tbd,de->tbe/dot_general | solution.py:188
  48.9 1.7 copy.135
  50.6 5.4 %fusion.93 = (f32[8,512]{1,0:T(8,128)S(1)}, f32[8,512,512]{1,2,0:T(8,128)}) fusion(pred[512,512]{0,1:T(8,128)(4,1)S(1)} %broadcast_compare_fusion, bf16[512,3,8,64]{0,3,2,1:T(8,128)(2,1)S(1)} %bitcast.247), kind=kOutput, calls=%fused_computation.148 | convolution fusion | flops 276824576 | bytes 9715712 | tf_op jit(solution)/shard_map/while/body/eval_jaxpr/sub | solution.py:39
  56.0 4.7 %fusion.6 = bf16[8,512,512]{1,2,0:T(8,128)(2,1)S(1)} fusion(f32[8,512,512]{1,2,0:T(8,128)} %get-tuple-element.50, f32[8,512]{1,0:T(8,128)S(1)} %get-tuple-element.49), kind=kLoop, calls=%fused_computation.11 | loop fusion | flops 4194304 | bytes 12599296 | tf_op jit(solution)/shard_map/while/body/eval_jaxpr/convert_element_type | solution.py:48
  61.5 1.4 fusion.37
  62.9 1.2 copy-done.1
  64.1 1.8 multiply_convert_fusion
  65.9 1.4 fusion.36
  72.7 2.7 %reduce.6 = bf16[512,512]{0,1:T(8,128)(2,1)} reduce(bf16[512,1,512]{0,2,1:T(8,128)(2,1)} %fusion.50, bf16[]{:T(256)} %broadcast.209), dimensions={1}, to_apply=%copy.143.reduce_sub_computation | reduce | bytes 1048578 | tf_op jit(solution)/shard_map/convert_element_type | solution.py:274
  75.4 2.0 %copy.208 = bf16[512,512]{1,0:T(8,128)(2,1)} copy(bf16[512,512]{0,1:T(8,128)(2,1)} %reduce.6) | data formatting | bytes 1048576
  77.4 2.2 %reshape.341 = bf16[16,2,8192]{2,1,0:T(2,128)(2,1)} reshape(bf16[512,512]{1,0:T(8,128)(2,1)} %copy.208) | data formatting | bytes 1048576
  79.7 4.5 %all-to-all-start.1 = ((bf16[16,2,8192]{2,1,0:T(2,128)(2,1)}), bf16[16,2,8192]{2,1,0:T(2,128)(2,1)}, u32[]{:S(2)}, u32[]{:S(2)}) async-start(bf16[16,2,8192]{2,1,0:T(2,128)(2,1)} %reshape.341), calls=%async_computation.1 | async-start | bytes 1048576 | tf_op jit(solution)/shard_map/all_to_all | solution.py:275
  84.1 1.2 fusion.62
  86.2 1.9 %copy-done = f32[512,2048]{1,0:T(8,128)} copy-done((f32[512,2048]{1,0:T(8,128)}, f32[512,2048]{1,0:T(8,128)S(1)}, u32[]{:S(2)}) %copy-start) | copy-done | bytes 4194328
  88.1 1.2 fusion.47
  89.3 9.1 %all-to-all-done.1 = bf16[16,2,8192]{2,1,0:T(2,128)(2,1)} async-done(((bf16[16,2,8192]{2,1,0:T(2,128)(2,1)}), bf16[16,2,8192]{2,1,0:T(2,128)(2,1)}, u32[]{:S(2)}, u32[]{:S(2)}) %all-to-all-start.1) | async-done | bytes 524320 | tf_op jit(solution)/shard_map/all_to_all | solution.py:275
  98.4 2.2 %reshape.342 = bf16[512,1,512]{2,1,0:T(2,128)(2,1)S(1)} reshape(bf16[16,2,8192]{2,1,0:T(2,128)(2,1)} %all-to-all-done.1) | data formatting | bytes 1048576
  101.0 1.6 convolution_bitcast_fusion
  103.4 2.3 %convolution_convert_fusion.8 = bf16[32,16,512]{2,1,0:T(8,128)(2,1)} fusion(bf16[32,16,512]{2,1,0:T(8,128)(2,1)S(1)} %bitcast.259, bf16[512,2048]{1,0:T(8,128)(2,1)} %param.11), kind=kOutput, calls=%fused_computation.58 | convolution fusion | flops 268697600 | bytes 1572864 | tf_op jit(solution)/shard_map/tbe,de->tbd/dot_general | solution.py:192
  105.7 2.4 %reshape.330 = bf16[32,16,8,64]{3,2,1,0:T(8,128)(2,1)} reshape(bf16[32,16,512]{2,1,0:T(8,128)(2,1)} %convolution_convert_fusion.8) | data formatting | bytes 1048576 | tf_op jit(solution)/shard_map/reshape | solution.py:156
  108.9 4.2 %all-to-all-start.2 = ((bf16[8,32,512]{2,1,0:T(8,128)(2,1)}), bf16[8,32,512]{2,1,0:T(8,128)(2,1)S(1)}, u32[]{:S(2)}, u32[]{:S(2)}) async-start(bf16[8,32,512]{2,1,0:T(8,128)(2,1)} %fusion.66), calls=%async_computation.2 | async-start | bytes 524288 | tf_op jit(solution)/shard_map/all_to_all | solution.py:210
  113.1 4.1 %fusion.9 = bf16[8,32,2048]{2,1,0:T(8,128)(2,1)} fusion(bf16[8,32,2048]{2,1,0:T(8,128)(2,1)} %collective-permute-done.1, f32[8,2,32,2048]{3,2,1,0:T(8,128)} %bitcast.239, pred[]{:T(512)S(6)} %eq.61), kind=kLoop, calls=%fused_computation.18 | loop fusion | flops 2097152 | bytes 6291457 | tf_op jit(solution)/shard_map/convert_element_type | solution.py:209
  117.2 5.2 %all-to-all-done.2 = bf16[8,32,512]{2,1,0:T(8,128)(2,1)S(1)} async-done(((bf16[8,32,512]{2,1,0:T(8,128)(2,1)}), bf16[8,32,512]{2,1,0:T(8,128)(2,1)S(1)}, u32[]{:S(2)}, u32[]{:S(2)}) %all-to-all-start.2) | async-done | bytes 262176 | tf_op jit(solution)/shard_map/all_to_all | solution.py:210
  122.4 4.2 %all-to-all-start.3 = ((bf16[8,32,2048]{2,1,0:T(8,128)(2,1)}), bf16[8,32,2048]{2,1,0:T(8,128)(2,1)}, u32[]{:S(2)}, u32[]{:S(2)}) async-start(bf16[8,32,2048]{2,1,0:T(8,128)(2,1)} %fusion.9), calls=%async_computation.3 | async-start | bytes 2097152 | tf_op jit(solution)/shard_map/all_to_all | solution.py:210
  126.7 2.0 %multiply_reduce_fusion = f32[32,8,16]{2,1,0:T(8,128)S(1)} fusion(bf16[32,8,16,64]{3,2,1,0:T(8,128)(2,1)S(1)} %copy-done.5, bf16[32,16,8,64]{3,2,1,0:T(8,128)(2,1)} %reshape.330), kind=kLoop, calls=%fused_computation.20 | loop fusion | flops 1044480 | bytes 1064960 | tf_op jit(solution)/shard_map/reduce_sum | solution.py:79
  128.7 2.4 %multiply_convert_fusion.1 = bf16[32,8,16,16]{2,3,1,0:T(8,128)(2,1)S(1)} fusion(f32[32,8,16]{2,1,0:T(8,128)S(1)} %multiply_reduce_fusion, bf16[32,16,1,8,64]{4,3,2,1,0:T(8,128)(2,1)S(1)} %copy-done.19, bf16[32,16,8,64]{3,2,1,0:T(8,128)(2,1)S(1)} %copy-done.8, f32[32,8,16,16]{2,3,1,0:T(8,128)} %copy-done.27, f32[32,8,16]{2,1,0:T(8,128)} %copy-done.29), kind=kOutput, calls=%fused_computation.19 | convolution fusion | flops 8716288 | bytes 1474560 | tf_op jit(solution)/shard_map/...uo,...ao->...ua/dot_general | solution.py:73
  135.4 2.5 %copy.157 = bf16[32,16,3,8,64]{4,3,2,1,0:T(8,128)(2,1)} copy(bf16[32,16,3,8,64]{4,1,3,0,2:T(8,128)(2,1)S(1)} %maximum_bitcast_fusion) | data formatting | bytes 3145728 | tf_op jit(solution)/shard_map/transpose | solution.py:169
  137.9 5.4 %reshape.331 = bf16[32,16,1536]{2,1,0:T(8,128)(2,1)} reshape(bf16[32,16,3,8,64]{4,3,2,1,0:T(8,128)(2,1)} %copy.157) | data formatting | bytes 3145728 | tf_op jit(solution)/shard_map/reshape | solution.py:169
  143.4 8.7 %all-to-all-done.3 = bf16[8,32,2048]{2,1,0:T(8,128)(2,1)} async-done(((bf16[8,32,2048]{2,1,0:T(8,128)(2,1)}), bf16[8,32,2048]{2,1,0:T(8,128)(2,1)}, u32[]{:S(2)}, u32[]{:S(2)}) %all-to-all-start.3) | async-done | bytes 1048608 | tf_op jit(solution)/shard_map/all_to_all | solution.py:210
  152.0 2.1 %convert_reduce_fusion = f32[32,2048]{1,0:T(8,128)} fusion(bf16[8,32,2048]{2,1,0:T(8,128)(2,1)} %all-to-all-done.3), kind=kLoop, calls=%fused_computation.21 | loop fusion | flops 983040 | bytes 1310720 | tf_op jit(solution)/shard_map/reduce_sum | solution.py:211
  154.1 2.5 %fusion.81 = f32[512,1536,1]{1,0,2:T(8,128)S(1)} fusion(bf16[32,16,1536]{2,1,0:T(8,128)(2,1)} %reshape.331, bf16[32,16,512]{2,1,0:T(8,128)(2,1)S(1)} %copy-done.12, f32[512]{0:T(512)S(1)} %copy-done.25, f32[32,16]{1,0:T(8,128)S(1)} %add_rsqrt_fusion), kind=kOutput, calls=%fused_computation.128 | convolution fusion | flops 806354944 | bytes 5246976 | tf_op jit(solution)/shard_map/tbd,tbe->de/dot_general | solution.py:198
  156.9 2.3 %collective-permute-done.2 = bf16[8,32,1536]{2,1,0:T(8,128)(2,1)S(1)} collective-permute-done((bf16[8,32,1536]{2,1,0:T(8,128)(2,1)S(1)}, bf16[8,32,1536]{2,1,0:T(8,128)(2,1)S(1)}, u32[]{:S(2)}, u32[]{:S(2)}) %collective-permute-start.2) | collective-permute-done | bytes 786464 | tf_op jit(solution)/shard_map/ppermute | solution.py:208
  159.1 1.3 fusion.13
  160.4 3.5 %all-to-all-start.4 = ((bf16[8,32,1536]{2,1,0:T(8,128)(2,1)}), bf16[8,32,1536]{2,1,0:T(8,128)(2,1)S(1)}, u32[]{:S(2)}, u32[]{:S(2)}) async-start(bf16[8,32,1536]{2,1,0:T(8,128)(2,1)} %fusion.13), calls=%async_computation.4 | async-start | bytes 1572864 | tf_op jit(solution)/shard_map/all_to_all | solution.py:210
  164.0 2.4 %fusion.35 = bf16[512,1,512]{2,0,1:T(8,128)(2,1)} fusion(f32[512,512]{1,0:T(8,128)S(1)} %bitcast.242, bf16[512,512]{0,1:T(8,128)(2,1)S(1)} %bitcast.253, bf16[512,2048]{1,0:T(8,128)(2,1)} %param.12), kind=kOutput, calls=%fused_computation.66 | convolution fusion | flops 268959744 | bytes 2621440 | tf_op jit(solution)/shard_map/tbd,de->tbe/dot_general | solution.py:188
  166.4 2.5 %fusion.46 = (f32[32,16]{1,0:T(8,128)S(1)}, f32[32,16,512]{2,1,0:T(8,128)S(1)}) fusion(bf16[32,16,512]{2,1,0:T(8,128)(2,1)S(1)} %copy-done.12, f32[512]{0:T(512)S(1)} %copy-done.25, bf16[32,16,1536]{2,1,0:T(8,128)(2,1)S(1)} %copy-done.15, bf16[512,2048]{1,0:T(8,128)(2,1)} %param.11), kind=kOutput, calls=%fused_computation.77 | convolution fusion | flops 806354432 | bytes 4722688 | tf_op jit(solution)/shard_map/tbe,de->tbd/dot_general | solution.py:192
  168.9 1.2 fusion.44
  170.1 14.5 %all-to-all-done.4 = bf16[8,32,1536]{2,1,0:T(8,128)(2,1)S(1)} async-done(((bf16[8,32,1536]{2,1,0:T(8,128)(2,1)}), bf16[8,32,1536]{2,1,0:T(8,128)(2,1)S(1)}, u32[]{:S(2)}, u32[]{:S(2)}) %all-to-all-start.4) | async-done | bytes 786464 | tf_op jit(solution)/shard_map/all_to_all | solution.py:210
  (108 shorter events, 21.1 us)
Async XLA Ops:
  9.7 2.2 %copy-start.23 = (s32[16,16]{1,0:T(8,128)S(1)}, s32[16,16]{1,0:T(8,128)}, u32[]{:S(2)}) copy-start(s32[16,16]{1,0:T(8,128)} %param.15) | copy-start | bytes 3076
  9.7 2.3 %copy-start.22 = (s32[512]{0:T(512)S(1)}, s32[512]{0:T(512)}, u32[]{:S(2)}) copy-start(s32[512]{0:T(512)} %param.17) | copy-start | bytes 6148
  9.7 2.3 %copy-start.26 = (s32[4]{0:T(128)S(1)}, s32[4]{0:T(128)}, u32[]{:S(2)}) copy-start(s32[4]{0:T(128)} %param.16) | copy-start | bytes 52
  12.3 4.3 %copy-start.18 = (bf16[32,16,1,8,64]{4,3,2,1,0:T(8,128)(2,1)S(1)}, bf16[32,16,1,8,64]{4,3,2,1,0:T(8,128)(2,1)}, u32[]{:S(2)}) copy-start(bf16[32,16,1,8,64]{4,3,2,1,0:T(8,128)(2,1)} %get-tuple-element.46) | copy-start | bytes 1572868
  15.3 1.4 copy-start.27
  15.3 1.9 %copy-start.29 = (f32[32,8,16]{2,1,0:T(8,128)}, f32[32,8,16]{2,1,0:T(8,128)S(1)}, u32[]{:S(2)}) copy-start(f32[32,8,16]{2,1,0:T(8,128)S(1)} %get-tuple-element.47) | copy-start | bytes 49156
  17.2 1.0 copy-start.4
  17.2 1.9 %copy-start.11 = (bf16[32,16,512]{2,1,0:T(8,128)(2,1)S(1)}, bf16[32,16,512]{2,1,0:T(8,128)(2,1)}, u32[]{:S(2)}) copy-start(bf16[32,16,512]{2,1,0:T(8,128)(2,1)} %param.9) | copy-start | bytes 1572868
  19.1 2.8 %copy-start.20 = (bf16[32,16,512]{2,1,0:T(8,128)(2,1)}, bf16[32,16,512]{2,1,0:T(8,128)(2,1)S(1)}, u32[]{:S(2)}) copy-start(bf16[32,16,512]{2,1,0:T(8,128)(2,1)S(1)} %reshape.322) | copy-start | bytes 1572868
  19.1 10.2 %copy-start.9 = (bf16[512,1,512]{2,0,1:T(8,128)(2,1)S(1)}, bf16[512,1,512]{2,0,1:T(8,128)(2,1)}, u32[]{:S(2)}) copy-start(bf16[512,1,512]{2,0,1:T(8,128)(2,1)} %param.10) | copy-start | bytes 1572868
  21.9 21.9 %all-to-all-start = ((bf16[32,16,512]{2,0,1:T(8,128)(2,1)}), bf16[32,16,512]{2,0,1:T(8,128)(2,1)S(1)}, u32[]{:S(2)}, u32[]{:S(2)}) async-start(bf16[32,16,512]{2,0,1:T(8,128)(2,1)} %copy.131), calls=%async_computation | async-start | bytes 1048576 | tf_op jit(solution)/shard_map/all_to_all | solution.py:243
  32.8 12.4 %copy-start.24 = (f32[512]{0:T(512)S(1)}, f32[512]{0:T(512)}, u32[]{:S(2)}) copy-start(f32[512]{0:T(512)} %param.14) | copy-start | bytes 6148
  44.2 1.0 copy-start.6
  56.0 4.7 %copy-start.14 = (bf16[512,512]{0,1:T(8,128)(2,1)S(1)}, bf16[512,512]{0,1:T(8,128)(2,1)}, u32[]{:S(2)}) copy-start(bf16[512,512]{0,1:T(8,128)(2,1)} %convolution_convert_fusion.11) | copy-start | bytes 1572868
  60.7 3.4 %copy-start.1 = (f32[8,512,512]{1,2,0:T(8,128)S(1)}, f32[8,512,512]{1,2,0:T(8,128)}, u32[]{:S(2)}) copy-start(f32[8,512,512]{1,2,0:T(8,128)} %get-tuple-element.50) | copy-start | bytes 25165828
  68.1 1.2 copy-start.7
  68.1 1.9 %copy-start.21 = (bf16[512,2048]{1,0:T(8,128)(2,1)S(1)}, bf16[512,2048]{1,0:T(8,128)(2,1)}, u32[]{:S(2)}) copy-start(bf16[512,2048]{1,0:T(8,128)(2,1)} %param.12) | copy-start | bytes 6291460
  70.0 1.0 copy-start.13
  79.7 18.7 %all-to-all-start.1 = ((bf16[16,2,8192]{2,1,0:T(2,128)(2,1)}), bf16[16,2,8192]{2,1,0:T(2,128)(2,1)}, u32[]{:S(2)}, u32[]{:S(2)}) async-start(bf16[16,2,8192]{2,1,0:T(2,128)(2,1)} %reshape.341), calls=%async_computation.1 | async-start | bytes 1048576 | tf_op jit(solution)/shard_map/all_to_all | solution.py:275
  84.1 1.2 copy-start.10
  86.1 1.9 %copy-start = (f32[512,2048]{1,0:T(8,128)}, f32[512,2048]{1,0:T(8,128)S(1)}, u32[]{:S(2)}) copy-start(f32[512,2048]{1,0:T(8,128)S(1)} %pad_maximum_fusion) | copy-start | bytes 12582916
  89.2 23.9 %collective-permute-start.1 = (bf16[8,32,2048]{2,1,0:T(8,128)(2,1)}, bf16[8,32,2048]{2,1,0:T(8,128)(2,1)}, u32[]{:S(2)}, u32[]{:S(2)}) collective-permute-start(bf16[8,32,2048]{2,1,0:T(8,128)(2,1)} %fusion.47), channel_id=1, source_target_pairs={{0,1},{1,0},{2,3},{3,2},{4,5},{5,4},{6,7},{7,6},{8,9},{9,8},{10,11... | collective-permute-start | bytes 3145736 | tf_op jit(solution)/shard_map/ppermute | solution.py:208
  103.4 4.7 %collective-permute-start = (bf16[8,32,512]{2,1,0:T(8,128)(2,1)}, bf16[8,32,512]{2,1,0:T(8,128)(2,1)S(1)}, u32[]{:S(2)}, u32[]{:S(2)}) collective-permute-start(bf16[8,32,512]{2,1,0:T(8,128)(2,1)} %fusion.84), channel_id=1, source_target_pairs={{0,1},{1,0},{2,3},{3,2},{4,5},{5,4},{6,7},{7,6},{8,9},{9,8},{10,11... | collective-permute-start | bytes 786440 | tf_op jit(solution)/shard_map/ppermute | solution.py:208
  108.9 13.5 %all-to-all-start.2 = ((bf16[8,32,512]{2,1,0:T(8,128)(2,1)}), bf16[8,32,512]{2,1,0:T(8,128)(2,1)S(1)}, u32[]{:S(2)}, u32[]{:S(2)}) async-start(bf16[8,32,512]{2,1,0:T(8,128)(2,1)} %fusion.66), calls=%async_computation.2 | async-start | bytes 524288 | tf_op jit(solution)/shard_map/all_to_all | solution.py:210
  117.2 9.5 %copy-start.5 = (bf16[32,8,16,64]{3,2,1,0:T(8,128)(2,1)S(1)}, bf16[32,8,16,64]{3,2,1,0:T(8,128)(2,1)}, u32[]{:S(2)}) copy-start(bf16[32,8,16,64]{3,2,1,0:T(8,128)(2,1)} %copy-done.4) | copy-start | bytes 1572868
  122.4 6.3 %copy-start.16 = (bf16[8,32,512]{2,1,0:T(8,128)(2,1)}, bf16[8,32,512]{2,1,0:T(8,128)(2,1)S(1)}, u32[]{:S(2)}) copy-start(bf16[8,32,512]{2,1,0:T(8,128)(2,1)S(1)} %all-to-all-done.2) | copy-start | bytes 786436
  122.4 29.6 %all-to-all-start.3 = ((bf16[8,32,2048]{2,1,0:T(8,128)(2,1)}), bf16[8,32,2048]{2,1,0:T(8,128)(2,1)}, u32[]{:S(2)}, u32[]{:S(2)}) async-start(bf16[8,32,2048]{2,1,0:T(8,128)(2,1)} %fusion.9), calls=%async_computation.3 | async-start | bytes 2097152 | tf_op jit(solution)/shard_map/all_to_all | solution.py:210
  126.7 2.0 %copy-start.8 = (bf16[32,16,8,64]{3,2,1,0:T(8,128)(2,1)S(1)}, bf16[32,16,8,64]{3,2,1,0:T(8,128)(2,1)}, u32[]{:S(2)}) copy-start(bf16[32,16,8,64]{3,2,1,0:T(8,128)(2,1)} %reshape.330) | copy-start | bytes 1572868
  126.7 2.0 %copy-start.19 = (bf16[32,16,1,8,64]{4,3,2,1,0:T(8,128)(2,1)S(1)}, bf16[32,16,1,8,64]{4,3,2,1,0:T(8,128)(2,1)}, u32[]{:S(2)}) copy-start(bf16[32,16,1,8,64]{4,3,2,1,0:T(8,128)(2,1)} %get-tuple-element.46) | copy-start | bytes 1572868
  128.7 2.4 %copy-start.3 = (bf16[32,16,1,8,64]{4,3,2,1,0:T(8,128)(2,1)S(1)}, bf16[32,16,1,8,64]{4,3,2,1,0:T(8,128)(2,1)}, u32[]{:S(2)}) copy-start(bf16[32,16,1,8,64]{4,3,2,1,0:T(8,128)(2,1)} %get-tuple-element.44) | copy-start | bytes 1572868
  131.1 1.2 copy-start.2
  132.4 1.6 copy-start.28
  132.4 1.6 copy-start.30
  137.9 5.4 %copy-start.17 = (bf16[8,32,512]{2,1,0:T(8,128)(2,1)S(1)}, bf16[8,32,512]{2,1,0:T(8,128)(2,1)}, u32[]{:S(2)}) copy-start(bf16[8,32,512]{2,1,0:T(8,128)(2,1)} %copy-done.16) | copy-start | bytes 786436
  137.9 16.2 %copy-start.12 = (bf16[32,16,512]{2,1,0:T(8,128)(2,1)S(1)}, bf16[32,16,512]{2,1,0:T(8,128)(2,1)}, u32[]{:S(2)}) copy-start(bf16[32,16,512]{2,1,0:T(8,128)(2,1)} %param.9) | copy-start | bytes 1572868
  137.9 16.2 %copy-start.25 = (f32[512]{0:T(512)S(1)}, f32[512]{0:T(512)}, u32[]{:S(2)}) copy-start(f32[512]{0:T(512)} %param.13) | copy-start | bytes 6148
  156.8 2.4 %collective-permute-start.2 = (bf16[8,32,1536]{2,1,0:T(8,128)(2,1)S(1)}, bf16[8,32,1536]{2,1,0:T(8,128)(2,1)S(1)}, u32[]{:S(2)}, u32[]{:S(2)}) collective-permute-start(bf16[8,32,1536]{2,1,0:T(8,128)(2,1)S(1)} %fusion.60), channel_id=1, source_target_pairs={{0,1},{1,0},{2,3},{3,2},{4,5},{5,4},{6,7},{7,6},{8,9},{9,8},{10,11... | collective-permute-start | bytes 2359304 | tf_op jit(solution)/shard_map/ppermute | solution.py:208
  160.4 24.2 %all-to-all-start.4 = ((bf16[8,32,1536]{2,1,0:T(8,128)(2,1)}), bf16[8,32,1536]{2,1,0:T(8,128)(2,1)S(1)}, u32[]{:S(2)}, u32[]{:S(2)}) async-start(bf16[8,32,1536]{2,1,0:T(8,128)(2,1)} %fusion.13), calls=%async_computation.4 | async-start | bytes 1572864 | tf_op jit(solution)/shard_map/all_to_all | solution.py:210
  164.0 2.4 %copy-start.15 = (bf16[32,16,1536]{2,1,0:T(8,128)(2,1)S(1)}, bf16[32,16,1536]{2,1,0:T(8,128)(2,1)}, u32[]{:S(2)}) copy-start(bf16[32,16,1536]{2,1,0:T(8,128)(2,1)} %reshape.331) | copy-start | bytes 4718596

commit v7 on v5

--- a/solution.py
+++ b/solution.py
@@ -272,15 +272,15 @@
         grad_out.astype(jnp.float32)
         + norm_backward(middle_block, temporal_gain, inverse_two, grad_normed_two)
     ).astype(jnp.bfloat16)
-    grad_middle_time = lax.all_to_all(grad_middle, ("outer", "core"), split_axis=0, concat_axis=1, tiled=True)
     normed_cols = normed_two
     context_cols = temporal_context
-    temporal_grad = scatter_rows(
-        jnp.concatenate(
-            [weight_term(normed_cols, grad_temporal_proj), weight_term(context_cols, grad_out)],
-            axis=1,
-        )
-    )
+    temporal_partial = jnp.concatenate(
+        [weight_term(normed_cols, grad_temporal_proj), weight_term(context_cols, grad_out)],
+        axis=1,
+    ).astype(jnp.bfloat16)
+    temporal_partial, grad_middle = lax.optimization_barrier((temporal_partial, grad_middle))
+    temporal_grad = scatter_rows(temporal_partial)
+    grad_middle_time = lax.all_to_all(grad_middle, ("outer", "core"), split_axis=0, concat_axis=1, tiled=True)
     spatial_term = weight_term(spatial_context, grad_middle_time)
     spatial_term, grad_middle_time = lax.optimization_barrier((spatial_term, grad_middle_time))
     grad_spatial_context = project_back(

time: 174 us -> 179 us (1.029)
  waiting for transfers between devices: 45.6 us -> 51.2 us
    reduce_scatter x1, waiting for transfers between devices: 10.7 us -> 16.1 us  [scatter_rows(): lax.psum_scatter(partial.astype(jnp.bfloat16), ('outer', 'core'), scatter...]
    all_to_all x2, waiting for transfers between devices: 12.3 us -> 7.54 us  [reduce_rows(): pieces = lax.all_to_all(pieces, 'outer', 0, 0, tiled=True)]
    all_to_all x1, waiting for transfers between devices: 9.49 us -> 13.7 us  [per_device(): lax.all_to_all(grad_middle, ('outer', 'core'), split_axis=0, concat_axis=...]
    unnamed x82 -> x78, local copies, waits for them, and re-layouts: 12 us -> 10.9 us
  transfers between devices with their start and end apart: 7 -> 7, of which waited for: 6 -> 6; matrix products, arithmetic and copies ran while one was open for 21% -> 18% of each run, Pallas kernels for 0% -> 0%
where the time goes in v7:
time: 179 us; the launch traced here: 177 us
  waiting for transfers between devices  51.2 us (29%)
  matrix products  44.3 us (25%)
  local copies, waits for them, and re-layouts  27.7 us (15%)
  starting transfers between devices  20.5 us (11%)
  other arithmetic  19.1 us (11%)
  between operations  14.7 us (8%)
    reduce_scatter x1, waiting for transfers between devices, scatter_rows(): lax.psum_scatter(partial.astype(jnp.bfloat16), ('outer', 'core'), scatter...  16.1 us
    all_to_all x1, waiting for transfers between devices, per_device(): lax.all_to_all(grad_middle, ('outer', 'core'), split_axis=0, concat_axis=...  13.7 us
    dot_general x4, matrix products, project(): jnp.einsum('tbd,de->tbe', rows, coefficient_array, preferred_element_type...  11.5 us
    unnamed x78, local copies, waits for them, and re-layouts  10.9 us
    all_to_all x1, waiting for transfers between devices, per_device(): lax.all_to_all(middle, ('outer', 'core'), split_axis=1, concat_axis=0, ti...  10.9 us
    dot_general x4, matrix products, project_back(): jnp.einsum('tbe,de->tbd', derivative_collection, coefficient_array, prefe...  9.16 us
    all_to_all x2, starting transfers between devices, reduce_rows(): pieces = lax.all_to_all(pieces, 'outer', 0, 0, tiled=True)  8.89 us
    sub x2, matrix products, normalized_affinity(): expo = jnp.exp(unnormalized_affinities - row_max)  8.32 us
  transfers between devices with their start and end apart: 7, of which 6 were waited for; matrix products, arithmetic and copies ran while one was open for 18% of the time, Pallas kernels for 0%

profile of v7, /device:TPU:0, one launch (start us, length us, event | category | flops | bytes accessed | tf_op | source)
XLA Modules:
  0.0 177.5 jit_solution(10632374533232401935)
XLA Ops:
  7.2 1.2 fusion.42
  8.4 3.8 %convolution_convert_fusion.2 = bf16[32,16,1536]{2,1,0:T(8,128)(2,1)} fusion(bf16[512,2048]{1,0:T(8,128)(2,1)} %param.11, bf16[32,16,512]{2,1,0:T(8,128)(2,1)} %param.9, f32[512]{0:T(512)} %param.13, f32[32,16]{1,0:T(8,128)S(1)} %add_rsqrt_fusion), kind=kOutput, calls=%fused_computation.14 | convolution fusion | flops 807141376 | bytes 3674112 | tf_op jit(solution)/shard_map/tbd,de->tbe/dot_general | solution.py:188
  12.2 4.0 %reshape.313 = bf16[32,16,3,8,64]{4,3,2,1,0:T(8,128)(2,1)S(1)} reshape(bf16[32,16,1536]{2,1,0:T(8,128)(2,1)} %convolution_convert_fusion.2) | data formatting | bytes 3145728 | tf_op jit(solution)/shard_map/reshape | solution.py:136
  16.2 2.1 %fusion.85 = (bf16[32,16,1,8,64]{4,3,2,1,0:T(8,128)(2,1)}, bf16[32,16,1,8,64]{4,3,2,1,0:T(8,128)(2,1)}, bf16[32,16,1,8,64]{4,3,2,1,0:T(8,128)(2,1)}) fusion(bf16[32,16,3,8,64]{4,3,2,1,0:T(8,128)(2,1)S(1)} %reshape.313), kind=kLoop, calls=%fused_computation.139 | loop fusion | bytes 3145728 | tf_op jit(solution)/shard_map/slice | solution.py:139
  18.8 2.9 %fusion.86 = (f32[32,8,16]{2,1,0:T(8,128)S(1)}, f32[32,8,16,16]{2,3,1,0:T(8,128)S(1)}) fusion(pred[32,16,16]{1,2,0:T(8,128)(4,1)S(1)} %and_or_fusion, bf16[32,16,1,8,64]{4,3,2,1,0:T(8,128)(2,1)} %get-tuple-element.47, bf16[32,16,1,8,64]{4,3,2,1,0:T(8,128)(2,1)} %get-tuple-element.46), kind=kOutput, calls=%fused_computation.140 | convolution fusion | flops 8650767 | bytes 1335296 | tf_op jit(solution)/shard_map/sub | solution.py:39
  21.8 1.3 copy-done.32
  23.7 1.0 copy-done.7
  25.6 1.7 fusion.28
  27.3 1.1 copy.119
  28.3 7.4 %all-to-all-start = ((bf16[32,16,512]{2,0,1:T(8,128)(2,1)}), bf16[32,16,512]{2,0,1:T(8,128)(2,1)S(1)}, u32[]{:S(2)}, u32[]{:S(2)}) async-start(bf16[32,16,512]{2,0,1:T(8,128)(2,1)} %copy.119), calls=%async_computation | async-start | bytes 1048576 | tf_op jit(solution)/shard_map/all_to_all | solution.py:243
  35.8 1.0 copy.130
  37.0 2.3 %convolution_convert_fusion.13 = bf16[512,512]{0,1:T(8,128)(2,1)} fusion(bf16[512,1,512]{2,0,1:T(8,128)(2,1)S(1)} %copy-done.13, bf16[512,2048]{1,0:T(8,128)(2,1)} %param.12), kind=kOutput, calls=%fused_computation.57 | convolution fusion | flops 268697600 | bytes 1572864 | tf_op jit(solution)/shard_map/tbe,de->tbd/dot_general | solution.py:192
  39.3 10.9 %all-to-all-done = bf16[32,16,512]{2,0,1:T(8,128)(2,1)S(1)} async-done(((bf16[32,16,512]{2,0,1:T(8,128)(2,1)}), bf16[32,16,512]{2,0,1:T(8,128)(2,1)S(1)}, u32[]{:S(2)}, u32[]{:S(2)}) %all-to-all-start) | async-done | bytes 524320 | tf_op jit(solution)/shard_map/all_to_all | solution.py:243
  51.7 3.7 %convolution_convert_fusion.1 = bf16[512,1536]{1,0:T(8,128)(2,1)} fusion(bf16[512,2048]{1,0:T(8,128)(2,1)} %param.12, f32[512,512]{0,1:T(8,128)S(1)} %copy.122, f32[512]{0:T(512)S(1)} %copy-done.29, f32[512]{0:T(512)S(1)} %rsqrt.21), kind=kOutput, calls=%fused_computation.13 | convolution fusion | flops 806879232 | bytes 4198400 | tf_op jit(solution)/shard_map/tbd,de->tbe/dot_general | solution.py:188
  55.3 1.7 copy.123
  57.1 5.4 %fusion.87 = (f32[8,512]{1,0:T(8,128)S(1)}, f32[8,512,512]{1,2,0:T(8,128)}) fusion(pred[512,512]{0,1:T(8,128)(4,1)S(1)} %broadcast_compare_fusion, bf16[512,3,8,64]{0,3,2,1:T(8,128)(2,1)S(1)} %bitcast.218), kind=kOutput, calls=%fused_computation.141 | convolution fusion | flops 276824576 | bytes 9715712 | tf_op jit(solution)/shard_map/while/body/eval_jaxpr/sub | solution.py:39
  62.5 4.7 %fusion.6 = bf16[8,512,512]{1,2,0:T(8,128)(2,1)S(1)} fusion(f32[8,512,512]{1,2,0:T(8,128)} %get-tuple-element.52, f32[8,512]{1,0:T(8,128)S(1)} %get-tuple-element.51), kind=kLoop, calls=%fused_computation.10 | loop fusion | flops 4194304 | bytes 12599296 | tf_op jit(solution)/shard_map/while/body/eval_jaxpr/convert_element_type | solution.py:48
  68.0 1.4 fusion.34
  69.3 1.4 copy-done.2
  70.7 1.8 %multiply_convert_fusion = bf16[8,512,512]{1,2,0:T(8,128)(2,1)S(1)} fusion(f32[8,512]{1,0:T(8,128)S(1)} %get-tuple-element.53, f32[8,512,512]{1,2,0:T(8,128)S(1)} %copy-done.2, f32[8,512]{1,0:T(8,128)S(1)} %get-tuple-element.51, bf16[8,512,64]{1,2,0:T(8,128)(2,1)S(1)} %bitcast.233, bf16[512,3,8,64]{0,3,2,1:T(8,128)(2,1)S(1)} %bitcast.220), kind=kOutput, calls=%fused_computation.2 | convolution fusion | flops 278921216 | bytes 13664256 | tf_op jit(solution)/shard_map/while/body/eval_jaxpr/...uo,...ao->...ua/dot_general | solution.py:73
  72.5 1.4 fusion.33
  73.9 0.8 fusion.35
  76.6 2.0 %multiply_reduce_fusion.1 = (f32[512]{0:T(512)S(1)}, f32[512,512]{0,1:T(8,128)}) fusion(f32[512,512]{0,1:T(8,128)S(1)} %copy-done.10, f32[512]{0:T(512)S(1)} %copy-done.29, bf16[512,1536]{0,1:T(8,128)(2,1)S(1)} %bitcast.234, bf16[512,2048]{1,0:T(8,128)(2,1)S(1)} %copy-done.26), kind=kOutput, calls=%fused_computation.81 | convolution fusion | flops 806092288 | bytes 5246976 | tf_op jit(solution)/shard_map/tbe,de->tbd/dot_general | solution.py:192
  78.6 1.2 convolution_convert_fusion
  79.9 1.6 pad_maximum_fusion
  81.5 1.5 fusion.46
  83.5 1.0 reduce.6
  84.8 1.2 reshape.332
  85.9 4.1 %all-to-all-start.1 = ((bf16[16,2,8192]{2,1,0:T(2,128)(2,1)}), bf16[16,2,8192]{2,1,0:T(2,128)(2,1)S(1)}, u32[]{:S(2)}, u32[]{:S(2)}) async-start(bf16[16,2,8192]{2,1,0:T(2,128)(2,1)} %reshape.332), calls=%async_computation.1 | async-start | bytes 1048576 | tf_op jit(solution)/shard_map/all_to_all | solution.py:283
  90.8 13.7 %all-to-all-done.1 = bf16[16,2,8192]{2,1,0:T(2,128)(2,1)S(1)} async-done(((bf16[16,2,8192]{2,1,0:T(2,128)(2,1)}), bf16[16,2,8192]{2,1,0:T(2,128)(2,1)S(1)}, u32[]{:S(2)}, u32[]{:S(2)}) %all-to-all-start.1) | async-done | bytes 524320 | tf_op jit(solution)/shard_map/all_to_all | solution.py:283
  107.5 2.3 %convolution_convert_fusion.9 = bf16[32,16,512]{2,1,0:T(8,128)(2,1)} fusion(bf16[32,16,512]{2,1,0:T(8,128)(2,1)S(1)} %bitcast.230, bf16[512,2048]{1,0:T(8,128)(2,1)} %param.11), kind=kOutput, calls=%fused_computation.53 | convolution fusion | flops 268697600 | bytes 1572864 | tf_op jit(solution)/shard_map/tbe,de->tbd/dot_general | solution.py:192
  109.9 1.7 reshape.321
  112.3 1.0 copy-done.33
  114.0 1.7 fusion.24
  115.7 0.8 fusion.61
  116.6 4.4 %all-to-all-start.2 = ((bf16[8,32,512]{2,1,0:T(8,128)(2,1)}), bf16[8,32,512]{2,1,0:T(8,128)(2,1)S(1)}, u32[]{:S(2)}, u32[]{:S(2)}) async-start(bf16[8,32,512]{2,1,0:T(8,128)(2,1)} %fusion.61), calls=%async_computation.2 | async-start | bytes 524288 | tf_op jit(solution)/shard_map/all_to_all | solution.py:210
  123.5 0.8 copy.141
  124.3 3.0 %reshape.322 = bf16[32,16,1536]{2,1,0:T(8,128)(2,1)} reshape(bf16[32,16,3,8,64]{4,3,2,1,0:T(8,128)(2,1)S(1)} %copy.141) | data formatting | bytes 3145728 | tf_op jit(solution)/shard_map/reshape | solution.py:169
  127.3 6.9 %all-to-all-done.2 = bf16[8,32,512]{2,1,0:T(8,128)(2,1)S(1)} async-done(((bf16[8,32,512]{2,1,0:T(8,128)(2,1)}), bf16[8,32,512]{2,1,0:T(8,128)(2,1)S(1)}, u32[]{:S(2)}, u32[]{:S(2)}) %all-to-all-start.2) | async-done | bytes 262176 | tf_op jit(solution)/shard_map/all_to_all | solution.py:210
  134.2 2.7 %fusion.75 = f32[512,1536,1]{1,0,2:T(8,128)S(1)} fusion(bf16[32,16,1536]{2,1,0:T(8,128)(2,1)} %reshape.322, bf16[32,16,512]{2,1,0:T(8,128)(2,1)} %param.9, f32[512]{0:T(512)S(1)} %copy-done.30, f32[32,16]{1,0:T(8,128)S(1)} %add_rsqrt_fusion), kind=kOutput, calls=%fused_computation.121 | convolution fusion | flops 806354944 | bytes 5246976 | tf_op jit(solution)/shard_map/tbd,tbe->de/dot_general | solution.py:198
  137.2 2.3 %collective-permute-done.1 = bf16[8,32,1536]{2,1,0:T(8,128)(2,1)S(1)} collective-permute-done((bf16[8,32,1536]{2,1,0:T(8,128)(2,1)S(1)}, bf16[8,32,1536]{2,1,0:T(8,128)(2,1)S(1)}, u32[]{:S(2)}, u32[]{:S(2)}) %collective-permute-start.1) | collective-permute-done | bytes 786464 | tf_op jit(solution)/shard_map/ppermute | solution.py:208
  139.5 1.2 fusion.10
  140.7 4.5 %all-to-all-start.3 = ((bf16[8,32,1536]{2,1,0:T(8,128)(2,1)}), bf16[8,32,1536]{2,1,0:T(8,128)(2,1)S(1)}, u32[]{:S(2)}, u32[]{:S(2)}) async-start(bf16[8,32,1536]{2,1,0:T(8,128)(2,1)} %fusion.10), calls=%async_computation.3 | async-start | bytes 1572864 | tf_op jit(solution)/shard_map/all_to_all | solution.py:210
  145.2 2.4 %fusion.32 = bf16[512,1,512]{2,0,1:T(8,128)(2,1)} fusion(f32[512,512]{1,0:T(8,128)S(1)} %bitcast.215, bf16[512,512]{0,1:T(8,128)(2,1)S(1)} %bitcast.224, bf16[512,2048]{1,0:T(8,128)(2,1)} %param.12), kind=kOutput, calls=%fused_computation.62 | convolution fusion | flops 268959744 | bytes 2621440 | tf_op jit(solution)/shard_map/tbd,de->tbe/dot_general | solution.py:188
  147.6 2.5 %fusion.43 = (f32[32,16]{1,0:T(8,128)S(1)}, f32[32,16,512]{2,1,0:T(8,128)S(1)}) fusion(bf16[32,16,512]{2,1,0:T(8,128)(2,1)S(1)} %copy-done.15, f32[512]{0:T(512)S(1)} %copy-done.30, bf16[32,16,1536]{2,1,0:T(8,128)(2,1)S(1)} %copy-done.20, bf16[512,2048]{1,0:T(8,128)(2,1)} %param.11), kind=kOutput, calls=%fused_computation.73 | convolution fusion | flops 806354432 | bytes 4722688 | tf_op jit(solution)/shard_map/tbe,de->tbd/dot_general | solution.py:192
  150.2 1.2 fusion.41
  151.4 16.1 %reduce-scatter.2.cloned.1.call-done = bf16[32,2048]{1,0:T(8,128)(2,1)} async-done(((bf16[512,2048]{1,0:T(8,128)(2,1)}), bf16[32,2048]{1,0:T(8,128)(2,1)}) %reduce-scatter.2.cloned.1.call-update) | async-done | bytes 131088 | tf_op jit(solution)/shard_map/reduce_scatter | solution.py:215
  167.5 1.6 convert_element_type.266
  (115 shorter events, 16.4 us)
Async XLA Ops:
  16.2 2.2 %copy-start.28 = (s32[16,16]{1,0:T(8,128)S(1)}, s32[16,16]{1,0:T(8,128)}, u32[]{:S(2)}) copy-start(s32[16,16]{1,0:T(8,128)} %param.15) | copy-start | bytes 3076
  16.2 2.2 %copy-start.27 = (s32[512]{0:T(512)S(1)}, s32[512]{0:T(512)}, u32[]{:S(2)}) copy-start(s32[512]{0:T(512)} %param.17) | copy-start | bytes 6148
  16.2 2.3 %copy-start.31 = (s32[4]{0:T(128)S(1)}, s32[4]{0:T(128)}, u32[]{:S(2)}) copy-start(s32[4]{0:T(128)} %param.16) | copy-start | bytes 52
  18.8 4.3 %copy-start.21 = (bf16[32,16,1,8,64]{4,3,2,1,0:T(8,128)(2,1)S(1)}, bf16[32,16,1,8,64]{4,3,2,1,0:T(8,128)(2,1)}, u32[]{:S(2)}) copy-start(bf16[32,16,1,8,64]{4,3,2,1,0:T(8,128)(2,1)} %get-tuple-element.48) | copy-start | bytes 1572868
  21.8 1.4 copy-start.32
  21.8 1.9 %copy-start.34 = (f32[32,8,16]{2,1,0:T(8,128)}, f32[32,8,16]{2,1,0:T(8,128)S(1)}, u32[]{:S(2)}) copy-start(f32[32,8,16]{2,1,0:T(8,128)S(1)} %get-tuple-element.49) | copy-start | bytes 49156
  23.7 1.0 copy-start.7
  23.7 1.9 %copy-start.14 = (bf16[32,16,512]{2,1,0:T(8,128)(2,1)S(1)}, bf16[32,16,512]{2,1,0:T(8,128)(2,1)}, u32[]{:S(2)}) copy-start(bf16[32,16,512]{2,1,0:T(8,128)(2,1)} %param.9) | copy-start | bytes 1572868
  25.6 2.8 %copy-start.24 = (bf16[32,16,512]{2,1,0:T(8,128)(2,1)}, bf16[32,16,512]{2,1,0:T(8,128)(2,1)S(1)}, u32[]{:S(2)}) copy-start(bf16[32,16,512]{2,1,0:T(8,128)(2,1)S(1)} %reshape.314) | copy-start | bytes 1572868
  25.6 10.2 %copy-start.13 = (bf16[512,1,512]{2,0,1:T(8,128)(2,1)S(1)}, bf16[512,1,512]{2,0,1:T(8,128)(2,1)}, u32[]{:S(2)}) copy-start(bf16[512,1,512]{2,0,1:T(8,128)(2,1)} %param.10) | copy-start | bytes 1572868
  28.3 21.9 %all-to-all-start = ((bf16[32,16,512]{2,0,1:T(8,128)(2,1)}), bf16[32,16,512]{2,0,1:T(8,128)(2,1)S(1)}, u32[]{:S(2)}, u32[]{:S(2)}) async-start(bf16[32,16,512]{2,0,1:T(8,128)(2,1)} %copy.119), calls=%async_computation | async-start | bytes 1048576 | tf_op jit(solution)/shard_map/all_to_all | solution.py:243
  39.3 12.4 %copy-start.29 = (f32[512]{0:T(512)S(1)}, f32[512]{0:T(512)}, u32[]{:S(2)}) copy-start(f32[512]{0:T(512)} %param.14) | copy-start | bytes 6148
  50.3 28.3 %copy-start = (f32[32,16,512]{2,0,1:T(8,128)}, f32[32,16,512]{2,0,1:T(8,128)S(1)}, u32[]{:S(2)}) copy-start(f32[32,16,512]{2,0,1:T(8,128)S(1)} %convert_element_type.271) | copy-start | bytes 3145732
  50.7 1.0 copy-start.9
  62.5 4.7 %copy-start.19 = (bf16[512,512]{0,1:T(8,128)(2,1)S(1)}, bf16[512,512]{0,1:T(8,128)(2,1)}, u32[]{:S(2)}) copy-start(bf16[512,512]{0,1:T(8,128)(2,1)} %convolution_convert_fusion.13) | copy-start | bytes 1572868
  67.1 3.6 %copy-start.2 = (f32[8,512,512]{1,2,0:T(8,128)S(1)}, f32[8,512,512]{1,2,0:T(8,128)}, u32[]{:S(2)}) copy-start(f32[8,512,512]{1,2,0:T(8,128)} %get-tuple-element.52) | copy-start | bytes 25165828
  68.0 6.7 %copy-start.3 = (bf16[8,512,64]{1,2,0:T(8,128)(2,1)}, bf16[8,512,64]{1,2,0:T(8,128)(2,1)S(1)}, u32[]{:S(2)}) copy-start(bf16[8,512,64]{1,2,0:T(8,128)(2,1)S(1)} %get-tuple-element.54) | copy-start | bytes 1572868
  74.7 1.2 copy-start.10
  74.7 1.9 %copy-start.26 = (bf16[512,2048]{1,0:T(8,128)(2,1)S(1)}, bf16[512,2048]{1,0:T(8,128)(2,1)}, u32[]{:S(2)}) copy-start(bf16[512,2048]{1,0:T(8,128)(2,1)} %param.12) | copy-start | bytes 6291460
  79.9 1.6 copy-start.18
  85.9 18.6 %all-to-all-start.1 = ((bf16[16,2,8192]{2,1,0:T(2,128)(2,1)}), bf16[16,2,8192]{2,1,0:T(2,128)(2,1)S(1)}, u32[]{:S(2)}, u32[]{:S(2)}) async-start(bf16[16,2,8192]{2,1,0:T(2,128)(2,1)} %reshape.332), calls=%async_computation.1 | async-start | bytes 1048576 | tf_op jit(solution)/shard_map/all_to_all | solution.py:283
  90.0 77.5 %reduce-scatter.2.cloned.1.call-start = ((), (), s32[]{:S(2)}) async-start(), calls=%async_computation.5 | async-start | bytes 2228224 | tf_op jit(solution)/shard_map/reduce_scatter | solution.py:215
  90.8 14.4 %copy-start.25 = (bf16[32,16,512]{2,1,0:T(8,128)(2,1)S(1)}, bf16[32,16,512]{2,1,0:T(8,128)(2,1)}, u32[]{:S(2)}) copy-start(bf16[32,16,512]{2,1,0:T(8,128)(2,1)} %copy-done.24) | copy-start | bytes 1572868
  105.8 1.0 copy-start.11
  106.1 1.5 copy-start.16
  106.1 5.5 %copy-start.8 = (bf16[32,8,16,64]{3,2,1,0:T(8,128)(2,1)S(1)}, bf16[32,8,16,64]{3,2,1,0:T(8,128)(2,1)}, u32[]{:S(2)}) copy-start(bf16[32,8,16,64]{3,2,1,0:T(8,128)(2,1)} %copy-done.7) | copy-start | bytes 1572868
  107.5 8.2 %collective-permute-start = (bf16[8,32,512]{2,1,0:T(8,128)(2,1)}, bf16[8,32,512]{2,1,0:T(8,128)(2,1)S(1)}, u32[]{:S(2)}, u32[]{:S(2)}) collective-permute-start(bf16[8,32,512]{2,1,0:T(8,128)(2,1)} %fusion.78), channel_id=1, source_target_pairs={{0,1},{1,0},{2,3},{3,2},{4,5},{5,4},{6,7},{7,6},{8,9},{9,8},{10,11... | collective-permute-start | bytes 786440 | tf_op jit(solution)/shard_map/ppermute | solution.py:208
  109.9 2.4 %copy-start.22 = (bf16[32,16,1,8,64]{4,3,2,1,0:T(8,128)(2,1)S(1)}, bf16[32,16,1,8,64]{4,3,2,1,0:T(8,128)(2,1)}, u32[]{:S(2)}) copy-start(bf16[32,16,1,8,64]{4,3,2,1,0:T(8,128)(2,1)} %get-tuple-element.48) | copy-start | bytes 1572868
  109.9 2.4 %copy-start.35 = (f32[32,8,16]{2,1,0:T(8,128)S(1)}, f32[32,8,16]{2,1,0:T(8,128)}, u32[]{:S(2)}) copy-start(f32[32,8,16]{2,1,0:T(8,128)} %copy-done.34) | copy-start | bytes 49156
  111.6 1.6 copy-start.33
  114.0 1.7 copy-start.12
  115.7 5.3 %copy-start.6 = (bf16[32,16,1,8,64]{4,3,2,1,0:T(8,128)(2,1)S(1)}, bf16[32,16,1,8,64]{4,3,2,1,0:T(8,128)(2,1)}, u32[]{:S(2)}) copy-start(bf16[32,16,1,8,64]{4,3,2,1,0:T(8,128)(2,1)} %get-tuple-element.46) | copy-start | bytes 1572868
  116.6 5.0 %copy-start.5 = (bf16[32,16,1,8,64]{4,3,2,1,0:T(8,128)(2,1)S(1)}, bf16[32,16,1,8,64]{4,3,2,1,0:T(8,128)(2,1)}, u32[]{:S(2)}) copy-start(bf16[32,16,1,8,64]{4,3,2,1,0:T(8,128)(2,1)} %get-tuple-element.47) | copy-start | bytes 1572868
  116.6 17.6 %all-to-all-start.2 = ((bf16[8,32,512]{2,1,0:T(8,128)(2,1)}), bf16[8,32,512]{2,1,0:T(8,128)(2,1)S(1)}, u32[]{:S(2)}, u32[]{:S(2)}) async-start(bf16[8,32,512]{2,1,0:T(8,128)(2,1)} %fusion.61), calls=%async_computation.2 | async-start | bytes 524288 | tf_op jit(solution)/shard_map/all_to_all | solution.py:210
  121.5 1.2 copy-start.23
  124.3 9.9 %copy-start.30 = (f32[512]{0:T(512)S(1)}, f32[512]{0:T(512)}, u32[]{:S(2)}) copy-start(f32[512]{0:T(512)} %param.13) | copy-start | bytes 6148
  137.1 8.1 %copy-start.1 = (f32[32,16,512]{2,0,1:T(8,128)S(1)}, f32[32,16,512]{2,0,1:T(8,128)}, u32[]{:S(2)}) copy-start(f32[32,16,512]{2,0,1:T(8,128)} %copy-done) | copy-start | bytes 3145732
  137.1 8.1 %copy-start.4 = (bf16[8,512,64]{1,2,0:T(8,128)(2,1)S(1)}, bf16[8,512,64]{1,2,0:T(8,128)(2,1)}, u32[]{:S(2)}) copy-start(bf16[8,512,64]{1,2,0:T(8,128)(2,1)} %copy-done.3) | copy-start | bytes 1572868
  137.1 2.4 %collective-permute-start.1 = (bf16[8,32,1536]{2,1,0:T(8,128)(2,1)S(1)}, bf16[8,32,1536]{2,1,0:T(8,128)(2,1)S(1)}, u32[]{:S(2)}, u32[]{:S(2)}) collective-permute-start(bf16[8,32,1536]{2,1,0:T(8,128)(2,1)S(1)} %fusion.56), channel_id=1, source_target_pairs={{0,1},{1,0},{2,3},{3,2},{4,5},{5,4},{6,7},{7,6},{8,9},{9,8},{10,11... | collective-permute-start | bytes 2359304 | tf_op jit(solution)/shard_map/ppermute | solution.py:208
  140.7 6.9 %copy-start.15 = (bf16[32,16,512]{2,1,0:T(8,128)(2,1)S(1)}, bf16[32,16,512]{2,1,0:T(8,128)(2,1)}, u32[]{:S(2)}) copy-start(bf16[32,16,512]{2,1,0:T(8,128)(2,1)} %param.9) | copy-start | bytes 1572868
  140.7 29.1 %all-to-all-start.3 = ((bf16[8,32,1536]{2,1,0:T(8,128)(2,1)}), bf16[8,32,1536]{2,1,0:T(8,128)(2,1)S(1)}, u32[]{:S(2)}, u32[]{:S(2)}) async-start(bf16[8,32,1536]{2,1,0:T(8,128)(2,1)} %fusion.10), calls=%async_computation.3 | async-start | bytes 1572864 | tf_op jit(solution)/shard_map/all_to_all | solution.py:210
  145.2 2.5 %copy-start.20 = (bf16[32,16,1536]{2,1,0:T(8,128)(2,1)S(1)}, bf16[32,16,1536]{2,1,0:T(8,128)(2,1)}, u32[]{:S(2)}) copy-start(bf16[32,16,1536]{2,1,0:T(8,128)(2,1)} %reshape.322) | copy-start | bytes 4718596
  147.6 2.6 %copy-start.17 = (bf16[16,32,1,512]{3,0,1,2:T(8,128)(2,1)S(1)}, bf16[16,32,1,512]{3,0,1,2:T(8,128)(2,1)}, u32[]{:S(2)}) copy-start(bf16[16,32,1,512]{3,0,1,2:T(8,128)(2,1)} %copy-done.16) | copy-start | bytes 1572868
Sparse Core Ops, SparseCore 0:
  94.6 72.8 reduce-scatter.1

commit v8 on v5

--- a/solution.py
+++ b/solution.py
@@ -167,6 +167,81 @@
     )
     return (
         jnp.stack(derivative_collection, axis=0).transpose(1, 3, 0, 2, 4).reshape(bins, blocks, -1)
+    )
+
+
+def head_mask(width):
+    column_head = jnp.arange(width, dtype=jnp.int32) // (width // HEADS)
+    return column_head[None, :] == jnp.arange(HEADS, dtype=jnp.int32)[:, None]
+
+
+def masked_rows(rows):
+    keep = head_mask(rows.shape[-1])[None, :, None, :]
+    return jnp.where(keep, rows[:, None, :, :], jnp.zeros((), rows.dtype))
+
+
+def masked_cols(rows):
+    keep = head_mask(rows.shape[-1])[None, None, :, :]
+    return jnp.where(keep, rows[:, :, None, :], jnp.zeros((), rows.dtype))
+
+
+def spatial_probs(asking, lookup, admissible_pairs, sharpness_divisor):
+    scores = (
+        jnp.einsum(
+            "tbd,thcd->tbhc", asking, masked_rows(lookup), preferred_element_type=jnp.float32
+        )
+        * sharpness_divisor
+    )
+    scores = jnp.where(admissible_pairs[:, 0][:, :, None, :], scores, -1e30)
+    row_max = jnp.max(scores, axis=-1, keepdims=True)
+    expo = jnp.exp(scores - row_max)
+    return expo / jnp.sum(expo, axis=-1, keepdims=True)
+
+
+def spatial_forward_heads(projected, admissible_pairs):
+    width = projected.shape[-1] // 3
+    asking, lookup, payload = [projected[..., i * width : (i + 1) * width] for i in range(3)]
+    sharpness_divisor = float(width // HEADS) ** (-0.5)
+    probs = spatial_probs(asking, lookup, admissible_pairs, sharpness_divisor).astype(jnp.bfloat16)
+    return jnp.einsum(
+        "tbhc,thcd->tbd", probs, masked_rows(payload), preferred_element_type=jnp.float32
+    ).astype(jnp.bfloat16)
+
+
+def spatial_backward_heads(projected, admissible_pairs, combined_output, output_derivative):
+    width = projected.shape[-1] // 3
+    asking, lookup, payload = [projected[..., i * width : (i + 1) * width] for i in range(3)]
+    sharpness_divisor = float(width // HEADS) ** (-0.5)
+    bins, blocks = projected.shape[0], projected.shape[1]
+    probs = spatial_probs(asking, lookup, admissible_pairs, sharpness_divisor)
+    grad_values = jnp.einsum(
+        "tbhc,tbhd->tcd",
+        probs.astype(jnp.bfloat16),
+        masked_cols(output_derivative),
+        preferred_element_type=jnp.float32,
+    )
+    probs_derivative = jnp.einsum(
+        "tbd,thcd->tbhc", output_derivative, masked_rows(payload), preferred_element_type=jnp.float32
+    )
+    inner = jnp.einsum(
+        "tbd,hd->tbh",
+        output_derivative.astype(jnp.float32) * combined_output.astype(jnp.float32),
+        head_mask(width).astype(jnp.float32),
+        precision=lax.Precision.HIGHEST,
+        preferred_element_type=jnp.float32,
+    )[..., None]
+    scores_derivative = (probs * (probs_derivative - inner) * sharpness_divisor).astype(
+        jnp.bfloat16
+    )
+    grad_queries = jnp.einsum(
+        "tbhc,thcd->tbd", scores_derivative, masked_rows(lookup), preferred_element_type=jnp.float32
+    )
+    grad_keys = jnp.einsum(
+        "tbhc,tbhd->tcd", scores_derivative, masked_cols(asking), preferred_element_type=jnp.float32
+    )
+    return jnp.concatenate(
+        [grad_queries.astype(jnp.bfloat16), grad_keys.astype(jnp.bfloat16), grad_values.astype(jnp.bfloat16)],
+        axis=-1,
     )
 
 
@@ -235,7 +310,7 @@
     normed_one, inverse_one = norm_forward(activity, spatial_gain)
     spatial_proj = project(normed_one, spatial_weights[:, : 3 * model_width]).astype(jnp.bfloat16)
     allowed_space = spatial_allowed(sessions_here, channel_count, adjacency)
-    spatial_context = spatial_forward(spatial_proj, allowed_space)
+    spatial_context = spatial_forward_heads(spatial_proj, allowed_space)
     middle = (
         activity.astype(jnp.float32)
         + project(spatial_context, spatial_weights[:, 3 * model_width :])
@@ -286,7 +361,7 @@
     grad_spatial_context = project_back(
         grad_middle_time, spatial_weights[:, 3 * model_width :]
     ).astype(jnp.bfloat16)
-    grad_spatial_proj = spatial_backward(
+    grad_spatial_proj = spatial_backward_heads(
         spatial_proj, allowed_space, spatial_context, grad_spatial_context
     )
     spatial_term = reduce_rows(spatial_term)

time: 174 us -> 165 us (0.948)
  local copies, waits for them, and re-layouts: 28.8 us -> 13.4 us
  matrix products: 44.7 us -> 49.4 us
  waiting for transfers between devices: 45.6 us -> 48.7 us
    dot_general x0 -> x6, matrix products: none -> 10.3 us  [the longest x1 2.36 us: spatial_forward_heads(): jnp.einsum('tbhc,thcd->tbd', probs, masked_rows(payload), preferred_eleme...]
    reshape x4 -> x0, local copies, waits for them, and re-layouts: 9.32 us -> none  [the longest x1 3.97 us: spatial_split(): projected.reshape(projected.shape[0], projected.shape[1], 3, HEADS, proje...]
    unnamed x82 -> x66, local copies, waits for them, and re-layouts: 12 us -> 8.13 us
    all_to_all x2, waiting for transfers between devices: 12.3 us -> 15.6 us  [reduce_rows(): pieces = lax.all_to_all(pieces, 'outer', 0, 0, tiled=True)]
    sub x2 -> x1, matrix products: 8.31 us -> 5.43 us  [normalized_affinity(): expo = jnp.exp(unnormalized_affinities - row_max)]
    sub x0 -> x1, matrix products: none -> 2.64 us  [spatial_probs(): expo = jnp.exp(scores - row_max)]
where the time goes in v8:
time: 165 us; the launch traced here: 164 us
  matrix products  49.4 us (30%)
  waiting for transfers between devices  48.7 us (30%)
  starting transfers between devices  20.7 us (13%)
  other arithmetic  17.2 us (10%)
  between operations  14.6 us (9%)
  local copies, waits for them, and re-layouts  13.4 us (8%)
    all_to_all x2, waiting for transfers between devices, reduce_rows(): pieces = lax.all_to_all(pieces, 'outer', 0, 0, tiled=True)  15.6 us
    all_to_all x1, waiting for transfers between devices, per_device(): lax.all_to_all(middle, ('outer', 'core'), split_axis=1, concat_axis=0, ti...  10.9 us
    reduce_scatter x1, waiting for transfers between devices, scatter_rows(): lax.psum_scatter(partial.astype(jnp.bfloat16), ('outer', 'core'), scatter...  10.5 us
    dot_general x4, matrix products, project(): jnp.einsum('tbd,de->tbe', rows, coefficient_array, preferred_element_type...  10.4 us
    all_to_all x1, waiting for transfers between devices, per_device(): lax.all_to_all(grad_middle, ('outer', 'core'), split_axis=0, concat_axis=...  9.51 us
    all_to_all x2, starting transfers between devices, reduce_rows(): pieces = lax.all_to_all(pieces, 'outer', 0, 0, tiled=True)  8.78 us
    unnamed x66, local copies, waits for them, and re-layouts  8.13 us
    all_to_all x1, starting transfers between devices, per_device(): lax.all_to_all(middle, ('outer', 'core'), split_axis=1, concat_axis=0, ti...  7.4 us
  transfers between devices with their start and end apart: 7, of which 6 were waited for; matrix products, arithmetic and copies ran while one was open for 21% of the time, Pallas kernels for 0%

profile of v8, /device:TPU:0, one launch (start us, length us, event | category | flops | bytes accessed | tf_op | source)
XLA Modules:
  0.0 164.0 jit_solution(4869331812196107008)
XLA Ops:
  7.2 1.2 fusion.95
  8.5 2.6 %convolution_convert_fusion.2 = bf16[32,16,1536]{2,1,0:T(8,128)(2,1)S(1)} fusion(bf16[512,2048]{1,0:T(8,128)(2,1)} %param.11, bf16[32,16,512]{2,1,0:T(8,128)(2,1)} %param.9, f32[512]{0:T(512)} %param.13, f32[32,16]{1,0:T(8,128)S(1)} %add_rsqrt_fusion), kind=kOutput, calls=%fused_computation.31 | convolution fusion | flops 807141376 | bytes 3674112 | tf_op jit(solution)/shard_map/tbd,de->tbe/dot_general | solution.py:263
  11.1 1.0 fusion.150
  12.6 2.6 %fusion.151 = (f32[32,16,8]{1,2,0:T(8,128)S(1)}, f32[32,16,8,16]{1,3,2,0:T(8,128)}) fusion(pred[32,16,16]{1,2,0:T(8,128)(4,1)S(1)} %and_or_fusion, pred[8,512]{1,0:T(8,128)(4,1)S(1)} %iota_compare_fusion, bf16[32,16,512]{2,1,0:T(8,128)(2,1)S(1)} %get-tuple-element.44, bf16[32,16,1536]{2,1,0:T(8,128)(2,1)S(1)} %convolution_convert_fusion.2), kind=kOutput, calls=%fused_computation.184 | convolution fusion | flops 69468176 | bytes 1396736 | tf_op jit(solution)/shard_map/sub | solution.py:197
  15.3 2.4 %fusion.69 = bf16[32,16,512]{2,1,0:T(8,128)(2,1)S(1)} fusion(pred[8,512]{1,0:T(8,128)(4,1)S(1)} %iota_compare_fusion, bf16[32,16,512]{2,1,0:T(8,128)(2,1)S(1)} %get-tuple-element.43, f32[32,16,8,16]{1,3,2,0:T(8,128)} %get-tuple-element.46, f32[32,16,8]{1,2,0:T(8,128)S(1)} %get-tuple-element.45), kind=kOutput, calls=%fused_computation.84 | convolution fusion | flops 69599232 | bytes 1331200 | tf_op jit(solution)/shard_map/tbhc,thcd->tbd/dot_general | solution.py:206
  17.7 1.7 %fusion.81 = bf16[32,16,512]{2,1,0:T(8,128)(2,1)S(1)} fusion(bf16[32,16,512]{2,1,0:T(8,128)(2,1)S(1)} %fusion.69, bf16[32,16,512]{2,1,0:T(8,128)(2,1)S(1)} %copy-done.5, bf16[512,2048]{1,0:T(8,128)(2,1)} %param.11), kind=kOutput, calls=%fused_computation.88 | convolution fusion | flops 269221888 | bytes 2097152 | tf_op jit(solution)/shard_map/tbd,de->tbe/dot_general | solution.py:263
  19.4 1.1 copy.100
  20.4 7.4 %all-to-all-start = ((bf16[32,16,512]{2,0,1:T(8,128)(2,1)}), bf16[32,16,512]{2,0,1:T(8,128)(2,1)S(1)}, u32[]{:S(2)}, u32[]{:S(2)}) async-start(bf16[32,16,512]{2,0,1:T(8,128)(2,1)} %copy.100), calls=%async_computation | async-start | bytes 1048576 | tf_op jit(solution)/shard_map/all_to_all | solution.py:318
  27.9 1.0 copy.106
  29.1 2.3 %convolution_convert_fusion.9 = bf16[512,512]{0,1:T(8,128)(2,1)} fusion(bf16[512,1,512]{2,0,1:T(8,128)(2,1)S(1)} %copy-done.3, bf16[512,2048]{1,0:T(8,128)(2,1)} %param.12), kind=kOutput, calls=%fused_computation.83 | convolution fusion | flops 268697600 | bytes 1572864 | tf_op jit(solution)/shard_map/tbe,de->tbd/dot_general | solution.py:267
  31.4 10.9 %all-to-all-done = bf16[32,16,512]{2,0,1:T(8,128)(2,1)S(1)} async-done(((bf16[32,16,512]{2,0,1:T(8,128)(2,1)}), bf16[32,16,512]{2,0,1:T(8,128)(2,1)S(1)}, u32[]{:S(2)}, u32[]{:S(2)}) %all-to-all-start) | async-done | bytes 524320 | tf_op jit(solution)/shard_map/all_to_all | solution.py:318
  43.8 3.6 %convolution_convert_fusion.1 = bf16[512,1536]{1,0:T(8,128)(2,1)} fusion(bf16[512,2048]{1,0:T(8,128)(2,1)} %param.12, f32[512,512]{0,1:T(8,128)S(1)} %copy.103, f32[512]{0:T(512)S(1)} %copy-done.23, f32[512]{0:T(512)S(1)} %rsqrt.21), kind=kOutput, calls=%fused_computation.30 | convolution fusion | flops 806879232 | bytes 4198400 | tf_op jit(solution)/shard_map/tbd,de->tbe/dot_general | solution.py:263
  47.4 1.7 %copy.104 = bf16[512,1536]{0,1:T(8,128)(2,1)S(1)} copy(bf16[512,1536]{1,0:T(8,128)(2,1)} %convolution_convert_fusion.1) | data formatting | bytes 3145728 | tf_op jit(solution)/shard_map/convert_element_type | solution.py:320
  49.1 5.4 %fusion.152 = (f32[8,512]{1,0:T(8,128)S(1)}, f32[8,512,512]{1,2,0:T(8,128)}) fusion(pred[512,512]{0,1:T(8,128)(4,1)S(1)} %broadcast_compare_fusion, bf16[512,3,8,64]{0,3,2,1:T(8,128)(2,1)S(1)} %bitcast.210), kind=kOutput, calls=%fused_computation.185 | convolution fusion | flops 276824576 | bytes 9715712 | tf_op jit(solution)/shard_map/while/body/eval_jaxpr/sub | solution.py:39
  54.6 4.7 %fusion.24 = bf16[8,512,512]{1,2,0:T(8,128)(2,1)S(1)} fusion(f32[8,512,512]{1,2,0:T(8,128)} %get-tuple-element.48, f32[8,512]{1,0:T(8,128)S(1)} %get-tuple-element.47), kind=kLoop, calls=%fused_computation.28 | loop fusion | flops 4194304 | bytes 12599296 | tf_op jit(solution)/shard_map/while/body/eval_jaxpr/convert_element_type | solution.py:48
  60.1 1.4 fusion.87
  61.4 1.2 copy-done
  62.6 1.8 %multiply_convert_fusion = bf16[8,512,512]{1,2,0:T(8,128)(2,1)S(1)} fusion(f32[8,512]{1,0:T(8,128)S(1)} %get-tuple-element.49, f32[8,512,512]{1,2,0:T(8,128)S(1)} %copy-done, f32[8,512]{1,0:T(8,128)S(1)} %get-tuple-element.47, bf16[8,512,64]{1,2,0:T(8,128)(2,1)S(1)} %bitcast.224, bf16[512,3,8,64]{0,3,2,1:T(8,128)(2,1)S(1)} %bitcast.212), kind=kOutput, calls=%fused_computation.2 | convolution fusion | flops 278921216 | bytes 13664256 | tf_op jit(solution)/shard_map/while/body/eval_jaxpr/...uo,...ao->...ua/dot_general | solution.py:73
  64.4 1.4 fusion.86
  66.8 1.2 copy-done.2
  68.1 1.0 copy-done.20
  69.1 1.0 multiply_reduce_fusion
  71.0 1.1 reduce.6
  72.3 1.2 reshape.379
  73.5 4.1 %all-to-all-start.1 = ((bf16[16,2,8192]{2,1,0:T(2,128)(2,1)}), bf16[16,2,8192]{2,1,0:T(2,128)(2,1)S(1)}, u32[]{:S(2)}, u32[]{:S(2)}) async-start(bf16[16,2,8192]{2,1,0:T(2,128)(2,1)} %reshape.379), calls=%async_computation.1 | async-start | bytes 1048576 | tf_op jit(solution)/shard_map/all_to_all | solution.py:350
  78.3 2.6 %convolution_convert_fusion = bf16[512,1536]{1,0:T(8,128)(2,1)S(1)} fusion(bf16[512,1536]{0,1:T(8,128)(2,1)} %bitcast.226, f32[512,1,1,1,1,1,512]{6,0,5,4,3,2,1:T(8,128)S(1)} %bitcast.206, f32[512]{0:T(512)S(1)} %copy-done.23, f32[512]{0:T(512)S(1)} %rsqrt.21), kind=kOutput, calls=%fused_computation.29 | convolution fusion | flops 806879232 | bytes 4198400 | tf_op jit(solution)/shard_map/tbd,tbe->de/dot_general | solution.py:273
  80.9 1.6 pad_maximum_fusion
  82.5 9.5 %all-to-all-done.1 = bf16[16,2,8192]{2,1,0:T(2,128)(2,1)S(1)} async-done(((bf16[16,2,8192]{2,1,0:T(2,128)(2,1)}), bf16[16,2,8192]{2,1,0:T(2,128)(2,1)S(1)}, u32[]{:S(2)}, u32[]{:S(2)}) %all-to-all-start.1) | async-done | bytes 524320 | tf_op jit(solution)/shard_map/all_to_all | solution.py:350
  92.7 1.6 %convolution_bitcast_fusion = f32[512,512]{1,0:T(8,128)S(1)} fusion(bf16[32,16,512]{2,1,0:T(8,128)(2,1)} %copy-done.13, bf16[16,32,1,512]{3,1,0,2:T(8,128)(2,1)S(1)} %bitcast.219), kind=kOutput, calls=%fused_computation.69 | convolution fusion | flops 268435456 | bytes 2097152 | tf_op jit(solution)/shard_map/tbd,tbe->de/dot_general | solution.py:273
  95.5 1.5 convolution_convert_fusion.6
  97.1 1.4 fusion.75
  98.5 1.9 %fusion.98 = f32[32,16,8]{1,2,0:T(8,128)S(1)} fusion(bf16[32,16,512]{2,1,0:T(8,128)(2,1)S(1)} %copy-done.14, bf16[32,16,512]{2,1,0:T(8,128)(2,1)S(1)} %convolution_convert_fusion.6, s32[512]{0:T(512)S(1)} %add_select_fusion), kind=kOutput, calls=%fused_computation.107 | convolution fusion | flops 25956352 | bytes 1067008 | tf_op jit(solution)/shard_map/tbd,hd->tbh/dot_general | solution.py:226
  100.6 1.3 multiply_convert_fusion.1
  101.9 1.4 fusion.78
  104.2 4.3 %all-to-all-start.2 = ((bf16[8,32,512]{2,1,0:T(8,128)(2,1)}), bf16[8,32,512]{2,1,0:T(8,128)(2,1)S(1)}, u32[]{:S(2)}, u32[]{:S(2)}) async-start(bf16[8,32,512]{2,1,0:T(8,128)(2,1)} %fusion.113), calls=%async_computation.2 | async-start | bytes 524288 | tf_op jit(solution)/shard_map/all_to_all | solution.py:285
  108.4 1.9 %fusion.72 = bf16[32,16,512]{2,1,0:T(8,128)(2,1)S(1)} fusion(bf16[32,16,8,16]{1,3,2,0:T(8,128)(2,1)} %copy-done.26, pred[8,512]{1,0:T(8,128)(4,1)S(1)} %iota_compare_fusion, bf16[32,16,512]{2,1,0:T(8,128)(2,1)S(1)} %copy-done.16), kind=kOutput, calls=%fused_computation.85 | convolution fusion | flops 69468160 | bytes 1183744 | tf_op jit(solution)/shard_map/tbhc,thcd->tbd/dot_general | solution.py:236
  110.4 1.3 pad_maximum_fusion.2
  111.6 9.2 %all-to-all-done.2 = bf16[8,32,512]{2,1,0:T(8,128)(2,1)S(1)} async-done(((bf16[8,32,512]{2,1,0:T(8,128)(2,1)}), bf16[8,32,512]{2,1,0:T(8,128)(2,1)S(1)}, u32[]{:S(2)}, u32[]{:S(2)}) %all-to-all-start.2) | async-done | bytes 262176 | tf_op jit(solution)/shard_map/all_to_all | solution.py:285
  120.9 2.5 %fusion.129 = f32[512,1536,1]{1,0,2:T(8,128)S(1)} fusion(bf16[32,16,1536]{2,1,0:T(8,128)(2,1)} %pad_maximum_fusion.2, bf16[32,16,512]{2,1,0:T(8,128)(2,1)S(1)} %copy-done.6, f32[512]{0:T(512)S(1)} %copy-done.24, f32[32,16]{1,0:T(8,128)S(1)} %add_rsqrt_fusion), kind=kOutput, calls=%fused_computation.149 | convolution fusion | flops 806354944 | bytes 5246976 | tf_op jit(solution)/shard_map/tbd,tbe->de/dot_general | solution.py:273
  123.6 2.3 %collective-permute-done.1 = bf16[8,32,1536]{2,1,0:T(8,128)(2,1)S(1)} collective-permute-done((bf16[8,32,1536]{2,1,0:T(8,128)(2,1)S(1)}, bf16[8,32,1536]{2,1,0:T(8,128)(2,1)S(1)}, u32[]{:S(2)}, u32[]{:S(2)}) %collective-permute-start.1) | collective-permute-done | bytes 786464 | tf_op jit(solution)/shard_map/ppermute | solution.py:283
  125.9 1.3 fusion.40
  127.2 4.5 %all-to-all-start.3 = ((bf16[8,32,1536]{2,1,0:T(8,128)(2,1)}), bf16[8,32,1536]{2,1,0:T(8,128)(2,1)S(1)}, u32[]{:S(2)}, u32[]{:S(2)}) async-start(bf16[8,32,1536]{2,1,0:T(8,128)(2,1)} %fusion.40), calls=%async_computation.3 | async-start | bytes 1572864 | tf_op jit(solution)/shard_map/all_to_all | solution.py:285
  131.7 2.4 %fusion.85 = bf16[512,1,512]{2,0,1:T(8,128)(2,1)} fusion(f32[512,512]{1,0:T(8,128)S(1)} %bitcast.207, bf16[512,512]{0,1:T(8,128)(2,1)S(1)} %bitcast.216, bf16[512,2048]{1,0:T(8,128)(2,1)} %param.12), kind=kOutput, calls=%fused_computation.92 | convolution fusion | flops 268959744 | bytes 2621440 | tf_op jit(solution)/shard_map/tbd,de->tbe/dot_general | solution.py:263
  134.1 2.5 %fusion.96 = (f32[32,16]{1,0:T(8,128)S(1)}, f32[32,16,512]{2,1,0:T(8,128)S(1)}) fusion(bf16[32,16,512]{2,1,0:T(8,128)(2,1)S(1)} %copy-done.6, f32[512]{0:T(512)S(1)} %copy-done.24, bf16[32,16,1536]{2,1,0:T(8,128)(2,1)S(1)} %copy-done.12, bf16[512,2048]{1,0:T(8,128)(2,1)} %param.11), kind=kOutput, calls=%fused_computation.103 | convolution fusion | flops 806354432 | bytes 4722688 | tf_op jit(solution)/shard_map/tbe,de->tbd/dot_general | solution.py:267
  136.7 1.2 fusion.94
  137.9 10.5 %reduce-scatter.2.cloned.1.call-done = bf16[32,2048]{1,0:T(8,128)(2,1)} async-done(((bf16[512,2048]{1,0:T(8,128)(2,1)}), bf16[32,2048]{1,0:T(8,128)(2,1)}) %reduce-scatter.2.cloned.1.call-update) | async-done | bytes 131088 | tf_op jit(solution)/shard_map/reduce_scatter | solution.py:290
  148.4 1.6 convert_element_type.262
  150.0 6.4 %all-to-all-done.3 = bf16[8,32,1536]{2,1,0:T(8,128)(2,1)S(1)} async-done(((bf16[8,32,1536]{2,1,0:T(8,128)(2,1)}), bf16[8,32,1536]{2,1,0:T(8,128)(2,1)S(1)}, u32[]{:S(2)}, u32[]{:S(2)}) %all-to-all-start.3) | async-done | bytes 786464 | tf_op jit(solution)/shard_map/all_to_all | solution.py:285
  (99 shorter events, 9.7 us)
Async XLA Ops:
  11.1 1.0 copy-start.22
  11.1 1.1 copy-start.21
  11.1 1.2 copy-start.25
  12.1 3.1 %copy-start.15 = (bf16[32,16,512]{2,1,0:T(8,128)(2,1)}, bf16[32,16,512]{2,1,0:T(8,128)(2,1)S(1)}, u32[]{:S(2)}) copy-start(bf16[32,16,512]{2,1,0:T(8,128)(2,1)S(1)} %get-tuple-element.44) | copy-start | bytes 1572868
  12.1 3.1 %copy-start.18 = (bf16[32,16,512]{2,1,0:T(8,128)(2,1)}, bf16[32,16,512]{2,1,0:T(8,128)(2,1)S(1)}, u32[]{:S(2)}) copy-start(bf16[32,16,512]{2,1,0:T(8,128)(2,1)S(1)} %get-tuple-element.43) | copy-start | bytes 1572868
  15.2 2.4 %copy-start.28 = (f32[32,16,8]{1,2,0:T(8,128)}, f32[32,16,8]{1,2,0:T(8,128)S(1)}, u32[]{:S(2)}) copy-start(f32[32,16,8]{1,2,0:T(8,128)S(1)} %get-tuple-element.45) | copy-start | bytes 49156
  15.3 2.4 %copy-start.5 = (bf16[32,16,512]{2,1,0:T(8,128)(2,1)S(1)}, bf16[32,16,512]{2,1,0:T(8,128)(2,1)}, u32[]{:S(2)}) copy-start(bf16[32,16,512]{2,1,0:T(8,128)(2,1)} %param.9) | copy-start | bytes 1572868
  17.6 1.7 %copy-start.13 = (bf16[32,16,512]{2,1,0:T(8,128)(2,1)}, bf16[32,16,512]{2,1,0:T(8,128)(2,1)S(1)}, u32[]{:S(2)}) copy-start(bf16[32,16,512]{2,1,0:T(8,128)(2,1)S(1)} %fusion.69) | copy-start | bytes 1572868
  17.6 10.2 %copy-start.3 = (bf16[512,1,512]{2,0,1:T(8,128)(2,1)S(1)}, bf16[512,1,512]{2,0,1:T(8,128)(2,1)}, u32[]{:S(2)}) copy-start(bf16[512,1,512]{2,0,1:T(8,128)(2,1)} %param.10) | copy-start | bytes 1572868
  20.4 21.9 %all-to-all-start = ((bf16[32,16,512]{2,0,1:T(8,128)(2,1)}), bf16[32,16,512]{2,0,1:T(8,128)(2,1)S(1)}, u32[]{:S(2)}, u32[]{:S(2)}) async-start(bf16[32,16,512]{2,0,1:T(8,128)(2,1)} %copy.100), calls=%async_computation | async-start | bytes 1048576 | tf_op jit(solution)/shard_map/all_to_all | solution.py:318
  31.4 12.4 %copy-start.23 = (f32[512]{0:T(512)S(1)}, f32[512]{0:T(512)}, u32[]{:S(2)}) copy-start(f32[512]{0:T(512)} %param.14) | copy-start | bytes 6148
  42.8 1.0 copy-start.1
  54.6 4.7 %copy-start.10 = (bf16[512,512]{0,1:T(8,128)(2,1)S(1)}, bf16[512,512]{0,1:T(8,128)(2,1)}, u32[]{:S(2)}) copy-start(bf16[512,512]{0,1:T(8,128)(2,1)} %convolution_convert_fusion.9) | copy-start | bytes 1572868
  59.2 3.4 %copy-start = (f32[8,512,512]{1,2,0:T(8,128)S(1)}, f32[8,512,512]{1,2,0:T(8,128)}, u32[]{:S(2)}) copy-start(f32[8,512,512]{1,2,0:T(8,128)} %get-tuple-element.48) | copy-start | bytes 25165828
  66.6 1.5 copy-start.2
  66.6 2.5 %copy-start.20 = (bf16[512,2048]{1,0:T(8,128)(2,1)S(1)}, bf16[512,2048]{1,0:T(8,128)(2,1)}, u32[]{:S(2)}) copy-start(bf16[512,2048]{1,0:T(8,128)(2,1)} %param.12) | copy-start | bytes 6291460
  66.8 3.3 %copy-start.11 = (bf16[3,8,512,64]{2,3,1,0:T(8,128)(2,1)}, bf16[3,8,512,64]{2,3,1,0:T(8,128)(2,1)S(1)}, u32[]{:S(2)}) copy-start(bf16[3,8,512,64]{2,3,1,0:T(8,128)(2,1)S(1)} %pad_maximum_fusion.1) | copy-start | bytes 4718596
  69.1 1.0 copy-start.9
  71.0 6.9 %copy-start.4 = (bf16[512,1,512]{2,0,1:T(8,128)(2,1)S(1)}, bf16[512,1,512]{2,0,1:T(8,128)(2,1)}, u32[]{:S(2)}) copy-start(bf16[512,1,512]{2,0,1:T(8,128)(2,1)} %param.10) | copy-start | bytes 1572868
  73.5 18.6 %all-to-all-start.1 = ((bf16[16,2,8192]{2,1,0:T(2,128)(2,1)}), bf16[16,2,8192]{2,1,0:T(2,128)(2,1)S(1)}, u32[]{:S(2)}, u32[]{:S(2)}) async-start(bf16[16,2,8192]{2,1,0:T(2,128)(2,1)} %reshape.379), calls=%async_computation.1 | async-start | bytes 1048576 | tf_op jit(solution)/shard_map/all_to_all | solution.py:350
  77.6 70.8 %reduce-scatter.2.cloned.1.call-start = ((), (), s32[]{:S(2)}) async-start(), calls=%async_computation.5 | async-start | bytes 2228224 | tf_op jit(solution)/shard_map/reduce_scatter | solution.py:290
  94.4 2.7 %copy-start.27 = (f32[32,16,8,16]{1,3,2,0:T(8,128)S(1)}, f32[32,16,8,16]{1,3,2,0:T(8,128)}, u32[]{:S(2)}) copy-start(f32[32,16,8,16]{1,3,2,0:T(8,128)} %get-tuple-element.46) | copy-start | bytes 786436
  94.4 2.7 %copy-start.29 = (f32[32,16,8]{1,2,0:T(8,128)S(1)}, f32[32,16,8]{1,2,0:T(8,128)}, u32[]{:S(2)}) copy-start(f32[32,16,8]{1,2,0:T(8,128)} %copy-done.28) | copy-start | bytes 49156
  94.7 0.8 copy-start.7
  97.1 1.4 copy-start.14
  97.1 3.5 %copy-start.19 = (bf16[32,16,512]{2,1,0:T(8,128)(2,1)S(1)}, bf16[32,16,512]{2,1,0:T(8,128)(2,1)}, u32[]{:S(2)}) copy-start(bf16[32,16,512]{2,1,0:T(8,128)(2,1)} %copy-done.18) | copy-start | bytes 1572868
  100.5 1.4 copy-start.17
  100.5 2.8 %collective-permute-start = (bf16[8,32,512]{2,1,0:T(8,128)(2,1)S(1)}, bf16[8,32,512]{2,1,0:T(8,128)(2,1)S(1)}, u32[]{:S(2)}, u32[]{:S(2)}) collective-permute-start(bf16[8,32,512]{2,1,0:T(8,128)(2,1)S(1)} %fusion.132), channel_id=1, source_target_pairs={{0,1},{1,0},{2,3},{3,2},{4,5},{5,4},{6,7},{7,6},{8,9},{9,8},{10,11... | collective-permute-start | bytes 786440 | tf_op jit(solution)/shard_map/ppermute | solution.py:283
  101.9 1.4 copy-start.26
  103.3 5.1 %copy-start.16 = (bf16[32,16,512]{2,1,0:T(8,128)(2,1)S(1)}, bf16[32,16,512]{2,1,0:T(8,128)(2,1)}, u32[]{:S(2)}) copy-start(bf16[32,16,512]{2,1,0:T(8,128)(2,1)} %copy-done.15) | copy-start | bytes 1572868
  104.2 16.7 %all-to-all-start.2 = ((bf16[8,32,512]{2,1,0:T(8,128)(2,1)}), bf16[8,32,512]{2,1,0:T(8,128)(2,1)S(1)}, u32[]{:S(2)}, u32[]{:S(2)}) async-start(bf16[8,32,512]{2,1,0:T(8,128)(2,1)} %fusion.113), calls=%async_computation.2 | async-start | bytes 524288 | tf_op jit(solution)/shard_map/all_to_all | solution.py:285
  110.4 10.5 %copy-start.6 = (bf16[32,16,512]{2,1,0:T(8,128)(2,1)S(1)}, bf16[32,16,512]{2,1,0:T(8,128)(2,1)}, u32[]{:S(2)}) copy-start(bf16[32,16,512]{2,1,0:T(8,128)(2,1)} %param.9) | copy-start | bytes 1572868
  110.4 10.5 %copy-start.24 = (f32[512]{0:T(512)S(1)}, f32[512]{0:T(512)}, u32[]{:S(2)}) copy-start(f32[512]{0:T(512)} %param.13) | copy-start | bytes 6148
  123.6 2.4 %collective-permute-start.1 = (bf16[8,32,1536]{2,1,0:T(8,128)(2,1)S(1)}, bf16[8,32,1536]{2,1,0:T(8,128)(2,1)S(1)}, u32[]{:S(2)}, u32[]{:S(2)}) collective-permute-start(bf16[8,32,1536]{2,1,0:T(8,128)(2,1)S(1)} %fusion.108), channel_id=1, source_target_pairs={{0,1},{1,0},{2,3},{3,2},{4,5},{5,4},{6,7},{7,6},{8,9},{9,8},{10,11... | collective-permute-start | bytes 2359304 | tf_op jit(solution)/shard_map/ppermute | solution.py:283
  127.2 29.2 %all-to-all-start.3 = ((bf16[8,32,1536]{2,1,0:T(8,128)(2,1)}), bf16[8,32,1536]{2,1,0:T(8,128)(2,1)S(1)}, u32[]{:S(2)}, u32[]{:S(2)}) async-start(bf16[8,32,1536]{2,1,0:T(8,128)(2,1)} %fusion.40), calls=%async_computation.3 | async-start | bytes 1572864 | tf_op jit(solution)/shard_map/all_to_all | solution.py:285
  131.7 2.4 %copy-start.12 = (bf16[32,16,1536]{2,1,0:T(8,128)(2,1)S(1)}, bf16[32,16,1536]{2,1,0:T(8,128)(2,1)}, u32[]{:S(2)}) copy-start(bf16[32,16,1536]{2,1,0:T(8,128)(2,1)} %pad_maximum_fusion.2) | copy-start | bytes 4718596
  134.1 2.6 %copy-start.8 = (bf16[16,32,1,512]{3,0,1,2:T(8,128)(2,1)S(1)}, bf16[16,32,1,512]{3,0,1,2:T(8,128)(2,1)}, u32[]{:S(2)}) copy-start(bf16[16,32,1,512]{3,0,1,2:T(8,128)(2,1)} %copy-done.7) | copy-start | bytes 1572868
Sparse Core Ops, SparseCore 0:
  82.7 65.6 reduce-scatter.1

commit v9 on v8

--- a/solution.py
+++ b/solution.py
@@ -312,10 +312,17 @@
     allowed_space = spatial_allowed(sessions_here, channel_count, adjacency)
     spatial_context = spatial_forward_heads(spatial_proj, allowed_space)
     middle = (
-        activity.astype(jnp.float32)
-        + project(spatial_context, spatial_weights[:, 3 * model_width :])
-    ).astype(jnp.bfloat16)
-    middle_block = lax.all_to_all(middle, ("outer", "core"), split_axis=1, concat_axis=0, tiled=True)
+        jnp.swapaxes(activity, 0, 1).astype(jnp.float32)
+        + jnp.einsum(
+            "tbd,de->bte",
+            spatial_context,
+            spatial_weights[:, 3 * model_width :],
+            preferred_element_type=jnp.float32,
+        )
+    ).astype(jnp.bfloat16)
+    middle_block = lax.all_to_all(
+        middle, ("outer", "core"), split_axis=0, concat_axis=1, tiled=True
+    ).reshape(session_id.shape[0], 1, model_width)
     normed_two, inverse_two = norm_forward(middle_block, temporal_gain)
     temporal_proj = project(normed_two, temporal_weights[:, : 3 * model_width]).astype(jnp.bfloat16)
     allowed_time = session_id[:, None] == session_id[None, :]

time: 165 us -> 165 us (level)
    dot_general x0 -> x1, matrix products: none -> 1.68 us  [per_device(): jnp.einsum('tbd,de->bte', spatial_context, spatial_weights[:, 3 * model_w...]
    dot_general x4 -> x3, matrix products: 10.4 us -> 8.69 us  [project(): jnp.einsum('tbd,de->tbe', rows, coefficient_array, preferred_element_type...]
    unnamed x66 -> x65, local copies, waits for them, and re-layouts: 8.13 us -> 8.2 us
where the time goes in v9:
time: 165 us; the launch traced here: 164 us
  matrix products  49.4 us (30%)
  waiting for transfers between devices  48.7 us (30%)
  starting transfers between devices  20.7 us (13%)
  other arithmetic  17.2 us (10%)
  between operations  14.6 us (9%)
  local copies, waits for them, and re-layouts  13.4 us (8%)
    all_to_all x2, waiting for transfers between devices, reduce_rows(): pieces = lax.all_to_all(pieces, 'outer', 0, 0, tiled=True)  15.6 us
    all_to_all x1, waiting for transfers between devices, per_device(): lax.all_to_all(middle, ('outer', 'core'), split_axis=0, concat_axis=1, ti...  10.9 us
    reduce_scatter x1, waiting for transfers between devices, scatter_rows(): lax.psum_scatter(partial.astype(jnp.bfloat16), ('outer', 'core'), scatter...  10.5 us
    all_to_all x1, waiting for transfers between devices, per_device(): lax.all_to_all(grad_middle, ('outer', 'core'), split_axis=0, concat_axis=...  9.51 us
    all_to_all x2, starting transfers between devices, reduce_rows(): pieces = lax.all_to_all(pieces, 'outer', 0, 0, tiled=True)  8.78 us
    dot_general x3, matrix products, project(): jnp.einsum('tbd,de->tbe', rows, coefficient_array, preferred_element_type...  8.69 us
    unnamed x65, local copies, waits for them, and re-layouts  8.2 us
    all_to_all x1, starting transfers between devices, per_device(): lax.all_to_all(middle, ('outer', 'core'), split_axis=0, concat_axis=1, ti...  7.4 us
  transfers between devices with their start and end apart: 7, of which 6 were waited for; matrix products, arithmetic and copies ran while one was open for 21% of the time, Pallas kernels for 0%

profile of v9, /device:TPU:0, one launch (start us, length us, event | category | flops | bytes accessed | tf_op | source)
XLA Modules:
  0.0 164.0 jit_solution(12807247013711196686)
XLA Ops:
  7.2 1.2 fusion.96
  8.5 2.6 %convolution_convert_fusion.2 = bf16[32,16,1536]{2,1,0:T(8,128)(2,1)S(1)} fusion(bf16[512,2048]{1,0:T(8,128)(2,1)} %param.11, bf16[32,16,512]{2,1,0:T(8,128)(2,1)} %param.9, f32[512]{0:T(512)} %param.13, f32[32,16]{1,0:T(8,128)S(1)} %add_rsqrt_fusion), kind=kOutput, calls=%fused_computation.31 | convolution fusion | flops 807141376 | bytes 3674112 | tf_op jit(solution)/shard_map/tbd,de->tbe/dot_general | solution.py:263
  11.1 1.0 fusion.151
  12.6 2.6 %fusion.152 = (f32[32,16,8]{1,2,0:T(8,128)S(1)}, f32[32,16,8,16]{1,3,2,0:T(8,128)}) fusion(pred[32,16,16]{1,2,0:T(8,128)(4,1)S(1)} %and_or_fusion, pred[8,512]{1,0:T(8,128)(4,1)S(1)} %iota_compare_fusion, bf16[32,16,512]{2,1,0:T(8,128)(2,1)S(1)} %get-tuple-element.44, bf16[32,16,1536]{2,1,0:T(8,128)(2,1)S(1)} %convolution_convert_fusion.2), kind=kOutput, calls=%fused_computation.185 | convolution fusion | flops 69468176 | bytes 1396736 | tf_op jit(solution)/shard_map/sub | solution.py:197
  15.3 2.4 %fusion.69 = bf16[32,16,512]{2,1,0:T(8,128)(2,1)S(1)} fusion(pred[8,512]{1,0:T(8,128)(4,1)S(1)} %iota_compare_fusion, bf16[32,16,512]{2,1,0:T(8,128)(2,1)S(1)} %get-tuple-element.43, f32[32,16,8,16]{1,3,2,0:T(8,128)} %get-tuple-element.46, f32[32,16,8]{1,2,0:T(8,128)S(1)} %get-tuple-element.45), kind=kOutput, calls=%fused_computation.84 | convolution fusion | flops 69599232 | bytes 1331200 | tf_op jit(solution)/shard_map/tbhc,thcd->tbd/dot_general | solution.py:206
  17.7 1.7 %fusion.86 = bf16[16,32,512]{2,0,1:T(8,128)(2,1)S(1)} fusion(bf16[32,16,512]{2,1,0:T(8,128)(2,1)S(1)} %fusion.69, bf16[32,16,512]{2,1,0:T(8,128)(2,1)S(1)} %copy-done.5, bf16[512,2048]{1,0:T(8,128)(2,1)} %param.11), kind=kOutput, calls=%fused_computation.93 | convolution fusion | flops 269221888 | bytes 2097152 | tf_op jit(solution)/shard_map/tbd,de->bte/dot_general | solution.py:316
  19.4 1.1 copy.151
  20.4 7.4 %all-to-all-start = ((bf16[16,32,512]{2,1,0:T(8,128)(2,1)}), bf16[16,32,512]{2,1,0:T(8,128)(2,1)S(1)}, u32[]{:S(2)}, u32[]{:S(2)}) async-start(bf16[16,32,512]{2,1,0:T(8,128)(2,1)} %copy.151), calls=%async_computation | async-start | bytes 1048576 | tf_op jit(solution)/shard_map/all_to_all | solution.py:323
  27.9 1.0 copy.157
  29.1 2.3 %convolution_convert_fusion.9 = bf16[512,512]{0,1:T(8,128)(2,1)} fusion(bf16[512,1,512]{2,0,1:T(8,128)(2,1)S(1)} %copy-done.3, bf16[512,2048]{1,0:T(8,128)(2,1)} %param.12), kind=kOutput, calls=%fused_computation.83 | convolution fusion | flops 268697600 | bytes 1572864 | tf_op jit(solution)/shard_map/tbe,de->tbd/dot_general | solution.py:267
  31.4 10.9 %all-to-all-done = bf16[16,32,512]{2,1,0:T(8,128)(2,1)S(1)} async-done(((bf16[16,32,512]{2,1,0:T(8,128)(2,1)}), bf16[16,32,512]{2,1,0:T(8,128)(2,1)S(1)}, u32[]{:S(2)}, u32[]{:S(2)}) %all-to-all-start) | async-done | bytes 524320 | tf_op jit(solution)/shard_map/all_to_all | solution.py:323
  43.8 3.6 %convolution_convert_fusion.1 = bf16[512,1536]{1,0:T(8,128)(2,1)} fusion(bf16[512,2048]{1,0:T(8,128)(2,1)} %param.12, f32[512,512]{0,1:T(8,128)S(1)} %copy.154, f32[512]{0:T(512)S(1)} %copy-done.23, f32[512]{0:T(512)S(1)} %rsqrt.21), kind=kOutput, calls=%fused_computation.30 | convolution fusion | flops 806879232 | bytes 4198400 | tf_op jit(solution)/shard_map/tbd,de->tbe/dot_general | solution.py:263
  47.4 1.7 %copy.155 = bf16[512,1536]{0,1:T(8,128)(2,1)S(1)} copy(bf16[512,1536]{1,0:T(8,128)(2,1)} %convolution_convert_fusion.1) | data formatting | bytes 3145728 | tf_op jit(solution)/shard_map/convert_element_type | solution.py:327
  49.1 5.4 %fusion.153 = (f32[8,512]{1,0:T(8,128)S(1)}, f32[8,512,512]{1,2,0:T(8,128)}) fusion(pred[512,512]{0,1:T(8,128)(4,1)S(1)} %broadcast_compare_fusion, bf16[512,3,8,64]{0,3,2,1:T(8,128)(2,1)S(1)} %bitcast.205), kind=kOutput, calls=%fused_computation.186 | convolution fusion | flops 276824576 | bytes 9715712 | tf_op jit(solution)/shard_map/while/body/eval_jaxpr/sub | solution.py:39
  54.6 4.7 %fusion.24 = bf16[8,512,512]{1,2,0:T(8,128)(2,1)S(1)} fusion(f32[8,512,512]{1,2,0:T(8,128)} %get-tuple-element.48, f32[8,512]{1,0:T(8,128)S(1)} %get-tuple-element.47), kind=kLoop, calls=%fused_computation.28 | loop fusion | flops 4194304 | bytes 12599296 | tf_op jit(solution)/shard_map/while/body/eval_jaxpr/convert_element_type | solution.py:48
  60.1 1.4 fusion.88
  61.4 1.2 copy-done
  62.6 1.8 %multiply_convert_fusion = bf16[8,512,512]{1,2,0:T(8,128)(2,1)S(1)} fusion(f32[8,512]{1,0:T(8,128)S(1)} %get-tuple-element.49, f32[8,512,512]{1,2,0:T(8,128)S(1)} %copy-done, f32[8,512]{1,0:T(8,128)S(1)} %get-tuple-element.47, bf16[8,512,64]{1,2,0:T(8,128)(2,1)S(1)} %bitcast.219, bf16[512,3,8,64]{0,3,2,1:T(8,128)(2,1)S(1)} %bitcast.207), kind=kOutput, calls=%fused_computation.2 | convolution fusion | flops 278921216 | bytes 13664256 | tf_op jit(solution)/shard_map/while/body/eval_jaxpr/...uo,...ao->...ua/dot_general | solution.py:73
  64.4 1.4 fusion.87
  66.8 1.2 copy-done.2
  68.1 1.0 copy-done.20
  69.1 1.0 multiply_reduce_fusion
  71.0 1.1 reduce.6
  72.3 1.2 reshape.381
  73.5 4.1 %all-to-all-start.1 = ((bf16[16,2,8192]{2,1,0:T(2,128)(2,1)}), bf16[16,2,8192]{2,1,0:T(2,128)(2,1)S(1)}, u32[]{:S(2)}, u32[]{:S(2)}) async-start(bf16[16,2,8192]{2,1,0:T(2,128)(2,1)} %reshape.381), calls=%async_computation.1 | async-start | bytes 1048576 | tf_op jit(solution)/shard_map/all_to_all | solution.py:357
  78.3 2.6 %convolution_convert_fusion = bf16[512,1536]{1,0:T(8,128)(2,1)S(1)} fusion(bf16[512,1536]{0,1:T(8,128)(2,1)} %bitcast.221, f32[512,1,1,1,1,1,512]{6,0,5,4,3,2,1:T(8,128)S(1)} %bitcast.201, f32[512]{0:T(512)S(1)} %copy-done.23, f32[512]{0:T(512)S(1)} %rsqrt.21), kind=kOutput, calls=%fused_computation.29 | convolution fusion | flops 806879232 | bytes 4198400 | tf_op jit(solution)/shard_map/tbd,tbe->de/dot_general | solution.py:273
  80.9 1.6 pad_maximum_fusion
  82.5 9.5 %all-to-all-done.1 = bf16[16,2,8192]{2,1,0:T(2,128)(2,1)S(1)} async-done(((bf16[16,2,8192]{2,1,0:T(2,128)(2,1)}), bf16[16,2,8192]{2,1,0:T(2,128)(2,1)S(1)}, u32[]{:S(2)}, u32[]{:S(2)}) %all-to-all-start.1) | async-done | bytes 524320 | tf_op jit(solution)/shard_map/all_to_all | solution.py:357
  92.7 1.6 %convolution_bitcast_fusion = f32[512,512]{1,0:T(8,128)S(1)} fusion(bf16[32,16,512]{2,1,0:T(8,128)(2,1)} %copy-done.13, bf16[16,32,1,512]{3,1,0,2:T(8,128)(2,1)S(1)} %bitcast.214), kind=kOutput, calls=%fused_computation.69 | convolution fusion | flops 268435456 | bytes 2097152 | tf_op jit(solution)/shard_map/tbd,tbe->de/dot_general | solution.py:273
  95.5 1.5 convolution_convert_fusion.6
  97.1 1.4 fusion.75
  98.5 1.9 %fusion.99 = f32[32,16,8]{1,2,0:T(8,128)S(1)} fusion(bf16[32,16,512]{2,1,0:T(8,128)(2,1)S(1)} %copy-done.14, bf16[32,16,512]{2,1,0:T(8,128)(2,1)S(1)} %convolution_convert_fusion.6, s32[512]{0:T(512)S(1)} %add_select_fusion), kind=kOutput, calls=%fused_computation.108 | convolution fusion | flops 25956352 | bytes 1067008 | tf_op jit(solution)/shard_map/tbd,hd->tbh/dot_general | solution.py:226
  100.6 1.3 multiply_convert_fusion.1
  101.9 1.4 fusion.78
  104.2 4.3 %all-to-all-start.2 = ((bf16[8,32,512]{2,1,0:T(8,128)(2,1)}), bf16[8,32,512]{2,1,0:T(8,128)(2,1)S(1)}, u32[]{:S(2)}, u32[]{:S(2)}) async-start(bf16[8,32,512]{2,1,0:T(8,128)(2,1)} %fusion.114), calls=%async_computation.2 | async-start | bytes 524288 | tf_op jit(solution)/shard_map/all_to_all | solution.py:285
  108.4 1.9 %fusion.72 = bf16[32,16,512]{2,1,0:T(8,128)(2,1)S(1)} fusion(bf16[32,16,8,16]{1,3,2,0:T(8,128)(2,1)} %copy-done.26, pred[8,512]{1,0:T(8,128)(4,1)S(1)} %iota_compare_fusion, bf16[32,16,512]{2,1,0:T(8,128)(2,1)S(1)} %copy-done.16), kind=kOutput, calls=%fused_computation.85 | convolution fusion | flops 69468160 | bytes 1183744 | tf_op jit(solution)/shard_map/tbhc,thcd->tbd/dot_general | solution.py:236
  110.4 1.3 pad_maximum_fusion.2
  111.6 9.2 %all-to-all-done.2 = bf16[8,32,512]{2,1,0:T(8,128)(2,1)S(1)} async-done(((bf16[8,32,512]{2,1,0:T(8,128)(2,1)}), bf16[8,32,512]{2,1,0:T(8,128)(2,1)S(1)}, u32[]{:S(2)}, u32[]{:S(2)}) %all-to-all-start.2) | async-done | bytes 262176 | tf_op jit(solution)/shard_map/all_to_all | solution.py:285
  120.9 2.5 %fusion.130 = f32[512,1536,1]{1,0,2:T(8,128)S(1)} fusion(bf16[32,16,1536]{2,1,0:T(8,128)(2,1)} %pad_maximum_fusion.2, bf16[32,16,512]{2,1,0:T(8,128)(2,1)S(1)} %copy-done.6, f32[512]{0:T(512)S(1)} %copy-done.24, f32[32,16]{1,0:T(8,128)S(1)} %add_rsqrt_fusion), kind=kOutput, calls=%fused_computation.150 | convolution fusion | flops 806354944 | bytes 5246976 | tf_op jit(solution)/shard_map/tbd,tbe->de/dot_general | solution.py:273
  123.6 2.3 %collective-permute-done.1 = bf16[8,32,1536]{2,1,0:T(8,128)(2,1)S(1)} collective-permute-done((bf16[8,32,1536]{2,1,0:T(8,128)(2,1)S(1)}, bf16[8,32,1536]{2,1,0:T(8,128)(2,1)S(1)}, u32[]{:S(2)}, u32[]{:S(2)}) %collective-permute-start.1) | collective-permute-done | bytes 786464 | tf_op jit(solution)/shard_map/ppermute | solution.py:283
  125.9 1.3 fusion.40
  127.2 4.5 %all-to-all-start.3 = ((bf16[8,32,1536]{2,1,0:T(8,128)(2,1)}), bf16[8,32,1536]{2,1,0:T(8,128)(2,1)S(1)}, u32[]{:S(2)}, u32[]{:S(2)}) async-start(bf16[8,32,1536]{2,1,0:T(8,128)(2,1)} %fusion.40), calls=%async_computation.3 | async-start | bytes 1572864 | tf_op jit(solution)/shard_map/all_to_all | solution.py:285
  131.7 2.4 %fusion.85 = bf16[512,1,512]{2,0,1:T(8,128)(2,1)} fusion(f32[512,512]{1,0:T(8,128)S(1)} %bitcast.202, bf16[512,512]{0,1:T(8,128)(2,1)S(1)} %bitcast.211, bf16[512,2048]{1,0:T(8,128)(2,1)} %param.12), kind=kOutput, calls=%fused_computation.92 | convolution fusion | flops 268959744 | bytes 2621440 | tf_op jit(solution)/shard_map/tbd,de->tbe/dot_general | solution.py:263
  134.1 2.5 %fusion.97 = (f32[32,16]{1,0:T(8,128)S(1)}, f32[32,16,512]{2,1,0:T(8,128)S(1)}) fusion(bf16[32,16,512]{2,1,0:T(8,128)(2,1)S(1)} %copy-done.6, f32[512]{0:T(512)S(1)} %copy-done.24, bf16[32,16,1536]{2,1,0:T(8,128)(2,1)S(1)} %copy-done.12, bf16[512,2048]{1,0:T(8,128)(2,1)} %param.11), kind=kOutput, calls=%fused_computation.104 | convolution fusion | flops 806354432 | bytes 4722688 | tf_op jit(solution)/shard_map/tbe,de->tbd/dot_general | solution.py:267
  136.7 1.2 fusion.95
  137.9 10.5 %reduce-scatter.2.cloned.1.call-done = bf16[32,2048]{1,0:T(8,128)(2,1)} async-done(((bf16[512,2048]{1,0:T(8,128)(2,1)}), bf16[32,2048]{1,0:T(8,128)(2,1)}) %reduce-scatter.2.cloned.1.call-update) | async-done | bytes 131088 | tf_op jit(solution)/shard_map/reduce_scatter | solution.py:290
  148.4 1.6 convert_element_type.256
  150.0 6.4 %all-to-all-done.3 = bf16[8,32,1536]{2,1,0:T(8,128)(2,1)S(1)} async-done(((bf16[8,32,1536]{2,1,0:T(8,128)(2,1)}), bf16[8,32,1536]{2,1,0:T(8,128)(2,1)S(1)}, u32[]{:S(2)}, u32[]{:S(2)}) %all-to-all-start.3) | async-done | bytes 786464 | tf_op jit(solution)/shard_map/all_to_all | solution.py:285
  (97 shorter events, 9.7 us)
Async XLA Ops:
  11.1 1.0 copy-start.22
  11.1 1.1 copy-start.21
  11.1 1.2 copy-start.25
  12.1 3.1 %copy-start.15 = (bf16[32,16,512]{2,1,0:T(8,128)(2,1)}, bf16[32,16,512]{2,1,0:T(8,128)(2,1)S(1)}, u32[]{:S(2)}) copy-start(bf16[32,16,512]{2,1,0:T(8,128)(2,1)S(1)} %get-tuple-element.44) | copy-start | bytes 1572868
  12.1 3.1 %copy-start.18 = (bf16[32,16,512]{2,1,0:T(8,128)(2,1)}, bf16[32,16,512]{2,1,0:T(8,128)(2,1)S(1)}, u32[]{:S(2)}) copy-start(bf16[32,16,512]{2,1,0:T(8,128)(2,1)S(1)} %get-tuple-element.43) | copy-start | bytes 1572868
  15.2 2.4 %copy-start.28 = (f32[32,16,8]{1,2,0:T(8,128)}, f32[32,16,8]{1,2,0:T(8,128)S(1)}, u32[]{:S(2)}) copy-start(f32[32,16,8]{1,2,0:T(8,128)S(1)} %get-tuple-element.45) | copy-start | bytes 49156
  15.3 2.4 %copy-start.5 = (bf16[32,16,512]{2,1,0:T(8,128)(2,1)S(1)}, bf16[32,16,512]{2,1,0:T(8,128)(2,1)}, u32[]{:S(2)}) copy-start(bf16[32,16,512]{2,1,0:T(8,128)(2,1)} %param.9) | copy-start | bytes 1572868
  17.6 1.7 %copy-start.13 = (bf16[32,16,512]{2,1,0:T(8,128)(2,1)}, bf16[32,16,512]{2,1,0:T(8,128)(2,1)S(1)}, u32[]{:S(2)}) copy-start(bf16[32,16,512]{2,1,0:T(8,128)(2,1)S(1)} %fusion.69) | copy-start | bytes 1572868
  17.6 10.2 %copy-start.3 = (bf16[512,1,512]{2,0,1:T(8,128)(2,1)S(1)}, bf16[512,1,512]{2,0,1:T(8,128)(2,1)}, u32[]{:S(2)}) copy-start(bf16[512,1,512]{2,0,1:T(8,128)(2,1)} %param.10) | copy-start | bytes 1572868
  20.4 21.9 %all-to-all-start = ((bf16[16,32,512]{2,1,0:T(8,128)(2,1)}), bf16[16,32,512]{2,1,0:T(8,128)(2,1)S(1)}, u32[]{:S(2)}, u32[]{:S(2)}) async-start(bf16[16,32,512]{2,1,0:T(8,128)(2,1)} %copy.151), calls=%async_computation | async-start | bytes 1048576 | tf_op jit(solution)/shard_map/all_to_all | solution.py:323
  31.4 12.4 %copy-start.23 = (f32[512]{0:T(512)S(1)}, f32[512]{0:T(512)}, u32[]{:S(2)}) copy-start(f32[512]{0:T(512)} %param.14) | copy-start | bytes 6148
  42.8 1.0 copy-start.1
  54.6 4.7 %copy-start.10 = (bf16[512,512]{0,1:T(8,128)(2,1)S(1)}, bf16[512,512]{0,1:T(8,128)(2,1)}, u32[]{:S(2)}) copy-start(bf16[512,512]{0,1:T(8,128)(2,1)} %convolution_convert_fusion.9) | copy-start | bytes 1572868
  59.2 3.4 %copy-start = (f32[8,512,512]{1,2,0:T(8,128)S(1)}, f32[8,512,512]{1,2,0:T(8,128)}, u32[]{:S(2)}) copy-start(f32[8,512,512]{1,2,0:T(8,128)} %get-tuple-element.48) | copy-start | bytes 25165828
  66.6 1.5 copy-start.2
  66.6 2.5 %copy-start.20 = (bf16[512,2048]{1,0:T(8,128)(2,1)S(1)}, bf16[512,2048]{1,0:T(8,128)(2,1)}, u32[]{:S(2)}) copy-start(bf16[512,2048]{1,0:T(8,128)(2,1)} %param.12) | copy-start | bytes 6291460
  66.8 3.3 %copy-start.11 = (bf16[3,8,512,64]{2,3,1,0:T(8,128)(2,1)}, bf16[3,8,512,64]{2,3,1,0:T(8,128)(2,1)S(1)}, u32[]{:S(2)}) copy-start(bf16[3,8,512,64]{2,3,1,0:T(8,128)(2,1)S(1)} %pad_maximum_fusion.1) | copy-start | bytes 4718596
  69.1 1.0 copy-start.9
  71.0 6.9 %copy-start.4 = (bf16[512,1,512]{2,0,1:T(8,128)(2,1)S(1)}, bf16[512,1,512]{2,0,1:T(8,128)(2,1)}, u32[]{:S(2)}) copy-start(bf16[512,1,512]{2,0,1:T(8,128)(2,1)} %param.10) | copy-start | bytes 1572868
  73.5 18.6 %all-to-all-start.1 = ((bf16[16,2,8192]{2,1,0:T(2,128)(2,1)}), bf16[16,2,8192]{2,1,0:T(2,128)(2,1)S(1)}, u32[]{:S(2)}, u32[]{:S(2)}) async-start(bf16[16,2,8192]{2,1,0:T(2,128)(2,1)} %reshape.381), calls=%async_computation.1 | async-start | bytes 1048576 | tf_op jit(solution)/shard_map/all_to_all | solution.py:357
  77.6 70.8 %reduce-scatter.2.cloned.1.call-start = ((), (), s32[]{:S(2)}) async-start(), calls=%async_computation.5 | async-start | bytes 2228224 | tf_op jit(solution)/shard_map/reduce_scatter | solution.py:290
  94.4 2.7 %copy-start.27 = (f32[32,16,8,16]{1,3,2,0:T(8,128)S(1)}, f32[32,16,8,16]{1,3,2,0:T(8,128)}, u32[]{:S(2)}) copy-start(f32[32,16,8,16]{1,3,2,0:T(8,128)} %get-tuple-element.46) | copy-start | bytes 786436
  94.4 2.7 %copy-start.29 = (f32[32,16,8]{1,2,0:T(8,128)S(1)}, f32[32,16,8]{1,2,0:T(8,128)}, u32[]{:S(2)}) copy-start(f32[32,16,8]{1,2,0:T(8,128)} %copy-done.28) | copy-start | bytes 49156
  94.7 0.8 copy-start.7
  97.1 1.4 copy-start.14
  97.1 3.5 %copy-start.19 = (bf16[32,16,512]{2,1,0:T(8,128)(2,1)S(1)}, bf16[32,16,512]{2,1,0:T(8,128)(2,1)}, u32[]{:S(2)}) copy-start(bf16[32,16,512]{2,1,0:T(8,128)(2,1)} %copy-done.18) | copy-start | bytes 1572868
  100.5 1.4 copy-start.17
  100.5 2.8 %collective-permute-start = (bf16[8,32,512]{2,1,0:T(8,128)(2,1)S(1)}, bf16[8,32,512]{2,1,0:T(8,128)(2,1)S(1)}, u32[]{:S(2)}, u32[]{:S(2)}) collective-permute-start(bf16[8,32,512]{2,1,0:T(8,128)(2,1)S(1)} %fusion.133), channel_id=1, source_target_pairs={{0,1},{1,0},{2,3},{3,2},{4,5},{5,4},{6,7},{7,6},{8,9},{9,8},{10,11... | collective-permute-start | bytes 786440 | tf_op jit(solution)/shard_map/ppermute | solution.py:283
  101.9 1.4 copy-start.26
  103.3 5.1 %copy-start.16 = (bf16[32,16,512]{2,1,0:T(8,128)(2,1)S(1)}, bf16[32,16,512]{2,1,0:T(8,128)(2,1)}, u32[]{:S(2)}) copy-start(bf16[32,16,512]{2,1,0:T(8,128)(2,1)} %copy-done.15) | copy-start | bytes 1572868
  104.2 16.7 %all-to-all-start.2 = ((bf16[8,32,512]{2,1,0:T(8,128)(2,1)}), bf16[8,32,512]{2,1,0:T(8,128)(2,1)S(1)}, u32[]{:S(2)}, u32[]{:S(2)}) async-start(bf16[8,32,512]{2,1,0:T(8,128)(2,1)} %fusion.114), calls=%async_computation.2 | async-start | bytes 524288 | tf_op jit(solution)/shard_map/all_to_all | solution.py:285
  110.4 10.5 %copy-start.6 = (bf16[32,16,512]{2,1,0:T(8,128)(2,1)S(1)}, bf16[32,16,512]{2,1,0:T(8,128)(2,1)}, u32[]{:S(2)}) copy-start(bf16[32,16,512]{2,1,0:T(8,128)(2,1)} %param.9) | copy-start | bytes 1572868
  110.4 10.5 %copy-start.24 = (f32[512]{0:T(512)S(1)}, f32[512]{0:T(512)}, u32[]{:S(2)}) copy-start(f32[512]{0:T(512)} %param.13) | copy-start | bytes 6148
  123.6 2.4 %collective-permute-start.1 = (bf16[8,32,1536]{2,1,0:T(8,128)(2,1)S(1)}, bf16[8,32,1536]{2,1,0:T(8,128)(2,1)S(1)}, u32[]{:S(2)}, u32[]{:S(2)}) collective-permute-start(bf16[8,32,1536]{2,1,0:T(8,128)(2,1)S(1)} %fusion.109), channel_id=1, source_target_pairs={{0,1},{1,0},{2,3},{3,2},{4,5},{5,4},{6,7},{7,6},{8,9},{9,8},{10,11... | collective-permute-start | bytes 2359304 | tf_op jit(solution)/shard_map/ppermute | solution.py:283
  127.2 29.2 %all-to-all-start.3 = ((bf16[8,32,1536]{2,1,0:T(8,128)(2,1)}), bf16[8,32,1536]{2,1,0:T(8,128)(2,1)S(1)}, u32[]{:S(2)}, u32[]{:S(2)}) async-start(bf16[8,32,1536]{2,1,0:T(8,128)(2,1)} %fusion.40), calls=%async_computation.3 | async-start | bytes 1572864 | tf_op jit(solution)/shard_map/all_to_all | solution.py:285
  131.7 2.4 %copy-start.12 = (bf16[32,16,1536]{2,1,0:T(8,128)(2,1)S(1)}, bf16[32,16,1536]{2,1,0:T(8,128)(2,1)}, u32[]{:S(2)}) copy-start(bf16[32,16,1536]{2,1,0:T(8,128)(2,1)} %pad_maximum_fusion.2) | copy-start | bytes 4718596
  134.1 2.6 %copy-start.8 = (bf16[16,32,1,512]{3,0,1,2:T(8,128)(2,1)S(1)}, bf16[16,32,1,512]{3,0,1,2:T(8,128)(2,1)}, u32[]{:S(2)}) copy-start(bf16[16,32,1,512]{3,0,1,2:T(8,128)(2,1)} %copy-done.7) | copy-start | bytes 1572868
Sparse Core Ops, SparseCore 0:
  82.7 65.6 reduce-scatter.1

commit v10 on v8

--- a/solution.py
+++ b/solution.py
@@ -101,8 +101,10 @@
 
 
 def temporal_split(projected):
-    pieces = projected.reshape(projected.shape[0], 3, HEADS, projected.shape[1] // (3 * HEADS))
-    return [pieces[:, index].transpose(1, 0, 2) for index in range(3)]
+    return [
+        part.reshape(part.shape[0], HEADS, part.shape[1] // HEADS).transpose(1, 0, 2)
+        for part in projected
+    ]
 
 
 def temporal_forward(projected, admissible_pairs):
@@ -111,13 +113,13 @@
     combined_output = compute_affinity_outputs(
         asking_vectors, lookup_array, payload_array, admissible_pairs[None], sharpness_divisor
     )
-    return combined_output.transpose(1, 0, 2).reshape(projected.shape[0], -1)
+    return combined_output.transpose(1, 0, 2).reshape(projected[0].shape[0], -1)
 
 
 def temporal_backward(projected, admissible_pairs, combined_output, blended_output_derivative):
     asking_vectors, lookup_array, payload_array = temporal_split(projected)
     sharpness_divisor = float(asking_vectors.shape[-1]) ** (-0.5)
-    bins = projected.shape[0]
+    bins = projected[0].shape[0]
     subspace_outputs = combined_output.reshape(bins, HEADS, -1).transpose(1, 0, 2)
     subspace_derivative = blended_output_derivative.reshape(bins, HEADS, -1).transpose(1, 0, 2)
     derivative_collection = compute_affinity_derivatives(
@@ -317,9 +319,14 @@
     ).astype(jnp.bfloat16)
     middle_block = lax.all_to_all(middle, ("outer", "core"), split_axis=1, concat_axis=0, tiled=True)
     normed_two, inverse_two = norm_forward(middle_block, temporal_gain)
-    temporal_proj = project(normed_two, temporal_weights[:, : 3 * model_width]).astype(jnp.bfloat16)
+    temporal_proj = tuple(
+        project(normed_two, temporal_weights[:, i * model_width : (i + 1) * model_width]).astype(
+            jnp.bfloat16
+        )
+        for i in range(3)
+    )
     allowed_time = session_id[:, None] == session_id[None, :]
-    by_block = jnp.moveaxis(temporal_proj, 1, 0)
+    by_block = tuple(jnp.moveaxis(part, 1, 0) for part in temporal_proj)
     temporal_context = jnp.moveaxis(
         lax.map(lambda block_rows: temporal_forward(block_rows, allowed_time), by_block), 0, 1
     )

time: 165 us -> 170 us (1.030)
  matrix products: 49.4 us -> 52.2 us
  other arithmetic: 17.2 us -> 19.1 us
    reduce_scatter x1, waiting for transfers between devices: 10.5 us -> 16.1 us  [scatter_rows(): lax.psum_scatter(partial.astype(jnp.bfloat16), ('outer', 'core'), scatter...]
    all_to_all x2, waiting for transfers between devices: 15.6 us -> 10.8 us  [reduce_rows(): pieces = lax.all_to_all(pieces, 'outer', 0, 0, tiled=True)]
    sub x1, matrix products: 5.43 us -> 7.6 us  [normalized_affinity(): expo = jnp.exp(unnormalized_affinities - row_max)]
    convert_element_type x2, other arithmetic: 1.41 us -> 3.2 us  [per_device(): grad_middle = (grad_out.astype(jnp.float32) + norm_backward(middle_block,...]
    convert_element_type x1 -> x0, local copies, waits for them, and re-layouts: 1.71 us -> none  [per_device(): project(normed_two, temporal_weights[:, :3 * model_width])]
    unnamed x66 -> x72, local copies, waits for them, and re-layouts: 8.13 us -> 8.94 us
    dot_general x4 -> x6, matrix products: 10.4 us -> 11 us  [project(): jnp.einsum('tbd,de->tbe', rows, coefficient_array, preferred_element_type...]
where the time goes in v10:
time: 170 us; the launch traced here: 169 us
  matrix products  52.2 us (31%)
  waiting for transfers between devices  49.8 us (29%)
  starting transfers between devices  20.6 us (12%)
  other arithmetic  19.1 us (11%)
  between operations  14.7 us (9%)
  local copies, waits for them, and re-layouts  12.5 us (7%)
    reduce_scatter x1, waiting for transfers between devices, scatter_rows(): lax.psum_scatter(partial.astype(jnp.bfloat16), ('outer', 'core'), scatter...  16.1 us
    dot_general x6, matrix products, project(): jnp.einsum('tbd,de->tbe', rows, coefficient_array, preferred_element_type...  11 us
    all_to_all x1, waiting for transfers between devices, per_device(): lax.all_to_all(middle, ('outer', 'core'), split_axis=1, concat_axis=0, ti...  10.9 us
    all_to_all x2, waiting for transfers between devices, reduce_rows(): pieces = lax.all_to_all(pieces, 'outer', 0, 0, tiled=True)  10.8 us
    all_to_all x1, waiting for transfers between devices, per_device(): lax.all_to_all(grad_middle, ('outer', 'core'), split_axis=0, concat_axis=...  9.74 us
    unnamed x72, local copies, waits for them, and re-layouts  8.94 us
    all_to_all x2, starting transfers between devices, reduce_rows(): pieces = lax.all_to_all(pieces, 'outer', 0, 0, tiled=True)  8.57 us
    sub x1, matrix products, normalized_affinity(): expo = jnp.exp(unnormalized_affinities - row_max)  7.6 us
  transfers between devices with their start and end apart: 7, of which 6 were waited for; matrix products, arithmetic and copies ran while one was open for 21% of the time, Pallas kernels for 0%

profile of v10, /device:TPU:0, one launch (start us, length us, event | category | flops | bytes accessed | tf_op | source)
XLA Modules:
  0.0 168.9 jit_solution(4715777260050757060)
XLA Ops:
  7.2 1.2 fusion.94
  8.5 2.6 %convolution_convert_fusion.1 = bf16[32,16,1536]{2,1,0:T(8,128)(2,1)S(1)} fusion(bf16[512,2048]{1,0:T(8,128)(2,1)} %param.11, bf16[32,16,512]{2,1,0:T(8,128)(2,1)} %param.9, f32[512]{0:T(512)} %param.13, f32[32,16]{1,0:T(8,128)S(1)} %add_rsqrt_fusion), kind=kOutput, calls=%fused_computation.30 | convolution fusion | flops 807141376 | bytes 3674112 | tf_op jit(solution)/shard_map/tbd,de->tbe/dot_general | solution.py:265
  11.1 1.0 fusion.149
  12.6 2.6 %fusion.150 = (f32[32,16,8]{1,2,0:T(8,128)S(1)}, f32[32,16,8,16]{1,3,2,0:T(8,128)}) fusion(pred[32,16,16]{1,2,0:T(8,128)(4,1)S(1)} %and_or_fusion, pred[8,512]{1,0:T(8,128)(4,1)S(1)} %iota_compare_fusion, bf16[32,16,512]{2,1,0:T(8,128)(2,1)S(1)} %get-tuple-element.56, bf16[32,16,1536]{2,1,0:T(8,128)(2,1)S(1)} %convolution_convert_fusion.1), kind=kOutput, calls=%fused_computation.182 | convolution fusion | flops 69468176 | bytes 1396736 | tf_op jit(solution)/shard_map/sub | solution.py:199
  15.3 2.4 %fusion.68 = bf16[32,16,512]{2,1,0:T(8,128)(2,1)S(1)} fusion(pred[8,512]{1,0:T(8,128)(4,1)S(1)} %iota_compare_fusion, bf16[32,16,512]{2,1,0:T(8,128)(2,1)S(1)} %get-tuple-element.47, f32[32,16,8,16]{1,3,2,0:T(8,128)} %get-tuple-element.58, f32[32,16,8]{1,2,0:T(8,128)S(1)} %get-tuple-element.57), kind=kOutput, calls=%fused_computation.85 | convolution fusion | flops 69599232 | bytes 1331200 | tf_op jit(solution)/shard_map/tbhc,thcd->tbd/dot_general | solution.py:208
  17.7 1.7 fusion.80
  19.3 1.1 copy.95
  20.4 7.4 %all-to-all-start = ((bf16[32,16,512]{2,0,1:T(8,128)(2,1)}), bf16[32,16,512]{2,0,1:T(8,128)(2,1)S(1)}, u32[]{:S(2)}, u32[]{:S(2)}) async-start(bf16[32,16,512]{2,0,1:T(8,128)(2,1)} %copy.95), calls=%async_computation | async-start | bytes 1048576 | tf_op jit(solution)/shard_map/all_to_all | solution.py:320
  27.9 1.0 copy.100
  29.1 2.3 %convolution_convert_fusion.8 = bf16[512,512]{0,1:T(8,128)(2,1)} fusion(bf16[512,1,512]{2,0,1:T(8,128)(2,1)S(1)} %copy-done.1, bf16[512,2048]{1,0:T(8,128)(2,1)} %param.12), kind=kOutput, calls=%fused_computation.81 | convolution fusion | flops 268697600 | bytes 1572864 | tf_op jit(solution)/shard_map/tbe,de->tbd/dot_general | solution.py:269
  31.4 10.9 %all-to-all-done = bf16[32,16,512]{2,0,1:T(8,128)(2,1)S(1)} async-done(((bf16[32,16,512]{2,0,1:T(8,128)(2,1)}), bf16[32,16,512]{2,0,1:T(8,128)(2,1)S(1)}, u32[]{:S(2)}, u32[]{:S(2)}) %all-to-all-start) | async-done | bytes 524320 | tf_op jit(solution)/shard_map/all_to_all | solution.py:320
  43.4 2.4 %convolution_convert_fusion.9 = bf16[512,512]{0,1:T(8,128)(2,1)} fusion(bf16[512,512]{0,1:T(8,128)(2,1)S(1)} %multiply_convert_fusion.3, bf16[512,2048]{1,0:T(8,128)(2,1)} %param.12), kind=kOutput, calls=%fused_computation.82 | convolution fusion | flops 268697600 | bytes 1572864 | tf_op jit(solution)/shard_map/tbd,de->tbe/dot_general | solution.py:265
  45.8 1.3 convolution_convert_fusion.11
  47.6 7.6 %fusion.151 = (f32[8,512]{1,0:T(8,128)S(1)}, f32[8,512,512]{1,2,0:T(8,128)}) fusion(pred[512,512]{0,1:T(8,128)(4,1)S(1)} %broadcast_compare_fusion, bf16[8,512,64]{1,2,0:T(8,128)(2,1)} %bitcast.207, bf16[8,512,64]{1,2,0:T(8,128)(2,1)S(1)} %bitcast.205), kind=kOutput, calls=%fused_computation.183 | convolution fusion | flops 276824576 | bytes 9715712 | tf_op jit(solution)/shard_map/while/body/eval_jaxpr/sub | solution.py:39
  55.2 4.7 %fusion.24 = bf16[8,512,512]{1,2,0:T(8,128)(2,1)S(1)} fusion(f32[8,512,512]{1,2,0:T(8,128)} %get-tuple-element.60, f32[8,512]{1,0:T(8,128)S(1)} %get-tuple-element.59), kind=kLoop, calls=%fused_computation.28 | loop fusion | flops 4194304 | bytes 12599296 | tf_op jit(solution)/shard_map/while/body/eval_jaxpr/convert_element_type | solution.py:48
  60.7 1.4 fusion.86
  62.1 1.2 copy-done
  63.3 2.0 %multiply_convert_fusion = bf16[8,512,512]{1,2,0:T(8,128)(2,1)S(1)} fusion(f32[8,512]{1,0:T(8,128)S(1)} %get-tuple-element.61, f32[8,512,512]{1,2,0:T(8,128)S(1)} %copy-done, f32[8,512]{1,0:T(8,128)S(1)} %get-tuple-element.59, bf16[8,512,64]{1,2,0:T(8,128)(2,1)S(1)} %bitcast.202, bf16[8,512,64]{1,2,0:T(8,128)(2,1)S(1)} %bitcast.210), kind=kOutput, calls=%fused_computation.2 | convolution fusion | flops 278921216 | bytes 13664256 | tf_op jit(solution)/shard_map/while/body/eval_jaxpr/...uo,...ao->...ua/dot_general | solution.py:73
  65.3 1.4 fusion.85
  67.7 2.0 %copy-done.23 = bf16[512,2048]{1,0:T(8,128)(2,1)S(1)} copy-done((bf16[512,2048]{1,0:T(8,128)(2,1)S(1)}, bf16[512,2048]{1,0:T(8,128)(2,1)}, u32[]{:S(2)}) %copy-start.23) | copy-done | bytes 2097176
  69.7 1.0 multiply_reduce_fusion
  70.7 1.1 fusion.96
  72.3 2.1 %reduce.6 = bf16[512,512]{0,1:T(8,128)(2,1)S(1)} reduce(bf16[512,1,512]{0,2,1:T(8,128)(2,1)} %fusion.96, bf16[]{:T(256)} %broadcast.272), dimensions={1}, to_apply=%copy.106.reduce_sub_computation | reduce | bytes 1048578 | tf_op jit(solution)/shard_map/convert_element_type | solution.py:356
  74.6 1.2 reshape.417
  75.8 4.5 %all-to-all-start.1 = ((bf16[16,2,8192]{2,1,0:T(2,128)(2,1)}), bf16[16,2,8192]{2,1,0:T(2,128)(2,1)}, u32[]{:S(2)}, u32[]{:S(2)}) async-start(bf16[16,2,8192]{2,1,0:T(2,128)(2,1)} %reshape.417), calls=%async_computation.1 | async-start | bytes 1048576 | tf_op jit(solution)/shard_map/all_to_all | solution.py:357
  80.8 2.6 %convolution_convert_fusion = bf16[512,1536]{1,0:T(8,128)(2,1)S(1)} fusion(bf16[512,1536]{0,1:T(8,128)(2,1)} %bitcast.204, f32[512,1,1,1,1,1,512]{6,0,5,4,3,2,1:T(8,128)S(1)} %bitcast.189, f32[512]{0:T(512)S(1)} %copy-done.26, f32[512]{0:T(512)S(1)} %rsqrt.21), kind=kOutput, calls=%fused_computation.29 | convolution fusion | flops 806879232 | bytes 4198400 | tf_op jit(solution)/shard_map/tbd,tbe->de/dot_general | solution.py:275
  83.4 1.6 pad_maximum_fusion
  85.0 9.7 %all-to-all-done.1 = bf16[16,2,8192]{2,1,0:T(2,128)(2,1)} async-done(((bf16[16,2,8192]{2,1,0:T(2,128)(2,1)}), bf16[16,2,8192]{2,1,0:T(2,128)(2,1)}, u32[]{:S(2)}, u32[]{:S(2)}) %all-to-all-start.1) | async-done | bytes 524320 | tf_op jit(solution)/shard_map/all_to_all | solution.py:357
  94.8 2.2 %reshape.418 = bf16[512,1,512]{2,1,0:T(2,128)(2,1)S(1)} reshape(bf16[16,2,8192]{2,1,0:T(2,128)(2,1)} %all-to-all-done.1) | data formatting | bytes 1048576
  98.8 1.5 convolution_convert_fusion.5
  100.4 2.2 %fusion.74 = bf16[32,16,512]{2,1,0:T(8,128)(2,1)} fusion(pred[8,512]{1,0:T(8,128)(4,1)S(1)} %iota_compare_fusion, bf16[32,16,512]{2,1,0:T(8,128)(2,1)S(1)} %convolution_convert_fusion.5, f32[32,16,8,16]{1,3,2,0:T(8,128)S(1)} %copy-done.30, f32[32,16,8]{1,2,0:T(8,128)S(1)} %copy-done.32), kind=kOutput, calls=%fused_computation.87 | convolution fusion | flops 69599232 | bytes 1331200 | tf_op jit(solution)/shard_map/tbhc,tbhd->tcd/dot_general | solution.py:219
  102.6 1.9 %fusion.97 = f32[32,16,8]{1,2,0:T(8,128)S(1)} fusion(bf16[32,16,512]{2,1,0:T(8,128)(2,1)S(1)} %copy-done.14, bf16[32,16,512]{2,1,0:T(8,128)(2,1)S(1)} %convolution_convert_fusion.5, s32[512]{0:T(512)S(1)} %add_select_fusion), kind=kOutput, calls=%fused_computation.108 | convolution fusion | flops 25956352 | bytes 1067008 | tf_op jit(solution)/shard_map/tbd,hd->tbh/dot_general | solution.py:228
  104.7 1.3 multiply_convert_fusion.1
  106.0 1.4 fusion.77
  107.4 0.8 fusion.112
  108.3 4.2 %all-to-all-start.2 = ((bf16[8,32,512]{2,1,0:T(8,128)(2,1)}), bf16[8,32,512]{2,1,0:T(8,128)(2,1)S(1)}, u32[]{:S(2)}, u32[]{:S(2)}) async-start(bf16[8,32,512]{2,1,0:T(8,128)(2,1)} %fusion.112), calls=%async_computation.2 | async-start | bytes 524288 | tf_op jit(solution)/shard_map/all_to_all | solution.py:287
  112.5 2.0 %fusion.71 = bf16[32,16,512]{2,1,0:T(8,128)(2,1)S(1)} fusion(bf16[32,16,8,16]{1,3,2,0:T(8,128)(2,1)} %copy-done.29, pred[8,512]{1,0:T(8,128)(4,1)S(1)} %iota_compare_fusion, bf16[32,16,512]{2,1,0:T(8,128)(2,1)S(1)} %copy-done.16), kind=kOutput, calls=%fused_computation.86 | convolution fusion | flops 69468160 | bytes 1183744 | tf_op jit(solution)/shard_map/tbhc,thcd->tbd/dot_general | solution.py:238
  114.5 1.3 pad_maximum_fusion.2
  115.8 10.1 %all-to-all-done.2 = bf16[8,32,512]{2,1,0:T(8,128)(2,1)S(1)} async-done(((bf16[8,32,512]{2,1,0:T(8,128)(2,1)}), bf16[8,32,512]{2,1,0:T(8,128)(2,1)S(1)}, u32[]{:S(2)}, u32[]{:S(2)}) %all-to-all-start.2) | async-done | bytes 262176 | tf_op jit(solution)/shard_map/all_to_all | solution.py:287
  126.0 2.5 %fusion.128 = f32[512,1536,1]{1,0,2:T(8,128)S(1)} fusion(bf16[32,16,1536]{2,1,0:T(8,128)(2,1)} %pad_maximum_fusion.2, bf16[32,16,512]{2,1,0:T(8,128)(2,1)S(1)} %copy-done.3, f32[512]{0:T(512)S(1)} %copy-done.27, f32[32,16]{1,0:T(8,128)S(1)} %add_rsqrt_fusion), kind=kOutput, calls=%fused_computation.147 | convolution fusion | flops 806354944 | bytes 5246976 | tf_op jit(solution)/shard_map/tbd,tbe->de/dot_general | solution.py:275
  128.7 2.3 %collective-permute-done.1 = bf16[8,32,1536]{2,1,0:T(8,128)(2,1)S(1)} collective-permute-done((bf16[8,32,1536]{2,1,0:T(8,128)(2,1)S(1)}, bf16[8,32,1536]{2,1,0:T(8,128)(2,1)S(1)}, u32[]{:S(2)}, u32[]{:S(2)}) %collective-permute-start.1) | collective-permute-done | bytes 786464 | tf_op jit(solution)/shard_map/ppermute | solution.py:285
  131.0 1.2 fusion.40
  132.3 4.3 %all-to-all-start.3 = ((bf16[8,32,1536]{2,1,0:T(8,128)(2,1)}), bf16[8,32,1536]{2,1,0:T(8,128)(2,1)S(1)}, u32[]{:S(2)}, u32[]{:S(2)}) async-start(bf16[8,32,1536]{2,1,0:T(8,128)(2,1)} %fusion.40), calls=%async_computation.3 | async-start | bytes 1572864 | tf_op jit(solution)/shard_map/all_to_all | solution.py:287
  136.6 2.4 %fusion.84 = bf16[512,1,512]{2,0,1:T(8,128)(2,1)} fusion(f32[512,512]{1,0:T(8,128)S(1)} %bitcast.190, bf16[512,512]{0,1:T(8,128)(2,1)S(1)} %bitcast.194, bf16[512,2048]{1,0:T(8,128)(2,1)} %param.12), kind=kOutput, calls=%fused_computation.93 | convolution fusion | flops 268959744 | bytes 2621440 | tf_op jit(solution)/shard_map/tbd,de->tbe/dot_general | solution.py:265
  139.1 2.6 %fusion.95 = (f32[32,16]{1,0:T(8,128)S(1)}, f32[32,16,512]{2,1,0:T(8,128)S(1)}) fusion(bf16[32,16,512]{2,1,0:T(8,128)(2,1)S(1)} %copy-done.3, f32[512]{0:T(512)S(1)} %copy-done.27, bf16[32,16,1536]{2,1,0:T(8,128)(2,1)S(1)} %copy-done.9, bf16[512,2048]{1,0:T(8,128)(2,1)} %param.11), kind=kOutput, calls=%fused_computation.104 | convolution fusion | flops 806354432 | bytes 4722688 | tf_op jit(solution)/shard_map/tbe,de->tbd/dot_general | solution.py:269
  141.6 1.2 fusion.93
  142.8 16.1 %reduce-scatter.2.cloned.1.call-done = bf16[32,2048]{1,0:T(8,128)(2,1)} async-done(((bf16[512,2048]{1,0:T(8,128)(2,1)}), bf16[32,2048]{1,0:T(8,128)(2,1)}) %reduce-scatter.2.cloned.1.call-update) | async-done | bytes 131088 | tf_op jit(solution)/shard_map/reduce_scatter | solution.py:292
  158.9 1.6 convert_element_type.276
  (107 shorter events, 9.1 us)
Async XLA Ops:
  11.1 1.0 copy-start.25
  11.1 1.1 copy-start.24
  11.1 1.2 copy-start.28
  12.1 3.1 %copy-start.15 = (bf16[32,16,512]{2,1,0:T(8,128)(2,1)}, bf16[32,16,512]{2,1,0:T(8,128)(2,1)S(1)}, u32[]{:S(2)}) copy-start(bf16[32,16,512]{2,1,0:T(8,128)(2,1)S(1)} %get-tuple-element.56) | copy-start | bytes 1572868
  12.1 3.1 %copy-start.18 = (bf16[32,16,512]{2,1,0:T(8,128)(2,1)}, bf16[32,16,512]{2,1,0:T(8,128)(2,1)S(1)}, u32[]{:S(2)}) copy-start(bf16[32,16,512]{2,1,0:T(8,128)(2,1)S(1)} %get-tuple-element.47) | copy-start | bytes 1572868
  15.3 2.4 %copy-start.31 = (f32[32,16,8]{1,2,0:T(8,128)}, f32[32,16,8]{1,2,0:T(8,128)S(1)}, u32[]{:S(2)}) copy-start(f32[32,16,8]{1,2,0:T(8,128)S(1)} %get-tuple-element.57) | copy-start | bytes 49156
  15.3 2.4 %copy-start.2 = (bf16[32,16,512]{2,1,0:T(8,128)(2,1)S(1)}, bf16[32,16,512]{2,1,0:T(8,128)(2,1)}, u32[]{:S(2)}) copy-start(bf16[32,16,512]{2,1,0:T(8,128)(2,1)} %param.9) | copy-start | bytes 1572868
  17.6 2.8 %copy-start.13 = (bf16[32,16,512]{2,1,0:T(8,128)(2,1)}, bf16[32,16,512]{2,1,0:T(8,128)(2,1)S(1)}, u32[]{:S(2)}) copy-start(bf16[32,16,512]{2,1,0:T(8,128)(2,1)S(1)} %fusion.68) | copy-start | bytes 1572868
  17.7 10.2 %copy-start.1 = (bf16[512,1,512]{2,0,1:T(8,128)(2,1)S(1)}, bf16[512,1,512]{2,0,1:T(8,128)(2,1)}, u32[]{:S(2)}) copy-start(bf16[512,1,512]{2,0,1:T(8,128)(2,1)} %param.10) | copy-start | bytes 1572868
  20.4 21.9 %all-to-all-start = ((bf16[32,16,512]{2,0,1:T(8,128)(2,1)}), bf16[32,16,512]{2,0,1:T(8,128)(2,1)S(1)}, u32[]{:S(2)}, u32[]{:S(2)}) async-start(bf16[32,16,512]{2,0,1:T(8,128)(2,1)} %copy.95), calls=%async_computation | async-start | bytes 1048576 | tf_op jit(solution)/shard_map/all_to_all | solution.py:320
  31.4 11.8 %copy-start.26 = (f32[512]{0:T(512)S(1)}, f32[512]{0:T(512)}, u32[]{:S(2)}) copy-start(f32[512]{0:T(512)} %param.14) | copy-start | bytes 6148
  43.2 2.6 %copy-start.22 = (bf16[512,2048]{1,0:T(8,128)(2,1)S(1)}, bf16[512,2048]{1,0:T(8,128)(2,1)}, u32[]{:S(2)}) copy-start(bf16[512,2048]{1,0:T(8,128)(2,1)} %param.12) | copy-start | bytes 6291460
  47.6 7.6 %copy-start.10 = (bf16[512,512]{0,1:T(8,128)(2,1)}, bf16[512,512]{0,1:T(8,128)(2,1)S(1)}, u32[]{:S(2)}) copy-start(bf16[512,512]{0,1:T(8,128)(2,1)S(1)} %convolution_convert_fusion.10) | copy-start | bytes 1572868
  55.2 4.7 %copy-start.7 = (bf16[512,512]{0,1:T(8,128)(2,1)S(1)}, bf16[512,512]{0,1:T(8,128)(2,1)}, u32[]{:S(2)}) copy-start(bf16[512,512]{0,1:T(8,128)(2,1)} %convolution_convert_fusion.8) | copy-start | bytes 1572868
  55.2 4.7 %copy-start.21 = (bf16[512,512]{0,1:T(8,128)(2,1)S(1)}, bf16[512,512]{0,1:T(8,128)(2,1)}, u32[]{:S(2)}) copy-start(bf16[512,512]{0,1:T(8,128)(2,1)} %convolution_convert_fusion.9) | copy-start | bytes 1572868
  59.9 3.4 %copy-start = (f32[8,512,512]{1,2,0:T(8,128)S(1)}, f32[8,512,512]{1,2,0:T(8,128)}, u32[]{:S(2)}) copy-start(f32[8,512,512]{1,2,0:T(8,128)} %get-tuple-element.60) | copy-start | bytes 25165828
  63.3 2.0 %copy-start.12 = (bf16[512,512]{0,1:T(8,128)(2,1)S(1)}, bf16[512,512]{0,1:T(8,128)(2,1)}, u32[]{:S(2)}) copy-start(bf16[512,512]{0,1:T(8,128)(2,1)} %convolution_convert_fusion.11) | copy-start | bytes 1572868
  65.3 1.4 copy-start.11
  67.5 2.2 %copy-start.23 = (bf16[512,2048]{1,0:T(8,128)(2,1)S(1)}, bf16[512,2048]{1,0:T(8,128)(2,1)}, u32[]{:S(2)}) copy-start(bf16[512,2048]{1,0:T(8,128)(2,1)} %param.12) | copy-start | bytes 6291460
  67.7 3.0 %copy-start.8 = (bf16[3,8,512,64]{2,3,1,0:T(8,128)(2,1)}, bf16[3,8,512,64]{2,3,1,0:T(8,128)(2,1)S(1)}, u32[]{:S(2)}) copy-start(bf16[3,8,512,64]{2,3,1,0:T(8,128)(2,1)S(1)} %pad_maximum_fusion.1) | copy-start | bytes 4718596
  69.7 1.0 copy-start.6
  75.8 18.9 %all-to-all-start.1 = ((bf16[16,2,8192]{2,1,0:T(2,128)(2,1)}), bf16[16,2,8192]{2,1,0:T(2,128)(2,1)}, u32[]{:S(2)}, u32[]{:S(2)}) async-start(bf16[16,2,8192]{2,1,0:T(2,128)(2,1)} %reshape.417), calls=%async_computation.1 | async-start | bytes 1048576 | tf_op jit(solution)/shard_map/all_to_all | solution.py:357
  80.3 78.6 %reduce-scatter.2.cloned.1.call-start = ((), (), s32[]{:S(2)}) async-start(), calls=%async_computation.5 | async-start | bytes 2228224 | tf_op jit(solution)/shard_map/reduce_scatter | solution.py:292
  85.0 12.1 %copy-start.14 = (bf16[32,16,512]{2,1,0:T(8,128)(2,1)S(1)}, bf16[32,16,512]{2,1,0:T(8,128)(2,1)}, u32[]{:S(2)}) copy-start(bf16[32,16,512]{2,1,0:T(8,128)(2,1)} %copy-done.13) | copy-start | bytes 1572868
  97.7 2.7 %copy-start.30 = (f32[32,16,8,16]{1,3,2,0:T(8,128)S(1)}, f32[32,16,8,16]{1,3,2,0:T(8,128)}, u32[]{:S(2)}) copy-start(f32[32,16,8,16]{1,3,2,0:T(8,128)} %get-tuple-element.58) | copy-start | bytes 786436
  97.7 2.7 %copy-start.32 = (f32[32,16,8]{1,2,0:T(8,128)S(1)}, f32[32,16,8]{1,2,0:T(8,128)}, u32[]{:S(2)}) copy-start(f32[32,16,8]{1,2,0:T(8,128)} %copy-done.31) | copy-start | bytes 49156
  98.0 0.8 copy-start.4
  100.4 4.3 %copy-start.19 = (bf16[32,16,512]{2,1,0:T(8,128)(2,1)S(1)}, bf16[32,16,512]{2,1,0:T(8,128)(2,1)}, u32[]{:S(2)}) copy-start(bf16[32,16,512]{2,1,0:T(8,128)(2,1)} %copy-done.18) | copy-start | bytes 1572868
  104.6 1.4 copy-start.17
  104.6 2.8 %collective-permute-start = (bf16[8,32,512]{2,1,0:T(8,128)(2,1)S(1)}, bf16[8,32,512]{2,1,0:T(8,128)(2,1)S(1)}, u32[]{:S(2)}, u32[]{:S(2)}) collective-permute-start(bf16[8,32,512]{2,1,0:T(8,128)(2,1)S(1)} %fusion.131), channel_id=1, source_target_pairs={{0,1},{1,0},{2,3},{3,2},{4,5},{5,4},{6,7},{7,6},{8,9},{9,8},{10,11... | collective-permute-start | bytes 786440 | tf_op jit(solution)/shard_map/ppermute | solution.py:285
  106.0 1.4 copy-start.29
  107.4 5.1 %copy-start.16 = (bf16[32,16,512]{2,1,0:T(8,128)(2,1)S(1)}, bf16[32,16,512]{2,1,0:T(8,128)(2,1)}, u32[]{:S(2)}) copy-start(bf16[32,16,512]{2,1,0:T(8,128)(2,1)} %copy-done.15) | copy-start | bytes 1572868
  108.3 17.7 %all-to-all-start.2 = ((bf16[8,32,512]{2,1,0:T(8,128)(2,1)}), bf16[8,32,512]{2,1,0:T(8,128)(2,1)S(1)}, u32[]{:S(2)}, u32[]{:S(2)}) async-start(bf16[8,32,512]{2,1,0:T(8,128)(2,1)} %fusion.112), calls=%async_computation.2 | async-start | bytes 524288 | tf_op jit(solution)/shard_map/all_to_all | solution.py:287
  112.5 2.0 %copy-start.20 = (bf16[32,16,512]{2,1,0:T(8,128)(2,1)S(1)}, bf16[32,16,512]{2,1,0:T(8,128)(2,1)}, u32[]{:S(2)}) copy-start(bf16[32,16,512]{2,1,0:T(8,128)(2,1)} %fusion.74) | copy-start | bytes 1572868
  114.5 11.5 %copy-start.3 = (bf16[32,16,512]{2,1,0:T(8,128)(2,1)S(1)}, bf16[32,16,512]{2,1,0:T(8,128)(2,1)}, u32[]{:S(2)}) copy-start(bf16[32,16,512]{2,1,0:T(8,128)(2,1)} %param.9) | copy-start | bytes 1572868
  114.5 11.5 %copy-start.27 = (f32[512]{0:T(512)S(1)}, f32[512]{0:T(512)}, u32[]{:S(2)}) copy-start(f32[512]{0:T(512)} %param.13) | copy-start | bytes 6148
  128.7 2.4 %collective-permute-start.1 = (bf16[8,32,1536]{2,1,0:T(8,128)(2,1)S(1)}, bf16[8,32,1536]{2,1,0:T(8,128)(2,1)S(1)}, u32[]{:S(2)}, u32[]{:S(2)}) collective-permute-start(bf16[8,32,1536]{2,1,0:T(8,128)(2,1)S(1)} %fusion.107), channel_id=1, source_target_pairs={{0,1},{1,0},{2,3},{3,2},{4,5},{5,4},{6,7},{7,6},{8,9},{9,8},{10,11... | collective-permute-start | bytes 2359304 | tf_op jit(solution)/shard_map/ppermute | solution.py:285
  132.3 29.0 %all-to-all-start.3 = ((bf16[8,32,1536]{2,1,0:T(8,128)(2,1)}), bf16[8,32,1536]{2,1,0:T(8,128)(2,1)S(1)}, u32[]{:S(2)}, u32[]{:S(2)}) async-start(bf16[8,32,1536]{2,1,0:T(8,128)(2,1)} %fusion.40), calls=%async_computation.3 | async-start | bytes 1572864 | tf_op jit(solution)/shard_map/all_to_all | solution.py:287
  136.6 2.4 %copy-start.9 = (bf16[32,16,1536]{2,1,0:T(8,128)(2,1)S(1)}, bf16[32,16,1536]{2,1,0:T(8,128)(2,1)}, u32[]{:S(2)}) copy-start(bf16[32,16,1536]{2,1,0:T(8,128)(2,1)} %pad_maximum_fusion.2) | copy-start | bytes 4718596
  139.1 2.6 %copy-start.5 = (bf16[16,32,1,512]{3,0,1,2:T(8,128)(2,1)S(1)}, bf16[16,32,1,512]{3,0,1,2:T(8,128)(2,1)}, u32[]{:S(2)}) copy-start(bf16[16,32,1,512]{3,0,1,2:T(8,128)(2,1)} %copy-done.4) | copy-start | bytes 1572868
Sparse Core Ops, SparseCore 0:
  85.1 73.7 reduce-scatter.1

commit v11 on v8

--- a/solution.py
+++ b/solution.py
@@ -364,18 +364,18 @@
     grad_spatial_proj = spatial_backward_heads(
         spatial_proj, allowed_space, spatial_context, grad_spatial_context
     )
-    spatial_term = reduce_rows(spatial_term)
-    spatial_term, grad_spatial_proj = lax.optimization_barrier((spatial_term, grad_spatial_proj))
     grad_normed_one = project_back(grad_spatial_proj, spatial_weights[:, : 3 * model_width])
     grad_activity = (
         grad_middle_time.astype(jnp.float32)
         + norm_backward(activity, spatial_gain, inverse_one, grad_normed_one)
     ).astype(jnp.bfloat16)
-    normed_cols = normed_one
-    context_cols = spatial_context
+    normed_term = weight_term(normed_one, grad_spatial_proj)
+    spatial_term, normed_term, grad_activity = lax.optimization_barrier(
+        (reduce_rows(spatial_term), normed_term, grad_activity)
+    )
     spatial_grad = jnp.concatenate(
         [
-            reduce_rows(weight_term(normed_cols, grad_spatial_proj)),
+            reduce_rows(normed_term),
             spatial_term,
         ],
         axis=1,

time: 165 us -> 170 us (1.030)
  other arithmetic: 17.2 us -> 21 us
  waiting for transfers between devices: 48.7 us -> 51.5 us
  matrix products: 49.4 us -> 46.9 us
    all_to_all x2, waiting for transfers between devices: 15.6 us -> 18.8 us  [reduce_rows(): pieces = lax.all_to_all(pieces, 'outer', 0, 0, tiled=True)]
    convert_element_type x2, other arithmetic: 0.2 us -> 2.14 us  [reduce_rows(): given = jnp.where(first, pieces[:, 1], pieces[:, 0]).astype(jnp.bfloat16)]
    convert_element_type x2, other arithmetic: 2.11 us -> 4.04 us  [reduce_rows(): pieces = (kept + taken.astype(jnp.float32)).astype(jnp.bfloat16)]
    unnamed x66 -> x60, local copies, waits for them, and re-layouts: 8.13 us -> 8.48 us
where the time goes in v11:
time: 170 us; the launch traced here: 169 us
  waiting for transfers between devices  51.5 us (30%)
  matrix products  46.9 us (28%)
  starting transfers between devices  21.5 us (13%)
  other arithmetic  21 us (12%)
  between operations  14.5 us (9%)
  local copies, waits for them, and re-layouts  13.7 us (8%)
    all_to_all x2, waiting for transfers between devices, reduce_rows(): pieces = lax.all_to_all(pieces, 'outer', 0, 0, tiled=True)  18.8 us
    all_to_all x1, waiting for transfers between devices, per_device(): lax.all_to_all(middle, ('outer', 'core'), split_axis=1, concat_axis=0, ti...  10.9 us
    dot_general x4, matrix products, project(): jnp.einsum('tbd,de->tbe', rows, coefficient_array, preferred_element_type...  10.3 us
    reduce_scatter x1, waiting for transfers between devices, scatter_rows(): lax.psum_scatter(partial.astype(jnp.bfloat16), ('outer', 'core'), scatter...  9.96 us
    all_to_all x2, starting transfers between devices, reduce_rows(): pieces = lax.all_to_all(pieces, 'outer', 0, 0, tiled=True)  9.53 us
    all_to_all x1, waiting for transfers between devices, per_device(): lax.all_to_all(grad_middle, ('outer', 'core'), split_axis=0, concat_axis=...  9.5 us
    unnamed x60, local copies, waits for them, and re-layouts  8.48 us
    dot_general x4, matrix products, weight_term(): jnp.einsum('tbd,tbe->de', left, right, preferred_element_type=jnp.float32)  7.6 us
  transfers between devices with their start and end apart: 7, of which 6 were waited for; matrix products, arithmetic and copies ran while one was open for 21% of the time, Pallas kernels for 0%

profile of v11, /device:TPU:0, one launch (start us, length us, event | category | flops | bytes accessed | tf_op | source)
XLA Modules:
  0.0 169.1 jit_solution(7474178389932998084)
XLA Ops:
  7.2 1.2 fusion.95
  8.5 2.6 %convolution_convert_fusion.2 = bf16[32,16,1536]{2,1,0:T(8,128)(2,1)S(1)} fusion(bf16[512,2048]{1,0:T(8,128)(2,1)} %param.11, bf16[32,16,512]{2,1,0:T(8,128)(2,1)} %param.9, f32[512]{0:T(512)} %param.13, f32[32,16]{1,0:T(8,128)S(1)} %add_rsqrt_fusion), kind=kOutput, calls=%fused_computation.32 | convolution fusion | flops 807141376 | bytes 3674112 | tf_op jit(solution)/shard_map/tbd,de->tbe/dot_general | solution.py:263
  11.1 1.0 fusion.151
  12.6 2.6 %fusion.152 = (f32[32,16,8]{1,2,0:T(8,128)S(1)}, f32[32,16,8,16]{1,3,2,0:T(8,128)}) fusion(pred[32,16,16]{1,2,0:T(8,128)(4,1)S(1)} %and_or_fusion, pred[8,512]{1,0:T(8,128)(4,1)S(1)} %iota_compare_fusion, bf16[32,16,512]{2,1,0:T(8,128)(2,1)S(1)} %get-tuple-element.46, bf16[32,16,1536]{2,1,0:T(8,128)(2,1)S(1)} %convolution_convert_fusion.2), kind=kOutput, calls=%fused_computation.186 | convolution fusion | flops 69468176 | bytes 1396736 | tf_op jit(solution)/shard_map/sub | solution.py:197
  15.3 2.4 %fusion.69 = bf16[32,16,512]{2,1,0:T(8,128)(2,1)S(1)} fusion(pred[8,512]{1,0:T(8,128)(4,1)S(1)} %iota_compare_fusion, bf16[32,16,512]{2,1,0:T(8,128)(2,1)S(1)} %get-tuple-element.45, f32[32,16,8,16]{1,3,2,0:T(8,128)} %get-tuple-element.48, f32[32,16,8]{1,2,0:T(8,128)S(1)} %get-tuple-element.47), kind=kOutput, calls=%fused_computation.85 | convolution fusion | flops 69599232 | bytes 1331200 | tf_op jit(solution)/shard_map/tbhc,thcd->tbd/dot_general | solution.py:206
  17.7 1.7 fusion.81
  19.4 1.1 copy.100
  20.4 7.4 %all-to-all-start = ((bf16[32,16,512]{2,0,1:T(8,128)(2,1)}), bf16[32,16,512]{2,0,1:T(8,128)(2,1)S(1)}, u32[]{:S(2)}, u32[]{:S(2)}) async-start(bf16[32,16,512]{2,0,1:T(8,128)(2,1)} %copy.100), calls=%async_computation | async-start | bytes 1048576 | tf_op jit(solution)/shard_map/all_to_all | solution.py:318
  27.9 1.0 copy.106
  29.1 2.3 %convolution_convert_fusion.9 = bf16[512,512]{0,1:T(8,128)(2,1)} fusion(bf16[512,1,512]{2,0,1:T(8,128)(2,1)S(1)} %copy-done.3, bf16[512,2048]{1,0:T(8,128)(2,1)} %param.12), kind=kOutput, calls=%fused_computation.84 | convolution fusion | flops 268697600 | bytes 1572864 | tf_op jit(solution)/shard_map/tbe,de->tbd/dot_general | solution.py:267
  31.4 10.9 %all-to-all-done = bf16[32,16,512]{2,0,1:T(8,128)(2,1)S(1)} async-done(((bf16[32,16,512]{2,0,1:T(8,128)(2,1)}), bf16[32,16,512]{2,0,1:T(8,128)(2,1)S(1)}, u32[]{:S(2)}, u32[]{:S(2)}) %all-to-all-start) | async-done | bytes 524320 | tf_op jit(solution)/shard_map/all_to_all | solution.py:318
  43.8 3.7 %convolution_convert_fusion.1 = bf16[512,1536]{1,0:T(8,128)(2,1)} fusion(bf16[512,2048]{1,0:T(8,128)(2,1)} %param.12, f32[512,512]{0,1:T(8,128)S(1)} %copy.103, f32[512]{0:T(512)S(1)} %copy-done.21, f32[512]{0:T(512)S(1)} %rsqrt.21), kind=kOutput, calls=%fused_computation.31 | convolution fusion | flops 806879232 | bytes 4198400 | tf_op jit(solution)/shard_map/tbd,de->tbe/dot_general | solution.py:263
  47.4 1.7 %copy.104 = bf16[512,1536]{0,1:T(8,128)(2,1)S(1)} copy(bf16[512,1536]{1,0:T(8,128)(2,1)} %convolution_convert_fusion.1) | data formatting | bytes 3145728 | tf_op jit(solution)/shard_map/convert_element_type | solution.py:320
  49.1 5.4 %fusion.153 = (f32[8,512]{1,0:T(8,128)S(1)}, f32[8,512,512]{1,2,0:T(8,128)}) fusion(pred[512,512]{0,1:T(8,128)(4,1)S(1)} %broadcast_compare_fusion, bf16[512,3,8,64]{0,3,2,1:T(8,128)(2,1)S(1)} %bitcast.208), kind=kOutput, calls=%fused_computation.187 | convolution fusion | flops 276824576 | bytes 9715712 | tf_op jit(solution)/shard_map/while/body/eval_jaxpr/sub | solution.py:39
  54.6 4.7 %fusion.24 = bf16[8,512,512]{1,2,0:T(8,128)(2,1)S(1)} fusion(f32[8,512,512]{1,2,0:T(8,128)} %get-tuple-element.50, f32[8,512]{1,0:T(8,128)S(1)} %get-tuple-element.49), kind=kLoop, calls=%fused_computation.28 | loop fusion | flops 4194304 | bytes 12599296 | tf_op jit(solution)/shard_map/while/body/eval_jaxpr/convert_element_type | solution.py:48
  60.0 1.4 fusion.87
  61.4 1.2 copy-done
  62.6 1.8 %multiply_convert_fusion = bf16[8,512,512]{1,2,0:T(8,128)(2,1)S(1)} fusion(f32[8,512]{1,0:T(8,128)S(1)} %get-tuple-element.51, f32[8,512,512]{1,2,0:T(8,128)S(1)} %copy-done, f32[8,512]{1,0:T(8,128)S(1)} %get-tuple-element.49, bf16[8,512,64]{1,2,0:T(8,128)(2,1)S(1)} %bitcast.222, bf16[512,3,8,64]{0,3,2,1:T(8,128)(2,1)S(1)} %bitcast.210), kind=kOutput, calls=%fused_computation.2 | convolution fusion | flops 278921216 | bytes 13664256 | tf_op jit(solution)/shard_map/while/body/eval_jaxpr/...uo,...ao->...ua/dot_general | solution.py:73
  64.4 1.4 fusion.86
  66.8 1.2 copy-done.2
  68.1 1.0 copy-done.17
  69.1 1.0 multiply_reduce_fusion
  71.0 1.1 reduce.6
  72.3 1.2 reshape.379
  73.5 4.1 %all-to-all-start.1 = ((bf16[16,2,8192]{2,1,0:T(2,128)(2,1)}), bf16[16,2,8192]{2,1,0:T(2,128)(2,1)S(1)}, u32[]{:S(2)}, u32[]{:S(2)}) async-start(bf16[16,2,8192]{2,1,0:T(2,128)(2,1)} %reshape.379), calls=%async_computation.1 | async-start | bytes 1048576 | tf_op jit(solution)/shard_map/all_to_all | solution.py:350
  78.3 2.6 %convolution_convert_fusion = bf16[512,1536]{1,0:T(8,128)(2,1)S(1)} fusion(bf16[512,1536]{0,1:T(8,128)(2,1)} %bitcast.224, f32[512,1,1,1,1,1,512]{6,0,5,4,3,2,1:T(8,128)S(1)} %bitcast.204, f32[512]{0:T(512)S(1)} %copy-done.21, f32[512]{0:T(512)S(1)} %rsqrt.21), kind=kOutput, calls=%fused_computation.30 | convolution fusion | flops 806879232 | bytes 4198400 | tf_op jit(solution)/shard_map/tbd,tbe->de/dot_general | solution.py:273
  80.9 1.6 pad_maximum_fusion
  82.5 9.5 %all-to-all-done.1 = bf16[16,2,8192]{2,1,0:T(2,128)(2,1)S(1)} async-done(((bf16[16,2,8192]{2,1,0:T(2,128)(2,1)}), bf16[16,2,8192]{2,1,0:T(2,128)(2,1)S(1)}, u32[]{:S(2)}, u32[]{:S(2)}) %all-to-all-start.1) | async-done | bytes 524320 | tf_op jit(solution)/shard_map/all_to_all | solution.py:350
  92.7 1.8 %convolution_bitcast_fusion.1 = f32[512,512]{1,0:T(8,128)S(1)} fusion(bf16[32,16,512]{2,1,0:T(8,128)(2,1)} %copy-done.10, bf16[16,32,1,512]{3,1,0,2:T(8,128)(2,1)S(1)} %bitcast.217), kind=kOutput, calls=%fused_computation.70 | convolution fusion | flops 268435456 | bytes 2097152 | tf_op jit(solution)/shard_map/tbd,tbe->de/dot_general | solution.py:273
  95.3 0.8 copy-done.24
  96.2 1.4 fusion.75
  97.6 2.0 %fusion.98 = f32[32,16,8]{1,2,0:T(8,128)S(1)} fusion(bf16[32,16,512]{2,1,0:T(8,128)(2,1)S(1)} %copy-done.11, bf16[32,16,512]{2,1,0:T(8,128)(2,1)S(1)} %convolution_convert_fusion.6, s32[512]{0:T(512)S(1)} %add_select_fusion), kind=kOutput, calls=%fused_computation.108 | convolution fusion | flops 25956352 | bytes 1067008 | tf_op jit(solution)/shard_map/tbd,hd->tbh/dot_general | solution.py:226
  99.7 1.2 multiply_convert_fusion.1
  102.0 1.4 fusion.78
  103.4 2.8 %convolution_bitcast_fusion = f32[512,1536]{1,0:T(8,128)} fusion(bf16[32,16,512]{2,1,0:T(8,128)(2,1)S(1)} %fusion.75, bf16[32,16,512]{2,1,0:T(8,128)(2,1)S(1)} %fusion.78, bf16[32,16,512]{2,1,0:T(8,128)(2,1)S(1)} %fusion.72, bf16[32,16,512]{2,1,0:T(8,128)(2,1)S(1)} %copy-done.6, f32[512]{0:T(512)S(1)} %copy-done.22, f32[32,16]{1,0:T(8,128)S(1)} %add_rsqrt_fusion), kind=kOutput, calls=%fused_computation.29 | convolution fusion | flops 811073536 | bytes 5246976 | tf_op jit(solution)/shard_map/tbd,tbe->de/dot_general | solution.py:273
  106.2 2.0 %fusion.96 = (f32[32,16]{1,0:T(8,128)S(1)}, f32[32,16,512]{2,1,0:T(8,128)}) fusion(bf16[32,16,512]{2,1,0:T(8,128)(2,1)S(1)} %copy-done.6, f32[512]{0:T(512)S(1)} %copy-done.22, bf16[512,2048]{1,0:T(8,128)(2,1)S(1)} %copy-done.20, bf16[32,16,512]{2,1,0:T(8,128)(2,1)S(1)} %fusion.75, bf16[32,16,512]{2,1,0:T(8,128)(2,1)S(1)} %fusion.78, ...), kind=kOutput, calls=%fused_computation.104 | convolution fusion | flops 811073024 | bytes 4722688 | tf_op jit(solution)/shard_map/tbe,de->tbd/dot_general | solution.py:267
  108.2 0.8 fusion.113
  109.1 4.3 %all-to-all-start.2 = ((bf16[8,32,512]{2,1,0:T(8,128)(2,1)}), bf16[8,32,512]{2,1,0:T(8,128)(2,1)S(1)}, u32[]{:S(2)}, u32[]{:S(2)}) async-start(bf16[8,32,512]{2,1,0:T(8,128)(2,1)} %fusion.113), calls=%async_computation.2 | async-start | bytes 524288 | tf_op jit(solution)/shard_map/all_to_all | solution.py:285
  113.3 2.4 %fusion.94 = bf16[32,16,512]{2,1,0:T(8,128)(2,1)} fusion(bf16[32,16,512]{2,1,0:T(8,128)(2,1)S(1)} %copy-done.6, f32[32,16,512]{2,1,0:T(8,128)} %get-tuple-element.56, bf16[32,16,512]{2,1,0:T(8,128)(2,1)S(1)} %bitcast.220, f32[32,16]{1,0:T(8,128)S(1)} %broadcast_multiply_fusion, f32[32,16]{1,0:T(8,128)S(1)} %add_rsqrt_fusion), kind=kLoop, calls=%fused_computation.102 | loop fusion | flops 2621440 | bytes 2625536 | tf_op jit(solution)/shard_map/convert_element_type | solution.py:371
  115.8 9.6 %all-to-all-done.2 = bf16[8,32,512]{2,1,0:T(8,128)(2,1)S(1)} async-done(((bf16[8,32,512]{2,1,0:T(8,128)(2,1)}), bf16[8,32,512]{2,1,0:T(8,128)(2,1)S(1)}, u32[]{:S(2)}, u32[]{:S(2)}) %all-to-all-start.2) | async-done | bytes 262176 | tf_op jit(solution)/shard_map/all_to_all | solution.py:285
  125.4 2.1 %fusion.108 = bf16[8,32,1536]{2,1,0:T(8,128)(2,1)S(1)} fusion(f32[8,2,32,1536]{3,2,1,0:T(8,128)} %bitcast.206, pred[]{:T(512)S(6)} %eq.78), kind=kLoop, calls=%fused_computation.122 | loop fusion | flops 393216 | bytes 2359297 | tf_op jit(solution)/shard_map/convert_element_type | solution.py:282
  127.5 2.3 %collective-permute-done.1 = bf16[8,32,1536]{2,1,0:T(8,128)(2,1)S(1)} collective-permute-done((bf16[8,32,1536]{2,1,0:T(8,128)(2,1)S(1)}, bf16[8,32,1536]{2,1,0:T(8,128)(2,1)S(1)}, u32[]{:S(2)}, u32[]{:S(2)}) %collective-permute-start.1) | collective-permute-done | bytes 786464 | tf_op jit(solution)/shard_map/ppermute | solution.py:283
  129.8 3.2 %fusion.40 = bf16[8,32,1536]{2,1,0:T(8,128)(2,1)} fusion(bf16[8,32,1536]{2,1,0:T(8,128)(2,1)S(1)} %collective-permute-done.1, f32[8,2,32,1536]{3,2,1,0:T(8,128)} %bitcast.207, pred[]{:T(512)S(6)} %eq.78), kind=kLoop, calls=%fused_computation.59 | loop fusion | flops 1572864 | bytes 4718593 | tf_op jit(solution)/shard_map/convert_element_type | solution.py:284
  133.0 5.3 %all-to-all-start.3 = ((bf16[8,32,1536]{2,1,0:T(8,128)(2,1)}), bf16[8,32,1536]{2,1,0:T(8,128)(2,1)S(1)}, u32[]{:S(2)}, u32[]{:S(2)}) async-start(bf16[8,32,1536]{2,1,0:T(8,128)(2,1)} %fusion.40), calls=%async_computation.3 | async-start | bytes 1572864 | tf_op jit(solution)/shard_map/all_to_all | solution.py:285
  138.3 2.3 %fusion.85 = bf16[512,1,512]{2,0,1:T(8,128)(2,1)} fusion(f32[512,512]{1,0:T(8,128)S(1)} %bitcast.205, bf16[512,512]{0,1:T(8,128)(2,1)S(1)} %bitcast.214, bf16[512,2048]{1,0:T(8,128)(2,1)} %param.12), kind=kOutput, calls=%fused_computation.93 | convolution fusion | flops 268959744 | bytes 2621440 | tf_op jit(solution)/shard_map/tbd,de->tbe/dot_general | solution.py:263
  140.6 10.0 %reduce-scatter.2.cloned.1.call-done = bf16[32,2048]{1,0:T(8,128)(2,1)} async-done(((bf16[512,2048]{1,0:T(8,128)(2,1)}), bf16[32,2048]{1,0:T(8,128)(2,1)}) %reduce-scatter.2.cloned.1.call-update) | async-done | bytes 131088 | tf_op jit(solution)/shard_map/reduce_scatter | solution.py:290
  150.5 1.6 convert_element_type.262
  152.2 9.2 %all-to-all-done.3 = bf16[8,32,1536]{2,1,0:T(8,128)(2,1)S(1)} async-done(((bf16[8,32,1536]{2,1,0:T(8,128)(2,1)}), bf16[8,32,1536]{2,1,0:T(8,128)(2,1)S(1)}, u32[]{:S(2)}, u32[]{:S(2)}) %all-to-all-start.3) | async-done | bytes 786464 | tf_op jit(solution)/shard_map/all_to_all | solution.py:285
  (92 shorter events, 9.4 us)
Async XLA Ops:
  11.1 1.0 copy-start.19
  11.1 1.1 copy-start.18
  11.1 1.2 copy-start.23
  12.1 3.1 %copy-start.13 = (bf16[32,16,512]{2,1,0:T(8,128)(2,1)}, bf16[32,16,512]{2,1,0:T(8,128)(2,1)S(1)}, u32[]{:S(2)}) copy-start(bf16[32,16,512]{2,1,0:T(8,128)(2,1)S(1)} %get-tuple-element.46) | copy-start | bytes 1572868
  12.1 3.1 %copy-start.15 = (bf16[32,16,512]{2,1,0:T(8,128)(2,1)}, bf16[32,16,512]{2,1,0:T(8,128)(2,1)S(1)}, u32[]{:S(2)}) copy-start(bf16[32,16,512]{2,1,0:T(8,128)(2,1)S(1)} %get-tuple-element.45) | copy-start | bytes 1572868
  15.2 2.4 %copy-start.25 = (f32[32,16,8]{1,2,0:T(8,128)}, f32[32,16,8]{1,2,0:T(8,128)S(1)}, u32[]{:S(2)}) copy-start(f32[32,16,8]{1,2,0:T(8,128)S(1)} %get-tuple-element.47) | copy-start | bytes 49156
  15.2 2.4 %copy-start.5 = (bf16[32,16,512]{2,1,0:T(8,128)(2,1)S(1)}, bf16[32,16,512]{2,1,0:T(8,128)(2,1)}, u32[]{:S(2)}) copy-start(bf16[32,16,512]{2,1,0:T(8,128)(2,1)} %param.9) | copy-start | bytes 1572868
  17.6 1.7 %copy-start.10 = (bf16[32,16,512]{2,1,0:T(8,128)(2,1)}, bf16[32,16,512]{2,1,0:T(8,128)(2,1)S(1)}, u32[]{:S(2)}) copy-start(bf16[32,16,512]{2,1,0:T(8,128)(2,1)S(1)} %fusion.69) | copy-start | bytes 1572868
  17.6 10.2 %copy-start.3 = (bf16[512,1,512]{2,0,1:T(8,128)(2,1)S(1)}, bf16[512,1,512]{2,0,1:T(8,128)(2,1)}, u32[]{:S(2)}) copy-start(bf16[512,1,512]{2,0,1:T(8,128)(2,1)} %param.10) | copy-start | bytes 1572868
  20.4 21.9 %all-to-all-start = ((bf16[32,16,512]{2,0,1:T(8,128)(2,1)}), bf16[32,16,512]{2,0,1:T(8,128)(2,1)S(1)}, u32[]{:S(2)}, u32[]{:S(2)}) async-start(bf16[32,16,512]{2,0,1:T(8,128)(2,1)} %copy.100), calls=%async_computation | async-start | bytes 1048576 | tf_op jit(solution)/shard_map/all_to_all | solution.py:318
  31.4 12.3 %copy-start.21 = (f32[512]{0:T(512)S(1)}, f32[512]{0:T(512)}, u32[]{:S(2)}) copy-start(f32[512]{0:T(512)} %param.14) | copy-start | bytes 6148
  42.8 1.0 copy-start.1
  54.6 4.7 %copy-start.8 = (bf16[512,512]{0,1:T(8,128)(2,1)S(1)}, bf16[512,512]{0,1:T(8,128)(2,1)}, u32[]{:S(2)}) copy-start(bf16[512,512]{0,1:T(8,128)(2,1)} %convolution_convert_fusion.9) | copy-start | bytes 1572868
  59.2 3.4 %copy-start = (f32[8,512,512]{1,2,0:T(8,128)S(1)}, f32[8,512,512]{1,2,0:T(8,128)}, u32[]{:S(2)}) copy-start(f32[8,512,512]{1,2,0:T(8,128)} %get-tuple-element.50) | copy-start | bytes 25165828
  66.6 1.5 copy-start.2
  66.6 2.5 %copy-start.17 = (bf16[512,2048]{1,0:T(8,128)(2,1)S(1)}, bf16[512,2048]{1,0:T(8,128)(2,1)}, u32[]{:S(2)}) copy-start(bf16[512,2048]{1,0:T(8,128)(2,1)} %param.12) | copy-start | bytes 6291460
  66.8 3.3 %copy-start.9 = (bf16[3,8,512,64]{2,3,1,0:T(8,128)(2,1)}, bf16[3,8,512,64]{2,3,1,0:T(8,128)(2,1)S(1)}, u32[]{:S(2)}) copy-start(bf16[3,8,512,64]{2,3,1,0:T(8,128)(2,1)S(1)} %pad_maximum_fusion.1) | copy-start | bytes 4718596
  69.1 1.0 copy-start.7
  71.0 6.9 %copy-start.4 = (bf16[512,1,512]{2,0,1:T(8,128)(2,1)S(1)}, bf16[512,1,512]{2,0,1:T(8,128)(2,1)}, u32[]{:S(2)}) copy-start(bf16[512,1,512]{2,0,1:T(8,128)(2,1)} %param.10) | copy-start | bytes 1572868
  73.5 18.6 %all-to-all-start.1 = ((bf16[16,2,8192]{2,1,0:T(2,128)(2,1)}), bf16[16,2,8192]{2,1,0:T(2,128)(2,1)S(1)}, u32[]{:S(2)}, u32[]{:S(2)}) async-start(bf16[16,2,8192]{2,1,0:T(2,128)(2,1)} %reshape.379), calls=%async_computation.1 | async-start | bytes 1048576 | tf_op jit(solution)/shard_map/all_to_all | solution.py:350
  77.6 73.0 %reduce-scatter.2.cloned.1.call-start = ((), (), s32[]{:S(2)}) async-start(), calls=%async_computation.5 | async-start | bytes 2228224 | tf_op jit(solution)/shard_map/reduce_scatter | solution.py:290
  92.7 2.1 %copy-start.20 = (bf16[512,2048]{1,0:T(8,128)(2,1)S(1)}, bf16[512,2048]{1,0:T(8,128)(2,1)}, u32[]{:S(2)}) copy-start(bf16[512,2048]{1,0:T(8,128)(2,1)} %param.11) | copy-start | bytes 6291460
  94.5 1.7 copy-start.24
  94.5 1.7 copy-start.26
  96.2 1.4 copy-start.11
  96.2 3.5 %copy-start.16 = (bf16[32,16,512]{2,1,0:T(8,128)(2,1)S(1)}, bf16[32,16,512]{2,1,0:T(8,128)(2,1)}, u32[]{:S(2)}) copy-start(bf16[32,16,512]{2,1,0:T(8,128)(2,1)} %copy-done.15) | copy-start | bytes 1572868
  99.6 1.3 copy-start.14
  99.6 8.6 %collective-permute-start = (bf16[8,32,512]{2,1,0:T(8,128)(2,1)S(1)}, bf16[8,32,512]{2,1,0:T(8,128)(2,1)S(1)}, u32[]{:S(2)}, u32[]{:S(2)}) collective-permute-start(bf16[8,32,512]{2,1,0:T(8,128)(2,1)S(1)} %fusion.131), channel_id=1, source_target_pairs={{0,1},{1,0},{2,3},{3,2},{4,5},{5,4},{6,7},{7,6},{8,9},{9,8},{10,11... | collective-permute-start | bytes 786440 | tf_op jit(solution)/shard_map/ppermute | solution.py:283
  101.0 1.1 copy-start.12
  102.0 1.4 copy-start.6
  102.0 1.4 copy-start.22
  109.1 16.3 %all-to-all-start.2 = ((bf16[8,32,512]{2,1,0:T(8,128)(2,1)}), bf16[8,32,512]{2,1,0:T(8,128)(2,1)S(1)}, u32[]{:S(2)}, u32[]{:S(2)}) async-start(bf16[8,32,512]{2,1,0:T(8,128)(2,1)} %fusion.113), calls=%async_computation.2 | async-start | bytes 524288 | tf_op jit(solution)/shard_map/all_to_all | solution.py:285
  127.5 2.4 %collective-permute-start.1 = (bf16[8,32,1536]{2,1,0:T(8,128)(2,1)S(1)}, bf16[8,32,1536]{2,1,0:T(8,128)(2,1)S(1)}, u32[]{:S(2)}, u32[]{:S(2)}) collective-permute-start(bf16[8,32,1536]{2,1,0:T(8,128)(2,1)S(1)} %fusion.108), channel_id=1, source_target_pairs={{0,1},{1,0},{2,3},{3,2},{4,5},{5,4},{6,7},{7,6},{8,9},{9,8},{10,11... | collective-permute-start | bytes 2359304 | tf_op jit(solution)/shard_map/ppermute | solution.py:283
  133.0 28.4 %all-to-all-start.3 = ((bf16[8,32,1536]{2,1,0:T(8,128)(2,1)}), bf16[8,32,1536]{2,1,0:T(8,128)(2,1)S(1)}, u32[]{:S(2)}, u32[]{:S(2)}) async-start(bf16[8,32,1536]{2,1,0:T(8,128)(2,1)} %fusion.40), calls=%async_computation.3 | async-start | bytes 1572864 | tf_op jit(solution)/shard_map/all_to_all | solution.py:285
Sparse Core Ops, SparseCore 0:
  82.7 67.8 reduce-scatter.1

commit v12 on v8

--- a/solution.py
+++ b/solution.py
@@ -59,6 +59,7 @@
     sharpness_divisor,
     combined_output,
     blended_output_derivative,
+    paired_inner_sums=None,
 ):
     coefficient_array = normalized_affinity(
         asking_vectors, lookup_array, admissible_pairs, sharpness_divisor
@@ -76,11 +77,12 @@
         payload_array,
         preferred_element_type=jnp.float32,
     )
-    paired_inner_sums = jnp.sum(
-        blended_output_derivative.astype(jnp.float32) * combined_output.astype(jnp.float32),
-        axis=-1,
-        keepdims=True,
-    )
+    if paired_inner_sums is None:
+        paired_inner_sums = jnp.sum(
+            blended_output_derivative.astype(jnp.float32) * combined_output.astype(jnp.float32),
+            axis=-1,
+            keepdims=True,
+        )
     affinity_derivative = (
         coefficient_array * (coefficient_derivative - paired_inner_sums) * sharpness_divisor
     ).astype(jnp.bfloat16)
@@ -118,16 +120,23 @@
     asking_vectors, lookup_array, payload_array = temporal_split(projected)
     sharpness_divisor = float(asking_vectors.shape[-1]) ** (-0.5)
     bins = projected.shape[0]
-    subspace_outputs = combined_output.reshape(bins, HEADS, -1).transpose(1, 0, 2)
     subspace_derivative = blended_output_derivative.reshape(bins, HEADS, -1).transpose(1, 0, 2)
+    inner = jnp.einsum(
+        "td,hd->ht",
+        blended_output_derivative.astype(jnp.float32) * combined_output.astype(jnp.float32),
+        head_mask(combined_output.shape[-1]).astype(jnp.float32),
+        precision=lax.Precision.HIGHEST,
+        preferred_element_type=jnp.float32,
+    )[..., None]
     derivative_collection = compute_affinity_derivatives(
         asking_vectors,
         lookup_array,
         payload_array,
         admissible_pairs[None],
         sharpness_divisor,
-        subspace_outputs,
+        None,
         subspace_derivative,
+        inner,
     )
     return jnp.stack(derivative_collection, axis=0).transpose(2, 0, 1, 3).reshape(bins, -1)
 

time: 165 us -> 165 us (level)
    unnamed x66 -> x64, local copies, waits for them, and re-layouts: 8.13 us -> 6.73 us
where the time goes in v12:
time: 165 us; the launch traced here: 164 us
  matrix products  51 us (31%)
  waiting for transfers between devices  48.8 us (30%)
  starting transfers between devices  20.7 us (13%)
  other arithmetic  17.2 us (10%)
  between operations  14.6 us (9%)
  local copies, waits for them, and re-layouts  12 us (7%)
    all_to_all x2, waiting for transfers between devices, reduce_rows(): pieces = lax.all_to_all(pieces, 'outer', 0, 0, tiled=True)  15.7 us
    all_to_all x1, waiting for transfers between devices, per_device(): lax.all_to_all(middle, ('outer', 'core'), split_axis=1, concat_axis=0, ti...  10.9 us
    reduce_scatter x1, waiting for transfers between devices, scatter_rows(): lax.psum_scatter(partial.astype(jnp.bfloat16), ('outer', 'core'), scatter...  10.4 us
    dot_general x4, matrix products, project(): jnp.einsum('tbd,de->tbe', rows, coefficient_array, preferred_element_type...  10.4 us
    all_to_all x1, waiting for transfers between devices, per_device(): lax.all_to_all(grad_middle, ('outer', 'core'), split_axis=0, concat_axis=...  9.51 us
    all_to_all x2, starting transfers between devices, reduce_rows(): pieces = lax.all_to_all(pieces, 'outer', 0, 0, tiled=True)  8.81 us
    dot_general x4, matrix products, project_back(): jnp.einsum('tbe,de->tbd', derivative_collection, coefficient_array, prefe...  7.52 us
    all_to_all x1, starting transfers between devices, per_device(): lax.all_to_all(middle, ('outer', 'core'), split_axis=1, concat_axis=0, ti...  7.4 us
  transfers between devices with their start and end apart: 7, of which 6 were waited for; matrix products, arithmetic and copies ran while one was open for 21% of the time, Pallas kernels for 0%

profile of v12, /device:TPU:0, one launch (start us, length us, event | category | flops | bytes accessed | tf_op | source)
XLA Modules:
  0.0 164.2 jit_solution(14045394125671312998)
XLA Ops:
  7.2 1.2 fusion.95
  8.5 2.6 %convolution_convert_fusion.2 = bf16[32,16,1536]{2,1,0:T(8,128)(2,1)S(1)} fusion(bf16[512,2048]{1,0:T(8,128)(2,1)} %param.11, bf16[32,16,512]{2,1,0:T(8,128)(2,1)} %param.9, f32[512]{0:T(512)} %param.13, f32[32,16]{1,0:T(8,128)S(1)} %add_rsqrt_fusion), kind=kOutput, calls=%fused_computation.31 | convolution fusion | flops 807141376 | bytes 3674112 | tf_op jit(solution)/shard_map/tbd,de->tbe/dot_general | solution.py:272
  11.1 1.0 fusion.156
  12.6 2.6 %fusion.157 = (f32[32,16,8]{1,2,0:T(8,128)S(1)}, f32[32,16,8,16]{1,3,2,0:T(8,128)}) fusion(pred[32,16,16]{1,2,0:T(8,128)(4,1)S(1)} %and_or_fusion, pred[8,512]{1,0:T(8,128)(4,1)S(1)} %iota_compare_fusion, bf16[32,16,512]{2,1,0:T(8,128)(2,1)S(1)} %get-tuple-element.44, bf16[32,16,1536]{2,1,0:T(8,128)(2,1)S(1)} %convolution_convert_fusion.2), kind=kOutput, calls=%fused_computation.189 | convolution fusion | flops 69468176 | bytes 1396736 | tf_op jit(solution)/shard_map/sub | solution.py:206
  15.3 2.4 %fusion.69 = bf16[32,16,512]{2,1,0:T(8,128)(2,1)S(1)} fusion(pred[8,512]{1,0:T(8,128)(4,1)S(1)} %iota_compare_fusion, bf16[32,16,512]{2,1,0:T(8,128)(2,1)S(1)} %get-tuple-element.43, f32[32,16,8,16]{1,3,2,0:T(8,128)} %get-tuple-element.46, f32[32,16,8]{1,2,0:T(8,128)S(1)} %get-tuple-element.45), kind=kOutput, calls=%fused_computation.84 | convolution fusion | flops 69599232 | bytes 1331200 | tf_op jit(solution)/shard_map/tbhc,thcd->tbd/dot_general | solution.py:215
  17.7 1.7 %fusion.81 = bf16[32,16,512]{2,1,0:T(8,128)(2,1)S(1)} fusion(bf16[32,16,512]{2,1,0:T(8,128)(2,1)S(1)} %fusion.69, bf16[32,16,512]{2,1,0:T(8,128)(2,1)S(1)} %copy-done.6, bf16[512,2048]{1,0:T(8,128)(2,1)} %param.11), kind=kOutput, calls=%fused_computation.88 | convolution fusion | flops 269221888 | bytes 2097152 | tf_op jit(solution)/shard_map/tbd,de->tbe/dot_general | solution.py:272
  19.4 1.1 copy.100
  20.5 7.4 %all-to-all-start = ((bf16[32,16,512]{2,0,1:T(8,128)(2,1)}), bf16[32,16,512]{2,0,1:T(8,128)(2,1)S(1)}, u32[]{:S(2)}, u32[]{:S(2)}) async-start(bf16[32,16,512]{2,0,1:T(8,128)(2,1)} %copy.100), calls=%async_computation | async-start | bytes 1048576 | tf_op jit(solution)/shard_map/all_to_all | solution.py:327
  27.9 1.0 copy.106
  29.1 2.3 %convolution_convert_fusion.9 = bf16[512,512]{0,1:T(8,128)(2,1)} fusion(bf16[512,1,512]{2,0,1:T(8,128)(2,1)S(1)} %copy-done.3, bf16[512,2048]{1,0:T(8,128)(2,1)} %param.12), kind=kOutput, calls=%fused_computation.83 | convolution fusion | flops 268697600 | bytes 1572864 | tf_op jit(solution)/shard_map/tbe,de->tbd/dot_general | solution.py:276
  31.4 10.9 %all-to-all-done = bf16[32,16,512]{2,0,1:T(8,128)(2,1)S(1)} async-done(((bf16[32,16,512]{2,0,1:T(8,128)(2,1)}), bf16[32,16,512]{2,0,1:T(8,128)(2,1)S(1)}, u32[]{:S(2)}, u32[]{:S(2)}) %all-to-all-start) | async-done | bytes 524320 | tf_op jit(solution)/shard_map/all_to_all | solution.py:327
  43.8 3.7 %convolution_convert_fusion.1 = bf16[512,1536]{1,0:T(8,128)(2,1)} fusion(bf16[512,2048]{1,0:T(8,128)(2,1)} %param.12, f32[512,512]{0,1:T(8,128)S(1)} %copy.103, f32[512]{0:T(512)S(1)} %copy-done.22, f32[512]{0:T(512)S(1)} %rsqrt.21), kind=kOutput, calls=%fused_computation.30 | convolution fusion | flops 806879232 | bytes 4198400 | tf_op jit(solution)/shard_map/tbd,de->tbe/dot_general | solution.py:272
  47.4 1.7 %copy.104 = bf16[512,1536]{0,1:T(8,128)(2,1)S(1)} copy(bf16[512,1536]{1,0:T(8,128)(2,1)} %convolution_convert_fusion.1) | data formatting | bytes 3145728 | tf_op jit(solution)/shard_map/convert_element_type | solution.py:329
  49.1 5.4 %fusion.158 = (f32[8,512]{1,0:T(8,128)S(1)}, f32[8,512,512]{1,2,0:T(8,128)}) fusion(pred[512,512]{0,1:T(8,128)(4,1)S(1)} %broadcast_compare_fusion, bf16[512,3,8,64]{0,3,2,1:T(8,128)(2,1)S(1)} %bitcast.210), kind=kOutput, calls=%fused_computation.190 | convolution fusion | flops 276824576 | bytes 9715712 | tf_op jit(solution)/shard_map/while/body/eval_jaxpr/sub | solution.py:39
  54.6 4.7 %fusion.24 = bf16[8,512,512]{1,2,0:T(8,128)(2,1)S(1)} fusion(f32[8,512,512]{1,2,0:T(8,128)} %get-tuple-element.48, f32[8,512]{1,0:T(8,128)S(1)} %get-tuple-element.47), kind=kLoop, calls=%fused_computation.28 | loop fusion | flops 4194304 | bytes 12599296 | tf_op jit(solution)/shard_map/while/body/eval_jaxpr/convert_element_type | solution.py:48
  60.1 1.4 fusion.87
  62.6 1.8 %multiply_convert_fusion = bf16[8,512,512]{1,2,0:T(8,128)(2,1)S(1)} fusion(f32[8,512]{1,0:T(8,128)S(1)} %fusion.102, f32[8,512,512]{1,2,0:T(8,128)S(1)} %copy-done, f32[8,512]{1,0:T(8,128)S(1)} %get-tuple-element.47, bf16[8,512,64]{1,2,0:T(8,128)(2,1)S(1)} %bitcast.218, bf16[512,3,8,64]{0,3,2,1:T(8,128)(2,1)S(1)} %bitcast.212), kind=kOutput, calls=%fused_computation.2 | convolution fusion | flops 278921216 | bytes 13664256 | tf_op jit(solution)/shard_map/while/body/eval_jaxpr/...uo,...ao->...ua/dot_general | solution.py:74
  64.4 1.4 fusion.86
  66.8 1.2 copy-done.2
  68.1 1.0 copy-done.19
  69.1 1.0 multiply_reduce_fusion
  71.0 1.1 reduce.6
  72.3 1.2 reshape.377
  73.5 4.1 %all-to-all-start.1 = ((bf16[16,2,8192]{2,1,0:T(2,128)(2,1)}), bf16[16,2,8192]{2,1,0:T(2,128)(2,1)S(1)}, u32[]{:S(2)}, u32[]{:S(2)}) async-start(bf16[16,2,8192]{2,1,0:T(2,128)(2,1)} %reshape.377), calls=%async_computation.1 | async-start | bytes 1048576 | tf_op jit(solution)/shard_map/all_to_all | solution.py:359
  78.3 2.6 %convolution_convert_fusion = bf16[512,1536]{1,0:T(8,128)(2,1)S(1)} fusion(bf16[512,1536]{0,1:T(8,128)(2,1)} %bitcast.224, f32[512,1,1,1,1,1,512]{6,0,5,4,3,2,1:T(8,128)S(1)} %bitcast.203, f32[512]{0:T(512)S(1)} %copy-done.22, f32[512]{0:T(512)S(1)} %rsqrt.21), kind=kOutput, calls=%fused_computation.29 | convolution fusion | flops 806879232 | bytes 4198400 | tf_op jit(solution)/shard_map/tbd,tbe->de/dot_general | solution.py:282
  80.9 1.6 pad_maximum_fusion
  82.5 9.5 %all-to-all-done.1 = bf16[16,2,8192]{2,1,0:T(2,128)(2,1)S(1)} async-done(((bf16[16,2,8192]{2,1,0:T(2,128)(2,1)}), bf16[16,2,8192]{2,1,0:T(2,128)(2,1)S(1)}, u32[]{:S(2)}, u32[]{:S(2)}) %all-to-all-start.1) | async-done | bytes 524320 | tf_op jit(solution)/shard_map/all_to_all | solution.py:359
  92.7 1.6 convolution_bitcast_fusion
  94.7 1.7 %convolution_convert_fusion.6 = bf16[32,16,512]{2,1,0:T(8,128)(2,1)S(1)} fusion(bf16[32,16,512]{2,1,0:T(8,128)(2,1)S(1)} %bitcast.221, bf16[512,2048]{1,0:T(8,128)(2,1)} %param.11), kind=kOutput, calls=%fused_computation.80 | convolution fusion | flops 268697600 | bytes 1572864 | tf_op jit(solution)/shard_map/tbe,de->tbd/dot_general | solution.py:276
  96.5 1.4 fusion.75
  97.9 1.9 %fusion.98 = f32[32,16,8]{1,2,0:T(8,128)S(1)} fusion(bf16[32,16,512]{2,1,0:T(8,128)(2,1)S(1)} %copy-done.12, bf16[32,16,512]{2,1,0:T(8,128)(2,1)S(1)} %convolution_convert_fusion.6, s32[512]{0:T(512)S(1)} %add_select_fusion), kind=kOutput, calls=%fused_computation.107 | convolution fusion | flops 25956352 | bytes 1067008 | tf_op jit(solution)/shard_map/tbd,hd->tbh/dot_general | solution.py:235
  100.0 1.3 multiply_convert_fusion.1
  101.3 2.2 %fusion.78 = bf16[32,16,512]{2,1,0:T(8,128)(2,1)} fusion(bf16[32,16,8,16]{1,3,2,0:T(8,128)(2,1)S(1)} %multiply_convert_fusion.1, pred[8,512]{1,0:T(8,128)(4,1)S(1)} %iota_compare_fusion, bf16[32,16,512]{2,1,0:T(8,128)(2,1)S(1)} %copy-done.15), kind=kOutput, calls=%fused_computation.87 | convolution fusion | flops 69468160 | bytes 1183744 | tf_op jit(solution)/shard_map/tbhc,tbhd->tcd/dot_general | solution.py:248
  103.5 0.8 fusion.117
  104.3 4.3 %all-to-all-start.2 = ((bf16[8,32,512]{2,1,0:T(8,128)(2,1)}), bf16[8,32,512]{2,1,0:T(8,128)(2,1)S(1)}, u32[]{:S(2)}, u32[]{:S(2)}) async-start(bf16[8,32,512]{2,1,0:T(8,128)(2,1)} %fusion.117), calls=%async_computation.2 | async-start | bytes 524288 | tf_op jit(solution)/shard_map/all_to_all | solution.py:294
  108.6 2.0 %fusion.72 = bf16[32,16,512]{2,1,0:T(8,128)(2,1)S(1)} fusion(bf16[32,16,8,16]{1,3,2,0:T(8,128)(2,1)} %copy-done.25, pred[8,512]{1,0:T(8,128)(4,1)S(1)} %iota_compare_fusion, bf16[32,16,512]{2,1,0:T(8,128)(2,1)S(1)} %copy-done.14), kind=kOutput, calls=%fused_computation.85 | convolution fusion | flops 69468160 | bytes 1183744 | tf_op jit(solution)/shard_map/tbhc,thcd->tbd/dot_general | solution.py:245
  110.6 1.2 pad_maximum_fusion.2
  111.9 9.1 %all-to-all-done.2 = bf16[8,32,512]{2,1,0:T(8,128)(2,1)S(1)} async-done(((bf16[8,32,512]{2,1,0:T(8,128)(2,1)}), bf16[8,32,512]{2,1,0:T(8,128)(2,1)S(1)}, u32[]{:S(2)}, u32[]{:S(2)}) %all-to-all-start.2) | async-done | bytes 262176 | tf_op jit(solution)/shard_map/all_to_all | solution.py:294
  121.1 2.5 %fusion.133 = f32[512,1536,1]{1,0,2:T(8,128)S(1)} fusion(bf16[32,16,1536]{2,1,0:T(8,128)(2,1)} %pad_maximum_fusion.2, bf16[32,16,512]{2,1,0:T(8,128)(2,1)S(1)} %copy-done.7, f32[512]{0:T(512)S(1)} %copy-done.23, f32[32,16]{1,0:T(8,128)S(1)} %add_rsqrt_fusion), kind=kOutput, calls=%fused_computation.152 | convolution fusion | flops 806354944 | bytes 5246976 | tf_op jit(solution)/shard_map/tbd,tbe->de/dot_general | solution.py:282
  123.8 2.3 %collective-permute-done.1 = bf16[8,32,1536]{2,1,0:T(8,128)(2,1)S(1)} collective-permute-done((bf16[8,32,1536]{2,1,0:T(8,128)(2,1)S(1)}, bf16[8,32,1536]{2,1,0:T(8,128)(2,1)S(1)}, u32[]{:S(2)}, u32[]{:S(2)}) %collective-permute-start.1) | collective-permute-done | bytes 786464 | tf_op jit(solution)/shard_map/ppermute | solution.py:292
  126.1 1.3 fusion.40
  127.4 4.5 %all-to-all-start.3 = ((bf16[8,32,1536]{2,1,0:T(8,128)(2,1)}), bf16[8,32,1536]{2,1,0:T(8,128)(2,1)S(1)}, u32[]{:S(2)}, u32[]{:S(2)}) async-start(bf16[8,32,1536]{2,1,0:T(8,128)(2,1)} %fusion.40), calls=%async_computation.3 | async-start | bytes 1572864 | tf_op jit(solution)/shard_map/all_to_all | solution.py:294
  131.9 2.4 %fusion.85 = bf16[512,1,512]{2,0,1:T(8,128)(2,1)} fusion(f32[512,512]{1,0:T(8,128)S(1)} %bitcast.204, bf16[512,512]{0,1:T(8,128)(2,1)S(1)} %bitcast.207, bf16[512,2048]{1,0:T(8,128)(2,1)} %param.12), kind=kOutput, calls=%fused_computation.92 | convolution fusion | flops 268959744 | bytes 2621440 | tf_op jit(solution)/shard_map/tbd,de->tbe/dot_general | solution.py:272
  134.3 2.5 %fusion.96 = (f32[32,16]{1,0:T(8,128)S(1)}, f32[32,16,512]{2,1,0:T(8,128)S(1)}) fusion(bf16[32,16,512]{2,1,0:T(8,128)(2,1)S(1)} %copy-done.7, f32[512]{0:T(512)S(1)} %copy-done.23, bf16[32,16,1536]{2,1,0:T(8,128)(2,1)S(1)} %copy-done.10, bf16[512,2048]{1,0:T(8,128)(2,1)} %param.11), kind=kOutput, calls=%fused_computation.103 | convolution fusion | flops 806354432 | bytes 4722688 | tf_op jit(solution)/shard_map/tbe,de->tbd/dot_general | solution.py:276
  136.8 1.2 fusion.94
  138.0 10.4 %reduce-scatter.2.cloned.1.call-done = bf16[32,2048]{1,0:T(8,128)(2,1)} async-done(((bf16[512,2048]{1,0:T(8,128)(2,1)}), bf16[32,2048]{1,0:T(8,128)(2,1)}) %reduce-scatter.2.cloned.1.call-update) | async-done | bytes 131088 | tf_op jit(solution)/shard_map/reduce_scatter | solution.py:299
  148.4 1.6 convert_element_type.264
  150.1 6.5 %all-to-all-done.3 = bf16[8,32,1536]{2,1,0:T(8,128)(2,1)S(1)} async-done(((bf16[8,32,1536]{2,1,0:T(8,128)(2,1)}), bf16[8,32,1536]{2,1,0:T(8,128)(2,1)S(1)}, u32[]{:S(2)}, u32[]{:S(2)}) %all-to-all-start.3) | async-done | bytes 786464 | tf_op jit(solution)/shard_map/all_to_all | solution.py:294
  (98 shorter events, 9.2 us)
Async XLA Ops:
  11.1 1.0 copy-start.21
  11.1 1.1 copy-start.20
  11.1 1.2 copy-start.24
  12.1 3.1 %copy-start.13 = (bf16[32,16,512]{2,1,0:T(8,128)(2,1)}, bf16[32,16,512]{2,1,0:T(8,128)(2,1)S(1)}, u32[]{:S(2)}) copy-start(bf16[32,16,512]{2,1,0:T(8,128)(2,1)S(1)} %get-tuple-element.44) | copy-start | bytes 1572868
  12.1 3.1 %copy-start.16 = (bf16[32,16,512]{2,1,0:T(8,128)(2,1)}, bf16[32,16,512]{2,1,0:T(8,128)(2,1)S(1)}, u32[]{:S(2)}) copy-start(bf16[32,16,512]{2,1,0:T(8,128)(2,1)S(1)} %get-tuple-element.43) | copy-start | bytes 1572868
  15.3 2.4 %copy-start.27 = (f32[32,16,8]{1,2,0:T(8,128)}, f32[32,16,8]{1,2,0:T(8,128)S(1)}, u32[]{:S(2)}) copy-start(f32[32,16,8]{1,2,0:T(8,128)S(1)} %get-tuple-element.45) | copy-start | bytes 49156
  15.3 2.4 %copy-start.6 = (bf16[32,16,512]{2,1,0:T(8,128)(2,1)S(1)}, bf16[32,16,512]{2,1,0:T(8,128)(2,1)}, u32[]{:S(2)}) copy-start(bf16[32,16,512]{2,1,0:T(8,128)(2,1)} %param.9) | copy-start | bytes 1572868
  17.6 1.7 %copy-start.11 = (bf16[32,16,512]{2,1,0:T(8,128)(2,1)}, bf16[32,16,512]{2,1,0:T(8,128)(2,1)S(1)}, u32[]{:S(2)}) copy-start(bf16[32,16,512]{2,1,0:T(8,128)(2,1)S(1)} %fusion.69) | copy-start | bytes 1572868
  17.7 10.2 %copy-start.3 = (bf16[512,1,512]{2,0,1:T(8,128)(2,1)S(1)}, bf16[512,1,512]{2,0,1:T(8,128)(2,1)}, u32[]{:S(2)}) copy-start(bf16[512,1,512]{2,0,1:T(8,128)(2,1)} %param.10) | copy-start | bytes 1572868
  20.5 21.9 %all-to-all-start = ((bf16[32,16,512]{2,0,1:T(8,128)(2,1)}), bf16[32,16,512]{2,0,1:T(8,128)(2,1)S(1)}, u32[]{:S(2)}, u32[]{:S(2)}) async-start(bf16[32,16,512]{2,0,1:T(8,128)(2,1)} %copy.100), calls=%async_computation | async-start | bytes 1048576 | tf_op jit(solution)/shard_map/all_to_all | solution.py:327
  31.4 12.3 %copy-start.22 = (f32[512]{0:T(512)S(1)}, f32[512]{0:T(512)}, u32[]{:S(2)}) copy-start(f32[512]{0:T(512)} %param.14) | copy-start | bytes 6148
  42.8 1.0 copy-start.1
  54.6 5.5 %copy-start.5 = (bf16[512,512]{0,1:T(8,128)(2,1)S(1)}, bf16[512,512]{0,1:T(8,128)(2,1)}, u32[]{:S(2)}) copy-start(bf16[512,512]{0,1:T(8,128)(2,1)} %convolution_convert_fusion.9) | copy-start | bytes 1572868
  59.2 3.4 %copy-start = (f32[8,512,512]{1,2,0:T(8,128)S(1)}, f32[8,512,512]{1,2,0:T(8,128)}, u32[]{:S(2)}) copy-start(f32[8,512,512]{1,2,0:T(8,128)} %get-tuple-element.48) | copy-start | bytes 25165828
  66.6 1.5 copy-start.2
  66.6 2.5 %copy-start.19 = (bf16[512,2048]{1,0:T(8,128)(2,1)S(1)}, bf16[512,2048]{1,0:T(8,128)(2,1)}, u32[]{:S(2)}) copy-start(bf16[512,2048]{1,0:T(8,128)(2,1)} %param.12) | copy-start | bytes 6291460
  66.8 3.3 %copy-start.9 = (bf16[3,8,512,64]{2,3,1,0:T(8,128)(2,1)}, bf16[3,8,512,64]{2,3,1,0:T(8,128)(2,1)S(1)}, u32[]{:S(2)}) copy-start(bf16[3,8,512,64]{2,3,1,0:T(8,128)(2,1)S(1)} %pad_maximum_fusion.1) | copy-start | bytes 4718596
  69.1 1.0 copy-start.8
  71.0 6.9 %copy-start.4 = (bf16[512,1,512]{2,0,1:T(8,128)(2,1)S(1)}, bf16[512,1,512]{2,0,1:T(8,128)(2,1)}, u32[]{:S(2)}) copy-start(bf16[512,1,512]{2,0,1:T(8,128)(2,1)} %param.10) | copy-start | bytes 1572868
  73.5 18.6 %all-to-all-start.1 = ((bf16[16,2,8192]{2,1,0:T(2,128)(2,1)}), bf16[16,2,8192]{2,1,0:T(2,128)(2,1)S(1)}, u32[]{:S(2)}, u32[]{:S(2)}) async-start(bf16[16,2,8192]{2,1,0:T(2,128)(2,1)} %reshape.377), calls=%async_computation.1 | async-start | bytes 1048576 | tf_op jit(solution)/shard_map/all_to_all | solution.py:359
  77.6 70.8 %reduce-scatter.2.cloned.1.call-start = ((), (), s32[]{:S(2)}) async-start(), calls=%async_computation.5 | async-start | bytes 2228224 | tf_op jit(solution)/shard_map/reduce_scatter | solution.py:299
  94.4 2.1 %copy-start.26 = (f32[32,16,8,16]{1,3,2,0:T(8,128)S(1)}, f32[32,16,8,16]{1,3,2,0:T(8,128)}, u32[]{:S(2)}) copy-start(f32[32,16,8,16]{1,3,2,0:T(8,128)} %get-tuple-element.46) | copy-start | bytes 786436
  94.4 2.1 %copy-start.28 = (f32[32,16,8]{1,2,0:T(8,128)S(1)}, f32[32,16,8]{1,2,0:T(8,128)}, u32[]{:S(2)}) copy-start(f32[32,16,8]{1,2,0:T(8,128)} %copy-done.27) | copy-start | bytes 49156
  96.4 1.4 copy-start.12
  96.4 3.6 %copy-start.17 = (bf16[32,16,512]{2,1,0:T(8,128)(2,1)S(1)}, bf16[32,16,512]{2,1,0:T(8,128)(2,1)}, u32[]{:S(2)}) copy-start(bf16[32,16,512]{2,1,0:T(8,128)(2,1)} %copy-done.16) | copy-start | bytes 1572868
  99.9 1.4 copy-start.15
  99.9 3.6 %collective-permute-start = (bf16[8,32,512]{2,1,0:T(8,128)(2,1)S(1)}, bf16[8,32,512]{2,1,0:T(8,128)(2,1)S(1)}, u32[]{:S(2)}, u32[]{:S(2)}) collective-permute-start(bf16[8,32,512]{2,1,0:T(8,128)(2,1)S(1)} %fusion.136), channel_id=1, source_target_pairs={{0,1},{1,0},{2,3},{3,2},{4,5},{5,4},{6,7},{7,6},{8,9},{9,8},{10,11... | collective-permute-start | bytes 786440 | tf_op jit(solution)/shard_map/ppermute | solution.py:292
  101.3 2.2 %copy-start.25 = (bf16[32,16,8,16]{1,3,2,0:T(8,128)(2,1)}, bf16[32,16,8,16]{1,3,2,0:T(8,128)(2,1)S(1)}, u32[]{:S(2)}) copy-start(bf16[32,16,8,16]{1,3,2,0:T(8,128)(2,1)S(1)} %multiply_convert_fusion.1) | copy-start | bytes 393220
  103.5 5.1 %copy-start.14 = (bf16[32,16,512]{2,1,0:T(8,128)(2,1)S(1)}, bf16[32,16,512]{2,1,0:T(8,128)(2,1)}, u32[]{:S(2)}) copy-start(bf16[32,16,512]{2,1,0:T(8,128)(2,1)} %copy-done.13) | copy-start | bytes 1572868
  104.3 16.7 %all-to-all-start.2 = ((bf16[8,32,512]{2,1,0:T(8,128)(2,1)}), bf16[8,32,512]{2,1,0:T(8,128)(2,1)S(1)}, u32[]{:S(2)}, u32[]{:S(2)}) async-start(bf16[8,32,512]{2,1,0:T(8,128)(2,1)} %fusion.117), calls=%async_computation.2 | async-start | bytes 524288 | tf_op jit(solution)/shard_map/all_to_all | solution.py:294
  108.6 2.0 %copy-start.18 = (bf16[32,16,512]{2,1,0:T(8,128)(2,1)S(1)}, bf16[32,16,512]{2,1,0:T(8,128)(2,1)}, u32[]{:S(2)}) copy-start(bf16[32,16,512]{2,1,0:T(8,128)(2,1)} %fusion.78) | copy-start | bytes 1572868
  110.6 10.5 %copy-start.7 = (bf16[32,16,512]{2,1,0:T(8,128)(2,1)S(1)}, bf16[32,16,512]{2,1,0:T(8,128)(2,1)}, u32[]{:S(2)}) copy-start(bf16[32,16,512]{2,1,0:T(8,128)(2,1)} %param.9) | copy-start | bytes 1572868
  110.6 10.5 %copy-start.23 = (f32[512]{0:T(512)S(1)}, f32[512]{0:T(512)}, u32[]{:S(2)}) copy-start(f32[512]{0:T(512)} %param.13) | copy-start | bytes 6148
  123.8 2.4 %collective-permute-start.1 = (bf16[8,32,1536]{2,1,0:T(8,128)(2,1)S(1)}, bf16[8,32,1536]{2,1,0:T(8,128)(2,1)S(1)}, u32[]{:S(2)}, u32[]{:S(2)}) collective-permute-start(bf16[8,32,1536]{2,1,0:T(8,128)(2,1)S(1)} %fusion.112), channel_id=1, source_target_pairs={{0,1},{1,0},{2,3},{3,2},{4,5},{5,4},{6,7},{7,6},{8,9},{9,8},{10,11... | collective-permute-start | bytes 2359304 | tf_op jit(solution)/shard_map/ppermute | solution.py:292
  127.4 29.2 %all-to-all-start.3 = ((bf16[8,32,1536]{2,1,0:T(8,128)(2,1)}), bf16[8,32,1536]{2,1,0:T(8,128)(2,1)S(1)}, u32[]{:S(2)}, u32[]{:S(2)}) async-start(bf16[8,32,1536]{2,1,0:T(8,128)(2,1)} %fusion.40), calls=%async_computation.3 | async-start | bytes 1572864 | tf_op jit(solution)/shard_map/all_to_all | solution.py:294
  131.9 2.4 %copy-start.10 = (bf16[32,16,1536]{2,1,0:T(8,128)(2,1)S(1)}, bf16[32,16,1536]{2,1,0:T(8,128)(2,1)}, u32[]{:S(2)}) copy-start(bf16[32,16,1536]{2,1,0:T(8,128)(2,1)} %pad_maximum_fusion.2) | copy-start | bytes 4718596
Sparse Core Ops, SparseCore 0:
  82.7 65.7 reduce-scatter.1

commit v13 on v8

--- a/solution.py
+++ b/solution.py
@@ -357,7 +357,6 @@
         )
     )
     spatial_term = weight_term(spatial_context, grad_middle_time)
-    spatial_term, grad_middle_time = lax.optimization_barrier((spatial_term, grad_middle_time))
     grad_spatial_context = project_back(
         grad_middle_time, spatial_weights[:, 3 * model_width :]
     ).astype(jnp.bfloat16)

time: 165 us -> 170 us (1.030)
  local copies, waits for them, and re-layouts: 13.4 us -> 20.4 us
  waiting for transfers between devices: 48.7 us -> 44.5 us
  matrix products: 49.4 us -> 52 us
    reduce_scatter x1, waiting for transfers between devices: 10.5 us -> 21.1 us  [scatter_rows(): lax.psum_scatter(partial.astype(jnp.bfloat16), ('outer', 'core'), scatter...]
    all_to_all x2, waiting for transfers between devices: 15.6 us -> 6.12 us  [reduce_rows(): pieces = lax.all_to_all(pieces, 'outer', 0, 0, tiled=True)]
    all_to_all x1, waiting for transfers between devices: 9.51 us -> 3.27 us  [per_device(): lax.all_to_all(grad_middle, ('outer', 'core'), split_axis=0, concat_axis=...]
    dot_general x0 -> x1, local copies, waits for them, and re-layouts: none -> 5.04 us  [weight_term(): jnp.einsum('tbd,tbe->de', left, right, preferred_element_type=jnp.float32)]
    unnamed x66 -> x64, local copies, waits for them, and re-layouts: 8.13 us -> 10.2 us
  transfers between devices with their start and end apart: 7 -> 7, of which waited for: 6 -> 5; matrix products, arithmetic and copies ran while one was open for 21% -> 26% of each run, Pallas kernels for 0% -> 0%
where the time goes in v13:
time: 170 us; the launch traced here: 169 us
  matrix products  52 us (31%)
  waiting for transfers between devices  44.5 us (26%)
  local copies, waits for them, and re-layouts  20.4 us (12%)
  starting transfers between devices  19.9 us (12%)
  other arithmetic  17.3 us (10%)
  between operations  14.6 us (9%)
    reduce_scatter x1, waiting for transfers between devices, scatter_rows(): lax.psum_scatter(partial.astype(jnp.bfloat16), ('outer', 'core'), scatter...  21.1 us
    all_to_all x1, waiting for transfers between devices, per_device(): lax.all_to_all(middle, ('outer', 'core'), split_axis=1, concat_axis=0, ti...  11.7 us
    dot_general x4, matrix products, project(): jnp.einsum('tbd,de->tbe', rows, coefficient_array, preferred_element_type...  10.4 us
    unnamed x64, local copies, waits for them, and re-layouts  10.2 us
    all_to_all x2, starting transfers between devices, reduce_rows(): pieces = lax.all_to_all(pieces, 'outer', 0, 0, tiled=True)  7.86 us
    dot_general x4, matrix products, weight_term(): jnp.einsum('tbd,tbe->de', left, right, preferred_element_type=jnp.float32)  7.75 us
    dot_general x4, matrix products, project_back(): jnp.einsum('tbe,de->tbd', derivative_collection, coefficient_array, prefe...  7.61 us
    all_to_all x1, starting transfers between devices, per_device(): lax.all_to_all(middle, ('outer', 'core'), split_axis=1, concat_axis=0, ti...  7.39 us
  transfers between devices with their start and end apart: 7, of which 5 were waited for; matrix products, arithmetic and copies ran while one was open for 26% of the time, Pallas kernels for 0%

profile of v13, /device:TPU:0, one launch (start us, length us, event | category | flops | bytes accessed | tf_op | source)
XLA Modules:
  0.0 168.6 jit_solution(5943084156144235284)
XLA Ops:
  7.2 1.2 fusion.100
  8.5 2.6 %convolution_convert_fusion.2 = bf16[32,16,1536]{2,1,0:T(8,128)(2,1)S(1)} fusion(bf16[512,2048]{1,0:T(8,128)(2,1)} %param.11, bf16[32,16,512]{2,1,0:T(8,128)(2,1)} %param.9, f32[512]{0:T(512)} %param.13, f32[32,16]{1,0:T(8,128)S(1)} %add_rsqrt_fusion), kind=kOutput, calls=%fused_computation.31 | convolution fusion | flops 807141376 | bytes 3674112 | tf_op jit(solution)/shard_map/tbd,de->tbe/dot_general | solution.py:263
  11.1 1.2 fusion.158
  12.8 2.6 %fusion.159 = (f32[32,16,8]{1,2,0:T(8,128)S(1)}, f32[32,16,8,16]{1,3,2,0:T(8,128)}) fusion(pred[32,16,16]{1,2,0:T(8,128)(4,1)S(1)} %and_or_fusion, pred[8,512]{1,0:T(8,128)(4,1)S(1)} %iota_compare_fusion, bf16[32,16,512]{2,1,0:T(8,128)(2,1)S(1)} %get-tuple-element.40, bf16[32,16,1536]{2,1,0:T(8,128)(2,1)S(1)} %convolution_convert_fusion.2), kind=kOutput, calls=%fused_computation.188 | convolution fusion | flops 69468176 | bytes 1396736 | tf_op jit(solution)/shard_map/sub | solution.py:197
  15.4 2.4 %fusion.74 = bf16[32,16,512]{2,1,0:T(8,128)(2,1)S(1)} fusion(pred[8,512]{1,0:T(8,128)(4,1)S(1)} %iota_compare_fusion, bf16[32,16,512]{2,1,0:T(8,128)(2,1)} %get-tuple-element.33, f32[32,16,8,16]{1,3,2,0:T(8,128)} %get-tuple-element.42, f32[32,16,8]{1,2,0:T(8,128)S(1)} %get-tuple-element.41), kind=kOutput, calls=%fused_computation.86 | convolution fusion | flops 69599232 | bytes 1331200 | tf_op jit(solution)/shard_map/tbhc,thcd->tbd/dot_general | solution.py:206
  17.9 1.7 fusion.86
  19.6 1.1 copy.102
  20.7 7.4 %all-to-all-start = ((bf16[32,16,512]{2,0,1:T(8,128)(2,1)}), bf16[32,16,512]{2,0,1:T(8,128)(2,1)S(1)}, u32[]{:S(2)}, u32[]{:S(2)}) async-start(bf16[32,16,512]{2,0,1:T(8,128)(2,1)} %copy.102), calls=%async_computation | async-start | bytes 1048576 | tf_op jit(solution)/shard_map/all_to_all | solution.py:318
  28.6 2.3 %convolution_convert_fusion.9 = bf16[512,512]{0,1:T(8,128)(2,1)} fusion(bf16[512,1,512]{2,0,1:T(8,128)(2,1)S(1)} %copy-done.6, bf16[512,2048]{1,0:T(8,128)(2,1)} %param.12), kind=kOutput, calls=%fused_computation.85 | convolution fusion | flops 268697600 | bytes 1572864 | tf_op jit(solution)/shard_map/tbe,de->tbd/dot_general | solution.py:267
  30.9 11.7 %all-to-all-done = bf16[32,16,512]{2,0,1:T(8,128)(2,1)S(1)} async-done(((bf16[32,16,512]{2,0,1:T(8,128)(2,1)}), bf16[32,16,512]{2,0,1:T(8,128)(2,1)S(1)}, u32[]{:S(2)}, u32[]{:S(2)}) %all-to-all-start) | async-done | bytes 524320 | tf_op jit(solution)/shard_map/all_to_all | solution.py:318
  44.0 3.7 %convolution_convert_fusion.1 = bf16[512,1536]{1,0:T(8,128)(2,1)} fusion(bf16[512,2048]{1,0:T(8,128)(2,1)} %param.12, f32[512,512]{0,1:T(8,128)S(1)} %copy.105, f32[512]{0:T(512)S(1)} %copy-done.22, f32[512]{0:T(512)S(1)} %rsqrt.21), kind=kOutput, calls=%fused_computation.30 | convolution fusion | flops 806879232 | bytes 4198400 | tf_op jit(solution)/shard_map/tbd,de->tbe/dot_general | solution.py:263
  47.7 1.7 %copy.106 = bf16[512,1536]{0,1:T(8,128)(2,1)S(1)} copy(bf16[512,1536]{1,0:T(8,128)(2,1)} %convolution_convert_fusion.1) | data formatting | bytes 3145728 | tf_op jit(solution)/shard_map/convert_element_type | solution.py:320
  49.4 5.4 %fusion.160 = (f32[8,512]{1,0:T(8,128)S(1)}, f32[8,512,512]{1,2,0:T(8,128)}) fusion(pred[512,512]{0,1:T(8,128)(4,1)S(1)} %broadcast_compare_fusion, bf16[512,3,8,64]{0,3,2,1:T(8,128)(2,1)S(1)} %bitcast.215), kind=kOutput, calls=%fused_computation.189 | convolution fusion | flops 276824576 | bytes 9715712 | tf_op jit(solution)/shard_map/while/body/eval_jaxpr/sub | solution.py:39
  54.8 4.7 %fusion.24 = bf16[8,512,512]{1,2,0:T(8,128)(2,1)S(1)} fusion(f32[8,512,512]{1,2,0:T(8,128)} %get-tuple-element.44, f32[8,512]{1,0:T(8,128)S(1)} %get-tuple-element.43), kind=kLoop, calls=%fused_computation.28 | loop fusion | flops 4194304 | bytes 12599296 | tf_op jit(solution)/shard_map/while/body/eval_jaxpr/convert_element_type | solution.py:48
  59.5 1.6 multiply_reduce_fusion.1
  61.1 1.4 fusion.92
  63.1 1.8 %multiply_convert_fusion = bf16[8,512,512]{1,2,0:T(8,128)(2,1)S(1)} fusion(f32[8,512]{1,0:T(8,128)S(1)} %get-tuple-element.45, f32[8,512,512]{1,2,0:T(8,128)S(1)} %copy-done, f32[8,512]{1,0:T(8,128)S(1)} %get-tuple-element.43, bf16[8,512,64]{1,2,0:T(8,128)(2,1)S(1)} %bitcast.227, bf16[512,3,8,64]{0,3,2,1:T(8,128)(2,1)S(1)} %bitcast.217), kind=kOutput, calls=%fused_computation.2 | convolution fusion | flops 278921216 | bytes 13664256 | tf_op jit(solution)/shard_map/while/body/eval_jaxpr/...uo,...ao->...ua/dot_general | solution.py:73
  64.9 1.4 fusion.91
  67.3 1.2 copy-done.5
  68.5 1.0 copy-done.19
  71.5 1.0 reduce.6
  72.7 1.2 reshape.378
  73.9 4.2 %all-to-all-start.1 = ((bf16[16,2,8192]{2,1,0:T(2,128)(2,1)}), bf16[16,2,8192]{2,1,0:T(2,128)(2,1)}, u32[]{:S(2)}, u32[]{:S(2)}) async-start(bf16[16,2,8192]{2,1,0:T(2,128)(2,1)} %reshape.378), calls=%async_computation.1 | async-start | bytes 1048576 | tf_op jit(solution)/shard_map/all_to_all | solution.py:350
  78.4 5.0 %dot_general.100 = bf16[8,2,32,16,32]{2,1,0,3,4:T(2,128)(2,1)S(1)} reshape(bf16[512,16,32]{0,1,2:T(8,128)(2,1)} %bitcast.225) | data formatting | bytes 1048576 | tf_op jit(solution)/shard_map/tbd,tbe->de/dot_general | solution.py:273
  83.4 1.6 convolution_convert_fusion.5
  85.1 2.6 %convolution_convert_fusion = bf16[512,1536]{1,0:T(8,128)(2,1)S(1)} fusion(bf16[512,1536]{0,1:T(8,128)(2,1)} %bitcast.229, f32[512,1,1,1,1,1,512]{6,0,5,4,3,2,1:T(8,128)S(1)} %bitcast.211, f32[512]{0:T(512)S(1)} %copy-done.22, f32[512]{0:T(512)S(1)} %rsqrt.21), kind=kOutput, calls=%fused_computation.29 | convolution fusion | flops 806879232 | bytes 4198400 | tf_op jit(solution)/shard_map/tbd,tbe->de/dot_general | solution.py:273
  87.7 1.6 pad_maximum_fusion
  89.3 3.3 %all-to-all-done.1 = bf16[16,2,8192]{2,1,0:T(2,128)(2,1)} async-done(((bf16[16,2,8192]{2,1,0:T(2,128)(2,1)}), bf16[16,2,8192]{2,1,0:T(2,128)(2,1)}, u32[]{:S(2)}, u32[]{:S(2)}) %all-to-all-start.1) | async-done | bytes 524320 | tf_op jit(solution)/shard_map/all_to_all | solution.py:350
  92.6 3.5 %reshape.379 = bf16[512,1,512]{2,1,0:T(2,128)(2,1)} reshape(bf16[16,2,8192]{2,1,0:T(2,128)(2,1)} %all-to-all-done.1) | data formatting | bytes 1048576
  96.1 1.5 copy.151
  97.6 1.7 %convolution_convert_fusion.6 = bf16[32,16,512]{2,1,0:T(8,128)(2,1)S(1)} fusion(bf16[16,32,1,512]{3,1,0,2:T(8,128)(2,1)S(1)} %bitcast.220, bf16[512,2048]{1,0:T(8,128)(2,1)} %param.11), kind=kOutput, calls=%fused_computation.82 | convolution fusion | flops 268697600 | bytes 1572864 | tf_op jit(solution)/shard_map/tbe,de->tbd/dot_general | solution.py:267
  99.4 2.2 %fusion.80 = bf16[32,16,512]{2,1,0:T(8,128)(2,1)} fusion(pred[8,512]{1,0:T(8,128)(4,1)S(1)} %iota_compare_fusion, bf16[32,16,512]{2,1,0:T(8,128)(2,1)S(1)} %convolution_convert_fusion.6, f32[32,16,8,16]{1,3,2,0:T(8,128)S(1)} %copy-done.26, f32[32,16,8]{1,2,0:T(8,128)S(1)} %copy-done.28), kind=kOutput, calls=%fused_computation.88 | convolution fusion | flops 69599232 | bytes 1331200 | tf_op jit(solution)/shard_map/tbhc,tbhd->tcd/dot_general | solution.py:217
  101.6 1.9 %fusion.103 = f32[32,16,8]{1,2,0:T(8,128)S(1)} fusion(bf16[32,16,512]{2,1,0:T(8,128)(2,1)S(1)} %copy-done.8, bf16[32,16,512]{2,1,0:T(8,128)(2,1)S(1)} %convolution_convert_fusion.6, s32[512]{0:T(512)S(1)} %add_select_fusion), kind=kOutput, calls=%fused_computation.109 | convolution fusion | flops 25956352 | bytes 1067008 | tf_op jit(solution)/shard_map/tbd,hd->tbh/dot_general | solution.py:226
  104.7 1.2 multiply_convert_fusion.1
  106.0 1.4 fusion.83
  108.2 4.2 %all-to-all-start.2 = ((bf16[8,32,512]{2,1,0:T(8,128)(2,1)}), bf16[8,32,512]{2,1,0:T(8,128)(2,1)S(1)}, u32[]{:S(2)}, u32[]{:S(2)}) async-start(bf16[8,32,512]{2,1,0:T(8,128)(2,1)} %fusion.118), calls=%async_computation.2 | async-start | bytes 524288 | tf_op jit(solution)/shard_map/all_to_all | solution.py:285
  112.5 2.0 %fusion.77 = bf16[32,16,512]{2,1,0:T(8,128)(2,1)S(1)} fusion(bf16[32,16,8,16]{1,3,2,0:T(8,128)(2,1)} %copy-done.25, pred[8,512]{1,0:T(8,128)(4,1)S(1)} %iota_compare_fusion, bf16[32,16,512]{2,1,0:T(8,128)(2,1)S(1)} %copy-done.15), kind=kOutput, calls=%fused_computation.87 | convolution fusion | flops 69468160 | bytes 1183744 | tf_op jit(solution)/shard_map/tbhc,thcd->tbd/dot_general | solution.py:236
  114.5 1.3 pad_maximum_fusion.2
  115.7 6.1 %all-to-all-done.2 = bf16[8,32,512]{2,1,0:T(8,128)(2,1)S(1)} async-done(((bf16[8,32,512]{2,1,0:T(8,128)(2,1)}), bf16[8,32,512]{2,1,0:T(8,128)(2,1)S(1)}, u32[]{:S(2)}, u32[]{:S(2)}) %all-to-all-start.2) | async-done | bytes 262176 | tf_op jit(solution)/shard_map/all_to_all | solution.py:285
  121.9 2.5 %fusion.137 = f32[512,1536,1]{1,0,2:T(8,128)S(1)} fusion(bf16[32,16,1536]{2,1,0:T(8,128)(2,1)} %pad_maximum_fusion.2, bf16[32,16,512]{2,1,0:T(8,128)(2,1)S(1)} %copy-done.10, f32[512]{0:T(512)S(1)} %copy-done.23, f32[32,16]{1,0:T(8,128)S(1)} %add_rsqrt_fusion), kind=kOutput, calls=%fused_computation.153 | convolution fusion | flops 806354944 | bytes 5246976 | tf_op jit(solution)/shard_map/tbd,tbe->de/dot_general | solution.py:273
  124.6 2.3 %collective-permute-done.1 = bf16[8,32,1536]{2,1,0:T(8,128)(2,1)S(1)} collective-permute-done((bf16[8,32,1536]{2,1,0:T(8,128)(2,1)S(1)}, bf16[8,32,1536]{2,1,0:T(8,128)(2,1)S(1)}, u32[]{:S(2)}, u32[]{:S(2)}) %collective-permute-start.1) | collective-permute-done | bytes 786464 | tf_op jit(solution)/shard_map/ppermute | solution.py:283
  126.9 1.3 fusion.42
  128.2 3.7 %all-to-all-start.3 = ((bf16[8,32,1536]{2,1,0:T(8,128)(2,1)}), bf16[8,32,1536]{2,1,0:T(8,128)(2,1)S(1)}, u32[]{:S(2)}, u32[]{:S(2)}) async-start(bf16[8,32,1536]{2,1,0:T(8,128)(2,1)} %fusion.42), calls=%async_computation.3 | async-start | bytes 1572864 | tf_op jit(solution)/shard_map/all_to_all | solution.py:285
  131.9 2.4 %fusion.90 = bf16[512,1,512]{2,0,1:T(8,128)(2,1)} fusion(f32[512,512]{1,0:T(8,128)S(1)} %bitcast.212, bf16[512,512]{0,1:T(8,128)(2,1)S(1)} %bitcast.224, bf16[512,2048]{1,0:T(8,128)(2,1)} %param.12), kind=kOutput, calls=%fused_computation.94 | convolution fusion | flops 268959744 | bytes 2621440 | tf_op jit(solution)/shard_map/tbd,de->tbe/dot_general | solution.py:263
  134.3 2.6 %fusion.101 = (f32[32,16]{1,0:T(8,128)S(1)}, f32[32,16,512]{2,1,0:T(8,128)S(1)}) fusion(bf16[32,16,512]{2,1,0:T(8,128)(2,1)S(1)} %copy-done.10, f32[512]{0:T(512)S(1)} %copy-done.23, bf16[32,16,1536]{2,1,0:T(8,128)(2,1)S(1)} %copy-done.13, bf16[512,2048]{1,0:T(8,128)(2,1)} %param.11), kind=kOutput, calls=%fused_computation.105 | convolution fusion | flops 806354432 | bytes 4722688 | tf_op jit(solution)/shard_map/tbe,de->tbd/dot_general | solution.py:267
  136.9 1.3 fusion.99
  138.2 21.1 %reduce-scatter.2.cloned.1.call-done = bf16[32,2048]{1,0:T(8,128)(2,1)} async-done(((bf16[512,2048]{1,0:T(8,128)(2,1)}), bf16[32,2048]{1,0:T(8,128)(2,1)}) %reduce-scatter.2.cloned.1.call-update) | async-done | bytes 131088 | tf_op jit(solution)/shard_map/reduce_scatter | solution.py:290
  159.3 1.6 convert_element_type.267
  (97 shorter events, 9.5 us)
Async XLA Ops:
  11.1 1.2 copy-start.21
  11.1 1.3 copy-start.20
  11.1 1.4 copy-start.24
  12.3 3.1 %copy-start.14 = (bf16[32,16,512]{2,1,0:T(8,128)(2,1)}, bf16[32,16,512]{2,1,0:T(8,128)(2,1)S(1)}, u32[]{:S(2)}) copy-start(bf16[32,16,512]{2,1,0:T(8,128)(2,1)S(1)} %get-tuple-element.40) | copy-start | bytes 1572868
  15.4 2.5 %copy-start.27 = (f32[32,16,8]{1,2,0:T(8,128)}, f32[32,16,8]{1,2,0:T(8,128)S(1)}, u32[]{:S(2)}) copy-start(f32[32,16,8]{1,2,0:T(8,128)S(1)} %get-tuple-element.41) | copy-start | bytes 49156
  15.4 2.5 %copy-start.9 = (bf16[32,16,512]{2,1,0:T(8,128)(2,1)S(1)}, bf16[32,16,512]{2,1,0:T(8,128)(2,1)}, u32[]{:S(2)}) copy-start(bf16[32,16,512]{2,1,0:T(8,128)(2,1)} %param.9) | copy-start | bytes 1572868
  17.9 2.8 %copy-start.7 = (bf16[32,16,512]{2,1,0:T(8,128)(2,1)}, bf16[32,16,512]{2,1,0:T(8,128)(2,1)S(1)}, u32[]{:S(2)}) copy-start(bf16[32,16,512]{2,1,0:T(8,128)(2,1)S(1)} %fusion.74) | copy-start | bytes 1572868
  17.9 10.2 %copy-start.6 = (bf16[512,1,512]{2,0,1:T(8,128)(2,1)S(1)}, bf16[512,1,512]{2,0,1:T(8,128)(2,1)}, u32[]{:S(2)}) copy-start(bf16[512,1,512]{2,0,1:T(8,128)(2,1)} %param.10) | copy-start | bytes 1572868
  20.7 21.9 %all-to-all-start = ((bf16[32,16,512]{2,0,1:T(8,128)(2,1)}), bf16[32,16,512]{2,0,1:T(8,128)(2,1)S(1)}, u32[]{:S(2)}, u32[]{:S(2)}) async-start(bf16[32,16,512]{2,0,1:T(8,128)(2,1)} %copy.102), calls=%async_computation | async-start | bytes 1048576 | tf_op jit(solution)/shard_map/all_to_all | solution.py:318
  30.9 13.1 %copy-start.22 = (f32[512]{0:T(512)S(1)}, f32[512]{0:T(512)}, u32[]{:S(2)}) copy-start(f32[512]{0:T(512)} %param.14) | copy-start | bytes 6148
  43.1 1.0 copy-start.4
  54.8 4.7 %copy-start.11 = (bf16[512,512]{0,1:T(8,128)(2,1)S(1)}, bf16[512,512]{0,1:T(8,128)(2,1)}, u32[]{:S(2)}) copy-start(bf16[512,512]{0,1:T(8,128)(2,1)} %convolution_convert_fusion.9) | copy-start | bytes 1572868
  59.5 3.6 %copy-start = (f32[8,512,512]{1,2,0:T(8,128)S(1)}, f32[8,512,512]{1,2,0:T(8,128)}, u32[]{:S(2)}) copy-start(f32[8,512,512]{1,2,0:T(8,128)} %get-tuple-element.44) | copy-start | bytes 25165828
  67.1 1.5 copy-start.5
  67.1 2.5 %copy-start.19 = (bf16[512,2048]{1,0:T(8,128)(2,1)S(1)}, bf16[512,2048]{1,0:T(8,128)(2,1)}, u32[]{:S(2)}) copy-start(bf16[512,2048]{1,0:T(8,128)(2,1)} %param.12) | copy-start | bytes 6291460
  67.3 3.3 %copy-start.12 = (bf16[3,8,512,64]{2,3,1,0:T(8,128)(2,1)}, bf16[3,8,512,64]{2,3,1,0:T(8,128)(2,1)S(1)}, u32[]{:S(2)}) copy-start(bf16[3,8,512,64]{2,3,1,0:T(8,128)(2,1)S(1)} %pad_maximum_fusion.1) | copy-start | bytes 4718596
  73.9 18.7 %all-to-all-start.1 = ((bf16[16,2,8192]{2,1,0:T(2,128)(2,1)}), bf16[16,2,8192]{2,1,0:T(2,128)(2,1)}, u32[]{:S(2)}, u32[]{:S(2)}) async-start(bf16[16,2,8192]{2,1,0:T(2,128)(2,1)} %reshape.378), calls=%async_computation.1 | async-start | bytes 1048576 | tf_op jit(solution)/shard_map/all_to_all | solution.py:350
  78.1 81.2 %reduce-scatter.2.cloned.1.call-start = ((), (), s32[]{:S(2)}) async-start(), calls=%async_computation.5 | async-start | bytes 2228224 | tf_op jit(solution)/shard_map/reduce_scatter | solution.py:290
  96.1 3.3 %copy-start.26 = (f32[32,16,8,16]{1,3,2,0:T(8,128)S(1)}, f32[32,16,8,16]{1,3,2,0:T(8,128)}, u32[]{:S(2)}) copy-start(f32[32,16,8,16]{1,3,2,0:T(8,128)} %get-tuple-element.42) | copy-start | bytes 786436
  96.1 3.3 %copy-start.28 = (f32[32,16,8]{1,2,0:T(8,128)S(1)}, f32[32,16,8]{1,2,0:T(8,128)}, u32[]{:S(2)}) copy-start(f32[32,16,8]{1,2,0:T(8,128)} %copy-done.27) | copy-start | bytes 49156
  97.6 5.9 %copy-start.1 = (bf16[512,1,512]{2,0,1:T(8,128)(2,1)}, bf16[512,1,512]{2,0,1:T(8,128)(2,1)S(1)}, u32[]{:S(2)}) copy-start(bf16[512,1,512]{2,0,1:T(8,128)(2,1)S(1)} %copy.151) | copy-start | bytes 1572868
  99.4 2.2 %copy-start.8 = (bf16[32,16,512]{2,1,0:T(8,128)(2,1)S(1)}, bf16[32,16,512]{2,1,0:T(8,128)(2,1)}, u32[]{:S(2)}) copy-start(bf16[32,16,512]{2,1,0:T(8,128)(2,1)} %copy-done.7) | copy-start | bytes 1572868
  103.5 1.2 copy-start.17
  104.6 1.4 copy-start.16
  104.6 2.8 %collective-permute-start = (bf16[8,32,512]{2,1,0:T(8,128)(2,1)S(1)}, bf16[8,32,512]{2,1,0:T(8,128)(2,1)S(1)}, u32[]{:S(2)}, u32[]{:S(2)}) collective-permute-start(bf16[8,32,512]{2,1,0:T(8,128)(2,1)S(1)} %fusion.140), channel_id=1, source_target_pairs={{0,1},{1,0},{2,3},{3,2},{4,5},{5,4},{6,7},{7,6},{8,9},{9,8},{10,11... | collective-permute-start | bytes 786440 | tf_op jit(solution)/shard_map/ppermute | solution.py:283
  106.0 1.4 copy-start.25
  107.4 5.1 %copy-start.15 = (bf16[32,16,512]{2,1,0:T(8,128)(2,1)S(1)}, bf16[32,16,512]{2,1,0:T(8,128)(2,1)}, u32[]{:S(2)}) copy-start(bf16[32,16,512]{2,1,0:T(8,128)(2,1)} %copy-done.14) | copy-start | bytes 1572868
  108.2 13.6 %all-to-all-start.2 = ((bf16[8,32,512]{2,1,0:T(8,128)(2,1)}), bf16[8,32,512]{2,1,0:T(8,128)(2,1)S(1)}, u32[]{:S(2)}, u32[]{:S(2)}) async-start(bf16[8,32,512]{2,1,0:T(8,128)(2,1)} %fusion.118), calls=%async_computation.2 | async-start | bytes 524288 | tf_op jit(solution)/shard_map/all_to_all | solution.py:285
  112.4 2.0 %copy-start.18 = (bf16[32,16,512]{2,1,0:T(8,128)(2,1)S(1)}, bf16[32,16,512]{2,1,0:T(8,128)(2,1)}, u32[]{:S(2)}) copy-start(bf16[32,16,512]{2,1,0:T(8,128)(2,1)} %fusion.80) | copy-start | bytes 1572868
  114.4 7.4 %copy-start.10 = (bf16[32,16,512]{2,1,0:T(8,128)(2,1)S(1)}, bf16[32,16,512]{2,1,0:T(8,128)(2,1)}, u32[]{:S(2)}) copy-start(bf16[32,16,512]{2,1,0:T(8,128)(2,1)} %param.9) | copy-start | bytes 1572868
  114.5 7.4 %copy-start.23 = (f32[512]{0:T(512)S(1)}, f32[512]{0:T(512)}, u32[]{:S(2)}) copy-start(f32[512]{0:T(512)} %param.13) | copy-start | bytes 6148
  124.6 7.3 %copy-start.3 = (bf16[8,512,64]{1,2,0:T(8,128)(2,1)S(1)}, bf16[8,512,64]{1,2,0:T(8,128)(2,1)}, u32[]{:S(2)}) copy-start(bf16[8,512,64]{1,2,0:T(8,128)(2,1)} %get-tuple-element.46) | copy-start | bytes 1572868
  124.6 2.4 %collective-permute-start.1 = (bf16[8,32,1536]{2,1,0:T(8,128)(2,1)S(1)}, bf16[8,32,1536]{2,1,0:T(8,128)(2,1)S(1)}, u32[]{:S(2)}, u32[]{:S(2)}) collective-permute-start(bf16[8,32,1536]{2,1,0:T(8,128)(2,1)S(1)} %fusion.113), channel_id=1, source_target_pairs={{0,1},{1,0},{2,3},{3,2},{4,5},{5,4},{6,7},{7,6},{8,9},{9,8},{10,11... | collective-permute-start | bytes 2359304 | tf_op jit(solution)/shard_map/ppermute | solution.py:283
  128.2 32.8 %all-to-all-start.3 = ((bf16[8,32,1536]{2,1,0:T(8,128)(2,1)}), bf16[8,32,1536]{2,1,0:T(8,128)(2,1)S(1)}, u32[]{:S(2)}, u32[]{:S(2)}) async-start(bf16[8,32,1536]{2,1,0:T(8,128)(2,1)} %fusion.42), calls=%async_computation.3 | async-start | bytes 1572864 | tf_op jit(solution)/shard_map/all_to_all | solution.py:285
  131.9 2.4 %copy-start.13 = (bf16[32,16,1536]{2,1,0:T(8,128)(2,1)S(1)}, bf16[32,16,1536]{2,1,0:T(8,128)(2,1)}, u32[]{:S(2)}) copy-start(bf16[32,16,1536]{2,1,0:T(8,128)(2,1)} %pad_maximum_fusion.2) | copy-start | bytes 4718596
  134.3 2.6 %copy-start.2 = (bf16[512,1,512]{2,0,1:T(8,128)(2,1)S(1)}, bf16[512,1,512]{2,0,1:T(8,128)(2,1)}, u32[]{:S(2)}) copy-start(bf16[512,1,512]{2,0,1:T(8,128)(2,1)} %copy-done.1) | copy-start | bytes 1572868
Sparse Core Ops, SparseCore 0:
  89.4 69.8 reduce-scatter.1
